TPU v7x, 256 devices: a whole 4x4x8 slice. The times are simulated.
256 devices in a mesh: gx: 16 (over x, y), gy: 8 (over z), mode: 2 (over core).
Axes of the slice: x: 4, y: 4, z: 8, core: 2. Of those that a mesh axis runs over, the one named last changes fastest.
Arguments:
- state: float32 [4, 64, 512, 2048], P(None, None, 'gx', ('gy', 'mode')), may hold values from -6 to 6
- depth_class: int32 [512, 2048], P('gx', ('gy', 'mode')), may hold values from 0 to 4
- vertical_inverse: float32 [4, 64, 64], replicated, as said below
- height: float32 [512, 2048], P('gx', ('gy', 'mode')), may hold values from -4 to 4
- transport: float32 [2, 512, 2048], P(None, 'gx', ('gy', 'mode')), may hold values from -4 to 4
Outputs:
- state_next: float32 [4, 64, 512, 2048], P(None, None, 'gx', ('gy', 'mode'))
- height_next: float32 [512, 2048], P('gx', ('gy', 'mode'))
- transport_next: float32 [2, 512, 2048], P(None, 'gx', ('gy', 'mode'))
Inputs may be any that keep to these rules, and one draw needn't show every extreme that they name: `depth_class`: 0 marks land; a column of class c has its top c * 16 levels active. `vertical_inverse`: entry c is used for columns of class c + 1 and acts on all 64 levels.
All inputs are finite; a program needn't handle non-finite values.
Results may differ from a plain program's by a relative error of at most 0.0003.
Values sent between devices are 32-bit elements; how exact they have to be, the bound alone decides.
No kernel may reach another device: no remote copies, remote signals or barrier semaphores. Data moves between devices by JAX's collectives and lax.ppermute only.
A program may use at most 128 MiB of HBM per device.

v0:
```python
import jax
import jax.numpy as jnp
from jax import lax
from jax.sharding import PartitionSpec as P

SUB = 32


THERMAL = 0.8
HALINE = 0.6
PRESSURE_SCALE = 4.0
VISCOSITY = 0.1
STEP_TIME = 0.05
WAVE_STEP = 0.5
GRAVITY = 1.0
BOTTOM_DRAG = 0.05
CORIOLIS_BASE = 0.3
CORIOLIS_SLOPE = 0.4


def with_halo(cells, sides, width):
    for axis, dim in sides:
        count = lax.axis_size(axis)
        ends = count - 1
        head = lax.slice_in_dim(cells, 0, width, axis=dim)
        tail = lax.slice_in_dim(cells, cells.shape[dim] - width, cells.shape[dim], axis=dim)
        cells = jnp.concatenate(
            [
                lax.ppermute(tail, axis, [(i, (i + 1) % count) for i in range(ends)]),
                cells,
                lax.ppermute(head, axis, [((i + 1) % count, i) for i in range(ends)]),
            ],
            axis=dim,
        )
    return cells


def x_fourth(values):
    return (
        8.0 * (values[..., 3:-1, 2:-2] - values[..., 1:-3, 2:-2])
        - (values[..., 4:, 2:-2] - values[..., :-4, 2:-2])
    ) / 12.0


def y_fourth(values):
    return (
        8.0 * (values[..., 2:-2, 3:-1] - values[..., 2:-2, 1:-3])
        - (values[..., 2:-2, 4:] - values[..., 2:-2, :-4])
    ) / 12.0


def laplace(values):
    center = values[..., 2:-2, 2:-2]
    return (
        values[..., 3:-1, 2:-2]
        + values[..., 1:-3, 2:-2]
        + values[..., 2:-2, 3:-1]
        + values[..., 2:-2, 1:-3]
        - 4.0 * center
    )


def coriolis_row(anchor, number, total):
    position = (anchor + lax.broadcasted_iota(jnp.int32, (number,), 0)).astype(jnp.float32)
    return (CORIOLIS_BASE + CORIOLIS_SLOPE * (position + 0.5) / total)[None, :]


def baroclinic(state, padded, pressure, active, depth_class, inverse, coriolis):
    levels = state.shape[1]
    center = padded[:, :, 2:-2, 2:-2]
    east_vel = center[2]
    north_vel = center[3]
    tendency = -(east_vel * x_fourth(padded) + north_vel * y_fourth(padded)) + VISCOSITY * laplace(
        padded
    )
    zeros_field = jnp.zeros_like(east_vel)
    extra = jnp.stack(
        [
            zeros_field,
            zeros_field,
            -x_fourth(pressure) + coriolis * north_vel,
            -y_fourth(pressure) - coriolis * east_vel,
        ]
    )
    tendency = tendency + extra
    provisional = active * (center + STEP_TIME * tendency)
    solved = jnp.zeros_like(provisional)
    for class_index in range(inverse.shape[0]):
        chosen = (depth_class == class_index + 1).astype(jnp.float32)
        solved = solved + chosen * jnp.einsum(
            "kl,flxy->fkxy", inverse[class_index], provisional, precision=lax.Precision.HIGHEST
        )
    updated = active * solved + (1.0 - active) * state
    forcing = jnp.sum(active * tendency[2:4], axis=1) / levels
    return (updated, forcing)


def shrink(values):
    return values[..., 1:-1, 1:-1]


def x_slope(values):
    return (values[2:, 1:-1] - values[:-2, 1:-1]) * 0.5


def y_slope(values):
    return (values[1:-1, 2:] - values[1:-1, :-2]) * 0.5


def substep(moving, fixed_fields, coriolis):
    surface, east_flow, north_flow = (moving[0], moving[1], moving[2])
    column_depth = fixed_fields[2]
    sea_mask = (column_depth > 0.0).astype(jnp.float32)
    surface_mid = shrink(sea_mask) * (
        shrink(surface) - WAVE_STEP * (x_slope(east_flow) + y_slope(north_flow))
    )
    sea_inner = shrink(shrink(sea_mask))
    depth_inner = shrink(shrink(column_depth))
    force_east = shrink(shrink(fixed_fields[0]))
    force_north = shrink(shrink(fixed_fields[1]))
    coriolis_inner = coriolis[:, 2:-2]
    east_old = shrink(shrink(east_flow))
    north_old = shrink(shrink(north_flow))
    east_new = sea_inner * (
        east_old
        + WAVE_STEP
        * (
            -GRAVITY * depth_inner * x_slope(surface_mid)
            + coriolis_inner * north_old
            + force_east
            - BOTTOM_DRAG * east_old
        )
    )
    north_new = sea_inner * (
        north_old
        + WAVE_STEP
        * (
            -GRAVITY * depth_inner * y_slope(surface_mid)
            - coriolis_inner * east_new
            + force_north
            - BOTTOM_DRAG * north_old
        )
    )
    return jnp.stack([shrink(surface_mid), east_new, north_new])


def finish(updated, waves, active, depth_class, level_block, levels):
    counted = jnp.maximum(depth_class * level_block, 1).astype(jnp.float32)
    safe_depth = jnp.maximum(depth_class, 1).astype(jnp.float32) * level_block / levels
    column_means = jnp.sum(active * updated[2:4], axis=1) / counted
    carried = waves[1:3] / safe_depth
    velocity = updated[2:4] + active * (carried - column_means)[:, None]
    return jnp.concatenate([updated[0:2], velocity], axis=0)


def advance(moving, fixed_wide, coriolis_wide, refresh, exchanges):

    def group(index, current):
        extended = refresh(current)
        extended = substep(extended, fixed_wide, coriolis_wide)
        return extended

    return lax.fori_loop(0, exchanges, group, moving)


def body(state, depth_class, vertical_inverse, height, transport):
    levels = state.shape[1]
    level_block = levels // vertical_inverse.shape[0]
    y_cells = depth_class.shape[1]
    level_ids = lax.broadcasted_iota(jnp.int32, (levels, 1, 1), 0)
    active = (level_ids < depth_class[None] * level_block).astype(jnp.float32)
    masked = state * active[None]
    padded = with_halo(masked, (("gx", 2), (("gy", "mode"), 3)), 2)
    column_blocks = lax.axis_size(("gy", "mode"))
    anchor = lax.axis_index(("gy", "mode")) * y_cells
    coriolis = coriolis_row(anchor, y_cells, y_cells * column_blocks)[0]
    density = -THERMAL * padded[0] + HALINE * padded[1]
    row_ids = lax.broadcasted_iota(jnp.int32, (levels, levels), 0)
    col_ids = lax.broadcasted_iota(jnp.int32, (levels, levels), 1)
    lower_ones = (row_ids >= col_ids).astype(jnp.float32)
    pressure = (
        PRESSURE_SCALE
        / levels
        * jnp.einsum("kl,lxy->kxy", lower_ones, density, precision=lax.Precision.HIGHEST)
    )
    updated, forcing = baroclinic(
        state, padded, pressure, active, depth_class, vertical_inverse, coriolis
    )
    column_depth = depth_class.astype(jnp.float32) * level_block / levels
    sea_mask = (depth_class > 0).astype(jnp.float32)
    moving = jnp.stack([height, transport[0], transport[1]]) * sea_mask
    fixed_fields = jnp.stack([forcing[0], forcing[1], column_depth])
    per_exchange = 1
    depth_rim = 2 * per_exchange
    exchanges = SUB // per_exchange
    fixed_wide = with_halo(fixed_fields, (("gx", 1), (("gy", "mode"), 2)), depth_rim)
    coriolis_wide = coriolis_row(
        anchor - depth_rim, y_cells + 2 * depth_rim, y_cells * column_blocks
    )

    def refresh_block(current):
        return with_halo(current, (("gx", 1), (("gy", "mode"), 2)), depth_rim)

    waves = advance(moving, fixed_wide, coriolis_wide, refresh_block, exchanges)
    state_next = finish(updated, waves, active, depth_class, level_block, levels)
    return (state_next, waves[0], waves[1:3])


def solution(mesh):
    placed = (
        P(None, None, "gx", ("gy", "mode")),
        P("gx", ("gy", "mode")),
        P(),
        P("gx", ("gy", "mode")),
        P(None, "gx", ("gy", "mode")),
    )
    return jax.shard_map(
        body,
        mesh=mesh,
        in_specs=placed,
        out_specs=(
            P(None, None, "gx", ("gy", "mode")),
            P("gx", ("gy", "mode")),
            P(None, "gx", ("gy", "mode")),
        ),
        check_vma=False,
    )
```

profile of v0, /device:TPU:103, one launch (start us, length us, event | category | flops | bytes accessed | tf_op | source)
XLA Modules:
  0.0 738.4 jit_solution(9772777111910220226)
XLA Ops:
  52.9 6.8 fusion.47
  63.7 12.7 %add_multiply_fusion = (f32[4,64,32,128]{3,1,2,0:T(8,128)S(1)}, f32[4,64,32,128]{3,1,2,0:T(8,128)}) fusion(f32[64,32,128]{2,0,1:T(8,128)S(1)} %fusion.64, f32[4,64,32,128]{3,2,1,0:T(8,128)} %param.7, f32[1,64,32,128]{3,1,2,0:T(8,128)} %get-tuple-element.98, f32[1,64,32,128]{3,1,2,0:T(8,128)} %get-tuple-element.99, f32[4]{0:T(128)} %pad.27.clone, ...), kind=kLoop, calls=%fused_computation.68 | loop fusion | flops 44040192 | bytes 22691856 | tf_op jit(solution)/shard_map/mul | solution.py:86
  91.4 10.2 %fusion.31 = f32[4,64,32,128]{3,1,2,0:T(8,128)S(1)} fusion(f32[4,32,128,64]{2,3,1,0:T(8,128)S(1)} %fusion.68, f32[4,32,128,64]{2,3,1,0:T(8,128)} %fusion.70, f32[4,32,128,64]{2,3,1,0:T(8,128)} %fusion.72, f32[4,64,32,128]{3,2,1,0:T(8,128)S(1)} %copy-done.2, f32[4,64,32,128]{3,1,2,0:T(8,128)S(1)} %get-tuple-element.77, f32[64,32,128]{2,0,1:T(8,128)S(1)} %copy-done.4, ...), kind=kOutput, calls=%fused_computation.67 | convolution fusion | flops 815792128 | bytes 27361280 | tf_op jit(solution)/shard_map/kl,flxy->fkxy/dot_general | solution.py:90
  126.8 602.5 %while.12 = (s32[]{:T(128)}, f32[3,32,128]{2,1,0:T(8,128)S(1)}, f32[3,36,132]{2,1,0:T(8,128)S(1)}, f32[1,132]{1,0:T(1,128)S(1)}, s32[]{:T(128)}) while((s32[]{:T(128)}, f32[3,32,128]{2,1,0:T(8,128)S(1)}, f32[3,36,132]{2,1,0:T(8,128)S(1)}, f32[1,132]{1,0:T(1,128)S(1)}, s32[]{:T(128)}) %tuple.68), condition=%wide.region_2.0_spmd, body=%wide.region_1.0_spmd.sunk | while | flops 239482 | bytes 991181 | solution.py:163
  158.5 6.7 collective-permute-start.3
  196.0 6.6 collective-permute-start.3
  214.8 6.6 collective-permute-start.3
  233.5 6.6 collective-permute-start.3
  252.3 6.6 collective-permute-start.3
  271.0 6.6 collective-permute-start.3
  289.8 6.6 collective-permute-start.3
  308.5 6.6 collective-permute-start.3
  327.3 6.6 collective-permute-start.3
  346.0 6.6 collective-permute-start.3
  364.8 6.6 collective-permute-start.3
  383.5 6.6 collective-permute-start.3
  402.2 6.6 collective-permute-start.3
  421.0 6.6 collective-permute-start.3
  439.7 6.6 collective-permute-start.3
  458.5 6.6 collective-permute-start.3
  477.2 6.6 collective-permute-start.3
  496.0 6.6 collective-permute-start.3
  514.7 6.6 collective-permute-start.3
  552.2 6.6 collective-permute-start.3
  (664 shorter events, 571.2 us)
Async XLA Ops:
  8.2 9.9 %collective-permute-start.4 = (f32[4,64,2,128]{3,1,2,0:T(8,128)S(1)}, f32[4,64,2,128]{3,1,2,0:T(8,128)S(1)}, u32[]{:S(2)}, u32[]{:S(2)}) collective-permute-start(f32[4,64,2,128]{3,1,2,0:T(8,128)S(1)} %get-tuple-element.101), channel_id=1, source_target_pairs={{16,0},{32,16},{48,32},{64,48},{80,64},{96,80},{112,96},{128,112},... | collective-permute-start | bytes 786440 | tf_op jit(solution)/shard_map/ppermute | solution.py:31
  13.1 10.9 %collective-permute-start.5 = (f32[4,64,2,128]{3,1,2,0:T(8,128)S(1)}, f32[4,64,2,128]{3,1,2,0:T(8,128)S(1)}, u32[]{:S(2)}, u32[]{:S(2)}) collective-permute-start(f32[4,64,2,128]{3,1,2,0:T(8,128)S(1)} %get-tuple-element.100), channel_id=1, source_target_pairs={{0,16},{16,32},{32,48},{48,64},{64,80},{80,96},{96,112},{112,128},... | collective-permute-start | bytes 786440 | tf_op jit(solution)/shard_map/ppermute | solution.py:29
  35.1 11.9 %collective-permute-start.6 = (f32[4,64,36,2]{1,0,3,2:T(4,128)S(1)}, f32[4,64,36,2]{1,0,3,2:T(4,128)S(1)}, u32[]{:S(2)}, u32[]{:S(2)}) collective-permute-start(f32[4,64,36,2]{1,0,3,2:T(4,128)S(1)} %copy.12), channel_id=1, source_target_pairs={{1,0},{2,1},{3,2},{4,3},{5,4},{6,5},{7,6},{8,7},{9,8},{10,9},{11,1... | collective-permute-start | bytes 221192 | tf_op jit(solution)/shard_map/ppermute | solution.py:31
  156.6 8.7 %collective-permute-start.2 = (f32[3,36,2]{2,1,0:T(8,128)S(1)}, f32[3,36,2]{2,1,0:T(8,128)S(1)}, u32[]{:S(2)}, u32[]{:S(2)}) collective-permute-start(f32[3,36,2]{2,1,0:T(8,128)S(1)} %get-tuple-element.156), channel_id=1, source_target_pairs={{1,0},{2,1},{3,2},{4,3},{5,4},{6,5},{7,6},{8,7},{9,8},{10,9},{11,1... | collective-permute-start | bytes 2600 | tf_op jit(solution)/shard_map/while/body/eval_jaxpr/ppermute | solution.py:31
  175.4 8.6 %collective-permute-start.2 = (f32[3,36,2]{2,1,0:T(8,128)S(1)}, f32[3,36,2]{2,1,0:T(8,128)S(1)}, u32[]{:S(2)}, u32[]{:S(2)}) collective-permute-start(f32[3,36,2]{2,1,0:T(8,128)S(1)} %get-tuple-element.156), channel_id=1, source_target_pairs={{1,0},{2,1},{3,2},{4,3},{5,4},{6,5},{7,6},{8,7},{9,8},{10,9},{11,1... | collective-permute-start | bytes 2600 | tf_op jit(solution)/shard_map/while/body/eval_jaxpr/ppermute | solution.py:31
  194.1 8.6 %collective-permute-start.2 = (f32[3,36,2]{2,1,0:T(8,128)S(1)}, f32[3,36,2]{2,1,0:T(8,128)S(1)}, u32[]{:S(2)}, u32[]{:S(2)}) collective-permute-start(f32[3,36,2]{2,1,0:T(8,128)S(1)} %get-tuple-element.156), channel_id=1, source_target_pairs={{1,0},{2,1},{3,2},{4,3},{5,4},{6,5},{7,6},{8,7},{9,8},{10,9},{11,1... | collective-permute-start | bytes 2600 | tf_op jit(solution)/shard_map/while/body/eval_jaxpr/ppermute | solution.py:31
  212.9 8.6 %collective-permute-start.2 = (f32[3,36,2]{2,1,0:T(8,128)S(1)}, f32[3,36,2]{2,1,0:T(8,128)S(1)}, u32[]{:S(2)}, u32[]{:S(2)}) collective-permute-start(f32[3,36,2]{2,1,0:T(8,128)S(1)} %get-tuple-element.156), channel_id=1, source_target_pairs={{1,0},{2,1},{3,2},{4,3},{5,4},{6,5},{7,6},{8,7},{9,8},{10,9},{11,1... | collective-permute-start | bytes 2600 | tf_op jit(solution)/shard_map/while/body/eval_jaxpr/ppermute | solution.py:31
  231.6 8.6 %collective-permute-start.2 = (f32[3,36,2]{2,1,0:T(8,128)S(1)}, f32[3,36,2]{2,1,0:T(8,128)S(1)}, u32[]{:S(2)}, u32[]{:S(2)}) collective-permute-start(f32[3,36,2]{2,1,0:T(8,128)S(1)} %get-tuple-element.156), channel_id=1, source_target_pairs={{1,0},{2,1},{3,2},{4,3},{5,4},{6,5},{7,6},{8,7},{9,8},{10,9},{11,1... | collective-permute-start | bytes 2600 | tf_op jit(solution)/shard_map/while/body/eval_jaxpr/ppermute | solution.py:31
  250.4 8.6 %collective-permute-start.2 = (f32[3,36,2]{2,1,0:T(8,128)S(1)}, f32[3,36,2]{2,1,0:T(8,128)S(1)}, u32[]{:S(2)}, u32[]{:S(2)}) collective-permute-start(f32[3,36,2]{2,1,0:T(8,128)S(1)} %get-tuple-element.156), channel_id=1, source_target_pairs={{1,0},{2,1},{3,2},{4,3},{5,4},{6,5},{7,6},{8,7},{9,8},{10,9},{11,1... | collective-permute-start | bytes 2600 | tf_op jit(solution)/shard_map/while/body/eval_jaxpr/ppermute | solution.py:31
  269.1 8.6 %collective-permute-start.2 = (f32[3,36,2]{2,1,0:T(8,128)S(1)}, f32[3,36,2]{2,1,0:T(8,128)S(1)}, u32[]{:S(2)}, u32[]{:S(2)}) collective-permute-start(f32[3,36,2]{2,1,0:T(8,128)S(1)} %get-tuple-element.156), channel_id=1, source_target_pairs={{1,0},{2,1},{3,2},{4,3},{5,4},{6,5},{7,6},{8,7},{9,8},{10,9},{11,1... | collective-permute-start | bytes 2600 | tf_op jit(solution)/shard_map/while/body/eval_jaxpr/ppermute | solution.py:31
  287.8 8.6 %collective-permute-start.2 = (f32[3,36,2]{2,1,0:T(8,128)S(1)}, f32[3,36,2]{2,1,0:T(8,128)S(1)}, u32[]{:S(2)}, u32[]{:S(2)}) collective-permute-start(f32[3,36,2]{2,1,0:T(8,128)S(1)} %get-tuple-element.156), channel_id=1, source_target_pairs={{1,0},{2,1},{3,2},{4,3},{5,4},{6,5},{7,6},{8,7},{9,8},{10,9},{11,1... | collective-permute-start | bytes 2600 | tf_op jit(solution)/shard_map/while/body/eval_jaxpr/ppermute | solution.py:31
  306.6 8.6 %collective-permute-start.2 = (f32[3,36,2]{2,1,0:T(8,128)S(1)}, f32[3,36,2]{2,1,0:T(8,128)S(1)}, u32[]{:S(2)}, u32[]{:S(2)}) collective-permute-start(f32[3,36,2]{2,1,0:T(8,128)S(1)} %get-tuple-element.156), channel_id=1, source_target_pairs={{1,0},{2,1},{3,2},{4,3},{5,4},{6,5},{7,6},{8,7},{9,8},{10,9},{11,1... | collective-permute-start | bytes 2600 | tf_op jit(solution)/shard_map/while/body/eval_jaxpr/ppermute | solution.py:31
  325.3 8.6 %collective-permute-start.2 = (f32[3,36,2]{2,1,0:T(8,128)S(1)}, f32[3,36,2]{2,1,0:T(8,128)S(1)}, u32[]{:S(2)}, u32[]{:S(2)}) collective-permute-start(f32[3,36,2]{2,1,0:T(8,128)S(1)} %get-tuple-element.156), channel_id=1, source_target_pairs={{1,0},{2,1},{3,2},{4,3},{5,4},{6,5},{7,6},{8,7},{9,8},{10,9},{11,1... | collective-permute-start | bytes 2600 | tf_op jit(solution)/shard_map/while/body/eval_jaxpr/ppermute | solution.py:31
  344.1 8.6 %collective-permute-start.2 = (f32[3,36,2]{2,1,0:T(8,128)S(1)}, f32[3,36,2]{2,1,0:T(8,128)S(1)}, u32[]{:S(2)}, u32[]{:S(2)}) collective-permute-start(f32[3,36,2]{2,1,0:T(8,128)S(1)} %get-tuple-element.156), channel_id=1, source_target_pairs={{1,0},{2,1},{3,2},{4,3},{5,4},{6,5},{7,6},{8,7},{9,8},{10,9},{11,1... | collective-permute-start | bytes 2600 | tf_op jit(solution)/shard_map/while/body/eval_jaxpr/ppermute | solution.py:31
  362.8 8.6 %collective-permute-start.2 = (f32[3,36,2]{2,1,0:T(8,128)S(1)}, f32[3,36,2]{2,1,0:T(8,128)S(1)}, u32[]{:S(2)}, u32[]{:S(2)}) collective-permute-start(f32[3,36,2]{2,1,0:T(8,128)S(1)} %get-tuple-element.156), channel_id=1, source_target_pairs={{1,0},{2,1},{3,2},{4,3},{5,4},{6,5},{7,6},{8,7},{9,8},{10,9},{11,1... | collective-permute-start | bytes 2600 | tf_op jit(solution)/shard_map/while/body/eval_jaxpr/ppermute | solution.py:31
  381.6 8.6 %collective-permute-start.2 = (f32[3,36,2]{2,1,0:T(8,128)S(1)}, f32[3,36,2]{2,1,0:T(8,128)S(1)}, u32[]{:S(2)}, u32[]{:S(2)}) collective-permute-start(f32[3,36,2]{2,1,0:T(8,128)S(1)} %get-tuple-element.156), channel_id=1, source_target_pairs={{1,0},{2,1},{3,2},{4,3},{5,4},{6,5},{7,6},{8,7},{9,8},{10,9},{11,1... | collective-permute-start | bytes 2600 | tf_op jit(solution)/shard_map/while/body/eval_jaxpr/ppermute | solution.py:31
  400.3 8.6 %collective-permute-start.2 = (f32[3,36,2]{2,1,0:T(8,128)S(1)}, f32[3,36,2]{2,1,0:T(8,128)S(1)}, u32[]{:S(2)}, u32[]{:S(2)}) collective-permute-start(f32[3,36,2]{2,1,0:T(8,128)S(1)} %get-tuple-element.156), channel_id=1, source_target_pairs={{1,0},{2,1},{3,2},{4,3},{5,4},{6,5},{7,6},{8,7},{9,8},{10,9},{11,1... | collective-permute-start | bytes 2600 | tf_op jit(solution)/shard_map/while/body/eval_jaxpr/ppermute | solution.py:31
  419.1 8.6 %collective-permute-start.2 = (f32[3,36,2]{2,1,0:T(8,128)S(1)}, f32[3,36,2]{2,1,0:T(8,128)S(1)}, u32[]{:S(2)}, u32[]{:S(2)}) collective-permute-start(f32[3,36,2]{2,1,0:T(8,128)S(1)} %get-tuple-element.156), channel_id=1, source_target_pairs={{1,0},{2,1},{3,2},{4,3},{5,4},{6,5},{7,6},{8,7},{9,8},{10,9},{11,1... | collective-permute-start | bytes 2600 | tf_op jit(solution)/shard_map/while/body/eval_jaxpr/ppermute | solution.py:31
  437.8 8.6 %collective-permute-start.2 = (f32[3,36,2]{2,1,0:T(8,128)S(1)}, f32[3,36,2]{2,1,0:T(8,128)S(1)}, u32[]{:S(2)}, u32[]{:S(2)}) collective-permute-start(f32[3,36,2]{2,1,0:T(8,128)S(1)} %get-tuple-element.156), channel_id=1, source_target_pairs={{1,0},{2,1},{3,2},{4,3},{5,4},{6,5},{7,6},{8,7},{9,8},{10,9},{11,1... | collective-permute-start | bytes 2600 | tf_op jit(solution)/shard_map/while/body/eval_jaxpr/ppermute | solution.py:31
  456.6 8.6 %collective-permute-start.2 = (f32[3,36,2]{2,1,0:T(8,128)S(1)}, f32[3,36,2]{2,1,0:T(8,128)S(1)}, u32[]{:S(2)}, u32[]{:S(2)}) collective-permute-start(f32[3,36,2]{2,1,0:T(8,128)S(1)} %get-tuple-element.156), channel_id=1, source_target_pairs={{1,0},{2,1},{3,2},{4,3},{5,4},{6,5},{7,6},{8,7},{9,8},{10,9},{11,1... | collective-permute-start | bytes 2600 | tf_op jit(solution)/shard_map/while/body/eval_jaxpr/ppermute | solution.py:31
  475.3 8.6 %collective-permute-start.2 = (f32[3,36,2]{2,1,0:T(8,128)S(1)}, f32[3,36,2]{2,1,0:T(8,128)S(1)}, u32[]{:S(2)}, u32[]{:S(2)}) collective-permute-start(f32[3,36,2]{2,1,0:T(8,128)S(1)} %get-tuple-element.156), channel_id=1, source_target_pairs={{1,0},{2,1},{3,2},{4,3},{5,4},{6,5},{7,6},{8,7},{9,8},{10,9},{11,1... | collective-permute-start | bytes 2600 | tf_op jit(solution)/shard_map/while/body/eval_jaxpr/ppermute | solution.py:31
  494.0 8.6 %collective-permute-start.2 = (f32[3,36,2]{2,1,0:T(8,128)S(1)}, f32[3,36,2]{2,1,0:T(8,128)S(1)}, u32[]{:S(2)}, u32[]{:S(2)}) collective-permute-start(f32[3,36,2]{2,1,0:T(8,128)S(1)} %get-tuple-element.156), channel_id=1, source_target_pairs={{1,0},{2,1},{3,2},{4,3},{5,4},{6,5},{7,6},{8,7},{9,8},{10,9},{11,1... | collective-permute-start | bytes 2600 | tf_op jit(solution)/shard_map/while/body/eval_jaxpr/ppermute | solution.py:31
  512.8 8.6 %collective-permute-start.2 = (f32[3,36,2]{2,1,0:T(8,128)S(1)}, f32[3,36,2]{2,1,0:T(8,128)S(1)}, u32[]{:S(2)}, u32[]{:S(2)}) collective-permute-start(f32[3,36,2]{2,1,0:T(8,128)S(1)} %get-tuple-element.156), channel_id=1, source_target_pairs={{1,0},{2,1},{3,2},{4,3},{5,4},{6,5},{7,6},{8,7},{9,8},{10,9},{11,1... | collective-permute-start | bytes 2600 | tf_op jit(solution)/shard_map/while/body/eval_jaxpr/ppermute | solution.py:31
  531.5 8.6 %collective-permute-start.2 = (f32[3,36,2]{2,1,0:T(8,128)S(1)}, f32[3,36,2]{2,1,0:T(8,128)S(1)}, u32[]{:S(2)}, u32[]{:S(2)}) collective-permute-start(f32[3,36,2]{2,1,0:T(8,128)S(1)} %get-tuple-element.156), channel_id=1, source_target_pairs={{1,0},{2,1},{3,2},{4,3},{5,4},{6,5},{7,6},{8,7},{9,8},{10,9},{11,1... | collective-permute-start | bytes 2600 | tf_op jit(solution)/shard_map/while/body/eval_jaxpr/ppermute | solution.py:31
  (125 other events, 864.0 us)
where the time goes:
time: 743 us; the launch traced here: 738 us
  starting transfers between devices  474 us (64%)
  waiting for transfers between devices  149 us (20%)
  other arithmetic  45.5 us (6%)
  local copies, waits for them, and re-layouts  33 us (4%)
  matrix products  32 us (4%)
    ppermute x68, starting transfers between devices, with_halo(): lax.ppermute(tail, axis, [(i, (i + 1) % count) for i in range(ends)])  331 us
    ppermute x68, starting transfers between devices, with_halo(): lax.ppermute(head, axis, [((i + 1) % count, i) for i in range(ends)])  143 us
    ppermute x68, waiting for transfers between devices, with_halo(): lax.ppermute(tail, axis, [(i, (i + 1) % count) for i in range(ends)])  143 us
    dot_general x4, matrix products, baroclinic(): jnp.einsum('kl,flxy->fkxy', inverse[class_index], provisional, precision=...  25.2 us
  transfers between devices with their start and end apart: 136, of which 68 were waited for; matrix products, arithmetic and copies ran while one was open for 2% of the time, Pallas kernels for 0%

commit v1 on v0

--- a/solution.py
+++ b/solution.py
@@ -153,14 +153,26 @@
     return jnp.concatenate([updated[0:2], velocity], axis=0)
 
 
-def advance(moving, fixed_wide, coriolis_wide, refresh, exchanges):
-
-    def group(index, current):
-        extended = refresh(current)
-        extended = substep(extended, fixed_wide, coriolis_wide)
-        return extended
-
-    return lax.fori_loop(0, exchanges, group, moving)
+def wide_halo(cells, axis, dim, width):
+    count = lax.axis_size(axis)
+    size = cells.shape[dim]
+    before, after = [], []
+    remaining, hop = width, 1
+    while remaining > 0:
+        take = min(size, remaining)
+        tail = lax.slice_in_dim(cells, size - take, size, axis=dim)
+        head = lax.slice_in_dim(cells, 0, take, axis=dim)
+        if hop < count:
+            from_before = lax.ppermute(tail, axis, [(i, i + hop) for i in range(count - hop)])
+            from_after = lax.ppermute(head, axis, [(i + hop, i) for i in range(count - hop)])
+        else:
+            from_before = jnp.zeros_like(tail)
+            from_after = jnp.zeros_like(head)
+        before.insert(0, from_before)
+        after.append(from_after)
+        remaining -= take
+        hop += 1
+    return jnp.concatenate(before + [cells] + after, axis=dim)
 
 
 def body(state, depth_class, vertical_inverse, height, transport):
@@ -189,19 +201,22 @@
     column_depth = depth_class.astype(jnp.float32) * level_block / levels
     sea_mask = (depth_class > 0).astype(jnp.float32)
     moving = jnp.stack([height, transport[0], transport[1]]) * sea_mask
-    fixed_fields = jnp.stack([forcing[0], forcing[1], column_depth])
-    per_exchange = 1
-    depth_rim = 2 * per_exchange
-    exchanges = SUB // per_exchange
-    fixed_wide = with_halo(fixed_fields, (("gx", 1), (("gy", "mode"), 2)), depth_rim)
+    fields = jnp.stack([moving[0], moving[1], moving[2], forcing[0], forcing[1], column_depth])
+    rim = 2 * SUB
+    fields = wide_halo(fields, "gx", 1, rim)
+    fields = wide_halo(fields, ("gy", "mode"), 2, rim)
+    moving_wide = fields[0:3]
+    fixed_wide = jnp.pad(fields[3:6], ((0, 0), (2, 2), (2, 2)))
     coriolis_wide = coriolis_row(
-        anchor - depth_rim, y_cells + 2 * depth_rim, y_cells * column_blocks
-    )
-
-    def refresh_block(current):
-        return with_halo(current, (("gx", 1), (("gy", "mode"), 2)), depth_rim)
-
-    waves = advance(moving, fixed_wide, coriolis_wide, refresh_block, exchanges)
+        anchor - rim - 2, y_cells + 2 * rim + 4, y_cells * column_blocks
+    )
+
+    def turn(index, current):
+        return substep(jnp.pad(current, ((0, 0), (2, 2), (2, 2))), fixed_wide, coriolis_wide)
+
+    waves_wide = lax.fori_loop(0, SUB, turn, moving_wide)
+    x_cells = depth_class.shape[0]
+    waves = waves_wide[:, rim : rim + x_cells, rim : rim + y_cells]
     state_next = finish(updated, waves, active, depth_class, level_block, levels)
     return (state_next, waves[0], waves[1:3])
 

time: 743 us -> 195 us (0.26)
  starting transfers between devices: 474 us -> 35.8 us
  waiting for transfers between devices: 149 us -> 18.7 us
  other arithmetic: 45.5 us -> 69.1 us
    ppermute x68 -> x2, starting transfers between devices: 331 us -> 6.75 us  [with_halo(): lax.ppermute(tail, axis, [(i, (i + 1) % count) for i in range(ends)])]
    ppermute x68 -> x2, waiting for transfers between devices: 143 us -> 5.91 us  [with_halo(): lax.ppermute(tail, axis, [(i, (i + 1) % count) for i in range(ends)])]
    ppermute x68 -> x2, starting transfers between devices: 143 us -> 8.68 us  [with_halo(): lax.ppermute(head, axis, [((i + 1) % count, i) for i in range(ends)])]
    ppermute x0 -> x6, starting transfers between devices: none -> 20.4 us  [the longest x3 11 us: wide_halo(): lax.ppermute(head, axis, [(i + hop, i) for i in range(count - hop)])]
    another operation x64, other arithmetic: 3.82 us -> 18 us  [substep(): return jnp.stack([shrink(surface_mid), east_new, north_new])]
    ppermute x0 -> x6, waiting for transfers between devices: none -> 12.6 us  [the longest x3 9.37 us: wide_halo(): lax.ppermute(head, axis, [(i + hop, i) for i in range(count - hop)])]
    mul x32, other arithmetic: 3.92 us -> 14.1 us  [substep(): shrink(sea_mask)]
    squeeze x32, local copies, waits for them, and re-layouts: 0.34 us -> 8.66 us  [substep(): surface, east_flow, north_flow = (moving[0], moving[1], moving[2])]
  transfers between devices with their start and end apart: 136 -> 10, of which waited for: 68 -> 5; matrix products, arithmetic and copies ran while one was open for 2% -> 5% of each run, Pallas kernels for 0% -> 0%
where the time goes in v1:
time: 195 us
  other arithmetic  69.1 us (35%)
  local copies, waits for them, and re-layouts  37 us (19%)
  starting transfers between devices  35.8 us (18%)
  matrix products  32 us (16%)
  waiting for transfers between devices  18.7 us (10%)
    dot_general x4, matrix products, baroclinic(): jnp.einsum('kl,flxy->fkxy', inverse[class_index], provisional, precision=...  25.2 us
    another operation x64, other arithmetic, substep(): return jnp.stack([shrink(surface_mid), east_new, north_new])  18 us
    mul x32, other arithmetic, substep(): shrink(sea_mask)  14.1 us
    mul x1, other arithmetic, baroclinic(): provisional = active * (center + STEP_TIME * tendency)  12.7 us
    ppermute x3, starting transfers between devices, wide_halo(): lax.ppermute(head, axis, [(i + hop, i) for i in range(count - hop)])  11 us
    ppermute x3, waiting for transfers between devices, wide_halo(): lax.ppermute(head, axis, [(i + hop, i) for i in range(count - hop)])  9.37 us
    ppermute x3, starting transfers between devices, wide_halo(): lax.ppermute(tail, axis, [(i, i + hop) for i in range(count - hop)])  9.33 us
    ppermute x2, starting transfers between devices, with_halo(): lax.ppermute(head, axis, [((i + 1) % count, i) for i in range(ends)])  8.68 us
  transfers between devices with their start and end apart: 10, of which 5 were waited for; matrix products, arithmetic and copies ran while one was open for 5% of the time, Pallas kernels for 0%

profile of v1, /device:TPU:103, one launch (start us, length us, event | category | flops | bytes accessed | tf_op | source)
XLA Modules:
  0.0 194.9 jit_solution(8577079485865242761)
XLA Ops:
  1.5 4.6 %copy_multiply_fusion = f32[4,64,32,128]{3,1,2,0:T(8,128)S(1)} fusion(f32[4,64,32,128]{3,2,1,0:T(8,128)} %param.7, f32[64,32,128]{2,0,1:T(8,128)S(1)} %fusion.67), kind=kLoop, calls=%fused_computation.69 | loop fusion | flops 1048576 | bytes 9437184 | tf_op jit(solution)/shard_map/mul | solution.py:184
  8.2 4.9 %collective-permute-start = (f32[4,64,2,128]{3,1,2,0:T(8,128)S(1)}, f32[4,64,2,128]{3,1,2,0:T(8,128)S(1)}, u32[]{:S(2)}, u32[]{:S(2)}) collective-permute-start(f32[4,64,2,128]{3,1,2,0:T(8,128)S(1)} %get-tuple-element.101), channel_id=1, source_target_pairs={{16,0},{32,16},{48,32},{64,48},{80,64},{96,80},{112,96},{128,112},... | collective-permute-start | bytes 786440 | tf_op jit(solution)/shard_map/ppermute | solution.py:31
  18.1 5.9 %collective-permute-done.1 = f32[4,64,2,128]{3,1,2,0:T(8,128)S(1)} collective-permute-done((f32[4,64,2,128]{3,1,2,0:T(8,128)S(1)}, f32[4,64,2,128]{3,1,2,0:T(8,128)S(1)}, u32[]{:S(2)}, u32[]{:S(2)}) %collective-permute-start.1) | collective-permute-done | bytes 262176 | tf_op jit(solution)/shard_map/ppermute | solution.py:29
  26.7 5.2 %fusion.88 = (f32[4,64,36,2]{3,1,2,0:T(8,128)}, f32[4,64,36,2]{3,1,2,0:T(8,128)}) fusion(f32[4,64,36,128]{3,1,2,0:T(8,128)S(1)} %pad_maximum_fusion.1), kind=kLoop, calls=%fused_computation.156 | loop fusion | bytes 294912 | tf_op jit(solution)/shard_map/slice | solution.py:26
  31.9 3.2 %copy.12 = f32[4,64,36,2]{1,0,3,2:T(4,128)S(1)} copy(f32[4,64,36,2]{3,1,2,0:T(8,128)} %get-tuple-element.93) | data formatting | bytes 147456 | tf_op jit(solution)/shard_map/slice | solution.py:25
  35.1 3.8 %collective-permute-start.2 = (f32[4,64,36,2]{1,0,3,2:T(4,128)S(1)}, f32[4,64,36,2]{1,0,3,2:T(4,128)S(1)}, u32[]{:S(2)}, u32[]{:S(2)}) collective-permute-start(f32[4,64,36,2]{1,0,3,2:T(4,128)S(1)} %copy.12), channel_id=1, source_target_pairs={{1,0},{2,1},{3,2},{4,3},{5,4},{6,5},{7,6},{8,7},{9,8},{10,9},{11,1... | collective-permute-start | bytes 221192 | tf_op jit(solution)/shard_map/ppermute | solution.py:31
  38.9 3.2 %copy.14 = f32[4,64,36,2]{1,0,3,2:T(4,128)S(1)} copy(f32[4,64,36,2]{3,1,2,0:T(8,128)} %get-tuple-element.92) | data formatting | bytes 147456 | tf_op jit(solution)/shard_map/slice | solution.py:26
  42.1 4.8 %collective-permute-start.3 = (f32[4,64,36,2]{1,0,3,2:T(4,128)S(1)}, f32[4,64,36,2]{1,0,3,2:T(4,128)S(1)}, u32[]{:S(2)}, u32[]{:S(2)}) collective-permute-start(f32[4,64,36,2]{1,0,3,2:T(4,128)S(1)} %copy.14), channel_id=1, source_target_pairs={{0,1},{1,2},{2,3},{3,4},{4,5},{5,6},{6,7},{7,8},{8,9},{9,10},{10,1... | collective-permute-start | bytes 221192 | tf_op jit(solution)/shard_map/ppermute | solution.py:29
  53.0 6.8 %fusion.50 = f32[64,36,132]{2,0,1:T(8,128)S(1)} fusion(f32[4,64,36,2]{3,1,2,0:T(8,128)} %copy.13, f32[4,64,36,2]{3,1,2,0:T(8,128)} %copy.15, f32[4,64,2,128]{3,1,2,0:T(8,128)S(1)} %collective-permute-done, f32[4,64,32,128]{3,1,2,0:T(8,128)} %copy-done, f32[4,64,2,128]{3,1,2,0:T(8,128)} %copy-done.5), kind=kOutput, calls=%fused_computation.92 | convolution fusion | flops 237223936 | bytes 6082560 | tf_op jit(solution)/shard_map/kl,lxy->kxy/dot_general | solution.py:196
  59.8 3.9 %fusion.68 = (f32[64,32,128]{2,0,1:T(8,128)}, f32[64,32,128]{2,0,1:T(8,128)}, f32[1,64,32,128]{3,1,2,0:T(8,128)}, f32[1,64,32,128]{3,1,2,0:T(8,128)}) fusion(f32[4,64,32,128]{3,1,2,0:T(8,128)S(1)} %copy-done.1, f32[128]{0:T(128)S(1)} %multiply_add_fusion.2, f32[64,36,132]{2,0,1:T(8,128)S(1)} %fusion.50), kind=kLoop, calls=%fused_computation.115 | loop fusion | flops 4718592 | bytes 14680576 | tf_op jit(solution)/shard_map/mul | solution.py:73
  63.7 12.7 %add_multiply_fusion = (f32[4,64,32,128]{3,1,2,0:T(8,128)S(1)}, f32[4,64,32,128]{3,1,2,0:T(8,128)}) fusion(f32[64,32,128]{2,0,1:T(8,128)S(1)} %fusion.67, f32[4,64,32,128]{3,2,1,0:T(8,128)} %param.7, f32[1,64,32,128]{3,1,2,0:T(8,128)} %get-tuple-element.98, f32[1,64,32,128]{3,1,2,0:T(8,128)} %get-tuple-element.99, f32[4]{0:T(128)} %pad.27.clone, ...), kind=kLoop, calls=%fused_computation.68 | loop fusion | flops 44040192 | bytes 22691856 | tf_op jit(solution)/shard_map/mul | solution.py:86
  76.4 4.0 %fusion.71 = f32[4,32,128,64]{2,3,1,0:T(8,128)S(1)} fusion(f32[4,64,32,128]{3,1,2,0:T(8,128)S(1)} %get-tuple-element.78, f32[4,64,64]{2,1,0:T(8,128)S(1)} %copy-done.7), kind=kOutput, calls=%fused_computation.122 | convolution fusion | flops 805306368 | bytes 8421376 | tf_op jit(solution)/shard_map/kl,flxy->fkxy/dot_general | solution.py:90
  80.4 5.6 %fusion.73 = f32[4,32,128,64]{2,3,1,0:T(8,128)} fusion(f32[4,64,32,128]{3,1,2,0:T(8,128)S(1)} %get-tuple-element.78, f32[4,64,64]{2,1,0:T(8,128)S(1)} %copy-done.7), kind=kOutput, calls=%fused_computation.124 | convolution fusion | flops 805306368 | bytes 8421376 | tf_op jit(solution)/shard_map/kl,flxy->fkxy/dot_general | solution.py:90
  86.0 5.5 %fusion.75 = f32[4,32,128,64]{2,3,1,0:T(8,128)} fusion(f32[4,64,32,128]{3,1,2,0:T(8,128)S(1)} %get-tuple-element.78, f32[4,64,64]{2,1,0:T(8,128)S(1)} %copy-done.7), kind=kOutput, calls=%fused_computation.126 | convolution fusion | flops 805306368 | bytes 8421376 | tf_op jit(solution)/shard_map/kl,flxy->fkxy/dot_general | solution.py:90
  91.5 10.2 %fusion.34 = f32[4,64,32,128]{3,1,2,0:T(8,128)S(1)} fusion(f32[4,32,128,64]{2,3,1,0:T(8,128)S(1)} %fusion.71, f32[4,32,128,64]{2,3,1,0:T(8,128)} %fusion.73, f32[4,32,128,64]{2,3,1,0:T(8,128)} %fusion.75, f32[4,64,32,128]{3,2,1,0:T(8,128)S(1)} %copy-done.2, f32[4,64,32,128]{3,1,2,0:T(8,128)S(1)} %get-tuple-element.78, f32[64,32,128]{2,0,1:T(8,128)S(1)} %copy-done.4, ...), kind=kOutput, calls=%fused_computation.67 | convolution fusion | flops 815792128 | bytes 27361280 | tf_op jit(solution)/shard_map/kl,flxy->fkxy/dot_general | solution.py:90
  101.7 4.0 %fusion.49 = (f32[2,32,128]{2,1,0:T(8,128)S(1)}, f32[2,32,128]{2,1,0:T(8,128)S(1)}) fusion(f32[4,64,32,128]{3,1,2,0:T(8,128)} %get-tuple-element.79, f32[64,32,128]{2,0,1:T(8,128)S(1)} %fusion.67, f32[4,64,32,128]{3,1,2,0:T(8,128)S(1)} %fusion.34), kind=kLoop, calls=%fused_computation.89 | loop fusion | flops 2080768 | bytes 5308416 | tf_op jit(solution)/shard_map/reduce_sum | solution.py:94
  109.6 5.5 %collective-permute-start.6 = (f32[6,32,128]{2,1,0:T(8,128)S(1)}, f32[6,32,128]{2,1,0:T(8,128)S(1)}, u32[]{:S(2)}, u32[]{:S(2)}) collective-permute-start(f32[6,32,128]{2,1,0:T(8,128)S(1)} %pad_maximum_fusion.21), channel_id=1, source_target_pairs={{16,0},{32,16},{48,32},{64,48},{80,64},{96,80},{112,96},{128,112},... | collective-permute-start | bytes 294920 | tf_op jit(solution)/shard_map/ppermute | solution.py:167
  115.0 3.7 %collective-permute-start.7 = (f32[6,32,128]{2,1,0:T(8,128)S(1)}, f32[6,32,128]{2,1,0:T(8,128)S(1)}, u32[]{:S(2)}, u32[]{:S(2)}) collective-permute-start(f32[6,32,128]{2,1,0:T(8,128)S(1)} %pad_maximum_fusion.21), channel_id=1, source_target_pairs={{32,0},{48,16},{64,32},{80,48},{96,64},{112,80},{128,96},{144,112}... | collective-permute-start | bytes 294920 | tf_op jit(solution)/shard_map/ppermute | solution.py:167
  118.8 3.8 %collective-permute-done.7 = f32[6,32,128]{2,1,0:T(8,128)S(1)} collective-permute-done((f32[6,32,128]{2,1,0:T(8,128)S(1)}, f32[6,32,128]{2,1,0:T(8,128)S(1)}, u32[]{:S(2)}, u32[]{:S(2)}) %collective-permute-start.7) | collective-permute-done | bytes 98336 | tf_op jit(solution)/shard_map/ppermute | solution.py:167
  122.8 5.5 %collective-permute-start.8 = (f32[6,160,64]{2,1,0:T(8,128)S(1)}, f32[6,160,64]{2,1,0:T(8,128)S(1)}, u32[]{:S(2)}, u32[]{:S(2)}) collective-permute-start(f32[6,160,64]{2,1,0:T(8,128)S(1)} %get-tuple-element.104), channel_id=1, source_target_pairs={{0,1},{1,2},{2,3},{3,4},{4,5},{5,6},{6,7},{7,8},{8,9},{9,10},{10,1... | collective-permute-start | bytes 737288 | tf_op jit(solution)/shard_map/ppermute | solution.py:166
  130.8 3.2 %collective-permute-done.8 = f32[6,160,64]{2,1,0:T(8,128)S(1)} collective-permute-done((f32[6,160,64]{2,1,0:T(8,128)S(1)}, f32[6,160,64]{2,1,0:T(8,128)S(1)}, u32[]{:S(2)}, u32[]{:S(2)}) %collective-permute-start.8) | collective-permute-done | bytes 245792 | tf_op jit(solution)/shard_map/ppermute | solution.py:166
  134.0 5.6 %collective-permute-done.9 = f32[6,160,64]{2,1,0:T(8,128)S(1)} collective-permute-done((f32[6,160,64]{2,1,0:T(8,128)S(1)}, f32[6,160,64]{2,1,0:T(8,128)S(1)}, u32[]{:S(2)}, u32[]{:S(2)}) %collective-permute-start.9) | collective-permute-done | bytes 245792 | tf_op jit(solution)/shard_map/ppermute | solution.py:167
  140.5 45.1 %while.12 = (s32[]{:T(128)}, f32[3,160,256]{2,1,0:T(8,128)S(1)}, f32[3,164,260]{2,1,0:T(8,128)S(1)}, f32[1,260]{1,0:T(1,128)S(1)}, s32[]{:T(128)}) while((s32[]{:T(128)}, f32[3,160,256]{2,1,0:T(8,128)S(1)}, f32[3,164,260]{2,1,0:T(8,128)S(1)}, f32[1,260]{1,0:T(1,128)S(1)}, s32[]{:T(128)}) %tuple.66), condition=%wide.region_2.3_spmd, body=%wide.region_1.2_spmd.sunk | while | flops 1523898 | bytes 6817901 | solution.py:217
  190.4 4.4 %copy.19 = f32[4,64,32,128]{3,2,1,0:T(8,128)} copy(f32[4,64,32,128]{3,1,2,0:T(8,128)S(1)} %pad_maximum_fusion.12) | data formatting | bytes 8388608
  (264 shorter events, 72.6 us)
Async XLA Ops:
  1.5 13.6 %copy-start.6 = (s32[32,128]{1,0:T(8,128)S(1)}, s32[32,128]{1,0:T(8,128)}, u32[]{:S(2)}) copy-start(s32[32,128]{1,0:T(8,128)} %param.8) | copy-start | bytes 49156
  1.5 14.2 %copy-start.11 = (f32[2,32,128]{2,1,0:T(8,128)S(1)}, f32[2,32,128]{2,1,0:T(8,128)}, u32[]{:S(2)}) copy-start(f32[2,32,128]{2,1,0:T(8,128)} %param.11) | copy-start | bytes 98308
  1.5 14.2 %copy-start.13 = (f32[32,128]{1,0:T(8,128)S(1)}, f32[32,128]{1,0:T(8,128)}, u32[]{:S(2)}) copy-start(f32[32,128]{1,0:T(8,128)} %param.10) | copy-start | bytes 49156
  8.2 9.9 %collective-permute-start = (f32[4,64,2,128]{3,1,2,0:T(8,128)S(1)}, f32[4,64,2,128]{3,1,2,0:T(8,128)S(1)}, u32[]{:S(2)}, u32[]{:S(2)}) collective-permute-start(f32[4,64,2,128]{3,1,2,0:T(8,128)S(1)} %get-tuple-element.101), channel_id=1, source_target_pairs={{16,0},{32,16},{48,32},{64,48},{80,64},{96,80},{112,96},{128,112},... | collective-permute-start | bytes 786440 | tf_op jit(solution)/shard_map/ppermute | solution.py:31
  13.1 10.9 %collective-permute-start.1 = (f32[4,64,2,128]{3,1,2,0:T(8,128)S(1)}, f32[4,64,2,128]{3,1,2,0:T(8,128)S(1)}, u32[]{:S(2)}, u32[]{:S(2)}) collective-permute-start(f32[4,64,2,128]{3,1,2,0:T(8,128)S(1)} %get-tuple-element.100), channel_id=1, source_target_pairs={{0,16},{16,32},{32,48},{48,64},{64,80},{80,96},{96,112},{112,128},... | collective-permute-start | bytes 786440 | tf_op jit(solution)/shard_map/ppermute | solution.py:29
  35.1 11.9 %collective-permute-start.2 = (f32[4,64,36,2]{1,0,3,2:T(4,128)S(1)}, f32[4,64,36,2]{1,0,3,2:T(4,128)S(1)}, u32[]{:S(2)}, u32[]{:S(2)}) collective-permute-start(f32[4,64,36,2]{1,0,3,2:T(4,128)S(1)} %copy.12), channel_id=1, source_target_pairs={{1,0},{2,1},{3,2},{4,3},{5,4},{6,5},{7,6},{8,7},{9,8},{10,9},{11,1... | collective-permute-start | bytes 221192 | tf_op jit(solution)/shard_map/ppermute | solution.py:31
  42.1 7.9 %collective-permute-start.3 = (f32[4,64,36,2]{1,0,3,2:T(4,128)S(1)}, f32[4,64,36,2]{1,0,3,2:T(4,128)S(1)}, u32[]{:S(2)}, u32[]{:S(2)}) collective-permute-start(f32[4,64,36,2]{1,0,3,2:T(4,128)S(1)} %copy.14), channel_id=1, source_target_pairs={{0,1},{1,2},{2,3},{3,4},{4,5},{5,6},{6,7},{7,8},{8,9},{9,10},{10,1... | collective-permute-start | bytes 221192 | tf_op jit(solution)/shard_map/ppermute | solution.py:29
  50.0 13.7 %slice-start = ((s8[4718592]{0:T(1024)(128)(4,1)}), s8[524288]{0:T(1024)(128)(4,1)S(1)}, s32[]{:S(2)}) async-start(s8[4718592]{0:T(1024)(128)(4,1)} %bitcast.95), calls=%async_computation | async-start | bytes 1048576
  53.0 6.8 %copy-start.1 = (f32[4,64,32,128]{3,1,2,0:T(8,128)S(1)}, f32[4,64,32,128]{3,1,2,0:T(8,128)}, u32[]{:S(2)}) copy-start(f32[4,64,32,128]{3,1,2,0:T(8,128)} %copy-done) | copy-start | bytes 12582916
  53.0 10.7 %slice-start.1 = ((s8[4718592]{0:T(1024)(128)(4,1)}), s8[4194304]{0:T(1024)(128)(4,1)S(1)}, s32[]{:S(2)}) async-start(s8[4718592]{0:T(1024)(128)(4,1)} %bitcast.95), calls=%async_computation.1 | async-start | bytes 8388608
  63.7 12.7 %copy-start.7 = (f32[4,64,64]{2,1,0:T(8,128)S(1)}, f32[4,64,64]{2,1,0:T(8,128)}, u32[]{:S(2)}) copy-start(f32[4,64,64]{2,1,0:T(8,128)} %param.9) | copy-start | bytes 196612
  86.0 5.5 %copy-start.2 = (f32[4,64,32,128]{3,2,1,0:T(8,128)S(1)}, f32[4,64,32,128]{3,2,1,0:T(8,128)}, u32[]{:S(2)}) copy-start(f32[4,64,32,128]{3,2,1,0:T(8,128)} %param.7) | copy-start | bytes 12582916
  86.0 5.5 %copy-start.4 = (f32[64,32,128]{2,0,1:T(8,128)S(1)}, f32[64,32,128]{2,0,1:T(8,128)}, u32[]{:S(2)}) copy-start(f32[64,32,128]{2,0,1:T(8,128)} %broadcast_subtract_fusion) | copy-start | bytes 3145732
  86.0 5.5 %copy-start.9 = (f32[32,128]{1,0:T(8,128)S(1)}, f32[32,128]{1,0:T(8,128)}, u32[]{:S(2)}) copy-start(f32[32,128]{1,0:T(8,128)} %get-tuple-element.109) | copy-start | bytes 49156
  86.0 5.5 %copy-start.10 = (f32[32,128]{1,0:T(8,128)S(1)}, f32[32,128]{1,0:T(8,128)}, u32[]{:S(2)}) copy-start(f32[32,128]{1,0:T(8,128)} %get-tuple-element.110) | copy-start | bytes 49156
  101.7 21.1 %copy-start.3 = (f32[4,64,32,128]{3,1,2,0:T(8,128)}, f32[4,64,32,128]{3,1,2,0:T(8,128)S(1)}, u32[]{:S(2)}) copy-start(f32[4,64,32,128]{3,1,2,0:T(8,128)S(1)} %fusion.34) | copy-start | bytes 12582916
  105.7 13.0 %collective-permute-start.4 = (f32[6,32,128]{2,1,0:T(8,128)S(1)}, f32[6,32,128]{2,1,0:T(8,128)S(1)}, u32[]{:S(2)}, u32[]{:S(2)}) collective-permute-start(f32[6,32,128]{2,1,0:T(8,128)S(1)} %pad_maximum_fusion.21), channel_id=1, source_target_pairs={{0,32},{16,48},{32,64},{48,80},{64,96},{80,112},{96,128},{112,144}... | collective-permute-start | bytes 294920 | tf_op jit(solution)/shard_map/ppermute | solution.py:166
  107.6 11.1 %collective-permute-start.5 = (f32[6,32,128]{2,1,0:T(8,128)S(1)}, f32[6,32,128]{2,1,0:T(8,128)S(1)}, u32[]{:S(2)}, u32[]{:S(2)}) collective-permute-start(f32[6,32,128]{2,1,0:T(8,128)S(1)} %pad_maximum_fusion.21), channel_id=1, source_target_pairs={{0,16},{16,32},{32,48},{48,64},{64,80},{80,96},{96,112},{112,128},... | collective-permute-start | bytes 294920 | tf_op jit(solution)/shard_map/ppermute | solution.py:166
  109.6 9.2 %collective-permute-start.6 = (f32[6,32,128]{2,1,0:T(8,128)S(1)}, f32[6,32,128]{2,1,0:T(8,128)S(1)}, u32[]{:S(2)}, u32[]{:S(2)}) collective-permute-start(f32[6,32,128]{2,1,0:T(8,128)S(1)} %pad_maximum_fusion.21), channel_id=1, source_target_pairs={{16,0},{32,16},{48,32},{64,48},{80,64},{96,80},{112,96},{128,112},... | collective-permute-start | bytes 294920 | tf_op jit(solution)/shard_map/ppermute | solution.py:167
  115.0 7.5 %collective-permute-start.7 = (f32[6,32,128]{2,1,0:T(8,128)S(1)}, f32[6,32,128]{2,1,0:T(8,128)S(1)}, u32[]{:S(2)}, u32[]{:S(2)}) collective-permute-start(f32[6,32,128]{2,1,0:T(8,128)S(1)} %pad_maximum_fusion.21), channel_id=1, source_target_pairs={{32,0},{48,16},{64,32},{80,48},{96,64},{112,80},{128,96},{144,112}... | collective-permute-start | bytes 294920 | tf_op jit(solution)/shard_map/ppermute | solution.py:167
  122.8 11.2 %collective-permute-start.8 = (f32[6,160,64]{2,1,0:T(8,128)S(1)}, f32[6,160,64]{2,1,0:T(8,128)S(1)}, u32[]{:S(2)}, u32[]{:S(2)}) collective-permute-start(f32[6,160,64]{2,1,0:T(8,128)S(1)} %get-tuple-element.104), channel_id=1, source_target_pairs={{0,1},{1,2},{2,3},{3,4},{4,5},{5,6},{6,7},{7,8},{8,9},{9,10},{10,1... | collective-permute-start | bytes 737288 | tf_op jit(solution)/shard_map/ppermute | solution.py:166
  128.3 11.4 %collective-permute-start.9 = (f32[6,160,64]{2,1,0:T(8,128)S(1)}, f32[6,160,64]{2,1,0:T(8,128)S(1)}, u32[]{:S(2)}, u32[]{:S(2)}) collective-permute-start(f32[6,160,64]{2,1,0:T(8,128)S(1)} %get-tuple-element.105), channel_id=1, source_target_pairs={{1,0},{2,1},{3,2},{4,3},{5,4},{6,5},{7,6},{8,7},{9,8},{10,9},{11,1... | collective-permute-start | bytes 737288 | tf_op jit(solution)/shard_map/ppermute | solution.py:167
  134.0 6.4 %copy-start.12 = (f32[1,260]{1,0:T(1,128)S(1)}, f32[1,260]{1,0:T(1,128)}, u32[]{:S(2)}) copy-start(f32[1,260]{1,0:T(1,128)} %multiply_add_fusion.1) | copy-start | bytes 3124
  140.4 45.8 %copy-start.8 = (f32[32,128]{1,0:T(8,128)S(1)}, f32[32,128]{1,0:T(8,128)}, u32[]{:S(2)}) copy-start(f32[32,128]{1,0:T(8,128)} %get-tuple-element.112) | copy-start | bytes 49156
  (2 other events, 4.7 us)

commit v2 on v1

--- a/solution.py
+++ b/solution.py
@@ -1,6 +1,8 @@
 import jax
 import jax.numpy as jnp
 from jax import lax
+from jax.experimental import pallas as pl
+from jax.experimental.pallas import tpu as pltpu
 from jax.sharding import PartitionSpec as P
 
 SUB = 32
@@ -175,6 +177,71 @@
     return jnp.concatenate(before + [cells] + after, axis=dim)
 
 
+def wave_kernel(moving_ref, fixed_ref, coriolis_ref, out_ref):
+    rows, cols = moving_ref.shape[1], moving_ref.shape[2]
+    column_depth = fixed_ref[2]
+    sea_mask = (column_depth > 0.0).astype(jnp.float32)
+    force_east = fixed_ref[0]
+    force_north = fixed_ref[1]
+    coriolis = jnp.broadcast_to(coriolis_ref[0:1, :], (rows, cols))
+
+    def x_slope_rolled(values):
+        return (pltpu.roll(values, rows - 1, 0) - pltpu.roll(values, 1, 0)) * 0.5
+
+    def y_slope_rolled(values):
+        return (pltpu.roll(values, cols - 1, 1) - pltpu.roll(values, 1, 1)) * 0.5
+
+    out_ref[...] = moving_ref[...]
+
+    def step(index, carry):
+        surface = out_ref[0]
+        east_old = out_ref[1]
+        north_old = out_ref[2]
+        surface_mid = sea_mask * (
+            surface - WAVE_STEP * (x_slope_rolled(east_old) + y_slope_rolled(north_old))
+        )
+        east_new = sea_mask * (
+            east_old
+            + WAVE_STEP
+            * (
+                -GRAVITY * column_depth * x_slope_rolled(surface_mid)
+                + coriolis * north_old
+                + force_east
+                - BOTTOM_DRAG * east_old
+            )
+        )
+        north_new = sea_mask * (
+            north_old
+            + WAVE_STEP
+            * (
+                -GRAVITY * column_depth * y_slope_rolled(surface_mid)
+                - coriolis * east_new
+                + force_north
+                - BOTTOM_DRAG * north_old
+            )
+        )
+        out_ref[0] = surface_mid
+        out_ref[1] = east_new
+        out_ref[2] = north_new
+        return carry
+
+    lax.fori_loop(0, SUB, step, 0)
+
+
+def local_waves(moving, fixed, coriolis):
+    rows, cols = moving.shape[1], moving.shape[2]
+    elements = rows * cols
+    return pl.pallas_call(
+        wave_kernel,
+        out_shape=jax.ShapeDtypeStruct(moving.shape, jnp.float32),
+        in_specs=[pl.BlockSpec(memory_space=pltpu.VMEM)] * 3,
+        out_specs=pl.BlockSpec(memory_space=pltpu.VMEM),
+        cost_estimate=pl.CostEstimate(
+            flops=SUB * 40 * elements, transcendentals=0, bytes_accessed=4 * 9 * elements
+        ),
+    )(moving, fixed, coriolis)
+
+
 def body(state, depth_class, vertical_inverse, height, transport):
     levels = state.shape[1]
     level_block = levels // vertical_inverse.shape[0]
@@ -205,16 +272,10 @@
     rim = 2 * SUB
     fields = wide_halo(fields, "gx", 1, rim)
     fields = wide_halo(fields, ("gy", "mode"), 2, rim)
-    moving_wide = fields[0:3]
-    fixed_wide = jnp.pad(fields[3:6], ((0, 0), (2, 2), (2, 2)))
-    coriolis_wide = coriolis_row(
-        anchor - rim - 2, y_cells + 2 * rim + 4, y_cells * column_blocks
-    )
-
-    def turn(index, current):
-        return substep(jnp.pad(current, ((0, 0), (2, 2), (2, 2))), fixed_wide, coriolis_wide)
-
-    waves_wide = lax.fori_loop(0, SUB, turn, moving_wide)
+    coriolis_wide = jnp.broadcast_to(
+        coriolis_row(anchor - rim, y_cells + 2 * rim, y_cells * column_blocks), (8, y_cells + 2 * rim)
+    )
+    waves_wide = local_waves(fields[0:3], fields[3:6], coriolis_wide)
     x_cells = depth_class.shape[0]
     waves = waves_wide[:, rim : rim + x_cells, rim : rim + y_cells]
     state_next = finish(updated, waves, active, depth_class, level_block, levels)

time: 195 us -> 167 us (0.86)
  other arithmetic: 69.1 us -> 36.5 us
  Pallas kernels: 0 us -> 13.7 us
  local copies, waits for them, and re-layouts: 37 us -> 28.1 us
    another operation x64 -> x0, other arithmetic: 18 us -> none  [substep(): return jnp.stack([shrink(surface_mid), east_new, north_new])]
    mul x32 -> x0, other arithmetic: 14.1 us -> none  [substep(): shrink(sea_mask)]
    pallas_call x0 -> x1, Pallas kernels: none -> 13.7 us  [local_waves(): pl.pallas_call(wave_kernel, out_shape=jax.ShapeDtypeStruct(moving.shape,...]
    squeeze x32 -> x0, local copies, waits for them, and re-layouts: 8.66 us -> none  [substep(): surface, east_flow, north_flow = (moving[0], moving[1], moving[2])]
    unnamed x36 -> x32, local copies, waits for them, and re-layouts: 6.55 us -> 6.54 us
  transfers between devices with their start and end apart: 10 -> 10, of which waited for: 5 -> 5; matrix products, arithmetic and copies ran while one was open for 5% -> 6% of each run, Pallas kernels for 0% -> 0%
where the time goes in v2:
time: 167 us; the launch traced here: 166 us
  other arithmetic  36.5 us (22%)
  starting transfers between devices  35.8 us (21%)
  matrix products  32 us (19%)
  local copies, waits for them, and re-layouts  28.1 us (17%)
  waiting for transfers between devices  19.2 us (11%)
  Pallas kernels  13.7 us (8%)
    dot_general x4, matrix products, baroclinic(): jnp.einsum('kl,flxy->fkxy', inverse[class_index], provisional, precision=...  25.2 us
    pallas_call x1, Pallas kernels, local_waves(): pl.pallas_call(wave_kernel, out_shape=jax.ShapeDtypeStruct(moving.shape,...  13.7 us
    mul x1, other arithmetic, baroclinic(): provisional = active * (center + STEP_TIME * tendency)  12.6 us
    ppermute x3, starting transfers between devices, wide_halo(): lax.ppermute(head, axis, [(i + hop, i) for i in range(count - hop)])  11 us
    ppermute x3, waiting for transfers between devices, wide_halo(): lax.ppermute(head, axis, [(i + hop, i) for i in range(count - hop)])  9.41 us
    ppermute x3, starting transfers between devices, wide_halo(): lax.ppermute(tail, axis, [(i, i + hop) for i in range(count - hop)])  9.31 us
    ppermute x2, starting transfers between devices, with_halo(): lax.ppermute(head, axis, [((i + 1) % count, i) for i in range(ends)])  8.68 us
    slice x3, local copies, waits for them, and re-layouts, with_halo(): lax.slice_in_dim(cells, cells.shape[dim] - width, cells.shape[dim], axis=...  8.5 us
  transfers between devices with their start and end apart: 10, of which 5 were waited for; matrix products, arithmetic and copies ran while one was open for 6% of the time, Pallas kernels for 0%

profile of v2, /device:TPU:103, one launch (start us, length us, event | category | flops | bytes accessed | tf_op | source)
XLA Modules:
  0.0 166.4 jit_solution(1391843978755272807)
XLA Ops:
  1.5 4.6 %copy_multiply_fusion = f32[4,64,32,128]{3,1,2,0:T(8,128)S(1)} fusion(f32[4,64,32,128]{3,2,1,0:T(8,128)} %param.5, f32[64,32,128]{2,0,1:T(8,128)S(1)} %fusion.45), kind=kLoop, calls=%fused_computation.31 | loop fusion | flops 1048576 | bytes 9437184 | tf_op jit(solution)/shard_map/mul | solution.py:251
  8.2 4.9 %collective-permute-start = (f32[4,64,2,128]{3,1,2,0:T(8,128)S(1)}, f32[4,64,2,128]{3,1,2,0:T(8,128)S(1)}, u32[]{:S(2)}, u32[]{:S(2)}) collective-permute-start(f32[4,64,2,128]{3,1,2,0:T(8,128)S(1)} %get-tuple-element.26), channel_id=1, source_target_pairs={{16,0},{32,16},{48,32},{64,48},{80,64},{96,80},{112,96},{128,112},... | collective-permute-start | bytes 786440 | tf_op jit(solution)/shard_map/ppermute | solution.py:33
  18.1 5.9 %collective-permute-done.1 = f32[4,64,2,128]{3,1,2,0:T(8,128)S(1)} collective-permute-done((f32[4,64,2,128]{3,1,2,0:T(8,128)S(1)}, f32[4,64,2,128]{3,1,2,0:T(8,128)S(1)}, u32[]{:S(2)}, u32[]{:S(2)}) %collective-permute-start.1) | collective-permute-done | bytes 262176 | tf_op jit(solution)/shard_map/ppermute | solution.py:31
  26.7 5.2 %fusion.65 = (f32[4,64,36,2]{3,1,2,0:T(8,128)}, f32[4,64,36,2]{3,1,2,0:T(8,128)}) fusion(f32[4,64,36,128]{3,1,2,0:T(8,128)S(1)} %pad_maximum_fusion), kind=kLoop, calls=%fused_computation.118 | loop fusion | bytes 294912 | tf_op jit(solution)/shard_map/slice | solution.py:28
  31.9 3.2 %copy.12 = f32[4,64,36,2]{1,0,3,2:T(4,128)S(1)} copy(f32[4,64,36,2]{3,1,2,0:T(8,128)} %get-tuple-element.18) | data formatting | bytes 147456 | tf_op jit(solution)/shard_map/slice | solution.py:27
  35.1 3.8 %collective-permute-start.2 = (f32[4,64,36,2]{1,0,3,2:T(4,128)S(1)}, f32[4,64,36,2]{1,0,3,2:T(4,128)S(1)}, u32[]{:S(2)}, u32[]{:S(2)}) collective-permute-start(f32[4,64,36,2]{1,0,3,2:T(4,128)S(1)} %copy.12), channel_id=1, source_target_pairs={{1,0},{2,1},{3,2},{4,3},{5,4},{6,5},{7,6},{8,7},{9,8},{10,9},{11,1... | collective-permute-start | bytes 221192 | tf_op jit(solution)/shard_map/ppermute | solution.py:33
  38.9 3.2 %copy.14 = f32[4,64,36,2]{1,0,3,2:T(4,128)S(1)} copy(f32[4,64,36,2]{3,1,2,0:T(8,128)} %get-tuple-element.17) | data formatting | bytes 147456 | tf_op jit(solution)/shard_map/slice | solution.py:28
  42.1 4.8 %collective-permute-start.3 = (f32[4,64,36,2]{1,0,3,2:T(4,128)S(1)}, f32[4,64,36,2]{1,0,3,2:T(4,128)S(1)}, u32[]{:S(2)}, u32[]{:S(2)}) collective-permute-start(f32[4,64,36,2]{1,0,3,2:T(4,128)S(1)} %copy.14), channel_id=1, source_target_pairs={{0,1},{1,2},{2,3},{3,4},{4,5},{5,6},{6,7},{7,8},{8,9},{9,10},{10,1... | collective-permute-start | bytes 221192 | tf_op jit(solution)/shard_map/ppermute | solution.py:31
  53.0 6.8 %fusion.28 = f32[64,36,132]{2,0,1:T(8,128)S(1)} fusion(f32[4,64,36,2]{3,1,2,0:T(8,128)} %copy.13, f32[4,64,36,2]{3,1,2,0:T(8,128)} %copy.15, f32[4,64,2,128]{3,1,2,0:T(8,128)S(1)} %collective-permute-done, f32[4,64,32,128]{3,1,2,0:T(8,128)} %copy-done, f32[4,64,2,128]{3,1,2,0:T(8,128)} %copy-done.5), kind=kOutput, calls=%fused_computation.54 | convolution fusion | flops 237223936 | bytes 6082560 | tf_op jit(solution)/shard_map/kl,lxy->kxy/dot_general | solution.py:263
  59.8 4.0 %fusion.46 = (f32[64,32,128]{2,0,1:T(8,128)}, f32[64,32,128]{2,0,1:T(8,128)}, f32[1,64,32,128]{3,1,2,0:T(8,128)}, f32[1,64,32,128]{3,1,2,0:T(8,128)}) fusion(f32[4,64,32,128]{3,1,2,0:T(8,128)S(1)} %copy-done.1, f32[128]{0:T(128)S(1)} %multiply_add_fusion.2, f32[64,36,132]{2,0,1:T(8,128)S(1)} %fusion.28), kind=kLoop, calls=%fused_computation.77 | loop fusion | flops 4718592 | bytes 14680576 | tf_op jit(solution)/shard_map/mul | solution.py:75
  63.8 12.6 %add_multiply_fusion = (f32[4,64,32,128]{3,1,2,0:T(8,128)S(1)}, f32[4,64,32,128]{3,1,2,0:T(8,128)}) fusion(f32[64,32,128]{2,0,1:T(8,128)S(1)} %fusion.45, f32[4,64,32,128]{3,2,1,0:T(8,128)} %param.5, f32[1,64,32,128]{3,1,2,0:T(8,128)} %get-tuple-element.23, f32[1,64,32,128]{3,1,2,0:T(8,128)} %get-tuple-element.24, f32[4]{0:T(128)} %pad.13.clone, ...), kind=kLoop, calls=%fused_computation.30 | loop fusion | flops 44040192 | bytes 22691856 | tf_op jit(solution)/shard_map/mul | solution.py:88
  76.4 4.0 %fusion.49 = f32[4,32,128,64]{2,3,1,0:T(8,128)S(1)} fusion(f32[4,64,32,128]{3,1,2,0:T(8,128)S(1)} %get-tuple-element.13, f32[4,64,64]{2,1,0:T(8,128)S(1)} %copy-done.7), kind=kOutput, calls=%fused_computation.84 | convolution fusion | flops 805306368 | bytes 8421376 | tf_op jit(solution)/shard_map/kl,flxy->fkxy/dot_general | solution.py:92
  80.4 5.6 %fusion.51 = f32[4,32,128,64]{2,3,1,0:T(8,128)} fusion(f32[4,64,32,128]{3,1,2,0:T(8,128)S(1)} %get-tuple-element.13, f32[4,64,64]{2,1,0:T(8,128)S(1)} %copy-done.7), kind=kOutput, calls=%fused_computation.86 | convolution fusion | flops 805306368 | bytes 8421376 | tf_op jit(solution)/shard_map/kl,flxy->fkxy/dot_general | solution.py:92
  86.0 5.4 %fusion.53 = f32[4,32,128,64]{2,3,1,0:T(8,128)} fusion(f32[4,64,32,128]{3,1,2,0:T(8,128)S(1)} %get-tuple-element.13, f32[4,64,64]{2,1,0:T(8,128)S(1)} %copy-done.7), kind=kOutput, calls=%fused_computation.88 | convolution fusion | flops 805306368 | bytes 8421376 | tf_op jit(solution)/shard_map/kl,flxy->fkxy/dot_general | solution.py:92
  91.5 10.2 %fusion.12 = f32[4,64,32,128]{3,1,2,0:T(8,128)S(1)} fusion(f32[4,32,128,64]{2,3,1,0:T(8,128)S(1)} %fusion.49, f32[4,32,128,64]{2,3,1,0:T(8,128)} %fusion.51, f32[4,32,128,64]{2,3,1,0:T(8,128)} %fusion.53, f32[4,64,32,128]{3,2,1,0:T(8,128)S(1)} %copy-done.2, f32[4,64,32,128]{3,1,2,0:T(8,128)S(1)} %get-tuple-element.13, f32[64,32,128]{2,0,1:T(8,128)S(1)} %copy-done.4, ...), kind=kOutput, calls=%fused_computation.29 | convolution fusion | flops 815792128 | bytes 27361280 | tf_op jit(solution)/shard_map/kl,flxy->fkxy/dot_general | solution.py:92
  101.7 4.0 %fusion.27 = (f32[2,32,128]{2,1,0:T(8,128)S(1)}, f32[2,32,128]{2,1,0:T(8,128)S(1)}) fusion(f32[4,64,32,128]{3,1,2,0:T(8,128)} %get-tuple-element.14, f32[64,32,128]{2,0,1:T(8,128)S(1)} %fusion.45, f32[4,64,32,128]{3,1,2,0:T(8,128)S(1)} %fusion.12), kind=kLoop, calls=%fused_computation.51 | loop fusion | flops 2080768 | bytes 5308416 | tf_op jit(solution)/shard_map/reduce_sum | solution.py:96
  109.5 5.5 %collective-permute-start.6 = (f32[6,32,128]{2,1,0:T(8,128)S(1)}, f32[6,32,128]{2,1,0:T(8,128)S(1)}, u32[]{:S(2)}, u32[]{:S(2)}) collective-permute-start(f32[6,32,128]{2,1,0:T(8,128)S(1)} %pad_maximum_fusion.20), channel_id=1, source_target_pairs={{16,0},{32,16},{48,32},{64,48},{80,64},{96,80},{112,96},{128,112},... | collective-permute-start | bytes 294920 | tf_op jit(solution)/shard_map/ppermute | solution.py:169
  115.0 3.7 %collective-permute-start.7 = (f32[6,32,128]{2,1,0:T(8,128)S(1)}, f32[6,32,128]{2,1,0:T(8,128)S(1)}, u32[]{:S(2)}, u32[]{:S(2)}) collective-permute-start(f32[6,32,128]{2,1,0:T(8,128)S(1)} %pad_maximum_fusion.20), channel_id=1, source_target_pairs={{32,0},{48,16},{64,32},{80,48},{96,64},{112,80},{128,96},{144,112}... | collective-permute-start | bytes 294920 | tf_op jit(solution)/shard_map/ppermute | solution.py:169
  118.8 3.8 %collective-permute-done.7 = f32[6,32,128]{2,1,0:T(8,128)S(1)} collective-permute-done((f32[6,32,128]{2,1,0:T(8,128)S(1)}, f32[6,32,128]{2,1,0:T(8,128)S(1)}, u32[]{:S(2)}, u32[]{:S(2)}) %collective-permute-start.7) | collective-permute-done | bytes 98336 | tf_op jit(solution)/shard_map/ppermute | solution.py:169
  122.8 5.5 %collective-permute-start.8 = (f32[6,160,64]{2,1,0:T(8,128)S(1)}, f32[6,160,64]{2,1,0:T(8,128)S(1)}, u32[]{:S(2)}, u32[]{:S(2)}) collective-permute-start(f32[6,160,64]{2,1,0:T(8,128)S(1)} %get-tuple-element.29), channel_id=1, source_target_pairs={{0,1},{1,2},{2,3},{3,4},{4,5},{5,6},{6,7},{7,8},{8,9},{9,10},{10,1... | collective-permute-start | bytes 737288 | tf_op jit(solution)/shard_map/ppermute | solution.py:168
  130.2 3.8 %collective-permute-done.8 = f32[6,160,64]{2,1,0:T(8,128)S(1)} collective-permute-done((f32[6,160,64]{2,1,0:T(8,128)S(1)}, f32[6,160,64]{2,1,0:T(8,128)S(1)}, u32[]{:S(2)}, u32[]{:S(2)}) %collective-permute-start.8) | collective-permute-done | bytes 245792 | tf_op jit(solution)/shard_map/ppermute | solution.py:168
  134.0 5.6 %collective-permute-done.9 = f32[6,160,64]{2,1,0:T(8,128)S(1)} collective-permute-done((f32[6,160,64]{2,1,0:T(8,128)S(1)}, f32[6,160,64]{2,1,0:T(8,128)S(1)}, u32[]{:S(2)}, u32[]{:S(2)}) %collective-permute-start.9) | collective-permute-done | bytes 245792 | tf_op jit(solution)/shard_map/ppermute | solution.py:169
  141.7 13.7 %shard_map.76 = f32[3,160,256]{2,1,0:T(8,128)} custom-call(f32[3,160,256]{2,1,0:T(8,128)} %get-tuple-element.28.moving_ref, f32[3,160,256]{2,1,0:T(8,128)} %get-tuple-element.27.fixed_ref, f32[8,256]{1,0:T(8,128)} %broadcast_in_dim.2.coriolis_ref), custom_call_target="tpu_custom_call" | custom-call | flops 52428800 | bytes 1474560 | tf_op jit(solution)/shard_map/pallas_call | solution.py:234
  161.9 4.4 %copy.19 = f32[4,64,32,128]{3,2,1,0:T(8,128)} copy(f32[4,64,32,128]{3,1,2,0:T(8,128)S(1)} %pad_maximum_fusion.11) | data formatting | bytes 8388608
  (68 shorter events, 31.1 us)
Async XLA Ops:
  1.5 13.6 %copy-start.6 = (s32[32,128]{1,0:T(8,128)S(1)}, s32[32,128]{1,0:T(8,128)}, u32[]{:S(2)}) copy-start(s32[32,128]{1,0:T(8,128)} %param.6) | copy-start | bytes 49156
  1.5 14.2 %copy-start.10 = (f32[2,32,128]{2,1,0:T(8,128)S(1)}, f32[2,32,128]{2,1,0:T(8,128)}, u32[]{:S(2)}) copy-start(f32[2,32,128]{2,1,0:T(8,128)} %param.9) | copy-start | bytes 98308
  1.5 14.2 %copy-start.11 = (f32[32,128]{1,0:T(8,128)S(1)}, f32[32,128]{1,0:T(8,128)}, u32[]{:S(2)}) copy-start(f32[32,128]{1,0:T(8,128)} %param.8) | copy-start | bytes 49156
  6.1 2.0 %copy-start = (f32[4,64,32,128]{3,1,2,0:T(8,128)}, f32[4,64,32,128]{3,1,2,0:T(8,128)S(1)}, u32[]{:S(2)}) copy-start(f32[4,64,32,128]{3,1,2,0:T(8,128)S(1)} %copy_multiply_fusion) | copy-start | bytes 12582916
  8.2 9.9 %collective-permute-start = (f32[4,64,2,128]{3,1,2,0:T(8,128)S(1)}, f32[4,64,2,128]{3,1,2,0:T(8,128)S(1)}, u32[]{:S(2)}, u32[]{:S(2)}) collective-permute-start(f32[4,64,2,128]{3,1,2,0:T(8,128)S(1)} %get-tuple-element.26), channel_id=1, source_target_pairs={{16,0},{32,16},{48,32},{64,48},{80,64},{96,80},{112,96},{128,112},... | collective-permute-start | bytes 786440 | tf_op jit(solution)/shard_map/ppermute | solution.py:33
  13.1 10.9 %collective-permute-start.1 = (f32[4,64,2,128]{3,1,2,0:T(8,128)S(1)}, f32[4,64,2,128]{3,1,2,0:T(8,128)S(1)}, u32[]{:S(2)}, u32[]{:S(2)}) collective-permute-start(f32[4,64,2,128]{3,1,2,0:T(8,128)S(1)} %get-tuple-element.25), channel_id=1, source_target_pairs={{0,16},{16,32},{32,48},{48,64},{64,80},{80,96},{96,112},{112,128},... | collective-permute-start | bytes 786440 | tf_op jit(solution)/shard_map/ppermute | solution.py:31
  24.0 2.7 %copy-start.5 = (f32[4,64,2,128]{3,1,2,0:T(8,128)}, f32[4,64,2,128]{3,1,2,0:T(8,128)S(1)}, u32[]{:S(2)}) copy-start(f32[4,64,2,128]{3,1,2,0:T(8,128)S(1)} %collective-permute-done.1) | copy-start | bytes 786436
  35.1 11.9 %collective-permute-start.2 = (f32[4,64,36,2]{1,0,3,2:T(4,128)S(1)}, f32[4,64,36,2]{1,0,3,2:T(4,128)S(1)}, u32[]{:S(2)}, u32[]{:S(2)}) collective-permute-start(f32[4,64,36,2]{1,0,3,2:T(4,128)S(1)} %copy.12), channel_id=1, source_target_pairs={{1,0},{2,1},{3,2},{4,3},{5,4},{6,5},{7,6},{8,7},{9,8},{10,9},{11,1... | collective-permute-start | bytes 221192 | tf_op jit(solution)/shard_map/ppermute | solution.py:33
  42.1 7.9 %collective-permute-start.3 = (f32[4,64,36,2]{1,0,3,2:T(4,128)S(1)}, f32[4,64,36,2]{1,0,3,2:T(4,128)S(1)}, u32[]{:S(2)}, u32[]{:S(2)}) collective-permute-start(f32[4,64,36,2]{1,0,3,2:T(4,128)S(1)} %copy.14), channel_id=1, source_target_pairs={{0,1},{1,2},{2,3},{3,4},{4,5},{5,6},{6,7},{7,8},{8,9},{9,10},{10,1... | collective-permute-start | bytes 221192 | tf_op jit(solution)/shard_map/ppermute | solution.py:31
  50.0 13.8 %slice-start = ((s8[4718592]{0:T(1024)(128)(4,1)}), s8[524288]{0:T(1024)(128)(4,1)S(1)}, s32[]{:S(2)}) async-start(s8[4718592]{0:T(1024)(128)(4,1)} %bitcast.65), calls=%async_computation | async-start | bytes 1048576
  53.0 6.8 %copy-start.1 = (f32[4,64,32,128]{3,1,2,0:T(8,128)S(1)}, f32[4,64,32,128]{3,1,2,0:T(8,128)}, u32[]{:S(2)}) copy-start(f32[4,64,32,128]{3,1,2,0:T(8,128)} %copy-done) | copy-start | bytes 12582916
  53.0 10.8 %slice-start.1 = ((s8[4718592]{0:T(1024)(128)(4,1)}), s8[4194304]{0:T(1024)(128)(4,1)S(1)}, s32[]{:S(2)}) async-start(s8[4718592]{0:T(1024)(128)(4,1)} %bitcast.65), calls=%async_computation.1 | async-start | bytes 8388608
  63.8 12.6 %copy-start.7 = (f32[4,64,64]{2,1,0:T(8,128)S(1)}, f32[4,64,64]{2,1,0:T(8,128)}, u32[]{:S(2)}) copy-start(f32[4,64,64]{2,1,0:T(8,128)} %param.7) | copy-start | bytes 196612
  86.0 5.5 %copy-start.2 = (f32[4,64,32,128]{3,2,1,0:T(8,128)S(1)}, f32[4,64,32,128]{3,2,1,0:T(8,128)}, u32[]{:S(2)}) copy-start(f32[4,64,32,128]{3,2,1,0:T(8,128)} %param.5) | copy-start | bytes 12582916
  86.0 5.5 %copy-start.4 = (f32[64,32,128]{2,0,1:T(8,128)S(1)}, f32[64,32,128]{2,0,1:T(8,128)}, u32[]{:S(2)}) copy-start(f32[64,32,128]{2,0,1:T(8,128)} %broadcast_subtract_fusion) | copy-start | bytes 3145732
  86.0 5.5 %copy-start.8 = (f32[32,128]{1,0:T(8,128)S(1)}, f32[32,128]{1,0:T(8,128)}, u32[]{:S(2)}) copy-start(f32[32,128]{1,0:T(8,128)} %get-tuple-element.34) | copy-start | bytes 49156
  86.0 5.5 %copy-start.9 = (f32[32,128]{1,0:T(8,128)S(1)}, f32[32,128]{1,0:T(8,128)}, u32[]{:S(2)}) copy-start(f32[32,128]{1,0:T(8,128)} %get-tuple-element.35) | copy-start | bytes 49156
  101.7 21.1 %copy-start.3 = (f32[4,64,32,128]{3,1,2,0:T(8,128)}, f32[4,64,32,128]{3,1,2,0:T(8,128)S(1)}, u32[]{:S(2)}) copy-start(f32[4,64,32,128]{3,1,2,0:T(8,128)S(1)} %fusion.12) | copy-start | bytes 12582916
  105.7 13.0 %collective-permute-start.4 = (f32[6,32,128]{2,1,0:T(8,128)S(1)}, f32[6,32,128]{2,1,0:T(8,128)S(1)}, u32[]{:S(2)}, u32[]{:S(2)}) collective-permute-start(f32[6,32,128]{2,1,0:T(8,128)S(1)} %pad_maximum_fusion.20), channel_id=1, source_target_pairs={{0,32},{16,48},{32,64},{48,80},{64,96},{80,112},{96,128},{112,144}... | collective-permute-start | bytes 294920 | tf_op jit(solution)/shard_map/ppermute | solution.py:168
  107.6 11.1 %collective-permute-start.5 = (f32[6,32,128]{2,1,0:T(8,128)S(1)}, f32[6,32,128]{2,1,0:T(8,128)S(1)}, u32[]{:S(2)}, u32[]{:S(2)}) collective-permute-start(f32[6,32,128]{2,1,0:T(8,128)S(1)} %pad_maximum_fusion.20), channel_id=1, source_target_pairs={{0,16},{16,32},{32,48},{48,64},{64,80},{80,96},{96,112},{112,128},... | collective-permute-start | bytes 294920 | tf_op jit(solution)/shard_map/ppermute | solution.py:168
  109.5 9.2 %collective-permute-start.6 = (f32[6,32,128]{2,1,0:T(8,128)S(1)}, f32[6,32,128]{2,1,0:T(8,128)S(1)}, u32[]{:S(2)}, u32[]{:S(2)}) collective-permute-start(f32[6,32,128]{2,1,0:T(8,128)S(1)} %pad_maximum_fusion.20), channel_id=1, source_target_pairs={{16,0},{32,16},{48,32},{64,48},{80,64},{96,80},{112,96},{128,112},... | collective-permute-start | bytes 294920 | tf_op jit(solution)/shard_map/ppermute | solution.py:169
  115.0 7.6 %collective-permute-start.7 = (f32[6,32,128]{2,1,0:T(8,128)S(1)}, f32[6,32,128]{2,1,0:T(8,128)S(1)}, u32[]{:S(2)}, u32[]{:S(2)}) collective-permute-start(f32[6,32,128]{2,1,0:T(8,128)S(1)} %pad_maximum_fusion.20), channel_id=1, source_target_pairs={{32,0},{48,16},{64,32},{80,48},{96,64},{112,80},{128,96},{144,112}... | collective-permute-start | bytes 294920 | tf_op jit(solution)/shard_map/ppermute | solution.py:169
  122.8 11.2 %collective-permute-start.8 = (f32[6,160,64]{2,1,0:T(8,128)S(1)}, f32[6,160,64]{2,1,0:T(8,128)S(1)}, u32[]{:S(2)}, u32[]{:S(2)}) collective-permute-start(f32[6,160,64]{2,1,0:T(8,128)S(1)} %get-tuple-element.29), channel_id=1, source_target_pairs={{0,1},{1,2},{2,3},{3,4},{4,5},{5,6},{6,7},{7,8},{8,9},{9,10},{10,1... | collective-permute-start | bytes 737288 | tf_op jit(solution)/shard_map/ppermute | solution.py:168
  128.3 11.4 %collective-permute-start.9 = (f32[6,160,64]{2,1,0:T(8,128)S(1)}, f32[6,160,64]{2,1,0:T(8,128)S(1)}, u32[]{:S(2)}, u32[]{:S(2)}) collective-permute-start(f32[6,160,64]{2,1,0:T(8,128)S(1)} %get-tuple-element.30), channel_id=1, source_target_pairs={{1,0},{2,1},{3,2},{4,3},{5,4},{6,5},{7,6},{8,7},{9,8},{10,9},{11,1... | collective-permute-start | bytes 737288 | tf_op jit(solution)/shard_map/ppermute | solution.py:169

commit v3 on v2

--- a/solution.py
+++ b/solution.py
@@ -37,6 +37,28 @@
     return cells
 
 
+def cross_halo(cells, x_axis, x_dim, y_axis, y_dim, width):
+    pieces = []
+    for axis, dim in ((x_axis, x_dim), (y_axis, y_dim)):
+        count = lax.axis_size(axis)
+        ends = count - 1
+        head = lax.slice_in_dim(cells, 0, width, axis=dim)
+        tail = lax.slice_in_dim(cells, cells.shape[dim] - width, cells.shape[dim], axis=dim)
+        pieces.append(
+            (
+                lax.ppermute(tail, axis, [(i, (i + 1) % count) for i in range(ends)]),
+                lax.ppermute(head, axis, [((i + 1) % count, i) for i in range(ends)]),
+            )
+        )
+    (west, east), (south, north) = pieces
+    cells = jnp.concatenate([west, cells, east], axis=x_dim)
+    rim = [(0, 0)] * cells.ndim
+    rim[x_dim] = (width, width)
+    south = jnp.pad(south, rim)
+    north = jnp.pad(north, rim)
+    return jnp.concatenate([south, cells, north], axis=y_dim)
+
+
 def x_fourth(values):
     return (
         8.0 * (values[..., 3:-1, 2:-2] - values[..., 1:-3, 2:-2])
@@ -86,12 +108,16 @@
     )
     tendency = tendency + extra
     provisional = active * (center + STEP_TIME * tendency)
+    classes = inverse.shape[0]
+    levels_out = inverse.shape[1]
+    stacked = inverse.reshape(classes * levels_out, inverse.shape[2])
+    every = jnp.einsum(
+        "kl,flxy->fkxy", stacked, provisional, precision=lax.Precision.HIGHEST
+    )
     solved = jnp.zeros_like(provisional)
-    for class_index in range(inverse.shape[0]):
+    for class_index in range(classes):
         chosen = (depth_class == class_index + 1).astype(jnp.float32)
-        solved = solved + chosen * jnp.einsum(
-            "kl,flxy->fkxy", inverse[class_index], provisional, precision=lax.Precision.HIGHEST
-        )
+        solved = solved + chosen * every[:, class_index * levels_out : (class_index + 1) * levels_out]
     updated = active * solved + (1.0 - active) * state
     forcing = jnp.sum(active * tendency[2:4], axis=1) / levels
     return (updated, forcing)
@@ -249,7 +275,7 @@
     level_ids = lax.broadcasted_iota(jnp.int32, (levels, 1, 1), 0)
     active = (level_ids < depth_class[None] * level_block).astype(jnp.float32)
     masked = state * active[None]
-    padded = with_halo(masked, (("gx", 2), (("gy", "mode"), 3)), 2)
+    padded = cross_halo(masked, "gx", 2, ("gy", "mode"), 3, 2)
     column_blocks = lax.axis_size(("gy", "mode"))
     anchor = lax.axis_index(("gy", "mode")) * y_cells
     coriolis = coriolis_row(anchor, y_cells, y_cells * column_blocks)[0]

time: 167 us -> 163 us (0.976)
  matrix products: 32 us -> 22 us
  local copies, waits for them, and re-layouts: 28.1 us -> 38 us
  waiting for transfers between devices: 19.2 us -> 13.7 us
  other arithmetic: 36.5 us -> 39.7 us
    add x0 -> x2, other arithmetic: none -> 19.5 us  [the longest x1 11.5 us: baroclinic(): tendency = tendency + extra]
    mul x1 -> x0, other arithmetic: 12.6 us -> none  [baroclinic(): provisional = active * (center + STEP_TIME * tendency)]
    pad x0 -> x2, local copies, waits for them, and re-layouts: none -> 8.48 us  [the longest x1 5.26 us: cross_halo(): north = jnp.pad(north, rim)]
    dot_general x4 -> x1, matrix products: 25.2 us -> 19.2 us  [baroclinic(): jnp.einsum('kl,flxy->fkxy', stacked, provisional, precision=lax.Precision...]
    ppermute x4, waiting for transfers between devices: 5.96 us -> 0.01 us  [the longest x2 0.01 us: cross_halo(): lax.ppermute(head, axis, [((i + 1) % count, i) for i in range(ends)])]
    dot_general x1, matrix products: 6.77 us -> 2.79 us  [body(): jnp.einsum('kl,lxy->kxy', lower_ones, density, precision=lax.Precision.HI...]
    concatenate x1 -> x0, other arithmetic: 2.66 us -> none  [with_halo(): jnp.concatenate([lax.ppermute(tail, axis, [(i, (i + 1) % count) for i in...]
    unnamed x32 -> x34, local copies, waits for them, and re-layouts: 6.54 us -> 7.68 us
  transfers between devices with their start and end apart: 10 -> 10, of which waited for: 5 -> 3; matrix products, arithmetic and copies ran while one was open for 6% -> 13% of each run, Pallas kernels for 0% -> 0%
where the time goes in v3:
time: 163 us; the launch traced here: 162 us
  other arithmetic  39.7 us (24%)
  local copies, waits for them, and re-layouts  38 us (23%)
  starting transfers between devices  34.4 us (21%)
  matrix products  22 us (13%)
  waiting for transfers between devices  13.7 us (8%)
  Pallas kernels  13.5 us (8%)
    dot_general x1, matrix products, baroclinic(): jnp.einsum('kl,flxy->fkxy', stacked, provisional, precision=lax.Precision...  19.2 us
    pallas_call x1, Pallas kernels, local_waves(): pl.pallas_call(wave_kernel, out_shape=jax.ShapeDtypeStruct(moving.shape,...  13.5 us
    add x1, other arithmetic, baroclinic(): tendency = tendency + extra  11.5 us
    ppermute x3, starting transfers between devices, wide_halo(): lax.ppermute(head, axis, [(i + hop, i) for i in range(count - hop)])  10.5 us
    ppermute x3, waiting for transfers between devices, wide_halo(): lax.ppermute(head, axis, [(i + hop, i) for i in range(count - hop)])  9.58 us
    ppermute x3, starting transfers between devices, wide_halo(): lax.ppermute(tail, axis, [(i, i + hop) for i in range(count - hop)])  9.48 us
    add x1, other arithmetic, baroclinic(): updated = active * solved + (1.0 - active) * state  8.01 us
    slice x2, local copies, waits for them, and re-layouts, cross_halo(): head = lax.slice_in_dim(cells, 0, width, axis=dim)  7.69 us
  transfers between devices with their start and end apart: 10, of which 3 were waited for; matrix products, arithmetic and copies ran while one was open for 13% of the time, Pallas kernels for 0%

profile of v3, /device:TPU:103, one launch (start us, length us, event | category | flops | bytes accessed | tf_op | source)
XLA Modules:
  0.0 162.3 jit_solution(5401865056288235081)
XLA Ops:
  1.5 4.6 %copy_multiply_fusion = f32[4,64,32,128]{3,1,2,0:T(8,128)S(1)} fusion(f32[4,64,32,128]{3,2,1,0:T(8,128)} %param.5, f32[64,32,128]{2,0,1:T(8,128)S(1)} %fusion.54), kind=kLoop, calls=%fused_computation.40 | loop fusion | flops 1048576 | bytes 9437184 | tf_op jit(solution)/shard_map/mul | solution.py:277
  6.2 4.7 %fusion.64 = (f32[4,64,32,2]{3,1,2,0:T(8,128)}, f32[4,64,32,2]{3,1,2,0:T(8,128)}) fusion(f32[4,64,32,128]{3,1,2,0:T(8,128)S(1)} %copy_multiply_fusion), kind=kLoop, calls=%fused_computation.120 | loop fusion | bytes 262144 | tf_op jit(solution)/shard_map/slice | solution.py:45
  10.9 3.0 %copy.14 = f32[4,64,32,2]{1,2,3,0:T(8,128)S(1)} copy(f32[4,64,32,2]{3,1,2,0:T(8,128)} %get-tuple-element.21) | data formatting | bytes 131072 | tf_op jit(solution)/shard_map/slice | solution.py:45
  16.6 3.0 %copy.16 = f32[4,64,32,2]{1,2,3,0:T(8,128)S(1)} copy(f32[4,64,32,2]{3,1,2,0:T(8,128)} %get-tuple-element.22) | data formatting | bytes 131072 | tf_op jit(solution)/shard_map/slice | solution.py:46
  19.6 4.7 %collective-permute-start.3 = (f32[4,64,32,2]{1,2,3,0:T(8,128)S(1)}, f32[4,64,32,2]{1,2,3,0:T(8,128)S(1)}, u32[]{:S(2)}, u32[]{:S(2)}) collective-permute-start(f32[4,64,32,2]{1,2,3,0:T(8,128)S(1)} %copy.16), channel_id=1, source_target_pairs={{0,1},{1,2},{2,3},{3,4},{4,5},{5,6},{6,7},{7,8},{8,9},{9,10},{10,1... | collective-permute-start | bytes 196616 | tf_op jit(solution)/shard_map/ppermute | solution.py:49
  25.3 4.9 %collective-permute-start = (f32[4,64,2,128]{3,1,2,0:T(8,128)S(1)}, f32[4,64,2,128]{3,1,2,0:T(8,128)S(1)}, u32[]{:S(2)}, u32[]{:S(2)}) collective-permute-start(f32[4,64,2,128]{3,1,2,0:T(8,128)S(1)} %get-tuple-element.24), channel_id=1, source_target_pairs={{16,0},{32,16},{48,32},{64,48},{80,64},{96,80},{112,96},{128,112},... | collective-permute-start | bytes 786440 | tf_op jit(solution)/shard_map/ppermute | solution.py:50
  35.3 2.7 %copy.15 = f32[4,64,32,2]{3,1,2,0:T(8,128)} copy(f32[4,64,32,2]{1,2,3,0:T(8,128)S(1)} %collective-permute-done.2) | data formatting | bytes 131072 | tf_op jit(solution)/shard_map/ppermute | solution.py:50
  38.0 5.3 %pad.7 = f32[4,64,36,2]{3,1,2,0:T(8,128)} pad(f32[4,64,32,2]{3,1,2,0:T(8,128)} %copy.15, f32[]{:T(128)} %constant.29.clone.1), padding=0_0x0_0x2_2x0_0 | pad | bytes 139268 | tf_op jit(solution)/shard_map/jit(_pad)/pad | solution.py:58
  46.0 3.2 %pad.8 = f32[4,64,36,2]{3,1,2,0:T(8,128)S(1)} pad(f32[4,64,32,2]{3,1,2,0:T(8,128)} %copy.17, f32[]{:T(128)} %constant.29.clone.1), padding=0_0x0_0x2_2x0_0 | pad | bytes 139268 | tf_op jit(solution)/shard_map/jit(_pad)/pad | solution.py:57
  52.4 2.8 %fusion.37 = f32[64,36,132]{2,0,1:T(8,128)S(1)} fusion(f32[4,64,36,2]{3,1,2,0:T(8,128)S(1)} %copy-done.4, f32[4,64,36,2]{3,1,2,0:T(8,128)S(1)} %pad.8, f32[4,64,2,128]{3,1,2,0:T(8,128)S(1)} %collective-permute-done, f32[4,64,32,128]{3,1,2,0:T(8,128)S(1)} %copy-done.3, f32[4,64,2,128]{3,1,2,0:T(8,128)S(1)} %collective-permute-done.1), kind=kOutput, calls=%fused_computation.65 | convolution fusion | flops 237223936 | bytes 6082560 | tf_op jit(solution)/shard_map/kl,lxy->kxy/dot_general | solution.py:289
  55.2 4.5 %fusion.55 = (f32[64,32,128]{2,0,1:T(8,128)}, f32[64,32,128]{2,0,1:T(8,128)}, f32[1,64,32,128]{3,1,2,0:T(8,128)}, f32[1,64,32,128]{3,1,2,0:T(8,128)}) fusion(f32[4,64,32,128]{3,1,2,0:T(8,128)S(1)} %copy-done.3, f32[128]{0:T(128)} %multiply_add_fusion.2, f32[64,36,132]{2,0,1:T(8,128)S(1)} %fusion.37), kind=kLoop, calls=%fused_computation.88 | loop fusion | flops 4718592 | bytes 14680576 | tf_op jit(solution)/shard_map/mul | solution.py:97
  59.7 11.5 %fusion.13 = f32[4,64,32,128]{3,1,2,0:T(8,128)} fusion(f32[4,64,36,2]{3,1,2,0:T(8,128)} %copy-done.5, f32[4,64,2,128]{3,1,2,0:T(8,128)S(1)} %collective-permute-done, f32[4,64,32,128]{3,1,2,0:T(8,128)S(1)} %copy-done.3, f32[4,64,2,128]{3,1,2,0:T(8,128)S(1)} %collective-permute-done.1, f32[4,64,36,2]{3,1,2,0:T(8,128)S(1)} %copy-done.4, ...), kind=kLoop, calls=%fused_computation.23 | loop fusion | flops 39845888 | bytes 13254672 | tf_op jit(solution)/shard_map/add | solution.py:109
  71.2 19.2 %convolution_bitcast_fusion = f32[4,256,32,128]{3,1,2,0:T(8,128)S(1)} fusion(f32[256,64,1,1]{1,0,3,2:T(8,128)S(1)} %bitcast.35, f32[4,64,32,128]{3,1,2,0:T(8,128)} %fusion.13, f32[64,32,128]{2,0,1:T(8,128)S(1)} %fusion.54, f32[4,64,32,128]{3,2,1,0:T(8,128)} %param.5), kind=kOutput, calls=%fused_computation | convolution fusion | flops 3225419776 | bytes 26279936 | tf_op jit(solution)/shard_map/kl,flxy->fkxy/dot_general | solution.py:114
  90.5 8.0 %fusion.4 = f32[4,64,32,128]{3,1,2,0:T(8,128)} fusion(f32[4,256,32,128]{3,1,2,0:T(8,128)S(1)} %convolution_bitcast_fusion, f32[4,64,32,128]{3,2,1,0:T(8,128)S(1)} %copy-done.6, f32[64,32,128]{2,0,1:T(8,128)} %broadcast_subtract_fusion, f32[32,128]{1,0:T(8,128)S(1)} %copy-done.9, f32[32,128]{1,0:T(8,128)S(1)} %copy-done.10, f32[32,128]{1,0:T(8,128)S(1)} %copy-done.11, ...), kind=kLoop, calls=%fused_computation.10 | loop fusion | flops 10485760 | bytes 27328512 | tf_op jit(solution)/shard_map/add | solution.py:121
  101.0 3.3 %collective-permute-start.4 = (f32[6,32,128]{2,1,0:T(8,128)S(1)}, f32[6,32,128]{2,1,0:T(8,128)S(1)}, u32[]{:S(2)}, u32[]{:S(2)}) collective-permute-start(f32[6,32,128]{2,1,0:T(8,128)S(1)} %pad_maximum_fusion.19), channel_id=1, source_target_pairs={{0,32},{16,48},{32,64},{48,80},{64,96},{80,112},{96,128},{112,144}... | collective-permute-start | bytes 294920 | tf_op jit(solution)/shard_map/ppermute | solution.py:194
  106.2 5.5 %collective-permute-start.6 = (f32[6,32,128]{2,1,0:T(8,128)S(1)}, f32[6,32,128]{2,1,0:T(8,128)S(1)}, u32[]{:S(2)}, u32[]{:S(2)}) collective-permute-start(f32[6,32,128]{2,1,0:T(8,128)S(1)} %pad_maximum_fusion.19), channel_id=1, source_target_pairs={{16,0},{32,16},{48,32},{64,48},{80,64},{96,80},{112,96},{128,112},... | collective-permute-start | bytes 294920 | tf_op jit(solution)/shard_map/ppermute | solution.py:195
  111.7 3.1 %collective-permute-start.7 = (f32[6,32,128]{2,1,0:T(8,128)S(1)}, f32[6,32,128]{2,1,0:T(8,128)S(1)}, u32[]{:S(2)}, u32[]{:S(2)}) collective-permute-start(f32[6,32,128]{2,1,0:T(8,128)S(1)} %pad_maximum_fusion.19), channel_id=1, source_target_pairs={{32,0},{48,16},{64,32},{80,48},{96,64},{112,80},{128,96},{144,112}... | collective-permute-start | bytes 294920 | tf_op jit(solution)/shard_map/ppermute | solution.py:195
  114.9 4.3 %collective-permute-done.7 = f32[6,32,128]{2,1,0:T(8,128)S(1)} collective-permute-done((f32[6,32,128]{2,1,0:T(8,128)S(1)}, f32[6,32,128]{2,1,0:T(8,128)S(1)}, u32[]{:S(2)}, u32[]{:S(2)}) %collective-permute-start.7) | collective-permute-done | bytes 98336 | tf_op jit(solution)/shard_map/ppermute | solution.py:195
  120.2 4.3 %collective-permute-start.8 = (f32[6,160,64]{2,1,0:T(8,128)}, f32[6,160,64]{2,1,0:T(8,128)S(1)}, u32[]{:S(2)}, u32[]{:S(2)}) collective-permute-start(f32[6,160,64]{2,1,0:T(8,128)} %get-tuple-element.27), channel_id=1, source_target_pairs={{0,1},{1,2},{2,3},{3,4},{4,5},{5,6},{6,7},{7,8},{8,9},{9,10},{10,1... | collective-permute-start | bytes 737288 | tf_op jit(solution)/shard_map/ppermute | solution.py:194
  126.4 4.1 %collective-permute-done.8 = f32[6,160,64]{2,1,0:T(8,128)S(1)} collective-permute-done((f32[6,160,64]{2,1,0:T(8,128)}, f32[6,160,64]{2,1,0:T(8,128)S(1)}, u32[]{:S(2)}, u32[]{:S(2)}) %collective-permute-start.8) | collective-permute-done | bytes 245792 | tf_op jit(solution)/shard_map/ppermute | solution.py:194
  130.6 5.3 %collective-permute-done.9 = f32[6,160,64]{2,1,0:T(8,128)S(1)} collective-permute-done((f32[6,160,64]{2,1,0:T(8,128)S(1)}, f32[6,160,64]{2,1,0:T(8,128)S(1)}, u32[]{:S(2)}, u32[]{:S(2)}) %collective-permute-start.9) | collective-permute-done | bytes 245792 | tf_op jit(solution)/shard_map/ppermute | solution.py:195
  137.9 13.5 %shard_map.76 = f32[3,160,256]{2,1,0:T(8,128)} custom-call(f32[3,160,256]{2,1,0:T(8,128)} %get-tuple-element.26.moving_ref, f32[3,160,256]{2,1,0:T(8,128)} %get-tuple-element.25.fixed_ref, f32[8,256]{1,0:T(8,128)} %broadcast_in_dim.2.coriolis_ref), custom_call_target="tpu_custom_call" | custom-call | flops 52428800 | bytes 1474560 | tf_op jit(solution)/shard_map/pallas_call | solution.py:260
  154.3 2.9 %fusion.63 = (f32[2,64,32,128]{3,1,2,0:T(8,128)S(1)}, f32[2,64,32,128]{3,1,2,0:T(8,128)S(1)}) fusion(f32[4,64,32,128]{3,1,2,0:T(8,128)} %fusion.4, f32[2,32,128]{2,1,0:T(8,128)S(1)} %get-tuple-element.11, f32[64,32,128]{2,0,1:T(8,128)S(1)} %fusion.54), kind=kLoop, calls=%fused_computation.119 | loop fusion | flops 1048576 | bytes 9469952 | tf_op jit(solution)/shard_map/slice | solution.py:181
  157.8 4.4 %copy.21 = f32[4,64,32,128]{3,2,1,0:T(8,128)} copy(f32[4,64,32,128]{3,1,2,0:T(8,128)S(1)} %pad_maximum_fusion.10) | data formatting | bytes 8388608
  (68 shorter events, 28.5 us)
Async XLA Ops:
  0.6 70.5 %copy-start = (f32[4,64,64]{2,1,0:T(8,128)S(1)}, f32[4,64,64]{2,1,0:T(8,128)}, u32[]{:S(2)}) copy-start(f32[4,64,64]{2,1,0:T(8,128)} %param.7) | copy-start | bytes 196612
  6.2 4.7 %copy-start.2 = (f32[4,64,32,128]{3,1,2,0:T(8,128)}, f32[4,64,32,128]{3,1,2,0:T(8,128)S(1)}, u32[]{:S(2)}) copy-start(f32[4,64,32,128]{3,1,2,0:T(8,128)S(1)} %copy_multiply_fusion) | copy-start | bytes 12582916
  10.9 21.5 %copy-start.8 = (s32[32,128]{1,0:T(8,128)S(1)}, s32[32,128]{1,0:T(8,128)}, u32[]{:S(2)}) copy-start(s32[32,128]{1,0:T(8,128)} %param.6) | copy-start | bytes 49156
  13.9 20.8 %copy-start.13 = (f32[2,32,128]{2,1,0:T(8,128)S(1)}, f32[2,32,128]{2,1,0:T(8,128)}, u32[]{:S(2)}) copy-start(f32[2,32,128]{2,1,0:T(8,128)} %param.9) | copy-start | bytes 98308
  13.9 20.8 %copy-start.14 = (f32[32,128]{1,0:T(8,128)S(1)}, f32[32,128]{1,0:T(8,128)}, u32[]{:S(2)}) copy-start(f32[32,128]{1,0:T(8,128)} %param.8) | copy-start | bytes 49156
  13.9 21.4 %collective-permute-start.2 = (f32[4,64,32,2]{1,2,3,0:T(8,128)S(1)}, f32[4,64,32,2]{1,2,3,0:T(8,128)S(1)}, u32[]{:S(2)}, u32[]{:S(2)}) collective-permute-start(f32[4,64,32,2]{1,2,3,0:T(8,128)S(1)} %copy.14), channel_id=1, source_target_pairs={{1,0},{2,1},{3,2},{4,3},{5,4},{6,5},{7,6},{8,7},{9,8},{10,9},{11,1... | collective-permute-start | bytes 196616 | tf_op jit(solution)/shard_map/ppermute | solution.py:50
  19.6 23.7 %collective-permute-start.3 = (f32[4,64,32,2]{1,2,3,0:T(8,128)S(1)}, f32[4,64,32,2]{1,2,3,0:T(8,128)S(1)}, u32[]{:S(2)}, u32[]{:S(2)}) collective-permute-start(f32[4,64,32,2]{1,2,3,0:T(8,128)S(1)} %copy.16), channel_id=1, source_target_pairs={{0,1},{1,2},{2,3},{3,4},{4,5},{5,6},{6,7},{7,8},{8,9},{9,10},{10,1... | collective-permute-start | bytes 196616 | tf_op jit(solution)/shard_map/ppermute | solution.py:49
  25.3 23.9 %collective-permute-start = (f32[4,64,2,128]{3,1,2,0:T(8,128)S(1)}, f32[4,64,2,128]{3,1,2,0:T(8,128)S(1)}, u32[]{:S(2)}, u32[]{:S(2)}) collective-permute-start(f32[4,64,2,128]{3,1,2,0:T(8,128)S(1)} %get-tuple-element.24), channel_id=1, source_target_pairs={{16,0},{32,16},{48,32},{64,48},{80,64},{96,80},{112,96},{128,112},... | collective-permute-start | bytes 786440 | tf_op jit(solution)/shard_map/ppermute | solution.py:50
  30.2 19.0 %collective-permute-start.1 = (f32[4,64,2,128]{3,1,2,0:T(8,128)S(1)}, f32[4,64,2,128]{3,1,2,0:T(8,128)S(1)}, u32[]{:S(2)}, u32[]{:S(2)}) collective-permute-start(f32[4,64,2,128]{3,1,2,0:T(8,128)S(1)} %get-tuple-element.23), channel_id=1, source_target_pairs={{0,16},{16,32},{32,48},{48,64},{64,80},{80,96},{96,112},{112,128},... | collective-permute-start | bytes 786440 | tf_op jit(solution)/shard_map/ppermute | solution.py:49
  46.0 5.6 %copy-start.3 = (f32[4,64,32,128]{3,1,2,0:T(8,128)S(1)}, f32[4,64,32,128]{3,1,2,0:T(8,128)}, u32[]{:S(2)}) copy-start(f32[4,64,32,128]{3,1,2,0:T(8,128)} %copy-done.2) | copy-start | bytes 12582916
  46.0 6.4 %copy-start.4 = (f32[4,64,36,2]{3,1,2,0:T(8,128)S(1)}, f32[4,64,36,2]{3,1,2,0:T(8,128)}, u32[]{:S(2)}) copy-start(f32[4,64,36,2]{3,1,2,0:T(8,128)} %pad.7) | copy-start | bytes 221188
  71.2 19.2 %copy-start.6 = (f32[4,64,32,128]{3,2,1,0:T(8,128)S(1)}, f32[4,64,32,128]{3,2,1,0:T(8,128)}, u32[]{:S(2)}) copy-start(f32[4,64,32,128]{3,2,1,0:T(8,128)} %param.5) | copy-start | bytes 12582916
  71.2 19.2 %copy-start.9 = (f32[32,128]{1,0:T(8,128)S(1)}, f32[32,128]{1,0:T(8,128)}, u32[]{:S(2)}) copy-start(f32[32,128]{1,0:T(8,128)} %get-tuple-element.30) | copy-start | bytes 49156
  71.2 19.2 %copy-start.10 = (f32[32,128]{1,0:T(8,128)S(1)}, f32[32,128]{1,0:T(8,128)}, u32[]{:S(2)}) copy-start(f32[32,128]{1,0:T(8,128)} %get-tuple-element.31) | copy-start | bytes 49156
  71.2 19.2 %copy-start.11 = (f32[32,128]{1,0:T(8,128)S(1)}, f32[32,128]{1,0:T(8,128)}, u32[]{:S(2)}) copy-start(f32[32,128]{1,0:T(8,128)} %get-tuple-element.32) | copy-start | bytes 49156
  71.2 19.2 %copy-start.12 = (f32[32,128]{1,0:T(8,128)S(1)}, f32[32,128]{1,0:T(8,128)}, u32[]{:S(2)}) copy-start(f32[32,128]{1,0:T(8,128)} %get-tuple-element.33) | copy-start | bytes 49156
  90.5 8.0 %copy-start.7 = (f32[4,64,32,128]{3,1,2,0:T(8,128)S(1)}, f32[4,64,32,128]{3,1,2,0:T(8,128)}, u32[]{:S(2)}) copy-start(f32[4,64,32,128]{3,1,2,0:T(8,128)} %fusion.13) | copy-start | bytes 12582916
  101.0 13.9 %collective-permute-start.4 = (f32[6,32,128]{2,1,0:T(8,128)S(1)}, f32[6,32,128]{2,1,0:T(8,128)S(1)}, u32[]{:S(2)}, u32[]{:S(2)}) collective-permute-start(f32[6,32,128]{2,1,0:T(8,128)S(1)} %pad_maximum_fusion.19), channel_id=1, source_target_pairs={{0,32},{16,48},{32,64},{48,80},{64,96},{80,112},{96,128},{112,144}... | collective-permute-start | bytes 294920 | tf_op jit(solution)/shard_map/ppermute | solution.py:194
  104.3 10.6 %collective-permute-start.5 = (f32[6,32,128]{2,1,0:T(8,128)S(1)}, f32[6,32,128]{2,1,0:T(8,128)S(1)}, u32[]{:S(2)}, u32[]{:S(2)}) collective-permute-start(f32[6,32,128]{2,1,0:T(8,128)S(1)} %pad_maximum_fusion.19), channel_id=1, source_target_pairs={{0,16},{16,32},{32,48},{48,64},{64,80},{80,96},{96,112},{112,128},... | collective-permute-start | bytes 294920 | tf_op jit(solution)/shard_map/ppermute | solution.py:194
  106.2 8.7 %collective-permute-start.6 = (f32[6,32,128]{2,1,0:T(8,128)S(1)}, f32[6,32,128]{2,1,0:T(8,128)S(1)}, u32[]{:S(2)}, u32[]{:S(2)}) collective-permute-start(f32[6,32,128]{2,1,0:T(8,128)S(1)} %pad_maximum_fusion.19), channel_id=1, source_target_pairs={{16,0},{32,16},{48,32},{64,48},{80,64},{96,80},{112,96},{128,112},... | collective-permute-start | bytes 294920 | tf_op jit(solution)/shard_map/ppermute | solution.py:195
  111.7 7.5 %collective-permute-start.7 = (f32[6,32,128]{2,1,0:T(8,128)S(1)}, f32[6,32,128]{2,1,0:T(8,128)S(1)}, u32[]{:S(2)}, u32[]{:S(2)}) collective-permute-start(f32[6,32,128]{2,1,0:T(8,128)S(1)} %pad_maximum_fusion.19), channel_id=1, source_target_pairs={{32,0},{48,16},{64,32},{80,48},{96,64},{112,80},{128,96},{144,112}... | collective-permute-start | bytes 294920 | tf_op jit(solution)/shard_map/ppermute | solution.py:195
  120.2 10.3 %collective-permute-start.8 = (f32[6,160,64]{2,1,0:T(8,128)}, f32[6,160,64]{2,1,0:T(8,128)S(1)}, u32[]{:S(2)}, u32[]{:S(2)}) collective-permute-start(f32[6,160,64]{2,1,0:T(8,128)} %get-tuple-element.27), channel_id=1, source_target_pairs={{0,1},{1,2},{2,3},{3,4},{4,5},{5,6},{6,7},{7,8},{8,9},{9,10},{10,1... | collective-permute-start | bytes 737288 | tf_op jit(solution)/shard_map/ppermute | solution.py:194
  124.5 11.4 %collective-permute-start.9 = (f32[6,160,64]{2,1,0:T(8,128)S(1)}, f32[6,160,64]{2,1,0:T(8,128)S(1)}, u32[]{:S(2)}, u32[]{:S(2)}) collective-permute-start(f32[6,160,64]{2,1,0:T(8,128)S(1)} %get-tuple-element.28), channel_id=1, source_target_pairs={{1,0},{2,1},{3,2},{4,3},{5,4},{6,5},{7,6},{8,7},{9,8},{10,9},{11,1... | collective-permute-start | bytes 737288 | tf_op jit(solution)/shard_map/ppermute | solution.py:195
  157.2 5.0 %copy-start.1 = (f32[4,64,64]{2,1,0:T(8,128)S(1)}, f32[4,64,64]{2,1,0:T(8,128)}, u32[]{:S(2)}) copy-start(f32[4,64,64]{2,1,0:T(8,128)} %param.7) | copy-start | bytes 196612
  (1 other events, 2.3 us)

commit v4 on v3

--- a/solution.py
+++ b/solution.py
@@ -109,15 +109,21 @@
     tendency = tendency + extra
     provisional = active * (center + STEP_TIME * tendency)
     classes = inverse.shape[0]
-    levels_out = inverse.shape[1]
-    stacked = inverse.reshape(classes * levels_out, inverse.shape[2])
-    every = jnp.einsum(
-        "kl,flxy->fkxy", stacked, provisional, precision=lax.Precision.HIGHEST
-    )
-    solved = jnp.zeros_like(provisional)
-    for class_index in range(classes):
-        chosen = (depth_class == class_index + 1).astype(jnp.float32)
-        solved = solved + chosen * every[:, class_index * levels_out : (class_index + 1) * levels_out]
+    band = levels // classes
+    stacked = jnp.concatenate(
+        [inverse[class_index, : band * (class_index + 1)] for class_index in range(classes)], axis=0
+    )
+    every = jnp.einsum("kl,flxy->fkxy", stacked, provisional, precision=lax.Precision.HIGH)
+    starts = [band * class_index * (class_index + 1) // 2 for class_index in range(classes)]
+    chosen = [(depth_class == class_index + 1).astype(jnp.float32) for class_index in range(classes)]
+    bands = []
+    for level_band in range(classes):
+        part = jnp.zeros_like(provisional[:, :band])
+        for class_index in range(level_band, classes):
+            first = starts[class_index] + level_band * band
+            part = part + chosen[class_index] * every[:, first : first + band]
+        bands.append(part)
+    solved = jnp.concatenate(bands, axis=1)
     updated = active * solved + (1.0 - active) * state
     forcing = jnp.sum(active * tendency[2:4], axis=1) / levels
     return (updated, forcing)

time: 163 us -> 151 us (0.926)
  matrix products: 22 us -> 12.3 us
  other arithmetic: 39.7 us -> 36.9 us
    dot_general x1, matrix products: 19.2 us -> 9.47 us  [baroclinic(): jnp.einsum('kl,flxy->fkxy', stacked, provisional, precision=lax.Precision...]
    add x1, other arithmetic: 8.01 us -> 4.72 us  [baroclinic(): updated = active * solved + (1.0 - active) * state]
    unnamed x34 -> x40, local copies, waits for them, and re-layouts: 7.68 us -> 8.39 us
  transfers between devices with their start and end apart: 10 -> 10, of which waited for: 3 -> 3; matrix products, arithmetic and copies ran while one was open for 13% -> 15% of each run, Pallas kernels for 0% -> 0%
where the time goes in v4:
time: 151 us; the launch traced here: 150 us
  local copies, waits for them, and re-layouts  38 us (25%)
  other arithmetic  36.9 us (24%)
  starting transfers between devices  34.4 us (23%)
  waiting for transfers between devices  13.7 us (9%)
  Pallas kernels  13.4 us (9%)
  matrix products  12.3 us (8%)
    pallas_call x1, Pallas kernels, local_waves(): pl.pallas_call(wave_kernel, out_shape=jax.ShapeDtypeStruct(moving.shape,...  13.4 us
    add x1, other arithmetic, baroclinic(): tendency = tendency + extra  11.6 us
    ppermute x3, starting transfers between devices, wide_halo(): lax.ppermute(head, axis, [(i + hop, i) for i in range(count - hop)])  10.5 us
    ppermute x3, waiting for transfers between devices, wide_halo(): lax.ppermute(head, axis, [(i + hop, i) for i in range(count - hop)])  10.2 us
    ppermute x3, starting transfers between devices, wide_halo(): lax.ppermute(tail, axis, [(i, i + hop) for i in range(count - hop)])  9.48 us
    dot_general x1, matrix products, baroclinic(): jnp.einsum('kl,flxy->fkxy', stacked, provisional, precision=lax.Precision...  9.47 us
    unnamed x40, local copies, waits for them, and re-layouts  8.39 us
    slice x2, local copies, waits for them, and re-layouts, cross_halo(): head = lax.slice_in_dim(cells, 0, width, axis=dim)  7.73 us
  transfers between devices with their start and end apart: 10, of which 3 were waited for; matrix products, arithmetic and copies ran while one was open for 15% of the time, Pallas kernels for 0%

profile of v4, /device:TPU:103, one launch (start us, length us, event | category | flops | bytes accessed | tf_op | source)
XLA Modules:
  0.0 149.8 jit_solution(5580011708676479005)
XLA Ops:
  2.1 4.6 %copy_multiply_fusion = f32[4,64,32,128]{3,1,2,0:T(8,128)S(1)} fusion(f32[4,64,32,128]{3,2,1,0:T(8,128)} %param.5, f32[64,32,128]{2,0,1:T(8,128)S(1)} %fusion.60), kind=kLoop, calls=%fused_computation.33 | loop fusion | flops 1048576 | bytes 9437184 | tf_op jit(solution)/shard_map/mul | solution.py:283
  6.7 4.7 %fusion.77 = (f32[4,64,32,2]{3,1,2,0:T(8,128)}, f32[4,64,32,2]{3,1,2,0:T(8,128)}) fusion(f32[4,64,32,128]{3,1,2,0:T(8,128)S(1)} %copy_multiply_fusion), kind=kLoop, calls=%fused_computation.138 | loop fusion | bytes 262144 | tf_op jit(solution)/shard_map/slice | solution.py:45
  11.5 3.0 %copy.16 = f32[4,64,32,2]{1,2,3,0:T(8,128)S(1)} copy(f32[4,64,32,2]{3,1,2,0:T(8,128)} %get-tuple-element.25) | data formatting | bytes 131072 | tf_op jit(solution)/shard_map/slice | solution.py:45
  17.2 3.0 %copy.18 = f32[4,64,32,2]{1,2,3,0:T(8,128)S(1)} copy(f32[4,64,32,2]{3,1,2,0:T(8,128)} %get-tuple-element.26) | data formatting | bytes 131072 | tf_op jit(solution)/shard_map/slice | solution.py:46
  20.2 4.7 %collective-permute-start.3 = (f32[4,64,32,2]{1,2,3,0:T(8,128)S(1)}, f32[4,64,32,2]{1,2,3,0:T(8,128)S(1)}, u32[]{:S(2)}, u32[]{:S(2)}) collective-permute-start(f32[4,64,32,2]{1,2,3,0:T(8,128)S(1)} %copy.18), channel_id=1, source_target_pairs={{0,1},{1,2},{2,3},{3,4},{4,5},{5,6},{6,7},{7,8},{8,9},{9,10},{10,1... | collective-permute-start | bytes 196616 | tf_op jit(solution)/shard_map/ppermute | solution.py:49
  25.9 4.9 %collective-permute-start = (f32[4,64,2,128]{3,1,2,0:T(8,128)S(1)}, f32[4,64,2,128]{3,1,2,0:T(8,128)S(1)}, u32[]{:S(2)}, u32[]{:S(2)}) collective-permute-start(f32[4,64,2,128]{3,1,2,0:T(8,128)S(1)} %get-tuple-element.28), channel_id=1, source_target_pairs={{16,0},{32,16},{48,32},{64,48},{80,64},{96,80},{112,96},{128,112},... | collective-permute-start | bytes 786440 | tf_op jit(solution)/shard_map/ppermute | solution.py:50
  36.8 2.7 %copy.17 = f32[4,64,32,2]{3,1,2,0:T(8,128)} copy(f32[4,64,32,2]{1,2,3,0:T(8,128)S(1)} %collective-permute-done.2) | data formatting | bytes 131072 | tf_op jit(solution)/shard_map/ppermute | solution.py:50
  39.5 5.3 %pad.7 = f32[4,64,36,2]{3,1,2,0:T(8,128)} pad(f32[4,64,32,2]{3,1,2,0:T(8,128)} %copy.17, f32[]{:T(128)} %constant.29.clone.1), padding=0_0x0_0x2_2x0_0 | pad | bytes 139268 | tf_op jit(solution)/shard_map/jit(_pad)/pad | solution.py:58
  47.5 3.2 %pad.8 = f32[4,64,36,2]{3,1,2,0:T(8,128)S(1)} pad(f32[4,64,32,2]{3,1,2,0:T(8,128)} %copy.19, f32[]{:T(128)} %constant.29.clone.1), padding=0_0x0_0x2_2x0_0 | pad | bytes 139268 | tf_op jit(solution)/shard_map/jit(_pad)/pad | solution.py:57
  53.9 2.8 %fusion.37 = f32[64,36,132]{2,0,1:T(8,128)S(1)} fusion(f32[4,64,36,2]{3,1,2,0:T(8,128)S(1)} %copy-done.4, f32[4,64,36,2]{3,1,2,0:T(8,128)S(1)} %pad.8, f32[4,64,2,128]{3,1,2,0:T(8,128)S(1)} %collective-permute-done, f32[4,64,32,128]{3,1,2,0:T(8,128)S(1)} %copy-done.1, f32[4,64,2,128]{3,1,2,0:T(8,128)S(1)} %collective-permute-done.1), kind=kOutput, calls=%fused_computation.59 | convolution fusion | flops 237223936 | bytes 6082560 | tf_op jit(solution)/shard_map/kl,lxy->kxy/dot_general | solution.py:295
  56.7 4.5 %fusion.61 = (f32[64,32,128]{2,0,1:T(8,128)}, f32[64,32,128]{2,0,1:T(8,128)}, f32[1,64,32,128]{3,1,2,0:T(8,128)}, f32[1,64,32,128]{3,1,2,0:T(8,128)}) fusion(f32[4,64,32,128]{3,1,2,0:T(8,128)S(1)} %copy-done.1, f32[128]{0:T(128)} %multiply_add_fusion.2, f32[64,36,132]{2,0,1:T(8,128)S(1)} %fusion.37), kind=kLoop, calls=%fused_computation.98 | loop fusion | flops 4718592 | bytes 14680576 | tf_op jit(solution)/shard_map/mul | solution.py:97
  61.3 11.6 %fusion.8 = f32[4,64,32,128]{3,1,2,0:T(8,128)} fusion(f32[4,64,36,2]{3,1,2,0:T(8,128)} %copy-done.5, f32[4,64,2,128]{3,1,2,0:T(8,128)S(1)} %collective-permute-done, f32[4,64,32,128]{3,1,2,0:T(8,128)S(1)} %copy-done.1, f32[4,64,2,128]{3,1,2,0:T(8,128)S(1)} %collective-permute-done.1, f32[4,64,36,2]{3,1,2,0:T(8,128)S(1)} %copy-done.4, ...), kind=kLoop, calls=%fused_computation.13 | loop fusion | flops 39845888 | bytes 13254672 | tf_op jit(solution)/shard_map/add | solution.py:109
  72.9 9.5 %fusion.17 = f32[4,160,32,128]{3,1,2,0:T(8,128)S(1)} fusion(f32[4,64,32,128]{3,1,2,0:T(8,128)} %fusion.8, f32[64,32,128]{2,0,1:T(8,128)S(1)} %fusion.60, f32[64,64]{0,1:T(8,128)S(1)} %bitcast.42, f32[48,64]{0,1:T(8,128)S(1)} %bitcast.40, f32[32,64]{0,1:T(8,128)S(1)} %bitcast.43, f32[16,64]{0,1:T(8,128)S(1)} %bitcast.41, f32[4,64,32,128]{3,2,1,0:T(8,128)S(1)} %copy-done.2), kind=kOutput, calls=%fused_computation.34 | convolution fusion | flops 1010857984 | bytes 19963904 | tf_op jit(solution)/shard_map/kl,flxy->fkxy/dot_general | solution.py:116
  83.6 4.7 %fusion.12 = f32[4,64,32,128]{3,1,2,0:T(8,128)S(1)} fusion(f32[4,16,32,128]{3,1,2,0:T(8,128)S(1)} %get-tuple-element.16, f32[4,16,32,128]{3,1,2,0:T(8,128)S(1)} %get-tuple-element.15, f32[4,16,32,128]{3,1,2,0:T(8,128)S(1)} %get-tuple-element.14, f32[4,16,32,128]{3,1,2,0:T(8,128)S(1)} %get-tuple-element.13, f32[4,64,32,128]{3,2,1,0:T(8,128)S(1)} %copy-done.2, ...), kind=kLoop, calls=%fused_computation.27 | loop fusion | flops 6291456 | bytes 14680064 | tf_op jit(solution)/shard_map/add | solution.py:127
  89.3 3.3 %collective-permute-start.4 = (f32[6,32,128]{2,1,0:T(8,128)S(1)}, f32[6,32,128]{2,1,0:T(8,128)S(1)}, u32[]{:S(2)}, u32[]{:S(2)}) collective-permute-start(f32[6,32,128]{2,1,0:T(8,128)S(1)} %pad_maximum_fusion.19), channel_id=1, source_target_pairs={{0,32},{16,48},{32,64},{48,80},{64,96},{80,112},{96,128},{112,144}... | collective-permute-start | bytes 294920 | tf_op jit(solution)/shard_map/ppermute | solution.py:200
  94.5 5.5 %collective-permute-start.6 = (f32[6,32,128]{2,1,0:T(8,128)S(1)}, f32[6,32,128]{2,1,0:T(8,128)S(1)}, u32[]{:S(2)}, u32[]{:S(2)}) collective-permute-start(f32[6,32,128]{2,1,0:T(8,128)S(1)} %pad_maximum_fusion.19), channel_id=1, source_target_pairs={{16,0},{32,16},{48,32},{64,48},{80,64},{96,80},{112,96},{128,112},... | collective-permute-start | bytes 294920 | tf_op jit(solution)/shard_map/ppermute | solution.py:201
  100.0 2.9 %collective-permute-start.7 = (f32[6,32,128]{2,1,0:T(8,128)S(1)}, f32[6,32,128]{2,1,0:T(8,128)S(1)}, u32[]{:S(2)}, u32[]{:S(2)}) collective-permute-start(f32[6,32,128]{2,1,0:T(8,128)S(1)} %pad_maximum_fusion.19), channel_id=1, source_target_pairs={{32,0},{48,16},{64,32},{80,48},{96,64},{112,80},{128,96},{144,112}... | collective-permute-start | bytes 294920 | tf_op jit(solution)/shard_map/ppermute | solution.py:201
  103.0 4.5 %collective-permute-done.7 = f32[6,32,128]{2,1,0:T(8,128)S(1)} collective-permute-done((f32[6,32,128]{2,1,0:T(8,128)S(1)}, f32[6,32,128]{2,1,0:T(8,128)S(1)}, u32[]{:S(2)}, u32[]{:S(2)}) %collective-permute-start.7) | collective-permute-done | bytes 98336 | tf_op jit(solution)/shard_map/ppermute | solution.py:201
  107.7 4.3 %collective-permute-start.8 = (f32[6,160,64]{2,1,0:T(8,128)S(1)}, f32[6,160,64]{2,1,0:T(8,128)S(1)}, u32[]{:S(2)}, u32[]{:S(2)}) collective-permute-start(f32[6,160,64]{2,1,0:T(8,128)S(1)} %get-tuple-element.31), channel_id=1, source_target_pairs={{0,1},{1,2},{2,3},{3,4},{4,5},{5,6},{6,7},{7,8},{8,9},{9,10},{10,1... | collective-permute-start | bytes 737288 | tf_op jit(solution)/shard_map/ppermute | solution.py:200
  114.2 3.5 %collective-permute-done.8 = f32[6,160,64]{2,1,0:T(8,128)S(1)} collective-permute-done((f32[6,160,64]{2,1,0:T(8,128)S(1)}, f32[6,160,64]{2,1,0:T(8,128)S(1)}, u32[]{:S(2)}, u32[]{:S(2)}) %collective-permute-start.8) | collective-permute-done | bytes 245792 | tf_op jit(solution)/shard_map/ppermute | solution.py:200
  117.8 5.6 %collective-permute-done.9 = f32[6,160,64]{2,1,0:T(8,128)S(1)} collective-permute-done((f32[6,160,64]{2,1,0:T(8,128)S(1)}, f32[6,160,64]{2,1,0:T(8,128)S(1)}, u32[]{:S(2)}, u32[]{:S(2)}) %collective-permute-start.9) | collective-permute-done | bytes 245792 | tf_op jit(solution)/shard_map/ppermute | solution.py:201
  125.5 13.4 %shard_map.76 = f32[3,160,256]{2,1,0:T(8,128)} custom-call(f32[3,160,256]{2,1,0:T(8,128)} %get-tuple-element.30.moving_ref, f32[3,160,256]{2,1,0:T(8,128)} %get-tuple-element.29.fixed_ref, f32[8,256]{1,0:T(8,128)} %broadcast_in_dim.2.coriolis_ref), custom_call_target="tpu_custom_call" | custom-call | flops 52428800 | bytes 1474560 | tf_op jit(solution)/shard_map/pallas_call | solution.py:266
  141.9 2.9 %fusion.76 = (f32[2,64,32,128]{3,1,2,0:T(8,128)S(1)}, f32[2,64,32,128]{3,1,2,0:T(8,128)S(1)}) fusion(f32[4,64,32,128]{3,1,2,0:T(8,128)} %copy-done.6, f32[2,32,128]{2,1,0:T(8,128)S(1)} %get-tuple-element.11, f32[64,32,128]{2,0,1:T(8,128)S(1)} %fusion.60), kind=kLoop, calls=%fused_computation.137 | loop fusion | flops 1048576 | bytes 9469952 | tf_op jit(solution)/shard_map/slice | solution.py:187
  145.4 4.4 %copy.25 = f32[4,64,32,128]{3,2,1,0:T(8,128)} copy(f32[4,64,32,128]{3,1,2,0:T(8,128)S(1)} %pad_maximum_fusion.10) | data formatting | bytes 8388608
  (80 shorter events, 29.2 us)
Async XLA Ops:
  6.7 4.7 %copy-start = (f32[4,64,32,128]{3,1,2,0:T(8,128)}, f32[4,64,32,128]{3,1,2,0:T(8,128)S(1)}, u32[]{:S(2)}) copy-start(f32[4,64,32,128]{3,1,2,0:T(8,128)S(1)} %copy_multiply_fusion) | copy-start | bytes 12582916
  11.4 21.5 %copy-start.9 = (f32[4,64,64]{2,1,0:T(8,128)S(1)}, f32[4,64,64]{2,1,0:T(8,128)}, u32[]{:S(2)}) copy-start(f32[4,64,64]{2,1,0:T(8,128)} %param.7) | copy-start | bytes 196612
  11.4 21.6 %copy-start.8 = (s32[32,128]{1,0:T(8,128)S(1)}, s32[32,128]{1,0:T(8,128)}, u32[]{:S(2)}) copy-start(s32[32,128]{1,0:T(8,128)} %param.6) | copy-start | bytes 49156
  14.5 20.3 %slice-start = ((f32[4,64,64]{2,1,0:T(8,128)}), f32[1,64,64]{2,1,0:T(8,128)S(1)}, s32[]{:S(2)}) async-start(f32[4,64,64]{2,1,0:T(8,128)} %param.7), calls=%async_computation | async-start | bytes 65536 | tf_op jit(solution)/shard_map/slice | solution.py:114
  14.5 21.2 %copy-start.14 = (f32[2,32,128]{2,1,0:T(8,128)S(1)}, f32[2,32,128]{2,1,0:T(8,128)}, u32[]{:S(2)}) copy-start(f32[2,32,128]{2,1,0:T(8,128)} %param.9) | copy-start | bytes 98308
  14.5 21.2 %copy-start.15 = (f32[32,128]{1,0:T(8,128)S(1)}, f32[32,128]{1,0:T(8,128)}, u32[]{:S(2)}) copy-start(f32[32,128]{1,0:T(8,128)} %param.8) | copy-start | bytes 49156
  14.5 22.3 %collective-permute-start.2 = (f32[4,64,32,2]{1,2,3,0:T(8,128)S(1)}, f32[4,64,32,2]{1,2,3,0:T(8,128)S(1)}, u32[]{:S(2)}, u32[]{:S(2)}) collective-permute-start(f32[4,64,32,2]{1,2,3,0:T(8,128)S(1)} %copy.16), channel_id=1, source_target_pairs={{1,0},{2,1},{3,2},{4,3},{5,4},{6,5},{7,6},{8,7},{9,8},{10,9},{11,1... | collective-permute-start | bytes 196616 | tf_op jit(solution)/shard_map/ppermute | solution.py:50
  20.2 24.6 %collective-permute-start.3 = (f32[4,64,32,2]{1,2,3,0:T(8,128)S(1)}, f32[4,64,32,2]{1,2,3,0:T(8,128)S(1)}, u32[]{:S(2)}, u32[]{:S(2)}) collective-permute-start(f32[4,64,32,2]{1,2,3,0:T(8,128)S(1)} %copy.18), channel_id=1, source_target_pairs={{0,1},{1,2},{2,3},{3,4},{4,5},{5,6},{6,7},{7,8},{8,9},{9,10},{10,1... | collective-permute-start | bytes 196616 | tf_op jit(solution)/shard_map/ppermute | solution.py:49
  25.9 24.9 %collective-permute-start = (f32[4,64,2,128]{3,1,2,0:T(8,128)S(1)}, f32[4,64,2,128]{3,1,2,0:T(8,128)S(1)}, u32[]{:S(2)}, u32[]{:S(2)}) collective-permute-start(f32[4,64,2,128]{3,1,2,0:T(8,128)S(1)} %get-tuple-element.28), channel_id=1, source_target_pairs={{16,0},{32,16},{48,32},{64,48},{80,64},{96,80},{112,96},{128,112},... | collective-permute-start | bytes 786440 | tf_op jit(solution)/shard_map/ppermute | solution.py:50
  30.9 20.0 %collective-permute-start.1 = (f32[4,64,2,128]{3,1,2,0:T(8,128)S(1)}, f32[4,64,2,128]{3,1,2,0:T(8,128)S(1)}, u32[]{:S(2)}, u32[]{:S(2)}) collective-permute-start(f32[4,64,2,128]{3,1,2,0:T(8,128)S(1)} %get-tuple-element.27), channel_id=1, source_target_pairs={{0,16},{16,32},{32,48},{48,64},{64,80},{80,96},{96,112},{112,128},... | collective-permute-start | bytes 786440 | tf_op jit(solution)/shard_map/ppermute | solution.py:49
  47.5 5.6 %copy-start.1 = (f32[4,64,32,128]{3,1,2,0:T(8,128)S(1)}, f32[4,64,32,128]{3,1,2,0:T(8,128)}, u32[]{:S(2)}) copy-start(f32[4,64,32,128]{3,1,2,0:T(8,128)} %copy-done) | copy-start | bytes 12582916
  47.5 6.4 %copy-start.4 = (f32[4,64,36,2]{3,1,2,0:T(8,128)S(1)}, f32[4,64,36,2]{3,1,2,0:T(8,128)}, u32[]{:S(2)}) copy-start(f32[4,64,36,2]{3,1,2,0:T(8,128)} %pad.7) | copy-start | bytes 221188
  61.2 11.6 %copy-start.2 = (f32[4,64,32,128]{3,2,1,0:T(8,128)S(1)}, f32[4,64,32,128]{3,2,1,0:T(8,128)}, u32[]{:S(2)}) copy-start(f32[4,64,32,128]{3,2,1,0:T(8,128)} %param.5) | copy-start | bytes 12582916
  72.8 9.5 %copy-start.10 = (f32[32,128]{1,0:T(8,128)S(1)}, f32[32,128]{1,0:T(8,128)}, u32[]{:S(2)}) copy-start(f32[32,128]{1,0:T(8,128)} %get-tuple-element.36) | copy-start | bytes 49156
  72.8 9.5 %copy-start.11 = (f32[32,128]{1,0:T(8,128)S(1)}, f32[32,128]{1,0:T(8,128)}, u32[]{:S(2)}) copy-start(f32[32,128]{1,0:T(8,128)} %get-tuple-element.37) | copy-start | bytes 49156
  88.3 19.4 %copy-start.6 = (f32[4,64,32,128]{3,1,2,0:T(8,128)}, f32[4,64,32,128]{3,1,2,0:T(8,128)S(1)}, u32[]{:S(2)}) copy-start(f32[4,64,32,128]{3,1,2,0:T(8,128)S(1)} %fusion.12) | copy-start | bytes 12582916
  89.3 13.6 %collective-permute-start.4 = (f32[6,32,128]{2,1,0:T(8,128)S(1)}, f32[6,32,128]{2,1,0:T(8,128)S(1)}, u32[]{:S(2)}, u32[]{:S(2)}) collective-permute-start(f32[6,32,128]{2,1,0:T(8,128)S(1)} %pad_maximum_fusion.19), channel_id=1, source_target_pairs={{0,32},{16,48},{32,64},{48,80},{64,96},{80,112},{96,128},{112,144}... | collective-permute-start | bytes 294920 | tf_op jit(solution)/shard_map/ppermute | solution.py:200
  92.6 10.3 %collective-permute-start.5 = (f32[6,32,128]{2,1,0:T(8,128)S(1)}, f32[6,32,128]{2,1,0:T(8,128)S(1)}, u32[]{:S(2)}, u32[]{:S(2)}) collective-permute-start(f32[6,32,128]{2,1,0:T(8,128)S(1)} %pad_maximum_fusion.19), channel_id=1, source_target_pairs={{0,16},{16,32},{32,48},{48,64},{64,80},{80,96},{96,112},{112,128},... | collective-permute-start | bytes 294920 | tf_op jit(solution)/shard_map/ppermute | solution.py:200
  94.5 8.5 %collective-permute-start.6 = (f32[6,32,128]{2,1,0:T(8,128)S(1)}, f32[6,32,128]{2,1,0:T(8,128)S(1)}, u32[]{:S(2)}, u32[]{:S(2)}) collective-permute-start(f32[6,32,128]{2,1,0:T(8,128)S(1)} %pad_maximum_fusion.19), channel_id=1, source_target_pairs={{16,0},{32,16},{48,32},{64,48},{80,64},{96,80},{112,96},{128,112},... | collective-permute-start | bytes 294920 | tf_op jit(solution)/shard_map/ppermute | solution.py:201
  100.0 7.5 %collective-permute-start.7 = (f32[6,32,128]{2,1,0:T(8,128)S(1)}, f32[6,32,128]{2,1,0:T(8,128)S(1)}, u32[]{:S(2)}, u32[]{:S(2)}) collective-permute-start(f32[6,32,128]{2,1,0:T(8,128)S(1)} %pad_maximum_fusion.19), channel_id=1, source_target_pairs={{32,0},{48,16},{64,32},{80,48},{96,64},{112,80},{128,96},{144,112}... | collective-permute-start | bytes 294920 | tf_op jit(solution)/shard_map/ppermute | solution.py:201
  102.9 37.4 %copy-start.12 = (f32[32,128]{1,0:T(8,128)S(1)}, f32[32,128]{1,0:T(8,128)}, u32[]{:S(2)}) copy-start(f32[32,128]{1,0:T(8,128)} %get-tuple-element.40) | copy-start | bytes 49156
  107.7 10.0 %collective-permute-start.8 = (f32[6,160,64]{2,1,0:T(8,128)S(1)}, f32[6,160,64]{2,1,0:T(8,128)S(1)}, u32[]{:S(2)}, u32[]{:S(2)}) collective-permute-start(f32[6,160,64]{2,1,0:T(8,128)S(1)} %get-tuple-element.31), channel_id=1, source_target_pairs={{0,1},{1,2},{2,3},{3,4},{4,5},{5,6},{6,7},{7,8},{8,9},{9,10},{10,1... | collective-permute-start | bytes 737288 | tf_op jit(solution)/shard_map/ppermute | solution.py:200
  112.0 11.4 %collective-permute-start.9 = (f32[6,160,64]{2,1,0:T(8,128)S(1)}, f32[6,160,64]{2,1,0:T(8,128)S(1)}, u32[]{:S(2)}, u32[]{:S(2)}) collective-permute-start(f32[6,160,64]{2,1,0:T(8,128)S(1)} %get-tuple-element.32), channel_id=1, source_target_pairs={{1,0},{2,1},{3,2},{4,3},{5,4},{6,5},{7,6},{8,7},{9,8},{10,9},{11,1... | collective-permute-start | bytes 737288 | tf_op jit(solution)/shard_map/ppermute | solution.py:201
  117.8 22.6 %copy-start.13 = (f32[32,128]{1,0:T(8,128)S(1)}, f32[32,128]{1,0:T(8,128)}, u32[]{:S(2)}) copy-start(f32[32,128]{1,0:T(8,128)} %get-tuple-element.39) | copy-start | bytes 49156
  (3 other events, 8.3 us)

commit v5 on v4

v5 whole, which is shorter than its diff:
```python
import jax
import jax.numpy as jnp
from jax import lax
from jax.experimental import pallas as pl
from jax.experimental.pallas import tpu as pltpu
from jax.sharding import PartitionSpec as P

SUB = 32
LEVEL_CHUNK = 8


THERMAL = 0.8
HALINE = 0.6
PRESSURE_SCALE = 4.0
VISCOSITY = 0.1
STEP_TIME = 0.05
WAVE_STEP = 0.5
GRAVITY = 1.0
BOTTOM_DRAG = 0.05
CORIOLIS_BASE = 0.3
CORIOLIS_SLOPE = 0.4


def coriolis_row(anchor, number, total):
    position = (anchor + lax.broadcasted_iota(jnp.int32, (number,), 0)).astype(jnp.float32)
    return (CORIOLIS_BASE + CORIOLIS_SLOPE * (position + 0.5) / total)[None, :]


def vertical_solve(state, provisional, active, depth_class, inverse):
    levels = state.shape[1]
    classes = inverse.shape[0]
    band = levels // classes
    stacked = jnp.concatenate(
        [inverse[class_index, : band * (class_index + 1)] for class_index in range(classes)], axis=0
    )
    every = jnp.einsum("kl,flxy->fkxy", stacked, provisional, precision=lax.Precision.HIGH)
    starts = [band * class_index * (class_index + 1) // 2 for class_index in range(classes)]
    chosen = [(depth_class == class_index + 1).astype(jnp.float32) for class_index in range(classes)]
    bands = []
    for level_band in range(classes):
        part = jnp.zeros_like(provisional[:, :band])
        for class_index in range(level_band, classes):
            first = starts[class_index] + level_band * band
            part = part + chosen[class_index] * every[:, first : first + band]
        bands.append(part)
    solved = jnp.concatenate(bands, axis=1)
    return active * solved + (1.0 - active) * state


def edge_halo(state, active, axis, dim, width):
    count = lax.axis_size(axis)
    ends = count - 1
    size = state.shape[dim]
    head = lax.slice_in_dim(state, 0, width, axis=dim) * lax.slice_in_dim(active, 0, width, axis=dim - 1)
    tail = lax.slice_in_dim(state, size - width, size, axis=dim) * lax.slice_in_dim(
        active, size - width, size, axis=dim - 1
    )
    before = lax.ppermute(tail, axis, [(i, i + 1) for i in range(ends)])
    after = lax.ppermute(head, axis, [(i + 1, i) for i in range(ends)])
    return before, after


def finish(updated, waves, active, depth_class, level_block, levels):
    counted = jnp.maximum(depth_class * level_block, 1).astype(jnp.float32)
    safe_depth = jnp.maximum(depth_class, 1).astype(jnp.float32) * level_block / levels
    column_means = jnp.sum(active * updated[2:4], axis=1) / counted
    carried = waves[1:3] / safe_depth
    velocity = updated[2:4] + active * (carried - column_means)[:, None]
    return jnp.concatenate([updated[0:2], velocity], axis=0)


def wide_halo(cells, axis, dim, width):
    count = lax.axis_size(axis)
    size = cells.shape[dim]
    before, after = [], []
    remaining, hop = width, 1
    while remaining > 0:
        take = min(size, remaining)
        tail = lax.slice_in_dim(cells, size - take, size, axis=dim)
        head = lax.slice_in_dim(cells, 0, take, axis=dim)
        if hop < count:
            from_before = lax.ppermute(tail, axis, [(i, i + hop) for i in range(count - hop)])
            from_after = lax.ppermute(head, axis, [(i + hop, i) for i in range(count - hop)])
        else:
            from_before = jnp.zeros_like(tail)
            from_after = jnp.zeros_like(head)
        before.insert(0, from_before)
        after.append(from_after)
        remaining -= take
        hop += 1
    return jnp.concatenate(before + [cells] + after, axis=dim)


def stencil_kernel(depth_ref, coriolis_ref, state_ref, west_ref, east_ref, side_ref,
                   provisional_ref, forcing_ref, sums_ref):
    chunk = pl.program_id(0)
    fields, depth_levels, rows, cols = state_ref.shape
    levels = depth_levels * pl.num_programs(0)
    block = levels // 4

    @pl.when(chunk == 0)
    def _():
        sums_ref[...] = jnp.zeros_like(sums_ref)

    row = lax.broadcasted_iota(jnp.int32, (rows, cols), 0)
    lane = lax.broadcasted_iota(jnp.int32, (rows, cols), 1)
    reach = depth_ref[...] * block
    coriolis = coriolis_ref[0:1, :]

    def near(values, west, east, side):
        w0 = jnp.broadcast_to(west[0:1], (rows, cols))
        w1 = jnp.broadcast_to(west[1:2], (rows, cols))
        e0 = jnp.broadcast_to(east[0:1], (rows, cols))
        e1 = jnp.broadcast_to(east[1:2], (rows, cols))
        xm1 = jnp.where(row == 0, w1, pltpu.roll(values, 1, 0))
        xm2 = jnp.where(row == 0, w0, jnp.where(row == 1, w1, pltpu.roll(values, 2, 0)))
        xp1 = jnp.where(row == rows - 1, e0, pltpu.roll(values, rows - 1, 0))
        xp2 = jnp.where(row == rows - 2, e0, jnp.where(row == rows - 1, e1, pltpu.roll(values, rows - 2, 0)))
        ym1 = jnp.where(lane == 0, pltpu.roll(side, cols - 1, 1), pltpu.roll(values, 1, 1))
        ym2 = jnp.where(lane < 2, side, pltpu.roll(values, 2, 1))
        yp1 = jnp.where(lane == cols - 1, pltpu.roll(side, 1, 1), pltpu.roll(values, cols - 1, 1))
        yp2 = jnp.where(lane >= cols - 2, side, pltpu.roll(values, cols - 2, 1))
        return xm2, xm1, xp1, xp2, ym2, ym1, yp1, yp2

    def fourth(m2, m1, p1, p2):
        return (8.0 * (p1 - m1) - (p2 - m2)) / 12.0

    def level(k, carry):
        global_level = chunk * depth_levels + k
        active = (global_level < reach).astype(jnp.float32)
        masked = [state_ref[f, k] * active for f in range(fields)]
        west = [west_ref[f, k] for f in range(fields)]
        east = [east_ref[f, k] for f in range(fields)]
        side = [side_ref[f, k] for f in range(fields)]
        density = -THERMAL * masked[0] + HALINE * masked[1]
        density_w = -THERMAL * west[0] + HALINE * west[1]
        density_e = -THERMAL * east[0] + HALINE * east[1]
        density_s = -THERMAL * side[0] + HALINE * side[1]
        sums_ref[0] = sums_ref[0] + density
        sums_ref[1] = sums_ref[1] + density_s
        sums_ref[2, 0:2] = sums_ref[2, 0:2] + density_w
        sums_ref[2, 2:4] = sums_ref[2, 2:4] + density_e
        scale = PRESSURE_SCALE / levels
        pressure = scale * sums_ref[0]
        pressure_s = scale * sums_ref[1]
        pressure_w = scale * sums_ref[2, 0:2]
        pressure_e = scale * sums_ref[2, 2:4]
        east_vel = masked[2]
        north_vel = masked[3]
        pm2, pm1, pp1, pp2, qm2, qm1, qp1, qp2 = near(pressure, pressure_w, pressure_e, pressure_s)
        extra = [None, None,
                 -fourth(pm2, pm1, pp1, pp2) + coriolis * north_vel,
                 -fourth(qm2, qm1, qp1, qp2) - coriolis * east_vel]
        for f in range(fields):
            xm2, xm1, xp1, xp2, ym2, ym1, yp1, yp2 = near(masked[f], west[f], east[f], side[f])
            lap = xp1 + xm1 + yp1 + ym1 - 4.0 * masked[f]
            tendency = -(east_vel * fourth(xm2, xm1, xp1, xp2) + north_vel * fourth(ym2, ym1, yp1, yp2)) + VISCOSITY * lap
            if extra[f] is not None:
                tendency = tendency + extra[f]
                forcing_ref[f - 2] = forcing_ref[f - 2] + active * tendency
            provisional_ref[f, k] = active * (masked[f] + STEP_TIME * tendency)
        return carry

    @pl.when(chunk == 0)
    def _():
        forcing_ref[...] = jnp.zeros_like(forcing_ref)

    lax.fori_loop(0, depth_levels, level, 0)

    @pl.when(chunk == pl.num_programs(0) - 1)
    def _():
        forcing_ref[...] = forcing_ref[...] / levels


def stencil(state, depth_class, west, east, side, coriolis):
    fields, levels, rows, cols = state.shape
    steps = levels // LEVEL_CHUNK
    big = pl.BlockSpec((fields, LEVEL_CHUNK, rows, cols), lambda c: (0, c, 0, 0))
    rim = pl.BlockSpec((fields, LEVEL_CHUNK, 2, cols), lambda c: (0, c, 0, 0))
    flat = pl.BlockSpec((rows, cols), lambda c: (0, 0))
    return pl.pallas_call(
        stencil_kernel,
        grid=(steps,),
        out_shape=(jax.ShapeDtypeStruct(state.shape, jnp.float32),
                   jax.ShapeDtypeStruct((2, rows, cols), jnp.float32)),
        in_specs=[flat, pl.BlockSpec((8, cols), lambda c: (0, 0)), big, rim, rim, big],
        out_specs=(big, pl.BlockSpec((2, rows, cols), lambda c: (0, 0, 0))),
        scratch_shapes=[pltpu.VMEM((3, rows, cols), jnp.float32)],
        compiler_params=pltpu.CompilerParams(dimension_semantics=("arbitrary",)),
        cost_estimate=pl.CostEstimate(
            flops=60 * state.size, transcendentals=0, bytes_accessed=4 * 3 * state.size
        ),
    )(depth_class, coriolis, state, west, east, side)


def wave_kernel(moving_ref, fixed_ref, coriolis_ref, out_ref):
    rows, cols = moving_ref.shape[1], moving_ref.shape[2]
    column_depth = fixed_ref[2]
    sea_mask = (column_depth > 0.0).astype(jnp.float32)
    force_east = fixed_ref[0]
    force_north = fixed_ref[1]
    coriolis = jnp.broadcast_to(coriolis_ref[0:1, :], (rows, cols))

    def x_slope_rolled(values):
        return (pltpu.roll(values, rows - 1, 0) - pltpu.roll(values, 1, 0)) * 0.5

    def y_slope_rolled(values):
        return (pltpu.roll(values, cols - 1, 1) - pltpu.roll(values, 1, 1)) * 0.5

    out_ref[...] = moving_ref[...]

    def step(index, carry):
        surface = out_ref[0]
        east_old = out_ref[1]
        north_old = out_ref[2]
        surface_mid = sea_mask * (
            surface - WAVE_STEP * (x_slope_rolled(east_old) + y_slope_rolled(north_old))
        )
        east_new = sea_mask * (
            east_old
            + WAVE_STEP
            * (
                -GRAVITY * column_depth * x_slope_rolled(surface_mid)
                + coriolis * north_old
                + force_east
                - BOTTOM_DRAG * east_old
            )
        )
        north_new = sea_mask * (
            north_old
            + WAVE_STEP
            * (
                -GRAVITY * column_depth * y_slope_rolled(surface_mid)
                - coriolis * east_new
                + force_north
                - BOTTOM_DRAG * north_old
            )
        )
        out_ref[0] = surface_mid
        out_ref[1] = east_new
        out_ref[2] = north_new
        return carry

    lax.fori_loop(0, SUB, step, 0)


def local_waves(moving, fixed, coriolis):
    rows, cols = moving.shape[1], moving.shape[2]
    elements = rows * cols
    return pl.pallas_call(
        wave_kernel,
        out_shape=jax.ShapeDtypeStruct(moving.shape, jnp.float32),
        in_specs=[pl.BlockSpec(memory_space=pltpu.VMEM)] * 3,
        out_specs=pl.BlockSpec(memory_space=pltpu.VMEM),
        cost_estimate=pl.CostEstimate(
            flops=SUB * 40 * elements, transcendentals=0, bytes_accessed=4 * 9 * elements
        ),
    )(moving, fixed, coriolis)


def body(state, depth_class, vertical_inverse, height, transport):
    levels = state.shape[1]
    level_block = levels // vertical_inverse.shape[0]
    y_cells = depth_class.shape[1]
    level_ids = lax.broadcasted_iota(jnp.int32, (levels, 1, 1), 0)
    active = (level_ids < depth_class[None] * level_block).astype(jnp.float32)
    west, east = edge_halo(state, active, "gx", 2, 2)
    south, north = edge_halo(state, active, ("gy", "mode"), 3, 2)
    column_blocks = lax.axis_size(("gy", "mode"))
    anchor = lax.axis_index(("gy", "mode")) * y_cells
    coriolis = jnp.broadcast_to(coriolis_row(anchor, y_cells, y_cells * column_blocks), (8, y_cells))
    gap = jnp.zeros(south.shape[:3] + (y_cells - 4,), jnp.float32)
    side = jnp.concatenate([south, gap, north], axis=3)
    provisional, forcing = stencil(state, depth_class, west, east, side, coriolis)
    updated = vertical_solve(state, provisional, active, depth_class, vertical_inverse)
    column_depth = depth_class.astype(jnp.float32) * level_block / levels
    sea_mask = (depth_class > 0).astype(jnp.float32)
    moving = jnp.stack([height, transport[0], transport[1]]) * sea_mask
    fields = jnp.stack([moving[0], moving[1], moving[2], forcing[0], forcing[1], column_depth])
    rim = 2 * SUB
    fields = wide_halo(fields, "gx", 1, rim)
    fields = wide_halo(fields, ("gy", "mode"), 2, rim)
    coriolis_wide = jnp.broadcast_to(
        coriolis_row(anchor - rim, y_cells + 2 * rim, y_cells * column_blocks), (8, y_cells + 2 * rim)
    )
    waves_wide = local_waves(fields[0:3], fields[3:6], coriolis_wide)
    x_cells = depth_class.shape[0]
    waves = waves_wide[:, rim : rim + x_cells, rim : rim + y_cells]
    state_next = finish(updated, waves, active, depth_class, level_block, levels)
    return (state_next, waves[0], waves[1:3])


def solution(mesh):
    placed = (
        P(None, None, "gx", ("gy", "mode")),
        P("gx", ("gy", "mode")),
        P(),
        P("gx", ("gy", "mode")),
        P(None, "gx", ("gy", "mode")),
    )
    return jax.shard_map(
        body,
        mesh=mesh,
        in_specs=placed,
        out_specs=(
            P(None, None, "gx", ("gy", "mode")),
            P("gx", ("gy", "mode")),
            P(None, "gx", ("gy", "mode")),
        ),
        check_vma=False,
    )
```

time: 151 us -> 149 us (0.987)
  Pallas kernels: 13.4 us -> 30 us
  waiting for transfers between devices: 13.7 us -> 0.03 us
  other arithmetic: 36.9 us -> 27.2 us
  local copies, waits for them, and re-layouts: 38 us -> 45.1 us
  matrix products: 12.3 us -> 8.78 us
    pallas_call x0 -> x1, Pallas kernels: none -> 16.6 us  [stencil(): pl.pallas_call(stencil_kernel, grid=(steps,), out_shape=(jax.ShapeDtypeSt...]
    add x3 -> x2, other arithmetic: 17.1 us -> 5.54 us  [the longest x1 4.75 us: vertical_solve(): return active * solved + (1.0 - active) * state]
    ppermute x3, waiting for transfers between devices: 10.2 us -> 0.01 us  [wide_halo(): lax.ppermute(head, axis, [(i + hop, i) for i in range(count - hop)])]
    unnamed x40 -> x38, local copies, waits for them, and re-layouts: 8.39 us -> 17 us
    pad x2 -> x0, local copies, waits for them, and re-layouts: 8.5 us -> none  [the longest x1 5.28 us: cross_halo(): north = jnp.pad(north, rim)]
    concatenate x0 -> x1, other arithmetic: none -> 6.58 us  [body(): side = jnp.concatenate([south, gap, north], axis=3)]
    ppermute x2, local copies, waits for them, and re-layouts: 5.45 us -> 10.7 us  [the longest x1 5.38 us: edge_halo(): before = lax.ppermute(tail, axis, [(i, i + 1) for i in range(ends)])]
    mul x2 -> x3, other arithmetic: 9.14 us -> 4.73 us  [the longest x2 4.06 us: edge_halo(): lax.slice_in_dim(state, 0, width, axis=dim)]
  transfers between devices with their start and end apart: 10 -> 10, of which waited for: 3 -> 0; matrix products, arithmetic and copies ran while one was open for 15% -> 40% of each run, Pallas kernels for 0% -> 0%
where the time goes in v5:
time: 149 us; the launch traced here: 147 us
  local copies, waits for them, and re-layouts  45.1 us (30%)
  starting transfers between devices  35.3 us (24%)
  Pallas kernels  30 us (20%)
  other arithmetic  27.2 us (18%)
  matrix products  8.78 us (6%)
    unnamed x38, local copies, waits for them, and re-layouts  17 us
    pallas_call x1, Pallas kernels, stencil(): pl.pallas_call(stencil_kernel, grid=(steps,), out_shape=(jax.ShapeDtypeSt...  16.6 us
    pallas_call x1, Pallas kernels, local_waves(): pl.pallas_call(wave_kernel, out_shape=jax.ShapeDtypeStruct(moving.shape,...  13.4 us
    ppermute x3, starting transfers between devices, wide_halo(): lax.ppermute(tail, axis, [(i, i + hop) for i in range(count - hop)])  10.6 us
    ppermute x3, starting transfers between devices, wide_halo(): lax.ppermute(head, axis, [(i + hop, i) for i in range(count - hop)])  9.48 us
    dot_general x1, matrix products, vertical_solve(): jnp.einsum('kl,flxy->fkxy', stacked, provisional, precision=lax.Precision...  8.78 us
    slice x1, local copies, waits for them, and re-layouts, edge_halo(): lax.slice_in_dim(state, size - width, size, axis=dim)  8.03 us
    ppermute x2, starting transfers between devices, edge_halo(): before = lax.ppermute(tail, axis, [(i, i + 1) for i in range(ends)])  7.83 us
  transfers between devices with their start and end apart: 10, of which 0 were waited for; matrix products, arithmetic and copies ran while one was open for 40% of the time, Pallas kernels for 0%

profile of v5, /device:TPU:103, one launch (start us, length us, event | category | flops | bytes accessed | tf_op | source)
XLA Modules:
  0.0 147.5 jit_solution(16172489654560775453)
XLA Ops:
  2.7 2.6 %slice_multiply_fusion.10 = (f32[4,64,2,128]{3,2,1,0:T(2,128)}, f32[4,64,2,128]{3,2,1,0:T(2,128)}) fusion(f32[4,64,32,128]{3,2,1,0:T(8,128)} %state_ref.1, f32[64,2,128]{2,1,0:T(2,128)S(1)} %get-tuple-element.27, f32[64,2,128]{2,1,0:T(2,128)S(1)} %get-tuple-element.28), kind=kLoop, calls=%fused_computation.30 | loop fusion | flops 131072 | bytes 1179648 | tf_op jit(solution)/shard_map/mul | solution.py:54
  5.3 3.2 %collective-permute-start = (f32[4,64,2,128]{3,2,1,0:T(2,128)}, f32[4,64,2,128]{3,2,1,0:T(2,128)S(1)}, u32[]{:S(2)}, u32[]{:S(2)}) collective-permute-start(f32[4,64,2,128]{3,2,1,0:T(2,128)} %get-tuple-element.24), channel_id=1, source_target_pairs={{0,16},{16,32},{32,48},{48,64},{64,80},{80,96},{96,112},{112,128},... | collective-permute-start | bytes 786440 | tf_op jit(solution)/shard_map/ppermute | solution.py:58
  8.5 4.2 %collective-permute-start.1 = (f32[4,64,2,128]{3,2,1,0:T(2,128)}, f32[4,64,2,128]{3,2,1,0:T(2,128)}, u32[]{:S(2)}, u32[]{:S(2)}) collective-permute-start(f32[4,64,2,128]{3,2,1,0:T(2,128)} %get-tuple-element.23), channel_id=1, source_target_pairs={{16,0},{32,16},{48,32},{64,48},{80,64},{96,80},{112,96},{128,112},... | collective-permute-start | bytes 786440 | tf_op jit(solution)/shard_map/ppermute | solution.py:59
  12.7 8.0 %fusion.21 = (f32[4,64,32,2]{3,2,1,0:T(8,128)}, f32[4,64,32,2]{3,2,1,0:T(8,128)}) fusion(f32[4,64,32,128]{3,2,1,0:T(8,128)} %state_ref.1), kind=kLoop, calls=%fused_computation.63 | loop fusion | bytes 262144 | tf_op jit(solution)/shard_map/slice | solution.py:55
  21.1 3.7 %copy.36 = f32[4,64,32,2]{1,2,3,0:T(8,128)S(1)} copy(f32[4,64,32,2]{3,2,1,0:T(8,128)} %get-tuple-element.22) | data formatting | bytes 131072
  27.5 3.3 %collective-permute-start.3 = (f32[4,64,32,2]{1,2,3,0:T(8,128)}, f32[4,64,32,2]{1,2,3,0:T(8,128)}, u32[]{:S(2)}, u32[]{:S(2)}) collective-permute-start(f32[4,64,32,2]{1,2,3,0:T(8,128)} %broadcast_multiply_fusion), channel_id=1, source_target_pairs={{1,0},{2,1},{3,2},{4,3},{5,4},{6,5},{7,6},{8,7},{9,8},{10,9},{11,1... | collective-permute-start | bytes 196616 | tf_op jit(solution)/shard_map/ppermute | solution.py:59
  30.8 3.7 %copy.35 = f32[4,64,32,2]{1,2,3,0:T(8,128)S(1)} copy(f32[4,64,32,2]{3,2,1,0:T(8,128)} %get-tuple-element.21) | data formatting | bytes 131072
  35.8 4.6 %collective-permute-start.2 = (f32[4,64,32,2]{1,2,3,0:T(8,128)}, f32[4,64,32,2]{1,2,3,0:T(8,128)}, u32[]{:S(2)}, u32[]{:S(2)}) collective-permute-start(f32[4,64,32,2]{1,2,3,0:T(8,128)} %broadcast_multiply_fusion.1), channel_id=1, source_target_pairs={{0,1},{1,2},{2,3},{3,4},{4,5},{5,6},{6,7},{7,8},{8,9},{9,10},{10,1... | collective-permute-start | bytes 196616 | tf_op jit(solution)/shard_map/ppermute | solution.py:58
  48.3 5.3 %copy.24 = f32[4,64,32,2]{3,2,1,0:T(8,128)} copy(f32[4,64,32,2]{1,2,3,0:T(8,128)} %collective-permute-done.3) | data formatting | bytes 131072 | tf_op jit(solution)/shard_map/ppermute | solution.py:59
  53.6 5.4 %copy.23 = f32[4,64,32,2]{3,2,1,0:T(8,128)} copy(f32[4,64,32,2]{1,2,3,0:T(8,128)} %collective-permute-done.2) | data formatting | bytes 131072 | tf_op jit(solution)/shard_map/ppermute | solution.py:58
  58.9 6.6 %pad_maximum_fusion.side_ref = f32[4,64,32,128]{3,2,1,0:T(8,128)} fusion(f32[4,64,32,2]{3,2,1,0:T(8,128)} %copy.24, f32[4,64,32,2]{3,2,1,0:T(8,128)} %copy.23, f32[128]{0:T(128)S(1)} %pad.22.clone), kind=kLoop, calls=%fused_computation | loop fusion | flops 2097152 | bytes 4325888 | tf_op jit(solution)/shard_map/concatenate | solution.py:273
  66.2 16.6 %shard_map.76 = (f32[4,64,32,128]{3,2,1,0:T(8,128)}, f32[2,32,128]{2,1,0:T(8,128)}) custom-call(s32[32,128]{1,0:T(8,128)} %depth_ref.1, f32[8,128]{1,0:T(8,128)} %broadcast_in_dim.6.coriolis_ref, f32[4,64,32,128]{3,2,1,0:T(8,128)} %state_ref.1, f32[4,64,2,128]{3,2,1,0:T(2,128)} %copy-done.3, f32[4,64,2,128]{3,2,1,0:T(2,128)} %collective-permute-done.1.east_ref, ...), custom_call_target="tpu_custom_call" | custom-call | flops 62914560 | bytes 12582912 | tf_op jit(solution)/shard_map/pallas_call | solution.py:181
  83.6 2.7 %collective-permute-start.4 = (f32[6,32,128]{2,1,0:T(8,128)S(1)}, f32[6,32,128]{2,1,0:T(8,128)S(1)}, u32[]{:S(2)}, u32[]{:S(2)}) collective-permute-start(f32[6,32,128]{2,1,0:T(8,128)S(1)} %pad_maximum_fusion.3), channel_id=1, source_target_pairs={{0,32},{16,48},{32,64},{48,80},{64,96},{80,112},{96,128},{112,144}... | collective-permute-start | bytes 294920 | tf_op jit(solution)/shard_map/ppermute | solution.py:82
  86.3 3.0 %collective-permute-start.5 = (f32[6,32,128]{2,1,0:T(8,128)S(1)}, f32[6,32,128]{2,1,0:T(8,128)S(1)}, u32[]{:S(2)}, u32[]{:S(2)}) collective-permute-start(f32[6,32,128]{2,1,0:T(8,128)S(1)} %pad_maximum_fusion.3), channel_id=1, source_target_pairs={{0,16},{16,32},{32,48},{48,64},{64,80},{80,96},{96,112},{112,128},... | collective-permute-start | bytes 294920 | tf_op jit(solution)/shard_map/ppermute | solution.py:82
  89.3 4.4 %collective-permute-start.6 = (f32[6,32,128]{2,1,0:T(8,128)S(1)}, f32[6,32,128]{2,1,0:T(8,128)S(1)}, u32[]{:S(2)}, u32[]{:S(2)}) collective-permute-start(f32[6,32,128]{2,1,0:T(8,128)S(1)} %pad_maximum_fusion.3), channel_id=1, source_target_pairs={{16,0},{32,16},{48,32},{64,48},{80,64},{96,80},{112,96},{128,112},... | collective-permute-start | bytes 294920 | tf_op jit(solution)/shard_map/ppermute | solution.py:83
  93.7 3.0 %collective-permute-start.7 = (f32[6,32,128]{2,1,0:T(8,128)S(1)}, f32[6,32,128]{2,1,0:T(8,128)S(1)}, u32[]{:S(2)}, u32[]{:S(2)}) collective-permute-start(f32[6,32,128]{2,1,0:T(8,128)S(1)} %pad_maximum_fusion.3), channel_id=1, source_target_pairs={{32,0},{48,16},{64,32},{80,48},{96,64},{112,80},{128,96},{144,112}... | collective-permute-start | bytes 294920 | tf_op jit(solution)/shard_map/ppermute | solution.py:83
  96.8 8.8 %fusion.3 = f32[4,160,32,128]{3,1,2,0:T(8,128)S(1)} fusion(f32[4,64,32,128]{3,2,1,0:T(8,128)} %get-tuple-element.5, f32[64,64]{0,1:T(8,128)S(1)} %bitcast.18, f32[48,64]{0,1:T(8,128)S(1)} %bitcast.16, f32[32,64]{0,1:T(8,128)S(1)} %bitcast.19, f32[16,64]{0,1:T(8,128)S(1)} %bitcast.17), kind=kOutput, calls=%fused_computation.7 | convolution fusion | flops 1006663680 | bytes 14721024 | tf_op jit(solution)/shard_map/kl,flxy->fkxy/dot_general | solution.py:36
  106.8 2.1 %collective-permute-start.9 = (f32[6,160,64]{2,1,0:T(8,128)S(1)}, f32[6,160,64]{2,1,0:T(8,128)S(1)}, u32[]{:S(2)}, u32[]{:S(2)}) collective-permute-start(f32[6,160,64]{2,1,0:T(8,128)S(1)} %get-tuple-element.32), channel_id=1, source_target_pairs={{1,0},{2,1},{3,2},{4,3},{5,4},{6,5},{7,6},{8,7},{9,8},{10,9},{11,1... | collective-permute-start | bytes 737288 | tf_op jit(solution)/shard_map/ppermute | solution.py:83
  108.9 4.9 %collective-permute-start.8 = (f32[6,160,64]{2,1,0:T(8,128)S(1)}, f32[6,160,64]{2,1,0:T(8,128)S(1)}, u32[]{:S(2)}, u32[]{:S(2)}) collective-permute-start(f32[6,160,64]{2,1,0:T(8,128)S(1)} %get-tuple-element.31), channel_id=1, source_target_pairs={{0,1},{1,2},{2,3},{3,4},{4,5},{5,6},{6,7},{7,8},{8,9},{9,10},{10,1... | collective-permute-start | bytes 737288 | tf_op jit(solution)/shard_map/ppermute | solution.py:82
  113.7 4.7 %fusion = f32[4,64,32,128]{3,1,2,0:T(8,128)S(1)} fusion(f32[4,16,32,128]{3,1,2,0:T(8,128)S(1)} %get-tuple-element.18, f32[4,16,32,128]{3,1,2,0:T(8,128)S(1)} %get-tuple-element.17, f32[4,16,32,128]{3,1,2,0:T(8,128)S(1)} %get-tuple-element.16, f32[4,16,32,128]{3,1,2,0:T(8,128)S(1)} %get-tuple-element.15, f32[4,64,32,128]{3,2,1,0:T(8,128)S(1)} %copy-done, ...), kind=kLoop, calls=%fused_computation.2 | loop fusion | flops 6291456 | bytes 14680064 | tf_op jit(solution)/shard_map/add | solution.py:47
  118.5 2.0 %copy-done.1 = f32[4,64,32,128]{3,1,2,0:T(8,128)} copy-done((f32[4,64,32,128]{3,1,2,0:T(8,128)}, f32[4,64,32,128]{3,1,2,0:T(8,128)S(1)}, u32[]{:S(2)}) %copy-start.1) | copy-done | bytes 4194328
  123.1 13.4 %shard_map.77 = f32[3,160,256]{2,1,0:T(8,128)} custom-call(f32[3,160,256]{2,1,0:T(8,128)} %get-tuple-element.30.moving_ref, f32[3,160,256]{2,1,0:T(8,128)} %get-tuple-element.29.fixed_ref, f32[8,256]{1,0:T(8,128)} %broadcast_in_dim.8.coriolis_ref), custom_call_target="tpu_custom_call" | custom-call | flops 52428800 | bytes 1474560 | tf_op jit(solution)/shard_map/pallas_call | solution.py:250
  139.5 2.9 %fusion.20 = (f32[2,64,32,128]{3,1,2,0:T(8,128)S(1)}, f32[2,64,32,128]{3,1,2,0:T(8,128)S(1)}) fusion(f32[4,64,32,128]{3,1,2,0:T(8,128)} %copy-done.1, f32[2,32,128]{2,1,0:T(8,128)S(1)} %get-tuple-element.13, f32[64,32,128]{2,0,1:T(8,128)S(1)} %copy.18), kind=kLoop, calls=%fused_computation.62 | loop fusion | flops 1048576 | bytes 9469952 | tf_op jit(solution)/shard_map/slice | solution.py:69
  143.0 4.4 %copy.33 = f32[4,64,32,128]{3,2,1,0:T(8,128)} copy(f32[4,64,32,128]{3,1,2,0:T(8,128)S(1)} %pad_maximum_fusion.1) | data formatting | bytes 8388608
  (80 shorter events, 22.9 us)
Async XLA Ops:
  5.3 60.2 %collective-permute-start = (f32[4,64,2,128]{3,2,1,0:T(2,128)}, f32[4,64,2,128]{3,2,1,0:T(2,128)S(1)}, u32[]{:S(2)}, u32[]{:S(2)}) collective-permute-start(f32[4,64,2,128]{3,2,1,0:T(2,128)} %get-tuple-element.24), channel_id=1, source_target_pairs={{0,16},{16,32},{32,48},{48,64},{64,80},{80,96},{96,112},{112,128},... | collective-permute-start | bytes 786440 | tf_op jit(solution)/shard_map/ppermute | solution.py:58
  8.5 57.0 %collective-permute-start.1 = (f32[4,64,2,128]{3,2,1,0:T(2,128)}, f32[4,64,2,128]{3,2,1,0:T(2,128)}, u32[]{:S(2)}, u32[]{:S(2)}) collective-permute-start(f32[4,64,2,128]{3,2,1,0:T(2,128)} %get-tuple-element.23), channel_id=1, source_target_pairs={{16,0},{32,16},{48,32},{64,48},{80,64},{96,80},{112,96},{128,112},... | collective-permute-start | bytes 786440 | tf_op jit(solution)/shard_map/ppermute | solution.py:59
  24.8 17.4 %copy-start.2 = (s32[32,128]{1,0:T(8,128)S(1)}, s32[32,128]{1,0:T(8,128)}, u32[]{:S(2)}) copy-start(s32[32,128]{1,0:T(8,128)} %depth_ref.1) | copy-start | bytes 49156
  26.0 14.4 %copy-start.6 = (f32[4,64,64]{2,1,0:T(8,128)S(1)}, f32[4,64,64]{2,1,0:T(8,128)}, u32[]{:S(2)}) copy-start(f32[4,64,64]{2,1,0:T(8,128)} %param.7) | copy-start | bytes 196612
  27.5 15.4 %copy-start.5 = (s32[32,128]{1,0:T(8,128)S(1)}, s32[32,128]{1,0:T(8,128)}, u32[]{:S(2)}) copy-start(s32[32,128]{1,0:T(8,128)} %copy-done.4) | copy-start | bytes 49156
  27.5 20.7 %collective-permute-start.3 = (f32[4,64,32,2]{1,2,3,0:T(8,128)}, f32[4,64,32,2]{1,2,3,0:T(8,128)}, u32[]{:S(2)}, u32[]{:S(2)}) collective-permute-start(f32[4,64,32,2]{1,2,3,0:T(8,128)} %broadcast_multiply_fusion), channel_id=1, source_target_pairs={{1,0},{2,1},{3,2},{4,3},{5,4},{6,5},{7,6},{8,7},{9,8},{10,9},{11,1... | collective-permute-start | bytes 196616 | tf_op jit(solution)/shard_map/ppermute | solution.py:59
  30.8 13.5 %slice-start = ((f32[4,64,64]{2,1,0:T(8,128)}), f32[1,64,64]{2,1,0:T(8,128)S(1)}, s32[]{:S(2)}) async-start(f32[4,64,64]{2,1,0:T(8,128)} %param.7), calls=%async_computation | async-start | bytes 65536 | tf_op jit(solution)/shard_map/slice | solution.py:34
  35.8 17.8 %collective-permute-start.2 = (f32[4,64,32,2]{1,2,3,0:T(8,128)}, f32[4,64,32,2]{1,2,3,0:T(8,128)}, u32[]{:S(2)}, u32[]{:S(2)}) collective-permute-start(f32[4,64,32,2]{1,2,3,0:T(8,128)} %broadcast_multiply_fusion.1), channel_id=1, source_target_pairs={{0,1},{1,2},{2,3},{3,4},{4,5},{5,6},{6,7},{7,8},{8,9},{9,10},{10,1... | collective-permute-start | bytes 196616 | tf_op jit(solution)/shard_map/ppermute | solution.py:58
  65.5 0.7 copy-start.3
  83.6 22.9 %collective-permute-start.4 = (f32[6,32,128]{2,1,0:T(8,128)S(1)}, f32[6,32,128]{2,1,0:T(8,128)S(1)}, u32[]{:S(2)}, u32[]{:S(2)}) collective-permute-start(f32[6,32,128]{2,1,0:T(8,128)S(1)} %pad_maximum_fusion.3), channel_id=1, source_target_pairs={{0,32},{16,48},{32,64},{48,80},{64,96},{80,112},{96,128},{112,144}... | collective-permute-start | bytes 294920 | tf_op jit(solution)/shard_map/ppermute | solution.py:82
  86.3 20.2 %collective-permute-start.5 = (f32[6,32,128]{2,1,0:T(8,128)S(1)}, f32[6,32,128]{2,1,0:T(8,128)S(1)}, u32[]{:S(2)}, u32[]{:S(2)}) collective-permute-start(f32[6,32,128]{2,1,0:T(8,128)S(1)} %pad_maximum_fusion.3), channel_id=1, source_target_pairs={{0,16},{16,32},{32,48},{48,64},{64,80},{80,96},{96,112},{112,128},... | collective-permute-start | bytes 294920 | tf_op jit(solution)/shard_map/ppermute | solution.py:82
  89.3 17.2 %collective-permute-start.6 = (f32[6,32,128]{2,1,0:T(8,128)S(1)}, f32[6,32,128]{2,1,0:T(8,128)S(1)}, u32[]{:S(2)}, u32[]{:S(2)}) collective-permute-start(f32[6,32,128]{2,1,0:T(8,128)S(1)} %pad_maximum_fusion.3), channel_id=1, source_target_pairs={{16,0},{32,16},{48,32},{64,48},{80,64},{96,80},{112,96},{128,112},... | collective-permute-start | bytes 294920 | tf_op jit(solution)/shard_map/ppermute | solution.py:83
  93.7 12.9 %collective-permute-start.7 = (f32[6,32,128]{2,1,0:T(8,128)S(1)}, f32[6,32,128]{2,1,0:T(8,128)S(1)}, u32[]{:S(2)}, u32[]{:S(2)}) collective-permute-start(f32[6,32,128]{2,1,0:T(8,128)S(1)} %pad_maximum_fusion.3), channel_id=1, source_target_pairs={{32,0},{48,16},{64,32},{80,48},{96,64},{112,80},{128,96},{144,112}... | collective-permute-start | bytes 294920 | tf_op jit(solution)/shard_map/ppermute | solution.py:83
  96.8 8.8 %copy-start.8 = (f32[32,128]{1,0:T(8,128)S(1)}, f32[32,128]{1,0:T(8,128)}, u32[]{:S(2)}) copy-start(f32[32,128]{1,0:T(8,128)} %get-tuple-element.34) | copy-start | bytes 49156
  96.8 8.8 %copy-start.9 = (f32[32,128]{1,0:T(8,128)S(1)}, f32[32,128]{1,0:T(8,128)}, u32[]{:S(2)}) copy-start(f32[32,128]{1,0:T(8,128)} %get-tuple-element.35) | copy-start | bytes 49156
  96.8 8.8 %copy-start.10 = (f32[32,128]{1,0:T(8,128)S(1)}, f32[32,128]{1,0:T(8,128)}, u32[]{:S(2)}) copy-start(f32[32,128]{1,0:T(8,128)} %get-tuple-element.36) | copy-start | bytes 49156
  96.8 8.8 %copy-start.11 = (f32[32,128]{1,0:T(8,128)S(1)}, f32[32,128]{1,0:T(8,128)}, u32[]{:S(2)}) copy-start(f32[32,128]{1,0:T(8,128)} %get-tuple-element.37) | copy-start | bytes 49156
  105.6 0.9 copy-start.7
  105.6 8.1 %copy-start = (f32[4,64,32,128]{3,2,1,0:T(8,128)S(1)}, f32[4,64,32,128]{3,2,1,0:T(8,128)}, u32[]{:S(2)}) copy-start(f32[4,64,32,128]{3,2,1,0:T(8,128)} %state_ref.1) | copy-start | bytes 12582916
  106.8 14.2 %collective-permute-start.9 = (f32[6,160,64]{2,1,0:T(8,128)S(1)}, f32[6,160,64]{2,1,0:T(8,128)S(1)}, u32[]{:S(2)}, u32[]{:S(2)}) collective-permute-start(f32[6,160,64]{2,1,0:T(8,128)S(1)} %get-tuple-element.32), channel_id=1, source_target_pairs={{1,0},{2,1},{3,2},{4,3},{5,4},{6,5},{7,6},{8,7},{9,8},{10,9},{11,1... | collective-permute-start | bytes 737288 | tf_op jit(solution)/shard_map/ppermute | solution.py:83
  108.9 12.1 %collective-permute-start.8 = (f32[6,160,64]{2,1,0:T(8,128)S(1)}, f32[6,160,64]{2,1,0:T(8,128)S(1)}, u32[]{:S(2)}, u32[]{:S(2)}) collective-permute-start(f32[6,160,64]{2,1,0:T(8,128)S(1)} %get-tuple-element.31), channel_id=1, source_target_pairs={{0,1},{1,2},{2,3},{3,4},{4,5},{5,6},{6,7},{7,8},{8,9},{9,10},{10,1... | collective-permute-start | bytes 737288 | tf_op jit(solution)/shard_map/ppermute | solution.py:82
  118.5 2.0 %copy-start.1 = (f32[4,64,32,128]{3,1,2,0:T(8,128)}, f32[4,64,32,128]{3,1,2,0:T(8,128)S(1)}, u32[]{:S(2)}) copy-start(f32[4,64,32,128]{3,1,2,0:T(8,128)S(1)} %fusion) | copy-start | bytes 12582916
  120.5 17.5 %copy-start.12 = (f32[32,128]{1,0:T(8,128)S(1)}, f32[32,128]{1,0:T(8,128)}, u32[]{:S(2)}) copy-start(f32[32,128]{1,0:T(8,128)} %get-tuple-element.40) | copy-start | bytes 49156
  120.5 17.5 %copy-start.13 = (f32[32,128]{1,0:T(8,128)S(1)}, f32[32,128]{1,0:T(8,128)}, u32[]{:S(2)}) copy-start(f32[32,128]{1,0:T(8,128)} %get-tuple-element.39) | copy-start | bytes 49156
  (1 other events, 0.6 us)

commit v6 on v5

--- a/solution.py
+++ b/solution.py
@@ -7,6 +7,7 @@
 
 SUB = 32
 LEVEL_CHUNK = 8
+PACK = 32
 
 
 THERMAL = 0.8
@@ -131,7 +132,9 @@
         masked = [state_ref[f, k] * active for f in range(fields)]
         west = [west_ref[f, k] for f in range(fields)]
         east = [east_ref[f, k] for f in range(fields)]
-        side = [side_ref[f, k] for f in range(fields)]
+        packed_level = global_level % PACK
+        shift = (cols - 2 - 4 * packed_level) % cols
+        side = [pltpu.roll(side_ref[f, global_level // PACK], shift, 1) for f in range(fields)]
         density = -THERMAL * masked[0] + HALINE * masked[1]
         density_w = -THERMAL * west[0] + HALINE * west[1]
         density_e = -THERMAL * east[0] + HALINE * east[1]
@@ -178,19 +181,61 @@
     big = pl.BlockSpec((fields, LEVEL_CHUNK, rows, cols), lambda c: (0, c, 0, 0))
     rim = pl.BlockSpec((fields, LEVEL_CHUNK, 2, cols), lambda c: (0, c, 0, 0))
     flat = pl.BlockSpec((rows, cols), lambda c: (0, 0))
+    packed = pl.BlockSpec(side.shape, lambda c: (0, 0, 0, 0))
     return pl.pallas_call(
         stencil_kernel,
         grid=(steps,),
         out_shape=(jax.ShapeDtypeStruct(state.shape, jnp.float32),
                    jax.ShapeDtypeStruct((2, rows, cols), jnp.float32)),
-        in_specs=[flat, pl.BlockSpec((8, cols), lambda c: (0, 0)), big, rim, rim, big],
+        in_specs=[flat, pl.BlockSpec((8, cols), lambda c: (0, 0)), big, rim, rim, packed],
         out_specs=(big, pl.BlockSpec((2, rows, cols), lambda c: (0, 0, 0))),
         scratch_shapes=[pltpu.VMEM((3, rows, cols), jnp.float32)],
         compiler_params=pltpu.CompilerParams(dimension_semantics=("arbitrary",)),
         cost_estimate=pl.CostEstimate(
-            flops=60 * state.size, transcendentals=0, bytes_accessed=4 * 3 * state.size
+            flops=60 * state.size, transcendentals=0, bytes_accessed=4 * 2 * state.size
         ),
     )(depth_class, coriolis, state, west, east, side)
+
+
+def pack_kernel(depth_ref, state_ref, out_ref):
+    block_index = pl.program_id(0)
+    fields, depth_levels, rows, cols = state_ref.shape
+    block = depth_levels * pl.num_programs(0) // 4
+    lane = lax.broadcasted_iota(jnp.int32, (rows, cols), 1)
+    reach = depth_ref[...] * block
+    packed = [jnp.zeros((rows, cols), jnp.float32) for f in range(fields)]
+    for k in range(depth_levels):
+        active = (block_index * depth_levels + k < reach).astype(jnp.float32)
+        low = 4 * k
+        first = (lane == low) | (lane == low + 1)
+        second = (lane == low + 2) | (lane == low + 3)
+        for f in range(fields):
+            masked = state_ref[f, k] * active
+            near_end = pltpu.roll(masked, low, 1)
+            far_end = pltpu.roll(masked, (low + 4) % cols, 1)
+            packed[f] = jnp.where(first, near_end, jnp.where(second, far_end, packed[f]))
+    for f in range(fields):
+        out_ref[f, 0] = packed[f]
+
+
+def pack_edges(state, depth_class):
+    fields, levels, rows, cols = state.shape
+    return pl.pallas_call(
+        pack_kernel,
+        grid=(levels // PACK,),
+        out_shape=jax.ShapeDtypeStruct((fields, levels // PACK, rows, cols), jnp.float32),
+        in_specs=[pl.BlockSpec((rows, cols), lambda c: (0, 0)),
+                  pl.BlockSpec((fields, PACK, rows, cols), lambda c: (0, c, 0, 0))],
+        out_specs=pl.BlockSpec((fields, 1, rows, cols), lambda c: (0, c, 0, 0)),
+        cost_estimate=pl.CostEstimate(
+            flops=4 * state.size, transcendentals=0, bytes_accessed=4 * state.size
+        ),
+    )(depth_class, state)
+
+
+def combine(from_south, from_north):
+    lane = lax.broadcasted_iota(jnp.int32, from_south.shape, from_south.ndim - 1)
+    return jnp.where(lane % 4 >= 2, from_south, from_north)
 
 
 def wave_kernel(moving_ref, fixed_ref, coriolis_ref, out_ref):
@@ -265,12 +310,14 @@
     level_ids = lax.broadcasted_iota(jnp.int32, (levels, 1, 1), 0)
     active = (level_ids < depth_class[None] * level_block).astype(jnp.float32)
     west, east = edge_halo(state, active, "gx", 2, 2)
-    south, north = edge_halo(state, active, ("gy", "mode"), 3, 2)
     column_blocks = lax.axis_size(("gy", "mode"))
     anchor = lax.axis_index(("gy", "mode")) * y_cells
     coriolis = jnp.broadcast_to(coriolis_row(anchor, y_cells, y_cells * column_blocks), (8, y_cells))
-    gap = jnp.zeros(south.shape[:3] + (y_cells - 4,), jnp.float32)
-    side = jnp.concatenate([south, gap, north], axis=3)
+    edges = pack_edges(state, depth_class)
+    y_count = lax.axis_size(("gy", "mode"))
+    from_south = lax.ppermute(edges, ("gy", "mode"), [(i, i + 1) for i in range(y_count - 1)])
+    from_north = lax.ppermute(edges, ("gy", "mode"), [(i + 1, i) for i in range(y_count - 1)])
+    side = combine(from_south, from_north)
     provisional, forcing = stencil(state, depth_class, west, east, side, coriolis)
     updated = vertical_solve(state, provisional, active, depth_class, vertical_inverse)
     column_depth = depth_class.astype(jnp.float32) * level_block / levels

time: 149 us -> 122 us (0.82)
  local copies, waits for them, and re-layouts: 45.1 us -> 17.9 us
  other arithmetic: 27.2 us -> 20.7 us
  Pallas kernels: 30 us -> 36.1 us
    ppermute x2 -> x0, local copies, waits for them, and re-layouts: 10.7 us -> none  [the longest x1 5.38 us: edge_halo(): before = lax.ppermute(tail, axis, [(i, i + 1) for i in range(ends)])]
    slice x3 -> x0, local copies, waits for them, and re-layouts: 9.02 us -> none  [the longest x1 8.03 us: edge_halo(): lax.slice_in_dim(state, size - width, size, axis=dim)]
    ppermute x0 -> x2, starting transfers between devices: none -> 7.23 us  [the longest x1 5.31 us: body(): lax.ppermute(edges, ('gy', 'mode'), [(i, i + 1) for i in range(y_count -...]
    unnamed x38 -> x40, local copies, waits for them, and re-layouts: 17 us -> 10.2 us
    concatenate x1 -> x0, other arithmetic: 6.58 us -> none  [body(): side = jnp.concatenate([south, gap, north], axis=3)]
    pallas_call x0 -> x1, Pallas kernels: none -> 4.8 us  [pack_edges(): pl.pallas_call(pack_kernel, grid=(levels // PACK,), out_shape=jax.ShapeDt...]
    ppermute x2 -> x1, starting transfers between devices: 7.83 us -> 3.19 us  [edge_halo(): before = lax.ppermute(tail, axis, [(i, i + 1) for i in range(ends)])]
    ppermute x2 -> x1, starting transfers between devices: 7.45 us -> 4.19 us  [edge_halo(): after = lax.ppermute(head, axis, [(i + 1, i) for i in range(ends)])]
  transfers between devices with their start and end apart: 10 -> 10, of which waited for: 0 -> 0; matrix products, arithmetic and copies ran while one was open for 40% -> 25% of each run, Pallas kernels for 0% -> 0%
where the time goes in v6:
time: 122 us; the launch traced here: 121 us
  starting transfers between devices  36.3 us (30%)
  Pallas kernels  36.1 us (30%)
  other arithmetic  20.7 us (17%)
  local copies, waits for them, and re-layouts  17.9 us (15%)
  matrix products  8.77 us (7%)
    pallas_call x1, Pallas kernels, stencil(): pl.pallas_call(stencil_kernel, grid=(steps,), out_shape=(jax.ShapeDtypeSt...  17.9 us
    pallas_call x1, Pallas kernels, local_waves(): pl.pallas_call(wave_kernel, out_shape=jax.ShapeDtypeStruct(moving.shape,...  13.4 us
    ppermute x3, starting transfers between devices, wide_halo(): lax.ppermute(tail, axis, [(i, i + hop) for i in range(count - hop)])  11.7 us
    unnamed x40, local copies, waits for them, and re-layouts  10.2 us
    ppermute x3, starting transfers between devices, wide_halo(): lax.ppermute(head, axis, [(i + hop, i) for i in range(count - hop)])  10 us
    dot_general x1, matrix products, vertical_solve(): jnp.einsum('kl,flxy->fkxy', stacked, provisional, precision=lax.Precision...  8.77 us
    ppermute x1, starting transfers between devices, body(): lax.ppermute(edges, ('gy', 'mode'), [(i, i + 1) for i in range(y_count -...  5.31 us
    pallas_call x1, Pallas kernels, pack_edges(): pl.pallas_call(pack_kernel, grid=(levels // PACK,), out_shape=jax.ShapeDt...  4.8 us
  transfers between devices with their start and end apart: 10, of which 0 were waited for; matrix products, arithmetic and copies ran while one was open for 25% of the time, Pallas kernels for 0%

profile of v6, /device:TPU:103, one launch (start us, length us, event | category | flops | bytes accessed | tf_op | source)
XLA Modules:
  0.0 121.0 jit_solution(1917844190522173865)
XLA Ops:
  0.7 4.8 %shard_map.76 = f32[4,2,32,128]{3,2,1,0:T(8,128)} custom-call(s32[32,128]{1,0:T(8,128)} %depth_ref.3, f32[4,64,32,128]{3,2,1,0:T(8,128)} %state_ref.3), custom_call_target="tpu_custom_call" | custom-call | flops 4194304 | bytes 4194304 | tf_op jit(solution)/shard_map/pallas_call | solution.py:223
  5.5 5.3 %collective-permute-start.2 = (f32[4,2,32,128]{3,2,1,0:T(8,128)}, f32[4,2,32,128]{3,2,1,0:T(8,128)}, u32[]{:S(2)}, u32[]{:S(2)}) collective-permute-start(f32[4,2,32,128]{3,2,1,0:T(8,128)} %shard_map.76), channel_id=1, source_target_pairs={{0,1},{1,2},{2,3},{3,4},{4,5},{5,6},{6,7},{7,8},{8,9},{9,10},{10,1... | collective-permute-start | bytes 393224 | tf_op jit(solution)/shard_map/ppermute | solution.py:318
  10.8 1.9 %collective-permute-start.3 = (f32[4,2,32,128]{3,2,1,0:T(8,128)}, f32[4,2,32,128]{3,2,1,0:T(8,128)}, u32[]{:S(2)}, u32[]{:S(2)}) collective-permute-start(f32[4,2,32,128]{3,2,1,0:T(8,128)} %shard_map.76), channel_id=1, source_target_pairs={{1,0},{2,1},{3,2},{4,3},{5,4},{6,5},{7,6},{8,7},{9,8},{10,9},{11,1... | collective-permute-start | bytes 393224 | tf_op jit(solution)/shard_map/ppermute | solution.py:319
  13.5 2.5 %slice_multiply_fusion.10 = (f32[4,64,2,128]{3,2,1,0:T(2,128)}, f32[4,64,2,128]{3,2,1,0:T(2,128)}) fusion(f32[4,64,32,128]{3,2,1,0:T(8,128)} %state_ref.3, f32[64,2,128]{2,1,0:T(2,128)S(1)} %get-tuple-element.20, f32[64,2,128]{2,1,0:T(2,128)S(1)} %get-tuple-element.21), kind=kLoop, calls=%fused_computation.29 | loop fusion | flops 131072 | bytes 1179648 | tf_op jit(solution)/shard_map/mul | solution.py:55
  16.1 3.2 %collective-permute-start = (f32[4,64,2,128]{3,2,1,0:T(2,128)}, f32[4,64,2,128]{3,2,1,0:T(2,128)S(1)}, u32[]{:S(2)}, u32[]{:S(2)}) collective-permute-start(f32[4,64,2,128]{3,2,1,0:T(2,128)} %get-tuple-element.19), channel_id=1, source_target_pairs={{0,16},{16,32},{32,48},{48,64},{64,80},{80,96},{96,112},{112,128},... | collective-permute-start | bytes 786440 | tf_op jit(solution)/shard_map/ppermute | solution.py:59
  19.3 4.2 %collective-permute-start.1 = (f32[4,64,2,128]{3,2,1,0:T(2,128)}, f32[4,64,2,128]{3,2,1,0:T(2,128)}, u32[]{:S(2)}, u32[]{:S(2)}) collective-permute-start(f32[4,64,2,128]{3,2,1,0:T(2,128)} %get-tuple-element.18), channel_id=1, source_target_pairs={{16,0},{32,16},{48,32},{64,48},{80,64},{96,80},{112,96},{128,112},... | collective-permute-start | bytes 786440 | tf_op jit(solution)/shard_map/ppermute | solution.py:60
  31.0 1.4 %copy.20 = f32[1,32,64]{1,2,0:T(8,128)} copy(f32[1,32,64]{2,1,0:T(8,128)} %slice.98) | data formatting | bytes 16384
  33.8 1.6 %fusion.13.side_ref = f32[4,2,32,128]{3,2,1,0:T(8,128)} fusion(f32[4,2,32,128]{3,2,1,0:T(8,128)} %collective-permute-done.2, f32[4,2,32,128]{3,2,1,0:T(8,128)} %collective-permute-done.3, s32[128]{0:T(128)} %get-tuple-element.35, s32[128]{0:T(128)} %get-tuple-element.36, pred[128]{0:T(512)(128)(4,1)} %compare_and_fusion), kind=kLoop, calls=%fused_computation.32 | loop fusion | flops 98304 | bytes 394368 | tf_op jit(solution)/shard_map/jit(_where)/select_n | solution.py:238
  35.5 1.3 %broadcast_in_dim.4.coriolis_ref = f32[8,128]{1,0:T(8,128)} broadcast(f32[128]{0:T(128)} %multiply_add_fusion.2), dimensions={1} | broadcast | bytes 4608 | tf_op jit(solution)/shard_map/broadcast_in_dim | solution.py:315
  36.8 17.9 %shard_map.77 = (f32[4,64,32,128]{3,2,1,0:T(8,128)}, f32[2,32,128]{2,1,0:T(8,128)}) custom-call(s32[32,128]{1,0:T(8,128)} %depth_ref.3, f32[8,128]{1,0:T(8,128)} %broadcast_in_dim.4.coriolis_ref, f32[4,64,32,128]{3,2,1,0:T(8,128)} %state_ref.3, f32[4,64,2,128]{3,2,1,0:T(2,128)} %copy-done.3, f32[4,64,2,128]{3,2,1,0:T(2,128)} %collective-permute-done.1.east_ref, ...), custom_call_target="tpu_custom_call" | custom-call | flops 62914560 | bytes 8388608 | tf_op jit(solution)/shard_map/pallas_call | solution.py:185
  55.4 2.7 %collective-permute-start.4 = (f32[6,32,128]{2,1,0:T(8,128)S(1)}, f32[6,32,128]{2,1,0:T(8,128)S(1)}, u32[]{:S(2)}, u32[]{:S(2)}) collective-permute-start(f32[6,32,128]{2,1,0:T(8,128)S(1)} %pad_maximum_fusion.2), channel_id=1, source_target_pairs={{0,32},{16,48},{32,64},{48,80},{64,96},{80,112},{96,128},{112,144}... | collective-permute-start | bytes 294920 | tf_op jit(solution)/shard_map/ppermute | solution.py:83
  58.1 3.0 %collective-permute-start.5 = (f32[6,32,128]{2,1,0:T(8,128)S(1)}, f32[6,32,128]{2,1,0:T(8,128)S(1)}, u32[]{:S(2)}, u32[]{:S(2)}) collective-permute-start(f32[6,32,128]{2,1,0:T(8,128)S(1)} %pad_maximum_fusion.2), channel_id=1, source_target_pairs={{0,16},{16,32},{32,48},{48,64},{64,80},{80,96},{96,112},{112,128},... | collective-permute-start | bytes 294920 | tf_op jit(solution)/shard_map/ppermute | solution.py:83
  61.1 4.4 %collective-permute-start.6 = (f32[6,32,128]{2,1,0:T(8,128)S(1)}, f32[6,32,128]{2,1,0:T(8,128)S(1)}, u32[]{:S(2)}, u32[]{:S(2)}) collective-permute-start(f32[6,32,128]{2,1,0:T(8,128)S(1)} %pad_maximum_fusion.2), channel_id=1, source_target_pairs={{16,0},{32,16},{48,32},{64,48},{80,64},{96,80},{112,96},{128,112},... | collective-permute-start | bytes 294920 | tf_op jit(solution)/shard_map/ppermute | solution.py:84
  65.5 2.9 %collective-permute-start.7 = (f32[6,32,128]{2,1,0:T(8,128)S(1)}, f32[6,32,128]{2,1,0:T(8,128)S(1)}, u32[]{:S(2)}, u32[]{:S(2)}) collective-permute-start(f32[6,32,128]{2,1,0:T(8,128)S(1)} %pad_maximum_fusion.2), channel_id=1, source_target_pairs={{32,0},{48,16},{64,32},{80,48},{96,64},{112,80},{128,96},{144,112}... | collective-permute-start | bytes 294920 | tf_op jit(solution)/shard_map/ppermute | solution.py:84
  68.4 8.8 %fusion.3 = f32[4,160,32,128]{3,1,2,0:T(8,128)S(1)} fusion(f32[4,64,32,128]{3,2,1,0:T(8,128)} %get-tuple-element.5, f32[64,64]{0,1:T(8,128)S(1)} %bitcast.18, f32[48,64]{0,1:T(8,128)S(1)} %bitcast.16, f32[32,64]{0,1:T(8,128)S(1)} %bitcast.19, f32[16,64]{0,1:T(8,128)S(1)} %bitcast.17), kind=kOutput, calls=%fused_computation.6 | convolution fusion | flops 1006663680 | bytes 14721024 | tf_op jit(solution)/shard_map/kl,flxy->fkxy/dot_general | solution.py:37
  78.4 2.7 %collective-permute-start.9 = (f32[6,160,64]{2,1,0:T(8,128)S(1)}, f32[6,160,64]{2,1,0:T(8,128)S(1)}, u32[]{:S(2)}, u32[]{:S(2)}) collective-permute-start(f32[6,160,64]{2,1,0:T(8,128)S(1)} %get-tuple-element.25), channel_id=1, source_target_pairs={{1,0},{2,1},{3,2},{4,3},{5,4},{6,5},{7,6},{8,7},{9,8},{10,9},{11,1... | collective-permute-start | bytes 737288 | tf_op jit(solution)/shard_map/ppermute | solution.py:84
  81.2 6.0 %collective-permute-start.8 = (f32[6,160,64]{2,1,0:T(8,128)S(1)}, f32[6,160,64]{2,1,0:T(8,128)S(1)}, u32[]{:S(2)}, u32[]{:S(2)}) collective-permute-start(f32[6,160,64]{2,1,0:T(8,128)S(1)} %get-tuple-element.24), channel_id=1, source_target_pairs={{0,1},{1,2},{2,3},{3,4},{4,5},{5,6},{6,7},{7,8},{8,9},{9,10},{10,1... | collective-permute-start | bytes 737288 | tf_op jit(solution)/shard_map/ppermute | solution.py:83
  87.2 4.7 %fusion = f32[4,64,32,128]{3,1,2,0:T(8,128)S(1)} fusion(f32[4,16,32,128]{3,1,2,0:T(8,128)S(1)} %get-tuple-element.15, f32[4,16,32,128]{3,1,2,0:T(8,128)S(1)} %get-tuple-element.14, f32[4,16,32,128]{3,1,2,0:T(8,128)S(1)} %get-tuple-element.13, f32[4,16,32,128]{3,1,2,0:T(8,128)S(1)} %get-tuple-element.12, f32[4,64,32,128]{3,2,1,0:T(8,128)S(1)} %copy-done, ...), kind=kLoop, calls=%fused_computation.1 | loop fusion | flops 6291456 | bytes 14680064 | tf_op jit(solution)/shard_map/add | solution.py:48
  92.0 2.0 %copy-done.1 = f32[4,64,32,128]{3,1,2,0:T(8,128)} copy-done((f32[4,64,32,128]{3,1,2,0:T(8,128)}, f32[4,64,32,128]{3,1,2,0:T(8,128)S(1)}, u32[]{:S(2)}) %copy-start.1) | copy-done | bytes 4194328
  96.6 13.4 %shard_map.78 = f32[3,160,256]{2,1,0:T(8,128)} custom-call(f32[3,160,256]{2,1,0:T(8,128)} %get-tuple-element.23.moving_ref, f32[3,160,256]{2,1,0:T(8,128)} %get-tuple-element.22.fixed_ref, f32[8,256]{1,0:T(8,128)} %broadcast_in_dim.5.coriolis_ref), custom_call_target="tpu_custom_call" | custom-call | flops 52428800 | bytes 1474560 | tf_op jit(solution)/shard_map/pallas_call | solution.py:295
  110.0 1.4 %slice_bitcast_fusion = f32[32,128]{1,0:T(8,128)} fusion(f32[3,160,256]{2,1,0:T(8,128)} %shard_map.78), kind=kLoop, calls=%fused_computation.43 | loop fusion | bytes 32768 | tf_op jit(solution)/shard_map/squeeze | solution.py:337
  111.5 1.5 %divide_subtract_fusion = (f32[2,32,128]{2,1,0:T(8,128)S(1)}, f32[2,32,128]{2,1,0:T(8,128)}) fusion(f32[2,32,128]{2,1,0:T(8,128)S(1)} %multiply_reduce_fusion, f32[32,128]{1,0:T(8,128)S(1)} %copy-done.11, f32[32,128]{1,0:T(8,128)S(1)} %copy-done.12, f32[3,160,256]{2,1,0:T(8,128)} %shard_map.78), kind=kLoop, calls=%fused_computation.42 | loop fusion | flops 24576 | bytes 163840 | tf_op jit(solution)/shard_map/sub | solution.py:69
  113.0 2.9 %fusion.21 = (f32[2,64,32,128]{3,1,2,0:T(8,128)S(1)}, f32[2,64,32,128]{3,1,2,0:T(8,128)S(1)}) fusion(f32[4,64,32,128]{3,1,2,0:T(8,128)} %copy-done.1, f32[2,32,128]{2,1,0:T(8,128)S(1)} %get-tuple-element.10, f32[64,32,128]{2,0,1:T(8,128)S(1)} %copy.8), kind=kLoop, calls=%fused_computation.64 | loop fusion | flops 1048576 | bytes 9469952 | tf_op jit(solution)/shard_map/slice | solution.py:70
  116.5 4.4 %copy.17 = f32[4,64,32,128]{3,2,1,0:T(8,128)} copy(f32[4,64,32,128]{3,1,2,0:T(8,128)S(1)} %pad_maximum_fusion) | data formatting | bytes 8388608
  (75 shorter events, 14.7 us)
Async XLA Ops:
  0.6 12.1 %copy-start.2 = (s32[32,128]{1,0:T(8,128)S(1)}, s32[32,128]{1,0:T(8,128)}, u32[]{:S(2)}) copy-start(s32[32,128]{1,0:T(8,128)} %depth_ref.3) | copy-start | bytes 49156
  0.6 25.3 %copy-start.13 = (f32[2,32,128]{2,1,0:T(8,128)S(1)}, f32[2,32,128]{2,1,0:T(8,128)}, u32[]{:S(2)}) copy-start(f32[2,32,128]{2,1,0:T(8,128)} %param.9) | copy-start | bytes 98308
  0.7 25.3 %copy-start.14 = (f32[32,128]{1,0:T(8,128)S(1)}, f32[32,128]{1,0:T(8,128)}, u32[]{:S(2)}) copy-start(f32[32,128]{1,0:T(8,128)} %param.8) | copy-start | bytes 49156
  0.7 26.4 %copy-start.6 = (f32[4,64,64]{2,1,0:T(8,128)S(1)}, f32[4,64,64]{2,1,0:T(8,128)}, u32[]{:S(2)}) copy-start(f32[4,64,64]{2,1,0:T(8,128)} %param.7) | copy-start | bytes 196612
  0.7 28.8 %slice-start = ((f32[4,64,64]{2,1,0:T(8,128)}), f32[1,64,64]{2,1,0:T(8,128)S(1)}, s32[]{:S(2)}) async-start(f32[4,64,64]{2,1,0:T(8,128)} %param.7), calls=%async_computation | async-start | bytes 65536 | tf_op jit(solution)/shard_map/slice | solution.py:35
  5.5 28.3 %collective-permute-start.2 = (f32[4,2,32,128]{3,2,1,0:T(8,128)}, f32[4,2,32,128]{3,2,1,0:T(8,128)}, u32[]{:S(2)}, u32[]{:S(2)}) collective-permute-start(f32[4,2,32,128]{3,2,1,0:T(8,128)} %shard_map.76), channel_id=1, source_target_pairs={{0,1},{1,2},{2,3},{3,4},{4,5},{5,6},{6,7},{7,8},{8,9},{9,10},{10,1... | collective-permute-start | bytes 393224 | tf_op jit(solution)/shard_map/ppermute | solution.py:318
  10.8 23.0 %collective-permute-start.3 = (f32[4,2,32,128]{3,2,1,0:T(8,128)}, f32[4,2,32,128]{3,2,1,0:T(8,128)}, u32[]{:S(2)}, u32[]{:S(2)}) collective-permute-start(f32[4,2,32,128]{3,2,1,0:T(8,128)} %shard_map.76), channel_id=1, source_target_pairs={{1,0},{2,1},{3,2},{4,3},{5,4},{6,5},{7,6},{8,7},{9,8},{10,9},{11,1... | collective-permute-start | bytes 393224 | tf_op jit(solution)/shard_map/ppermute | solution.py:319
  16.1 19.4 %collective-permute-start = (f32[4,64,2,128]{3,2,1,0:T(2,128)}, f32[4,64,2,128]{3,2,1,0:T(2,128)S(1)}, u32[]{:S(2)}, u32[]{:S(2)}) collective-permute-start(f32[4,64,2,128]{3,2,1,0:T(2,128)} %get-tuple-element.19), channel_id=1, source_target_pairs={{0,16},{16,32},{32,48},{48,64},{64,80},{80,96},{96,112},{112,128},... | collective-permute-start | bytes 786440 | tf_op jit(solution)/shard_map/ppermute | solution.py:59
  19.3 16.2 %collective-permute-start.1 = (f32[4,64,2,128]{3,2,1,0:T(2,128)}, f32[4,64,2,128]{3,2,1,0:T(2,128)}, u32[]{:S(2)}, u32[]{:S(2)}) collective-permute-start(f32[4,64,2,128]{3,2,1,0:T(2,128)} %get-tuple-element.18), channel_id=1, source_target_pairs={{16,0},{32,16},{48,32},{64,48},{80,64},{96,80},{112,96},{128,112},... | collective-permute-start | bytes 786440 | tf_op jit(solution)/shard_map/ppermute | solution.py:60
  33.8 34.6 %copy-start.4 = (f32[1,64,64]{1,2,0:T(8,128)S(1)}, f32[1,64,64]{1,2,0:T(8,128)}, u32[]{:S(2)}) copy-start(f32[1,64,64]{1,2,0:T(8,128)} %copy.22) | copy-start | bytes 49156
  33.8 34.6 %copy-start.5 = (f32[1,32,64]{1,2,0:T(8,128)S(1)}, f32[1,32,64]{1,2,0:T(8,128)}, u32[]{:S(2)}) copy-start(f32[1,32,64]{1,2,0:T(8,128)} %copy.20) | copy-start | bytes 24580
  55.4 22.7 %collective-permute-start.4 = (f32[6,32,128]{2,1,0:T(8,128)S(1)}, f32[6,32,128]{2,1,0:T(8,128)S(1)}, u32[]{:S(2)}, u32[]{:S(2)}) collective-permute-start(f32[6,32,128]{2,1,0:T(8,128)S(1)} %pad_maximum_fusion.2), channel_id=1, source_target_pairs={{0,32},{16,48},{32,64},{48,80},{64,96},{80,112},{96,128},{112,144}... | collective-permute-start | bytes 294920 | tf_op jit(solution)/shard_map/ppermute | solution.py:83
  58.1 20.0 %collective-permute-start.5 = (f32[6,32,128]{2,1,0:T(8,128)S(1)}, f32[6,32,128]{2,1,0:T(8,128)S(1)}, u32[]{:S(2)}, u32[]{:S(2)}) collective-permute-start(f32[6,32,128]{2,1,0:T(8,128)S(1)} %pad_maximum_fusion.2), channel_id=1, source_target_pairs={{0,16},{16,32},{32,48},{48,64},{64,80},{80,96},{96,112},{112,128},... | collective-permute-start | bytes 294920 | tf_op jit(solution)/shard_map/ppermute | solution.py:83
  61.1 17.0 %collective-permute-start.6 = (f32[6,32,128]{2,1,0:T(8,128)S(1)}, f32[6,32,128]{2,1,0:T(8,128)S(1)}, u32[]{:S(2)}, u32[]{:S(2)}) collective-permute-start(f32[6,32,128]{2,1,0:T(8,128)S(1)} %pad_maximum_fusion.2), channel_id=1, source_target_pairs={{16,0},{32,16},{48,32},{64,48},{80,64},{96,80},{112,96},{128,112},... | collective-permute-start | bytes 294920 | tf_op jit(solution)/shard_map/ppermute | solution.py:84
  65.5 12.7 %collective-permute-start.7 = (f32[6,32,128]{2,1,0:T(8,128)S(1)}, f32[6,32,128]{2,1,0:T(8,128)S(1)}, u32[]{:S(2)}, u32[]{:S(2)}) collective-permute-start(f32[6,32,128]{2,1,0:T(8,128)S(1)} %pad_maximum_fusion.2), channel_id=1, source_target_pairs={{32,0},{48,16},{64,32},{80,48},{96,64},{112,80},{128,96},{144,112}... | collective-permute-start | bytes 294920 | tf_op jit(solution)/shard_map/ppermute | solution.py:84
  68.4 8.8 %copy-start.8 = (f32[32,128]{1,0:T(8,128)S(1)}, f32[32,128]{1,0:T(8,128)}, u32[]{:S(2)}) copy-start(f32[32,128]{1,0:T(8,128)} %get-tuple-element.28) | copy-start | bytes 49156
  68.4 8.8 %copy-start.9 = (f32[32,128]{1,0:T(8,128)S(1)}, f32[32,128]{1,0:T(8,128)}, u32[]{:S(2)}) copy-start(f32[32,128]{1,0:T(8,128)} %get-tuple-element.29) | copy-start | bytes 49156
  68.4 8.8 %copy-start.10 = (f32[32,128]{1,0:T(8,128)S(1)}, f32[32,128]{1,0:T(8,128)}, u32[]{:S(2)}) copy-start(f32[32,128]{1,0:T(8,128)} %get-tuple-element.30) | copy-start | bytes 49156
  77.3 9.9 %copy-start = (f32[4,64,32,128]{3,2,1,0:T(8,128)S(1)}, f32[4,64,32,128]{3,2,1,0:T(8,128)}, u32[]{:S(2)}) copy-start(f32[4,64,32,128]{3,2,1,0:T(8,128)} %state_ref.3) | copy-start | bytes 12582916
  78.4 16.0 %collective-permute-start.9 = (f32[6,160,64]{2,1,0:T(8,128)S(1)}, f32[6,160,64]{2,1,0:T(8,128)S(1)}, u32[]{:S(2)}, u32[]{:S(2)}) collective-permute-start(f32[6,160,64]{2,1,0:T(8,128)S(1)} %get-tuple-element.25), channel_id=1, source_target_pairs={{1,0},{2,1},{3,2},{4,3},{5,4},{6,5},{7,6},{8,7},{9,8},{10,9},{11,1... | collective-permute-start | bytes 737288 | tf_op jit(solution)/shard_map/ppermute | solution.py:84
  81.2 13.3 %collective-permute-start.8 = (f32[6,160,64]{2,1,0:T(8,128)S(1)}, f32[6,160,64]{2,1,0:T(8,128)S(1)}, u32[]{:S(2)}, u32[]{:S(2)}) collective-permute-start(f32[6,160,64]{2,1,0:T(8,128)S(1)} %get-tuple-element.24), channel_id=1, source_target_pairs={{0,1},{1,2},{2,3},{3,4},{4,5},{5,6},{6,7},{7,8},{8,9},{9,10},{10,1... | collective-permute-start | bytes 737288 | tf_op jit(solution)/shard_map/ppermute | solution.py:83
  94.0 2.0 %copy-start.15 = (f32[256]{0:T(256)S(1)}, f32[256]{0:T(256)}, u32[]{:S(2)}) copy-start(f32[256]{0:T(256)} %multiply_add_fusion.1) | copy-start | bytes 3076
  94.0 17.5 %copy-start.11 = (f32[32,128]{1,0:T(8,128)S(1)}, f32[32,128]{1,0:T(8,128)}, u32[]{:S(2)}) copy-start(f32[32,128]{1,0:T(8,128)} %get-tuple-element.33) | copy-start | bytes 49156
  94.0 17.5 %copy-start.12 = (f32[32,128]{1,0:T(8,128)S(1)}, f32[32,128]{1,0:T(8,128)}, u32[]{:S(2)}) copy-start(f32[32,128]{1,0:T(8,128)} %get-tuple-element.32) | copy-start | bytes 49156
  (3 other events, 4.2 us)

commit v7 on v6

--- a/solution.py
+++ b/solution.py
@@ -124,7 +124,7 @@
         return xm2, xm1, xp1, xp2, ym2, ym1, yp1, yp2
 
     def fourth(m2, m1, p1, p2):
-        return (8.0 * (p1 - m1) - (p2 - m2)) / 12.0
+        return (8.0 * (p1 - m1) - (p2 - m2)) * (1.0 / 12.0)
 
     def level(k, carry):
         global_level = chunk * depth_levels + k
@@ -313,6 +313,13 @@
     column_blocks = lax.axis_size(("gy", "mode"))
     anchor = lax.axis_index(("gy", "mode")) * y_cells
     coriolis = jnp.broadcast_to(coriolis_row(anchor, y_cells, y_cells * column_blocks), (8, y_cells))
+    rim = 2 * SUB
+    column_depth = depth_class.astype(jnp.float32) * level_block / levels
+    sea_mask = (depth_class > 0).astype(jnp.float32)
+    moving = jnp.stack([height, transport[0], transport[1]]) * sea_mask
+    early = jnp.concatenate([moving, column_depth[None]], axis=0)
+    early = wide_halo(early, "gx", 1, rim)
+    early = wide_halo(early, ("gy", "mode"), 2, rim)
     edges = pack_edges(state, depth_class)
     y_count = lax.axis_size(("gy", "mode"))
     from_south = lax.ppermute(edges, ("gy", "mode"), [(i, i + 1) for i in range(y_count - 1)])
@@ -320,13 +327,9 @@
     side = combine(from_south, from_north)
     provisional, forcing = stencil(state, depth_class, west, east, side, coriolis)
     updated = vertical_solve(state, provisional, active, depth_class, vertical_inverse)
-    column_depth = depth_class.astype(jnp.float32) * level_block / levels
-    sea_mask = (depth_class > 0).astype(jnp.float32)
-    moving = jnp.stack([height, transport[0], transport[1]]) * sea_mask
-    fields = jnp.stack([moving[0], moving[1], moving[2], forcing[0], forcing[1], column_depth])
-    rim = 2 * SUB
-    fields = wide_halo(fields, "gx", 1, rim)
-    fields = wide_halo(fields, ("gy", "mode"), 2, rim)
+    late = wide_halo(forcing, "gx", 1, rim)
+    late = wide_halo(late, ("gy", "mode"), 2, rim)
+    fields = jnp.concatenate([early[0:3], late, early[3:4]], axis=0)
     coriolis_wide = jnp.broadcast_to(
         coriolis_row(anchor - rim, y_cells + 2 * rim, y_cells * column_blocks), (8, y_cells + 2 * rim)
     )

time: 122 us -> 148 us (1.21)
  starting transfers between devices: 36.3 us -> 58.8 us
  waiting for transfers between devices: 0.03 us -> 3.94 us
    ppermute x3 -> x6, starting transfers between devices: 11.7 us -> 24.8 us  [wide_halo(): lax.ppermute(tail, axis, [(i, i + hop) for i in range(count - hop)])]
    ppermute x3 -> x6, starting transfers between devices: 10 us -> 19.4 us  [wide_halo(): lax.ppermute(head, axis, [(i + hop, i) for i in range(count - hop)])]
    ppermute x3 -> x6, waiting for transfers between devices: 0.01 us -> 2.38 us  [wide_halo(): lax.ppermute(tail, axis, [(i, i + hop) for i in range(count - hop)])]
    slice x5, local copies, waits for them, and re-layouts: 1.82 us -> 0.01 us  [vertical_solve(): inverse[class_index, :band * (class_index + 1)]]
    concatenate x0 -> x2, other arithmetic: none -> 1.66 us  [the longest x1 1.04 us: body(): fields = jnp.concatenate([early[0:3], late, early[3:4]], axis=0)]
    ppermute x3 -> x6, waiting for transfers between devices: 0.01 us -> 1.54 us  [wide_halo(): lax.ppermute(head, axis, [(i + hop, i) for i in range(count - hop)])]
    unnamed x40 -> x48, local copies, waits for them, and re-layouts: 10.2 us -> 11.2 us
  transfers between devices with their start and end apart: 10 -> 16, of which waited for: 0 -> 4; matrix products, arithmetic and copies ran while one was open for 25% -> 21% of each run, Pallas kernels for 0% -> 0%
where the time goes in v7:
time: 148 us; the launch traced here: 147 us
  starting transfers between devices  58.8 us (40%)
  Pallas kernels  36.1 us (24%)
  other arithmetic  20.1 us (14%)
  local copies, waits for them, and re-layouts  17.5 us (12%)
  matrix products  8.78 us (6%)
  waiting for transfers between devices  3.94 us (3%)
    ppermute x6, starting transfers between devices, wide_halo(): lax.ppermute(tail, axis, [(i, i + hop) for i in range(count - hop)])  24.8 us
    ppermute x6, starting transfers between devices, wide_halo(): lax.ppermute(head, axis, [(i + hop, i) for i in range(count - hop)])  19.4 us
    pallas_call x1, Pallas kernels, stencil(): pl.pallas_call(stencil_kernel, grid=(steps,), out_shape=(jax.ShapeDtypeSt...  17.9 us
    pallas_call x1, Pallas kernels, local_waves(): pl.pallas_call(wave_kernel, out_shape=jax.ShapeDtypeStruct(moving.shape,...  13.5 us
    unnamed x48, local copies, waits for them, and re-layouts  11.2 us
    dot_general x1, matrix products, vertical_solve(): jnp.einsum('kl,flxy->fkxy', stacked, provisional, precision=lax.Precision...  8.78 us
    ppermute x1, starting transfers between devices, body(): lax.ppermute(edges, ('gy', 'mode'), [(i, i + 1) for i in range(y_count -...  5.31 us
    ppermute x1, starting transfers between devices, edge_halo(): after = lax.ppermute(head, axis, [(i + 1, i) for i in range(ends)])  4.91 us
  transfers between devices with their start and end apart: 16, of which 4 were waited for; matrix products, arithmetic and copies ran while one was open for 21% of the time, Pallas kernels for 0%

profile of v7, /device:TPU:103, one launch (start us, length us, event | category | flops | bytes accessed | tf_op | source)
XLA Modules:
  0.0 146.5 jit_solution(3663302981872671584)
XLA Ops:
  0.7 4.8 %shard_map.76 = f32[4,2,32,128]{3,2,1,0:T(8,128)} custom-call(s32[32,128]{1,0:T(8,128)} %depth_ref.3, f32[4,64,32,128]{3,2,1,0:T(8,128)} %state_ref.3), custom_call_target="tpu_custom_call" | custom-call | flops 4194304 | bytes 4194304 | tf_op jit(solution)/shard_map/pallas_call | solution.py:223
  5.5 5.3 %collective-permute-start.2 = (f32[4,2,32,128]{3,2,1,0:T(8,128)}, f32[4,2,32,128]{3,2,1,0:T(8,128)}, u32[]{:S(2)}, u32[]{:S(2)}) collective-permute-start(f32[4,2,32,128]{3,2,1,0:T(8,128)} %shard_map.76), channel_id=1, source_target_pairs={{0,1},{1,2},{2,3},{3,4},{4,5},{5,6},{6,7},{7,8},{8,9},{9,10},{10,1... | collective-permute-start | bytes 393224 | tf_op jit(solution)/shard_map/ppermute | solution.py:325
  10.8 1.9 %collective-permute-start.3 = (f32[4,2,32,128]{3,2,1,0:T(8,128)}, f32[4,2,32,128]{3,2,1,0:T(8,128)}, u32[]{:S(2)}, u32[]{:S(2)}) collective-permute-start(f32[4,2,32,128]{3,2,1,0:T(8,128)} %shard_map.76), channel_id=1, source_target_pairs={{1,0},{2,1},{3,2},{4,3},{5,4},{6,5},{7,6},{8,7},{9,8},{10,9},{11,1... | collective-permute-start | bytes 393224 | tf_op jit(solution)/shard_map/ppermute | solution.py:326
  14.6 4.8 %collective-permute-start.4 = (f32[4,32,128]{2,1,0:T(8,128)}, f32[4,32,128]{2,1,0:T(8,128)}, u32[]{:S(2)}, u32[]{:S(2)}) collective-permute-start(f32[4,32,128]{2,1,0:T(8,128)} %pad_maximum_fusion.2), channel_id=1, source_target_pairs={{0,32},{16,48},{32,64},{48,80},{64,96},{80,112},{96,128},{112,144}... | collective-permute-start | bytes 196616 | tf_op jit(solution)/shard_map/ppermute | solution.py:83
  19.4 2.3 %collective-permute-start.5 = (f32[4,32,128]{2,1,0:T(8,128)}, f32[4,32,128]{2,1,0:T(8,128)}, u32[]{:S(2)}, u32[]{:S(2)}) collective-permute-start(f32[4,32,128]{2,1,0:T(8,128)} %pad_maximum_fusion.2), channel_id=1, source_target_pairs={{0,16},{16,32},{32,48},{48,64},{64,80},{80,96},{96,112},{112,128},... | collective-permute-start | bytes 196616 | tf_op jit(solution)/shard_map/ppermute | solution.py:83
  21.7 5.1 %collective-permute-start.6 = (f32[4,32,128]{2,1,0:T(8,128)}, f32[4,32,128]{2,1,0:T(8,128)}, u32[]{:S(2)}, u32[]{:S(2)}) collective-permute-start(f32[4,32,128]{2,1,0:T(8,128)} %pad_maximum_fusion.2), channel_id=1, source_target_pairs={{16,0},{32,16},{48,32},{64,48},{80,64},{96,80},{112,96},{128,112},... | collective-permute-start | bytes 196616 | tf_op jit(solution)/shard_map/ppermute | solution.py:84
  34.1 1.8 %slice_multiply_fusion.10 = (f32[4,64,2,128]{3,2,1,0:T(2,128)S(1)}, f32[4,64,2,128]{3,2,1,0:T(2,128)S(1)}) fusion(f32[4,64,32,128]{3,2,1,0:T(8,128)} %state_ref.3, f32[64,2,128]{2,1,0:T(2,128)} %get-tuple-element.20, f32[64,2,128]{2,1,0:T(2,128)} %get-tuple-element.21), kind=kLoop, calls=%fused_computation.33 | loop fusion | flops 131072 | bytes 1179648 | tf_op jit(solution)/shard_map/mul | solution.py:55
  35.9 1.9 %collective-permute-start.7 = (f32[4,32,128]{2,1,0:T(8,128)}, f32[4,32,128]{2,1,0:T(8,128)S(1)}, u32[]{:S(2)}, u32[]{:S(2)}) collective-permute-start(f32[4,32,128]{2,1,0:T(8,128)} %pad_maximum_fusion.2), channel_id=1, source_target_pairs={{32,0},{48,16},{64,32},{80,48},{96,64},{112,80},{128,96},{144,112}... | collective-permute-start | bytes 196616 | tf_op jit(solution)/shard_map/ppermute | solution.py:84
  38.6 2.5 %collective-permute-start = (f32[4,64,2,128]{3,2,1,0:T(2,128)S(1)}, f32[4,64,2,128]{3,2,1,0:T(2,128)S(1)}, u32[]{:S(2)}, u32[]{:S(2)}) collective-permute-start(f32[4,64,2,128]{3,2,1,0:T(2,128)S(1)} %get-tuple-element.19), channel_id=1, source_target_pairs={{0,16},{16,32},{32,48},{48,64},{64,80},{80,96},{96,112},{112,128},... | collective-permute-start | bytes 786440 | tf_op jit(solution)/shard_map/ppermute | solution.py:59
  42.0 4.9 %collective-permute-start.1 = (f32[4,64,2,128]{3,2,1,0:T(2,128)S(1)}, f32[4,64,2,128]{3,2,1,0:T(2,128)}, u32[]{:S(2)}, u32[]{:S(2)}) collective-permute-start(f32[4,64,2,128]{3,2,1,0:T(2,128)S(1)} %get-tuple-element.18), channel_id=1, source_target_pairs={{16,0},{32,16},{48,32},{64,48},{80,64},{96,80},{112,96},{128,112},... | collective-permute-start | bytes 786440 | tf_op jit(solution)/shard_map/ppermute | solution.py:60
  48.0 2.5 %collective-permute-start.9 = (f32[4,160,64]{2,1,0:T(8,128)S(1)}, f32[4,160,64]{2,1,0:T(8,128)S(1)}, u32[]{:S(2)}, u32[]{:S(2)}) collective-permute-start(f32[4,160,64]{2,1,0:T(8,128)S(1)} %get-tuple-element.23), channel_id=1, source_target_pairs={{1,0},{2,1},{3,2},{4,3},{5,4},{6,5},{7,6},{8,7},{9,8},{10,9},{11,1... | collective-permute-start | bytes 491528 | tf_op jit(solution)/shard_map/ppermute | solution.py:84
  50.5 5.8 %collective-permute-start.8 = (f32[4,160,64]{2,1,0:T(8,128)S(1)}, f32[4,160,64]{2,1,0:T(8,128)S(1)}, u32[]{:S(2)}, u32[]{:S(2)}) collective-permute-start(f32[4,160,64]{2,1,0:T(8,128)S(1)} %get-tuple-element.22), channel_id=1, source_target_pairs={{0,1},{1,2},{2,3},{3,4},{4,5},{5,6},{6,7},{7,8},{8,9},{9,10},{10,1... | collective-permute-start | bytes 491528 | tf_op jit(solution)/shard_map/ppermute | solution.py:83
  62.7 17.9 %shard_map.77 = (f32[4,64,32,128]{3,2,1,0:T(8,128)}, f32[2,32,128]{2,1,0:T(8,128)}) custom-call(s32[32,128]{1,0:T(8,128)} %depth_ref.3, f32[8,128]{1,0:T(8,128)} %broadcast_in_dim.6.coriolis_ref, f32[4,64,32,128]{3,2,1,0:T(8,128)} %state_ref.3, f32[4,64,2,128]{3,2,1,0:T(2,128)} %copy-done.3, f32[4,64,2,128]{3,2,1,0:T(2,128)} %collective-permute-done.1.east_ref, ...), custom_call_target="tpu_custom_call" | custom-call | flops 62914560 | bytes 8388608 | tf_op jit(solution)/shard_map/pallas_call | solution.py:185
  80.6 3.0 %collective-permute-start.10 = (f32[2,32,128]{2,1,0:T(8,128)}, f32[2,32,128]{2,1,0:T(8,128)S(1)}, u32[]{:S(2)}, u32[]{:S(2)}) collective-permute-start(f32[2,32,128]{2,1,0:T(8,128)} %get-tuple-element.6), channel_id=1, source_target_pairs={{0,32},{16,48},{32,64},{48,80},{64,96},{80,112},{96,128},{112,144}... | collective-permute-start | bytes 98312 | tf_op jit(solution)/shard_map/ppermute | solution.py:83
  83.6 1.9 %collective-permute-start.11 = (f32[2,32,128]{2,1,0:T(8,128)}, f32[2,32,128]{2,1,0:T(8,128)S(1)}, u32[]{:S(2)}, u32[]{:S(2)}) collective-permute-start(f32[2,32,128]{2,1,0:T(8,128)} %get-tuple-element.6), channel_id=1, source_target_pairs={{0,16},{16,32},{32,48},{48,64},{64,80},{80,96},{96,112},{112,128},... | collective-permute-start | bytes 98312 | tf_op jit(solution)/shard_map/ppermute | solution.py:83
  85.6 5.5 %collective-permute-start.12 = (f32[2,32,128]{2,1,0:T(8,128)}, f32[2,32,128]{2,1,0:T(8,128)S(1)}, u32[]{:S(2)}, u32[]{:S(2)}) collective-permute-start(f32[2,32,128]{2,1,0:T(8,128)} %get-tuple-element.6), channel_id=1, source_target_pairs={{16,0},{32,16},{48,32},{64,48},{80,64},{96,80},{112,96},{128,112},... | collective-permute-start | bytes 98312 | tf_op jit(solution)/shard_map/ppermute | solution.py:84
  91.0 2.5 %collective-permute-start.13 = (f32[2,32,128]{2,1,0:T(8,128)}, f32[2,32,128]{2,1,0:T(8,128)S(1)}, u32[]{:S(2)}, u32[]{:S(2)}) collective-permute-start(f32[2,32,128]{2,1,0:T(8,128)} %get-tuple-element.6), channel_id=1, source_target_pairs={{32,0},{48,16},{64,32},{80,48},{96,64},{112,80},{128,96},{144,112}... | collective-permute-start | bytes 98312 | tf_op jit(solution)/shard_map/ppermute | solution.py:84
  93.7 8.8 %fusion.3 = f32[4,160,32,128]{3,1,2,0:T(8,128)S(1)} fusion(f32[4,64,32,128]{3,2,1,0:T(8,128)} %get-tuple-element.5, f32[64,64]{0,1:T(8,128)S(1)} %bitcast.18, f32[48,64]{0,1:T(8,128)S(1)} %bitcast.16, f32[32,64]{0,1:T(8,128)S(1)} %bitcast.19, f32[16,64]{0,1:T(8,128)S(1)} %bitcast.17), kind=kOutput, calls=%fused_computation.6 | convolution fusion | flops 1006663680 | bytes 14721024 | tf_op jit(solution)/shard_map/kl,flxy->fkxy/dot_general | solution.py:37
  104.7 4.7 %fusion = f32[4,64,32,128]{3,1,2,0:T(8,128)S(1)} fusion(f32[4,16,32,128]{3,1,2,0:T(8,128)S(1)} %get-tuple-element.15, f32[4,16,32,128]{3,1,2,0:T(8,128)S(1)} %get-tuple-element.14, f32[4,16,32,128]{3,1,2,0:T(8,128)S(1)} %get-tuple-element.13, f32[4,16,32,128]{3,1,2,0:T(8,128)S(1)} %get-tuple-element.12, f32[4,64,32,128]{3,2,1,0:T(8,128)S(1)} %copy-done, ...), kind=kLoop, calls=%fused_computation.1 | loop fusion | flops 6291456 | bytes 14680064 | tf_op jit(solution)/shard_map/add | solution.py:48
  109.7 1.9 %collective-permute-start.15 = (f32[2,160,64]{2,1,0:T(8,128)S(1)}, f32[2,160,64]{2,1,0:T(8,128)S(1)}, u32[]{:S(2)}, u32[]{:S(2)}) collective-permute-start(f32[2,160,64]{2,1,0:T(8,128)S(1)} %get-tuple-element.25), channel_id=1, source_target_pairs={{1,0},{2,1},{3,2},{4,3},{5,4},{6,5},{7,6},{8,7},{9,8},{10,9},{11,1... | collective-permute-start | bytes 245768 | tf_op jit(solution)/shard_map/ppermute | solution.py:84
  111.6 6.9 %collective-permute-start.14 = (f32[2,160,64]{2,1,0:T(8,128)S(1)}, f32[2,160,64]{2,1,0:T(8,128)S(1)}, u32[]{:S(2)}, u32[]{:S(2)}) collective-permute-start(f32[2,160,64]{2,1,0:T(8,128)S(1)} %get-tuple-element.24), channel_id=1, source_target_pairs={{0,1},{1,2},{2,3},{3,4},{4,5},{5,6},{6,7},{7,8},{8,9},{9,10},{10,1... | collective-permute-start | bytes 245768 | tf_op jit(solution)/shard_map/ppermute | solution.py:83
  122.2 13.5 %shard_map.78 = f32[3,160,256]{2,1,0:T(8,128)} custom-call(f32[3,160,256]{2,1,0:T(8,128)} %slice.136.moving_ref, f32[3,160,256]{2,1,0:T(8,128)} %fusion.13.fixed_ref, f32[8,256]{1,0:T(8,128)} %broadcast_in_dim.8.coriolis_ref), custom_call_target="tpu_custom_call" | custom-call | flops 52428800 | bytes 1474560 | tf_op jit(solution)/shard_map/pallas_call | solution.py:295
  138.6 2.9 %fusion.22 = (f32[2,64,32,128]{3,1,2,0:T(8,128)S(1)}, f32[2,64,32,128]{3,1,2,0:T(8,128)S(1)}) fusion(f32[4,64,32,128]{3,1,2,0:T(8,128)} %copy-done.1, f32[2,32,128]{2,1,0:T(8,128)S(1)} %get-tuple-element.10, f32[64,32,128]{2,0,1:T(8,128)S(1)} %copy.8), kind=kLoop, calls=%fused_computation.73 | loop fusion | flops 1048576 | bytes 9469952 | tf_op jit(solution)/shard_map/slice | solution.py:70
  142.1 4.4 %copy.17 = f32[4,64,32,128]{3,2,1,0:T(8,128)} copy(f32[4,64,32,128]{3,1,2,0:T(8,128)S(1)} %pad_maximum_fusion) | data formatting | bytes 8388608
  (98 shorter events, 27.8 us)
Async XLA Ops:
  0.7 27.4 %copy-start.8 = (f32[4,64,64]{2,1,0:T(8,128)S(1)}, f32[4,64,64]{2,1,0:T(8,128)}, u32[]{:S(2)}) copy-start(f32[4,64,64]{2,1,0:T(8,128)} %param.7) | copy-start | bytes 196612
  0.7 29.5 %slice-start = ((f32[4,64,64]{2,1,0:T(8,128)}), f32[1,64,64]{2,1,0:T(8,128)S(1)}, s32[]{:S(2)}) async-start(f32[4,64,64]{2,1,0:T(8,128)} %param.7), calls=%async_computation | async-start | bytes 65536 | tf_op jit(solution)/shard_map/slice | solution.py:35
  5.5 45.0 %collective-permute-start.2 = (f32[4,2,32,128]{3,2,1,0:T(8,128)}, f32[4,2,32,128]{3,2,1,0:T(8,128)}, u32[]{:S(2)}, u32[]{:S(2)}) collective-permute-start(f32[4,2,32,128]{3,2,1,0:T(8,128)} %shard_map.76), channel_id=1, source_target_pairs={{0,1},{1,2},{2,3},{3,4},{4,5},{5,6},{6,7},{7,8},{8,9},{9,10},{10,1... | collective-permute-start | bytes 393224 | tf_op jit(solution)/shard_map/ppermute | solution.py:325
  10.8 45.5 %collective-permute-start.3 = (f32[4,2,32,128]{3,2,1,0:T(8,128)}, f32[4,2,32,128]{3,2,1,0:T(8,128)}, u32[]{:S(2)}, u32[]{:S(2)}) collective-permute-start(f32[4,2,32,128]{3,2,1,0:T(8,128)} %shard_map.76), channel_id=1, source_target_pairs={{1,0},{2,1},{3,2},{4,3},{5,4},{6,5},{7,6},{8,7},{9,8},{10,9},{11,1... | collective-permute-start | bytes 393224 | tf_op jit(solution)/shard_map/ppermute | solution.py:326
  14.6 21.3 %collective-permute-start.4 = (f32[4,32,128]{2,1,0:T(8,128)}, f32[4,32,128]{2,1,0:T(8,128)}, u32[]{:S(2)}, u32[]{:S(2)}) collective-permute-start(f32[4,32,128]{2,1,0:T(8,128)} %pad_maximum_fusion.2), channel_id=1, source_target_pairs={{0,32},{16,48},{32,64},{48,80},{64,96},{80,112},{96,128},{112,144}... | collective-permute-start | bytes 196616 | tf_op jit(solution)/shard_map/ppermute | solution.py:83
  19.4 19.2 %collective-permute-start.5 = (f32[4,32,128]{2,1,0:T(8,128)}, f32[4,32,128]{2,1,0:T(8,128)}, u32[]{:S(2)}, u32[]{:S(2)}) collective-permute-start(f32[4,32,128]{2,1,0:T(8,128)} %pad_maximum_fusion.2), channel_id=1, source_target_pairs={{0,16},{16,32},{32,48},{48,64},{64,80},{80,96},{96,112},{112,128},... | collective-permute-start | bytes 196616 | tf_op jit(solution)/shard_map/ppermute | solution.py:83
  21.7 20.3 %collective-permute-start.6 = (f32[4,32,128]{2,1,0:T(8,128)}, f32[4,32,128]{2,1,0:T(8,128)}, u32[]{:S(2)}, u32[]{:S(2)}) collective-permute-start(f32[4,32,128]{2,1,0:T(8,128)} %pad_maximum_fusion.2), channel_id=1, source_target_pairs={{16,0},{32,16},{48,32},{64,48},{80,64},{96,80},{112,96},{128,112},... | collective-permute-start | bytes 196616 | tf_op jit(solution)/shard_map/ppermute | solution.py:84
  35.9 11.9 %collective-permute-start.7 = (f32[4,32,128]{2,1,0:T(8,128)}, f32[4,32,128]{2,1,0:T(8,128)S(1)}, u32[]{:S(2)}, u32[]{:S(2)}) collective-permute-start(f32[4,32,128]{2,1,0:T(8,128)} %pad_maximum_fusion.2), channel_id=1, source_target_pairs={{32,0},{48,16},{64,32},{80,48},{96,64},{112,80},{128,96},{144,112}... | collective-permute-start | bytes 196616 | tf_op jit(solution)/shard_map/ppermute | solution.py:84
  38.6 22.8 %collective-permute-start = (f32[4,64,2,128]{3,2,1,0:T(2,128)S(1)}, f32[4,64,2,128]{3,2,1,0:T(2,128)S(1)}, u32[]{:S(2)}, u32[]{:S(2)}) collective-permute-start(f32[4,64,2,128]{3,2,1,0:T(2,128)S(1)} %get-tuple-element.19), channel_id=1, source_target_pairs={{0,16},{16,32},{32,48},{48,64},{64,80},{80,96},{96,112},{112,128},... | collective-permute-start | bytes 786440 | tf_op jit(solution)/shard_map/ppermute | solution.py:59
  42.0 19.4 %collective-permute-start.1 = (f32[4,64,2,128]{3,2,1,0:T(2,128)S(1)}, f32[4,64,2,128]{3,2,1,0:T(2,128)}, u32[]{:S(2)}, u32[]{:S(2)}) collective-permute-start(f32[4,64,2,128]{3,2,1,0:T(2,128)S(1)} %get-tuple-element.18), channel_id=1, source_target_pairs={{16,0},{32,16},{48,32},{64,48},{80,64},{96,80},{112,96},{128,112},... | collective-permute-start | bytes 786440 | tf_op jit(solution)/shard_map/ppermute | solution.py:60
  47.9 45.7 %copy-start.4 = (f32[1,48,64]{1,2,0:T(8,128)S(1)}, f32[1,48,64]{1,2,0:T(8,128)}, u32[]{:S(2)}) copy-start(f32[1,48,64]{1,2,0:T(8,128)} %copy.21) | copy-start | bytes 36868
  47.9 45.7 %copy-start.5 = (f32[1,16,64]{1,2,0:T(8,128)S(1)}, f32[1,16,64]{1,2,0:T(8,128)}, u32[]{:S(2)}) copy-start(f32[1,16,64]{1,2,0:T(8,128)} %copy.19) | copy-start | bytes 12292
  48.0 45.7 %copy-start.6 = (f32[1,64,64]{1,2,0:T(8,128)S(1)}, f32[1,64,64]{1,2,0:T(8,128)}, u32[]{:S(2)}) copy-start(f32[1,64,64]{1,2,0:T(8,128)} %copy.22) | copy-start | bytes 49156
  48.0 45.7 %copy-start.7 = (f32[1,32,64]{1,2,0:T(8,128)S(1)}, f32[1,32,64]{1,2,0:T(8,128)}, u32[]{:S(2)}) copy-start(f32[1,32,64]{1,2,0:T(8,128)} %copy.20) | copy-start | bytes 24580
  48.0 11.1 %collective-permute-start.9 = (f32[4,160,64]{2,1,0:T(8,128)S(1)}, f32[4,160,64]{2,1,0:T(8,128)S(1)}, u32[]{:S(2)}, u32[]{:S(2)}) collective-permute-start(f32[4,160,64]{2,1,0:T(8,128)S(1)} %get-tuple-element.23), channel_id=1, source_target_pairs={{1,0},{2,1},{3,2},{4,3},{5,4},{6,5},{7,6},{8,7},{9,8},{10,9},{11,1... | collective-permute-start | bytes 491528 | tf_op jit(solution)/shard_map/ppermute | solution.py:84
  50.5 9.8 %collective-permute-start.8 = (f32[4,160,64]{2,1,0:T(8,128)S(1)}, f32[4,160,64]{2,1,0:T(8,128)S(1)}, u32[]{:S(2)}, u32[]{:S(2)}) collective-permute-start(f32[4,160,64]{2,1,0:T(8,128)S(1)} %get-tuple-element.22), channel_id=1, source_target_pairs={{0,1},{1,2},{2,3},{3,4},{4,5},{5,6},{6,7},{7,8},{8,9},{9,10},{10,1... | collective-permute-start | bytes 491528 | tf_op jit(solution)/shard_map/ppermute | solution.py:83
  80.6 28.8 %collective-permute-start.10 = (f32[2,32,128]{2,1,0:T(8,128)}, f32[2,32,128]{2,1,0:T(8,128)S(1)}, u32[]{:S(2)}, u32[]{:S(2)}) collective-permute-start(f32[2,32,128]{2,1,0:T(8,128)} %get-tuple-element.6), channel_id=1, source_target_pairs={{0,32},{16,48},{32,64},{48,80},{64,96},{80,112},{96,128},{112,144}... | collective-permute-start | bytes 98312 | tf_op jit(solution)/shard_map/ppermute | solution.py:83
  83.6 25.8 %collective-permute-start.11 = (f32[2,32,128]{2,1,0:T(8,128)}, f32[2,32,128]{2,1,0:T(8,128)S(1)}, u32[]{:S(2)}, u32[]{:S(2)}) collective-permute-start(f32[2,32,128]{2,1,0:T(8,128)} %get-tuple-element.6), channel_id=1, source_target_pairs={{0,16},{16,32},{32,48},{48,64},{64,80},{80,96},{96,112},{112,128},... | collective-permute-start | bytes 98312 | tf_op jit(solution)/shard_map/ppermute | solution.py:83
  85.6 23.9 %collective-permute-start.12 = (f32[2,32,128]{2,1,0:T(8,128)}, f32[2,32,128]{2,1,0:T(8,128)S(1)}, u32[]{:S(2)}, u32[]{:S(2)}) collective-permute-start(f32[2,32,128]{2,1,0:T(8,128)} %get-tuple-element.6), channel_id=1, source_target_pairs={{16,0},{32,16},{48,32},{64,48},{80,64},{96,80},{112,96},{128,112},... | collective-permute-start | bytes 98312 | tf_op jit(solution)/shard_map/ppermute | solution.py:84
  91.0 18.5 %collective-permute-start.13 = (f32[2,32,128]{2,1,0:T(8,128)}, f32[2,32,128]{2,1,0:T(8,128)S(1)}, u32[]{:S(2)}, u32[]{:S(2)}) collective-permute-start(f32[2,32,128]{2,1,0:T(8,128)} %get-tuple-element.6), channel_id=1, source_target_pairs={{32,0},{48,16},{64,32},{80,48},{96,64},{112,80},{128,96},{144,112}... | collective-permute-start | bytes 98312 | tf_op jit(solution)/shard_map/ppermute | solution.py:84
  109.4 27.7 %copy-start.12 = (f32[32,128]{1,0:T(8,128)S(1)}, f32[32,128]{1,0:T(8,128)}, u32[]{:S(2)}) copy-start(f32[32,128]{1,0:T(8,128)} %get-tuple-element.32) | copy-start | bytes 49156
  109.4 27.7 %copy-start.13 = (f32[32,128]{1,0:T(8,128)S(1)}, f32[32,128]{1,0:T(8,128)}, u32[]{:S(2)}) copy-start(f32[32,128]{1,0:T(8,128)} %get-tuple-element.33) | copy-start | bytes 49156
  109.7 9.7 %collective-permute-start.15 = (f32[2,160,64]{2,1,0:T(8,128)S(1)}, f32[2,160,64]{2,1,0:T(8,128)S(1)}, u32[]{:S(2)}, u32[]{:S(2)}) collective-permute-start(f32[2,160,64]{2,1,0:T(8,128)S(1)} %get-tuple-element.25), channel_id=1, source_target_pairs={{1,0},{2,1},{3,2},{4,3},{5,4},{6,5},{7,6},{8,7},{9,8},{10,9},{11,1... | collective-permute-start | bytes 245768 | tf_op jit(solution)/shard_map/ppermute | solution.py:84
  111.6 9.0 %collective-permute-start.14 = (f32[2,160,64]{2,1,0:T(8,128)S(1)}, f32[2,160,64]{2,1,0:T(8,128)S(1)}, u32[]{:S(2)}, u32[]{:S(2)}) collective-permute-start(f32[2,160,64]{2,1,0:T(8,128)S(1)} %get-tuple-element.24), channel_id=1, source_target_pairs={{0,1},{1,2},{2,3},{3,4},{4,5},{5,6},{6,7},{7,8},{8,9},{9,10},{10,1... | collective-permute-start | bytes 245768 | tf_op jit(solution)/shard_map/ppermute | solution.py:83
  (11 other events, 94.8 us)

commit v8 on v6

--- a/solution.py
+++ b/solution.py
@@ -59,15 +59,6 @@
     before = lax.ppermute(tail, axis, [(i, i + 1) for i in range(ends)])
     after = lax.ppermute(head, axis, [(i + 1, i) for i in range(ends)])
     return before, after
-
-
-def finish(updated, waves, active, depth_class, level_block, levels):
-    counted = jnp.maximum(depth_class * level_block, 1).astype(jnp.float32)
-    safe_depth = jnp.maximum(depth_class, 1).astype(jnp.float32) * level_block / levels
-    column_means = jnp.sum(active * updated[2:4], axis=1) / counted
-    carried = waves[1:3] / safe_depth
-    velocity = updated[2:4] + active * (carried - column_means)[:, None]
-    return jnp.concatenate([updated[0:2], velocity], axis=0)
 
 
 def wide_halo(cells, axis, dim, width):
@@ -124,7 +115,7 @@
         return xm2, xm1, xp1, xp2, ym2, ym1, yp1, yp2
 
     def fourth(m2, m1, p1, p2):
-        return (8.0 * (p1 - m1) - (p2 - m2)) / 12.0
+        return (8.0 * (p1 - m1) - (p2 - m2)) * (1.0 / 12.0)
 
     def level(k, carry):
         global_level = chunk * depth_levels + k
@@ -238,69 +229,126 @@
     return jnp.where(lane % 4 >= 2, from_south, from_north)
 
 
-def wave_kernel(moving_ref, fixed_ref, coriolis_ref, out_ref):
+def wave_kernel(moving_ref, fixed_ref, coriolis_ref, out_ref, work_ref):
     rows, cols = moving_ref.shape[1], moving_ref.shape[2]
-    column_depth = fixed_ref[2]
-    sea_mask = (column_depth > 0.0).astype(jnp.float32)
-    force_east = fixed_ref[0]
-    force_north = fixed_ref[1]
-    coriolis = jnp.broadcast_to(coriolis_ref[0:1, :], (rows, cols))
-
-    def x_slope_rolled(values):
-        return (pltpu.roll(values, rows - 1, 0) - pltpu.roll(values, 1, 0)) * 0.5
-
-    def y_slope_rolled(values):
-        return (pltpu.roll(values, cols - 1, 1) - pltpu.roll(values, 1, 1)) * 0.5
-
-    out_ref[...] = moving_ref[...]
-
-    def step(index, carry):
-        surface = out_ref[0]
-        east_old = out_ref[1]
-        north_old = out_ref[2]
-        surface_mid = sea_mask * (
-            surface - WAVE_STEP * (x_slope_rolled(east_old) + y_slope_rolled(north_old))
-        )
-        east_new = sea_mask * (
-            east_old
-            + WAVE_STEP
-            * (
-                -GRAVITY * column_depth * x_slope_rolled(surface_mid)
-                + coriolis * north_old
-                + force_east
-                - BOTTOM_DRAG * east_old
+    inner_rows, inner_cols = out_ref.shape[1], out_ref.shape[2]
+    rim = (rows - inner_rows) // 2
+    groups = 4
+    per_group = SUB // groups
+    trim = 2 * per_group
+    work_ref[...] = moving_ref[...]
+    for group in range(groups):
+        low = trim * group
+        high = rows - trim * group
+        span = high - low
+        column_depth = fixed_ref[2, low:high]
+        sea_mask = (column_depth > 0.0).astype(jnp.float32)
+        force_east = fixed_ref[0, low:high]
+        force_north = fixed_ref[1, low:high]
+        coriolis = jnp.broadcast_to(coriolis_ref[0:1, :], (span, cols))
+
+        def x_slope_rolled(values):
+            return (pltpu.roll(values, span - 1, 0) - pltpu.roll(values, 1, 0)) * 0.5
+
+        def y_slope_rolled(values):
+            return (pltpu.roll(values, cols - 1, 1) - pltpu.roll(values, 1, 1)) * 0.5
+
+        def step(index, carry):
+            surface = work_ref[0, low:high]
+            east_old = work_ref[1, low:high]
+            north_old = work_ref[2, low:high]
+            surface_mid = sea_mask * (
+                surface - WAVE_STEP * (x_slope_rolled(east_old) + y_slope_rolled(north_old))
             )
-        )
-        north_new = sea_mask * (
-            north_old
-            + WAVE_STEP
-            * (
-                -GRAVITY * column_depth * y_slope_rolled(surface_mid)
-                - coriolis * east_new
-                + force_north
-                - BOTTOM_DRAG * north_old
+            east_new = sea_mask * (
+                east_old
+                + WAVE_STEP
+                * (
+                    -GRAVITY * column_depth * x_slope_rolled(surface_mid)
+                    + coriolis * north_old
+                    + force_east
+                    - BOTTOM_DRAG * east_old
+                )
             )
-        )
-        out_ref[0] = surface_mid
-        out_ref[1] = east_new
-        out_ref[2] = north_new
-        return carry
-
-    lax.fori_loop(0, SUB, step, 0)
-
-
-def local_waves(moving, fixed, coriolis):
+            north_new = sea_mask * (
+                north_old
+                + WAVE_STEP
+                * (
+                    -GRAVITY * column_depth * y_slope_rolled(surface_mid)
+                    - coriolis * east_new
+                    + force_north
+                    - BOTTOM_DRAG * north_old
+                )
+            )
+            work_ref[0, low:high] = surface_mid
+            work_ref[1, low:high] = east_new
+            work_ref[2, low:high] = north_new
+            return carry
+
+        lax.fori_loop(0, per_group, step, 0)
+    for field in range(3):
+        middle = work_ref[field, rim : rim + inner_rows]
+        out_ref[field] = pltpu.roll(middle, cols - rim, 1)[:, :inner_cols]
+
+
+def local_waves(moving, fixed, coriolis, inner_rows, inner_cols):
     rows, cols = moving.shape[1], moving.shape[2]
     elements = rows * cols
     return pl.pallas_call(
         wave_kernel,
-        out_shape=jax.ShapeDtypeStruct(moving.shape, jnp.float32),
+        out_shape=jax.ShapeDtypeStruct((3, inner_rows, inner_cols), jnp.float32),
         in_specs=[pl.BlockSpec(memory_space=pltpu.VMEM)] * 3,
         out_specs=pl.BlockSpec(memory_space=pltpu.VMEM),
+        scratch_shapes=[pltpu.VMEM(moving.shape, jnp.float32)],
         cost_estimate=pl.CostEstimate(
-            flops=SUB * 40 * elements, transcendentals=0, bytes_accessed=4 * 9 * elements
+            flops=SUB * 30 * elements, transcendentals=0, bytes_accessed=4 * 7 * elements
         ),
     )(moving, fixed, coriolis)
+
+
+def finish_kernel(depth_ref, waves_ref, updated_ref, out_ref):
+    field = pl.program_id(0)
+    levels = updated_ref.shape[1]
+    block = levels // 4
+    depth_class = depth_ref[...]
+
+    @pl.when(field < 2)
+    def _():
+        out_ref[...] = updated_ref[...]
+
+    @pl.when(field >= 2)
+    def _():
+        reach = depth_class * block
+        counted = jnp.maximum(reach, 1).astype(jnp.float32)
+        safe_depth = jnp.maximum(depth_class, 1).astype(jnp.float32) * block / levels
+        total = jnp.zeros(depth_class.shape, jnp.float32)
+        for k in range(levels):
+            active = (k < reach).astype(jnp.float32)
+            total = total + active * updated_ref[0, k]
+        carried = waves_ref[0] / safe_depth
+        shift = carried - total / counted
+        for k in range(levels):
+            active = (k < reach).astype(jnp.float32)
+            out_ref[0, k] = updated_ref[0, k] + active * shift
+
+
+def finish_state(updated, waves, depth_class):
+    fields, levels, rows, cols = updated.shape
+    whole = pl.BlockSpec((1, levels, rows, cols), lambda f: (f, 0, 0, 0))
+    return pl.pallas_call(
+        finish_kernel,
+        grid=(fields,),
+        out_shape=jax.ShapeDtypeStruct(updated.shape, jnp.float32),
+        in_specs=[
+            pl.BlockSpec((rows, cols), lambda f: (0, 0)),
+            pl.BlockSpec((1, rows, cols), lambda f: (jnp.maximum(f - 1, 0), 0, 0)),
+            whole,
+        ],
+        out_specs=whole,
+        cost_estimate=pl.CostEstimate(
+            flops=4 * updated.size, transcendentals=0, bytes_accessed=4 * 2 * updated.size
+        ),
+    )(depth_class, waves, updated)
 
 
 def body(state, depth_class, vertical_inverse, height, transport):
@@ -330,10 +378,9 @@
     coriolis_wide = jnp.broadcast_to(
         coriolis_row(anchor - rim, y_cells + 2 * rim, y_cells * column_blocks), (8, y_cells + 2 * rim)
     )
-    waves_wide = local_waves(fields[0:3], fields[3:6], coriolis_wide)
     x_cells = depth_class.shape[0]
-    waves = waves_wide[:, rim : rim + x_cells, rim : rim + y_cells]
-    state_next = finish(updated, waves, active, depth_class, level_block, levels)
+    waves = local_waves(fields[0:3], fields[3:6], coriolis_wide, x_cells, y_cells)
+    state_next = finish_state(updated, waves, depth_class)
     return (state_next, waves[0], waves[1:3])
 
 

time: 122 us -> 127 us (1.041)
  waiting for transfers between devices: 0.03 us -> 6.41 us
  other arithmetic: 20.7 us -> 16.9 us
  Pallas kernels: 36.1 us -> 39.2 us
    dot_general x0 -> x1, local copies, waits for them, and re-layouts: none -> 10.1 us  [vertical_solve(): jnp.einsum('kl,flxy->fkxy', stacked, provisional, precision=lax.Precision...]
    unnamed x40 -> x27, local copies, waits for them, and re-layouts: 10.2 us -> 1.12 us
    ppermute x3, waiting for transfers between devices: 0.01 us -> 5.61 us  [wide_halo(): lax.ppermute(head, axis, [(i + hop, i) for i in range(count - hop)])]
    add x1, other arithmetic: 0.79 us -> 5.68 us  [vertical_solve(): part = part + chosen[class_index] * every[:, first:first + band]]
    pallas_call x1 -> x2, Pallas kernels: 13.4 us -> 16.5 us  [the longest x1 11.5 us: local_waves(): pl.pallas_call(wave_kernel, out_shape=jax.ShapeDtypeStruct((3, inner_rows...]
    slice x1 -> x0, other arithmetic: 2.91 us -> none  [finish(): return jnp.concatenate([updated[0:2], velocity], axis=0)]
    add x1, other arithmetic: 4.75 us -> 2.81 us  [vertical_solve(): return active * solved + (1.0 - active) * state]
    sub x1 -> x0, other arithmetic: 1.53 us -> none  [finish(): velocity = updated[2:4] + active * (carried - column_means)[:, None]]
  transfers between devices with their start and end apart: 10 -> 10, of which waited for: 0 -> 2; matrix products, arithmetic and copies ran while one was open for 25% -> 29% of each run, Pallas kernels for 0% -> 0%
where the time goes in v8:
time: 127 us; the launch traced here: 126 us
  Pallas kernels  39.2 us (31%)
  starting transfers between devices  36.4 us (29%)
  local copies, waits for them, and re-layouts  17.6 us (14%)
  other arithmetic  16.9 us (13%)
  matrix products  8.76 us (7%)
  waiting for transfers between devices  6.41 us (5%)
    pallas_call x1, Pallas kernels, stencil(): pl.pallas_call(stencil_kernel, grid=(steps,), out_shape=(jax.ShapeDtypeSt...  17.9 us
    ppermute x3, starting transfers between devices, wide_halo(): lax.ppermute(tail, axis, [(i, i + hop) for i in range(count - hop)])  11.6 us
    pallas_call x1, Pallas kernels, local_waves(): pl.pallas_call(wave_kernel, out_shape=jax.ShapeDtypeStruct((3, inner_rows...  11.5 us
    ppermute x3, starting transfers between devices, wide_halo(): lax.ppermute(head, axis, [(i + hop, i) for i in range(count - hop)])  10.3 us
    dot_general x1, local copies, waits for them, and re-layouts, vertical_solve(): jnp.einsum('kl,flxy->fkxy', stacked, provisional, precision=lax.Precision...  10.1 us
    dot_general x1, matrix products, vertical_solve(): jnp.einsum('kl,flxy->fkxy', stacked, provisional, precision=lax.Precision...  8.76 us
    add x1, other arithmetic, vertical_solve(): part = part + chosen[class_index] * every[:, first:first + band]  5.68 us
    ppermute x3, waiting for transfers between devices, wide_halo(): lax.ppermute(head, axis, [(i + hop, i) for i in range(count - hop)])  5.61 us
  transfers between devices with their start and end apart: 10, of which 2 were waited for; matrix products, arithmetic and copies ran while one was open for 29% of the time, Pallas kernels for 0%

profile of v8, /device:TPU:103, one launch (start us, length us, event | category | flops | bytes accessed | tf_op | source)
XLA Modules:
  0.0 126.3 jit_solution(8776269959655036673)
XLA Ops:
  0.7 4.8 %shard_map.76 = f32[4,2,32,128]{3,2,1,0:T(8,128)} custom-call(s32[32,128]{1,0:T(8,128)} %depth_ref.5, f32[4,64,32,128]{3,2,1,0:T(8,128)} %state_ref.3), custom_call_target="tpu_custom_call" | custom-call | flops 4194304 | bytes 4194304 | tf_op jit(solution)/shard_map/pallas_call | solution.py:214
  5.5 5.3 %collective-permute-start.2 = (f32[4,2,32,128]{3,2,1,0:T(8,128)}, f32[4,2,32,128]{3,2,1,0:T(8,128)S(1)}, u32[]{:S(2)}, u32[]{:S(2)}) collective-permute-start(f32[4,2,32,128]{3,2,1,0:T(8,128)} %shard_map.76), channel_id=1, source_target_pairs={{0,1},{1,2},{2,3},{3,4},{4,5},{5,6},{6,7},{7,8},{8,9},{9,10},{10,1... | collective-permute-start | bytes 393224 | tf_op jit(solution)/shard_map/ppermute | solution.py:366
  10.8 1.9 %collective-permute-start.3 = (f32[4,2,32,128]{3,2,1,0:T(8,128)}, f32[4,2,32,128]{3,2,1,0:T(8,128)}, u32[]{:S(2)}, u32[]{:S(2)}) collective-permute-start(f32[4,2,32,128]{3,2,1,0:T(8,128)} %shard_map.76), channel_id=1, source_target_pairs={{1,0},{2,1},{3,2},{4,3},{5,4},{6,5},{7,6},{8,7},{9,8},{10,9},{11,1... | collective-permute-start | bytes 393224 | tf_op jit(solution)/shard_map/ppermute | solution.py:367
  12.9 1.8 %slice_multiply_fusion.10 = (f32[4,64,2,128]{3,2,1,0:T(2,128)S(1)}, f32[4,64,2,128]{3,2,1,0:T(2,128)S(1)}) fusion(f32[4,64,32,128]{3,2,1,0:T(8,128)} %state_ref.3, f32[64,2,128]{2,1,0:T(2,128)S(1)} %get-tuple-element.13, f32[64,2,128]{2,1,0:T(2,128)S(1)} %get-tuple-element.14), kind=kLoop, calls=%fused_computation.25 | loop fusion | flops 131072 | bytes 1179648 | tf_op jit(solution)/shard_map/mul | solution.py:55
  14.7 3.2 %collective-permute-start = (f32[4,64,2,128]{3,2,1,0:T(2,128)S(1)}, f32[4,64,2,128]{3,2,1,0:T(2,128)S(1)}, u32[]{:S(2)}, u32[]{:S(2)}) collective-permute-start(f32[4,64,2,128]{3,2,1,0:T(2,128)S(1)} %get-tuple-element.12), channel_id=1, source_target_pairs={{0,16},{16,32},{32,48},{48,64},{64,80},{80,96},{96,112},{112,128},... | collective-permute-start | bytes 786440 | tf_op jit(solution)/shard_map/ppermute | solution.py:59
  17.9 4.2 %collective-permute-start.1 = (f32[4,64,2,128]{3,2,1,0:T(2,128)S(1)}, f32[4,64,2,128]{3,2,1,0:T(2,128)S(1)}, u32[]{:S(2)}, u32[]{:S(2)}) collective-permute-start(f32[4,64,2,128]{3,2,1,0:T(2,128)S(1)} %get-tuple-element.11), channel_id=1, source_target_pairs={{16,0},{32,16},{48,32},{64,48},{80,64},{96,80},{112,96},{128,112},... | collective-permute-start | bytes 786440 | tf_op jit(solution)/shard_map/ppermute | solution.py:60
  27.5 1.6 %fusion.10.side_ref = f32[4,2,32,128]{3,2,1,0:T(8,128)} fusion(f32[4,2,32,128]{3,2,1,0:T(8,128)S(1)} %collective-permute-done.2, f32[4,2,32,128]{3,2,1,0:T(8,128)} %collective-permute-done.3, s32[128]{0:T(128)} %get-tuple-element.24, s32[128]{0:T(128)} %get-tuple-element.25, pred[128]{0:T(512)(128)(4,1)} %compare_and_fusion), kind=kLoop, calls=%fused_computation.28 | loop fusion | flops 98304 | bytes 394368 | tf_op jit(solution)/shard_map/jit(_where)/select_n | solution.py:229
  29.1 1.2 broadcast_in_dim.4.coriolis_ref
  30.4 17.9 %shard_map.77 = (f32[4,64,32,128]{3,2,1,0:T(8,128)}, f32[2,32,128]{2,1,0:T(8,128)}) custom-call(s32[32,128]{1,0:T(8,128)} %depth_ref.5, f32[8,128]{1,0:T(8,128)} %broadcast_in_dim.4.coriolis_ref, f32[4,64,32,128]{3,2,1,0:T(8,128)} %state_ref.3, f32[4,64,2,128]{3,2,1,0:T(2,128)} %copy-done.2, f32[4,64,2,128]{3,2,1,0:T(2,128)} %copy-done.3, ...), custom_call_target="tpu_custom_call" | custom-call | flops 62914560 | bytes 8388608 | tf_op jit(solution)/shard_map/pallas_call | solution.py:176
  49.0 3.0 %collective-permute-start.4 = (f32[6,32,128]{2,1,0:T(8,128)S(1)}, f32[6,32,128]{2,1,0:T(8,128)S(1)}, u32[]{:S(2)}, u32[]{:S(2)}) collective-permute-start(f32[6,32,128]{2,1,0:T(8,128)S(1)} %pad_maximum_fusion.1), channel_id=1, source_target_pairs={{0,32},{16,48},{32,64},{48,80},{64,96},{80,112},{96,128},{112,144}... | collective-permute-start | bytes 294920 | tf_op jit(solution)/shard_map/ppermute | solution.py:74
  52.0 2.0 %collective-permute-start.5 = (f32[6,32,128]{2,1,0:T(8,128)S(1)}, f32[6,32,128]{2,1,0:T(8,128)S(1)}, u32[]{:S(2)}, u32[]{:S(2)}) collective-permute-start(f32[6,32,128]{2,1,0:T(8,128)S(1)} %pad_maximum_fusion.1), channel_id=1, source_target_pairs={{0,16},{16,32},{32,48},{48,64},{64,80},{80,96},{96,112},{112,128},... | collective-permute-start | bytes 294920 | tf_op jit(solution)/shard_map/ppermute | solution.py:74
  54.0 5.4 %collective-permute-start.6 = (f32[6,32,128]{2,1,0:T(8,128)S(1)}, f32[6,32,128]{2,1,0:T(8,128)S(1)}, u32[]{:S(2)}, u32[]{:S(2)}) collective-permute-start(f32[6,32,128]{2,1,0:T(8,128)S(1)} %pad_maximum_fusion.1), channel_id=1, source_target_pairs={{16,0},{32,16},{48,32},{64,48},{80,64},{96,80},{112,96},{128,112},... | collective-permute-start | bytes 294920 | tf_op jit(solution)/shard_map/ppermute | solution.py:75
  59.4 2.7 %collective-permute-start.7 = (f32[6,32,128]{2,1,0:T(8,128)S(1)}, f32[6,32,128]{2,1,0:T(8,128)S(1)}, u32[]{:S(2)}, u32[]{:S(2)}) collective-permute-start(f32[6,32,128]{2,1,0:T(8,128)S(1)} %pad_maximum_fusion.1), channel_id=1, source_target_pairs={{32,0},{48,16},{64,32},{80,48},{96,64},{112,80},{128,96},{144,112}... | collective-permute-start | bytes 294920 | tf_op jit(solution)/shard_map/ppermute | solution.py:75
  62.2 8.8 %fusion.1 = f32[4,32,128,160]{2,3,1,0:T(8,128)S(1)} fusion(f32[4,64,32,128]{3,2,1,0:T(8,128)} %get-tuple-element.6, f32[64,64]{0,1:T(8,128)S(1)} %bitcast.20, f32[48,64]{0,1:T(8,128)S(1)} %bitcast.18, f32[32,64]{0,1:T(8,128)S(1)} %bitcast.21, f32[16,64]{0,1:T(8,128)S(1)} %bitcast.19), kind=kOutput, calls=%fused_computation.3 | convolution fusion | flops 1006663680 | bytes 14721024 | tf_op jit(solution)/shard_map/kl,flxy->fkxy/dot_general | solution.py:37
  71.0 10.1 %copy.22 = f32[4,32,128,160]{2,1,3,0:T(8,128)} copy(f32[4,32,128,160]{2,3,1,0:T(8,128)S(1)} %fusion.1) | data formatting | bytes 20971520 | tf_op jit(solution)/shard_map/kl,flxy->fkxy/dot_general | solution.py:37
  81.1 5.7 %fusion.6 = (f32[4,16,32,128]{3,2,1,0:T(8,128)S(1)}, f32[4,16,32,128]{3,2,1,0:T(8,128)S(1)}, f32[4,16,32,128]{3,2,1,0:T(8,128)S(1)}, f32[4,16,32,128]{3,2,1,0:T(8,128)S(1)}) fusion(f32[4,160,32,128]{3,2,1,0:T(8,128)} %bitcast.17, f32[32,128]{1,0:T(8,128)S(1)} %copy-done.8, f32[32,128]{1,0:T(8,128)S(1)} %copy-done.6, f32[32,128]{1,0:T(8,128)S(1)} %copy-done.7, ...), kind=kLoop, calls=%fused_computation.15 | loop fusion | flops 4194304 | bytes 14745600 | tf_op jit(solution)/shard_map/add | solution.py:45
  87.1 6.5 %collective-permute-start.8 = (f32[6,160,64]{2,1,0:T(8,128)S(1)}, f32[6,160,64]{2,1,0:T(8,128)S(1)}, u32[]{:S(2)}, u32[]{:S(2)}) collective-permute-start(f32[6,160,64]{2,1,0:T(8,128)S(1)} %get-tuple-element.17), channel_id=1, source_target_pairs={{0,1},{1,2},{2,3},{3,4},{4,5},{5,6},{6,7},{7,8},{8,9},{9,10},{10,1... | collective-permute-start | bytes 737288 | tf_op jit(solution)/shard_map/ppermute | solution.py:74
  93.6 2.1 %collective-permute-start.9 = (f32[6,160,64]{2,1,0:T(8,128)S(1)}, f32[6,160,64]{2,1,0:T(8,128)S(1)}, u32[]{:S(2)}, u32[]{:S(2)}) collective-permute-start(f32[6,160,64]{2,1,0:T(8,128)S(1)} %get-tuple-element.18), channel_id=1, source_target_pairs={{1,0},{2,1},{3,2},{4,3},{5,4},{6,5},{7,6},{8,7},{9,8},{10,9},{11,1... | collective-permute-start | bytes 737288 | tf_op jit(solution)/shard_map/ppermute | solution.py:75
  95.8 2.8 %fusion.updated_ref = f32[4,64,32,128]{3,2,1,0:T(8,128)} fusion(f32[4,16,32,128]{3,2,1,0:T(8,128)S(1)} %get-tuple-element.10, f32[4,16,32,128]{3,2,1,0:T(8,128)S(1)} %get-tuple-element.9, f32[4,16,32,128]{3,2,1,0:T(8,128)S(1)} %get-tuple-element.8, f32[4,16,32,128]{3,2,1,0:T(8,128)S(1)} %get-tuple-element.7, f32[4,64,32,128]{3,2,1,0:T(8,128)S(1)} %copy-done, ...), kind=kLoop, calls=%fused_computation.2 | loop fusion | flops 6291456 | bytes 14680064 | tf_op jit(solution)/shard_map/add | solution.py:48
  99.4 5.6 %collective-permute-done.9 = f32[6,160,64]{2,1,0:T(8,128)S(1)} collective-permute-done((f32[6,160,64]{2,1,0:T(8,128)S(1)}, f32[6,160,64]{2,1,0:T(8,128)S(1)}, u32[]{:S(2)}, u32[]{:S(2)}) %collective-permute-start.9) | collective-permute-done | bytes 245792 | tf_op jit(solution)/shard_map/ppermute | solution.py:75
  107.1 11.5 %shard_map.78.waves_ref = f32[3,32,128]{2,1,0:T(8,128)} custom-call(f32[3,160,256]{2,1,0:T(8,128)} %get-tuple-element.16.moving_ref, f32[3,160,256]{2,1,0:T(8,128)} %get-tuple-element.15.fixed_ref, f32[8,256]{1,0:T(8,128)} %broadcast_in_dim.5.coriolis_ref), custom_call_target="tpu_custom_call" | custom-call | flops 39321600 | bytes 1146880 | tf_op jit(solution)/shard_map/pallas_call | solution.py:297
  118.6 1.4 %slice.123 = f32[2,32,128]{2,1,0:T(8,128)} slice(f32[3,32,128]{2,1,0:T(8,128)} %shard_map.78.waves_ref), slice={[1:3], [0:32], [0:128]} | slice | bytes 65536 | tf_op jit(solution)/shard_map/slice | solution.py:384
  120.0 1.3 %slice_bitcast_fusion = f32[32,128]{1,0:T(8,128)} fusion(f32[3,32,128]{2,1,0:T(8,128)} %shard_map.78.waves_ref), kind=kLoop, calls=%fused_computation.38 | loop fusion | bytes 32768 | tf_op jit(solution)/shard_map/squeeze | solution.py:384
  121.3 5.0 %shard_map.79 = f32[4,64,32,128]{3,2,1,0:T(8,128)} custom-call(s32[32,128]{1,0:T(8,128)} %depth_ref.5, f32[3,32,128]{2,1,0:T(8,128)} %shard_map.78.waves_ref, f32[4,64,32,128]{3,2,1,0:T(8,128)} %fusion.updated_ref), custom_call_target="tpu_custom_call" | custom-call | flops 4194304 | bytes 8388608 | tf_op jit(solution)/shard_map/pallas_call | solution.py:338
  (59 shorter events, 9.4 us)
Async XLA Ops:
  0.6 12.1 %copy-start.1 = (s32[32,128]{1,0:T(8,128)S(1)}, s32[32,128]{1,0:T(8,128)}, u32[]{:S(2)}) copy-start(s32[32,128]{1,0:T(8,128)} %depth_ref.5) | copy-start | bytes 49156
  0.6 25.2 %copy-start.4 = (f32[4,64,64]{2,1,0:T(8,128)S(1)}, f32[4,64,64]{2,1,0:T(8,128)}, u32[]{:S(2)}) copy-start(f32[4,64,64]{2,1,0:T(8,128)} %param.7) | copy-start | bytes 196612
  0.7 25.8 %slice-start = ((f32[4,64,64]{2,1,0:T(8,128)}), f32[1,64,64]{2,1,0:T(8,128)S(1)}, s32[]{:S(2)}) async-start(f32[4,64,64]{2,1,0:T(8,128)} %param.7), calls=%async_computation | async-start | bytes 65536 | tf_op jit(solution)/shard_map/slice | solution.py:35
  5.5 22.0 %collective-permute-start.2 = (f32[4,2,32,128]{3,2,1,0:T(8,128)}, f32[4,2,32,128]{3,2,1,0:T(8,128)S(1)}, u32[]{:S(2)}, u32[]{:S(2)}) collective-permute-start(f32[4,2,32,128]{3,2,1,0:T(8,128)} %shard_map.76), channel_id=1, source_target_pairs={{0,1},{1,2},{2,3},{3,4},{4,5},{5,6},{6,7},{7,8},{8,9},{9,10},{10,1... | collective-permute-start | bytes 393224 | tf_op jit(solution)/shard_map/ppermute | solution.py:366
  10.8 16.7 %collective-permute-start.3 = (f32[4,2,32,128]{3,2,1,0:T(8,128)}, f32[4,2,32,128]{3,2,1,0:T(8,128)}, u32[]{:S(2)}, u32[]{:S(2)}) collective-permute-start(f32[4,2,32,128]{3,2,1,0:T(8,128)} %shard_map.76), channel_id=1, source_target_pairs={{1,0},{2,1},{3,2},{4,3},{5,4},{6,5},{7,6},{8,7},{9,8},{10,9},{11,1... | collective-permute-start | bytes 393224 | tf_op jit(solution)/shard_map/ppermute | solution.py:367
  14.7 14.4 %collective-permute-start = (f32[4,64,2,128]{3,2,1,0:T(2,128)S(1)}, f32[4,64,2,128]{3,2,1,0:T(2,128)S(1)}, u32[]{:S(2)}, u32[]{:S(2)}) collective-permute-start(f32[4,64,2,128]{3,2,1,0:T(2,128)S(1)} %get-tuple-element.12), channel_id=1, source_target_pairs={{0,16},{16,32},{32,48},{48,64},{64,80},{80,96},{96,112},{112,128},... | collective-permute-start | bytes 786440 | tf_op jit(solution)/shard_map/ppermute | solution.py:59
  17.9 11.2 %collective-permute-start.1 = (f32[4,64,2,128]{3,2,1,0:T(2,128)S(1)}, f32[4,64,2,128]{3,2,1,0:T(2,128)S(1)}, u32[]{:S(2)}, u32[]{:S(2)}) collective-permute-start(f32[4,64,2,128]{3,2,1,0:T(2,128)S(1)} %get-tuple-element.11), channel_id=1, source_target_pairs={{16,0},{32,16},{48,32},{64,48},{80,64},{96,80},{112,96},{128,112},... | collective-permute-start | bytes 786440 | tf_op jit(solution)/shard_map/ppermute | solution.py:60
  29.1 1.3 copy-start.2
  29.1 1.2 copy-start.3
  49.0 37.8 %collective-permute-start.4 = (f32[6,32,128]{2,1,0:T(8,128)S(1)}, f32[6,32,128]{2,1,0:T(8,128)S(1)}, u32[]{:S(2)}, u32[]{:S(2)}) collective-permute-start(f32[6,32,128]{2,1,0:T(8,128)S(1)} %pad_maximum_fusion.1), channel_id=1, source_target_pairs={{0,32},{16,48},{32,64},{48,80},{64,96},{80,112},{96,128},{112,144}... | collective-permute-start | bytes 294920 | tf_op jit(solution)/shard_map/ppermute | solution.py:74
  52.0 34.8 %collective-permute-start.5 = (f32[6,32,128]{2,1,0:T(8,128)S(1)}, f32[6,32,128]{2,1,0:T(8,128)S(1)}, u32[]{:S(2)}, u32[]{:S(2)}) collective-permute-start(f32[6,32,128]{2,1,0:T(8,128)S(1)} %pad_maximum_fusion.1), channel_id=1, source_target_pairs={{0,16},{16,32},{32,48},{48,64},{64,80},{80,96},{96,112},{112,128},... | collective-permute-start | bytes 294920 | tf_op jit(solution)/shard_map/ppermute | solution.py:74
  54.0 32.8 %collective-permute-start.6 = (f32[6,32,128]{2,1,0:T(8,128)S(1)}, f32[6,32,128]{2,1,0:T(8,128)S(1)}, u32[]{:S(2)}, u32[]{:S(2)}) collective-permute-start(f32[6,32,128]{2,1,0:T(8,128)S(1)} %pad_maximum_fusion.1), channel_id=1, source_target_pairs={{16,0},{32,16},{48,32},{64,48},{80,64},{96,80},{112,96},{128,112},... | collective-permute-start | bytes 294920 | tf_op jit(solution)/shard_map/ppermute | solution.py:75
  59.4 27.5 %collective-permute-start.7 = (f32[6,32,128]{2,1,0:T(8,128)S(1)}, f32[6,32,128]{2,1,0:T(8,128)S(1)}, u32[]{:S(2)}, u32[]{:S(2)}) collective-permute-start(f32[6,32,128]{2,1,0:T(8,128)S(1)} %pad_maximum_fusion.1), channel_id=1, source_target_pairs={{32,0},{48,16},{64,32},{80,48},{96,64},{112,80},{128,96},{144,112}... | collective-permute-start | bytes 294920 | tf_op jit(solution)/shard_map/ppermute | solution.py:75
  70.9 10.1 %copy-start.6 = (f32[32,128]{1,0:T(8,128)S(1)}, f32[32,128]{1,0:T(8,128)}, u32[]{:S(2)}) copy-start(f32[32,128]{1,0:T(8,128)} %get-tuple-element.20) | copy-start | bytes 49156
  71.0 10.1 %copy-start.7 = (f32[32,128]{1,0:T(8,128)S(1)}, f32[32,128]{1,0:T(8,128)}, u32[]{:S(2)}) copy-start(f32[32,128]{1,0:T(8,128)} %get-tuple-element.21) | copy-start | bytes 49156
  71.0 10.1 %copy-start.8 = (f32[32,128]{1,0:T(8,128)S(1)}, f32[32,128]{1,0:T(8,128)}, u32[]{:S(2)}) copy-start(f32[32,128]{1,0:T(8,128)} %get-tuple-element.23) | copy-start | bytes 49156
  81.1 5.8 %copy-start.5 = (f32[2,32,128]{2,1,0:T(8,128)S(1)}, f32[2,32,128]{2,1,0:T(8,128)}, u32[]{:S(2)}) copy-start(f32[2,32,128]{2,1,0:T(8,128)} %get-tuple-element.5) | copy-start | bytes 98308
  81.1 14.7 %copy-start = (f32[4,64,32,128]{3,2,1,0:T(8,128)S(1)}, f32[4,64,32,128]{3,2,1,0:T(8,128)}, u32[]{:S(2)}) copy-start(f32[4,64,32,128]{3,2,1,0:T(8,128)} %state_ref.3) | copy-start | bytes 12582916
  87.1 12.3 %collective-permute-start.8 = (f32[6,160,64]{2,1,0:T(8,128)S(1)}, f32[6,160,64]{2,1,0:T(8,128)S(1)}, u32[]{:S(2)}, u32[]{:S(2)}) collective-permute-start(f32[6,160,64]{2,1,0:T(8,128)S(1)} %get-tuple-element.17), channel_id=1, source_target_pairs={{0,1},{1,2},{2,3},{3,4},{4,5},{5,6},{6,7},{7,8},{8,9},{9,10},{10,1... | collective-permute-start | bytes 737288 | tf_op jit(solution)/shard_map/ppermute | solution.py:74
  93.6 11.4 %collective-permute-start.9 = (f32[6,160,64]{2,1,0:T(8,128)S(1)}, f32[6,160,64]{2,1,0:T(8,128)S(1)}, u32[]{:S(2)}, u32[]{:S(2)}) collective-permute-start(f32[6,160,64]{2,1,0:T(8,128)S(1)} %get-tuple-element.18), channel_id=1, source_target_pairs={{1,0},{2,1},{3,2},{4,3},{5,4},{6,5},{7,6},{8,7},{9,8},{10,9},{11,1... | collective-permute-start | bytes 737288 | tf_op jit(solution)/shard_map/ppermute | solution.py:75
  98.6 7.9 %copy-start.9 = (f32[256]{0:T(256)S(1)}, f32[256]{0:T(256)}, u32[]{:S(2)}) copy-start(f32[256]{0:T(256)} %multiply_add_fusion) | copy-start | bytes 3076

commit v9 on v8

--- a/solution.py
+++ b/solution.py
@@ -59,6 +59,15 @@
     before = lax.ppermute(tail, axis, [(i, i + 1) for i in range(ends)])
     after = lax.ppermute(head, axis, [(i + 1, i) for i in range(ends)])
     return before, after
+
+
+def finish(updated, transport_next, active, depth_class, level_block, levels):
+    counted = jnp.maximum(depth_class * level_block, 1).astype(jnp.float32)
+    safe_depth = jnp.maximum(depth_class, 1).astype(jnp.float32) * level_block / levels
+    column_means = jnp.sum(active * updated[2:4], axis=1) / counted
+    carried = transport_next / safe_depth
+    velocity = updated[2:4] + active * (carried - column_means)[:, None]
+    return jnp.concatenate([updated[0:2], velocity], axis=0)
 
 
 def wide_halo(cells, axis, dim, width):
@@ -229,9 +238,9 @@
     return jnp.where(lane % 4 >= 2, from_south, from_north)
 
 
-def wave_kernel(moving_ref, fixed_ref, coriolis_ref, out_ref, work_ref):
+def wave_kernel(moving_ref, fixed_ref, coriolis_ref, height_ref, transport_ref, work_ref):
     rows, cols = moving_ref.shape[1], moving_ref.shape[2]
-    inner_rows, inner_cols = out_ref.shape[1], out_ref.shape[2]
+    inner_rows, inner_cols = height_ref.shape[0], height_ref.shape[1]
     rim = (rows - inner_rows) // 2
     groups = 4
     per_group = SUB // groups
@@ -288,7 +297,11 @@
         lax.fori_loop(0, per_group, step, 0)
     for field in range(3):
         middle = work_ref[field, rim : rim + inner_rows]
-        out_ref[field] = pltpu.roll(middle, cols - rim, 1)[:, :inner_cols]
+        inner = pltpu.roll(middle, cols - rim, 1)[:, :inner_cols]
+        if field == 0:
+            height_ref[...] = inner
+        else:
+            transport_ref[field - 1] = inner
 
 
 def local_waves(moving, fixed, coriolis, inner_rows, inner_cols):
@@ -296,59 +309,17 @@
     elements = rows * cols
     return pl.pallas_call(
         wave_kernel,
-        out_shape=jax.ShapeDtypeStruct((3, inner_rows, inner_cols), jnp.float32),
+        out_shape=(
+            jax.ShapeDtypeStruct((inner_rows, inner_cols), jnp.float32),
+            jax.ShapeDtypeStruct((2, inner_rows, inner_cols), jnp.float32),
+        ),
         in_specs=[pl.BlockSpec(memory_space=pltpu.VMEM)] * 3,
-        out_specs=pl.BlockSpec(memory_space=pltpu.VMEM),
+        out_specs=(pl.BlockSpec(memory_space=pltpu.VMEM), pl.BlockSpec(memory_space=pltpu.VMEM)),
         scratch_shapes=[pltpu.VMEM(moving.shape, jnp.float32)],
         cost_estimate=pl.CostEstimate(
             flops=SUB * 30 * elements, transcendentals=0, bytes_accessed=4 * 7 * elements
         ),
     )(moving, fixed, coriolis)
-
-
-def finish_kernel(depth_ref, waves_ref, updated_ref, out_ref):
-    field = pl.program_id(0)
-    levels = updated_ref.shape[1]
-    block = levels // 4
-    depth_class = depth_ref[...]
-
-    @pl.when(field < 2)
-    def _():
-        out_ref[...] = updated_ref[...]
-
-    @pl.when(field >= 2)
-    def _():
-        reach = depth_class * block
-        counted = jnp.maximum(reach, 1).astype(jnp.float32)
-        safe_depth = jnp.maximum(depth_class, 1).astype(jnp.float32) * block / levels
-        total = jnp.zeros(depth_class.shape, jnp.float32)
-        for k in range(levels):
-            active = (k < reach).astype(jnp.float32)
-            total = total + active * updated_ref[0, k]
-        carried = waves_ref[0] / safe_depth
-        shift = carried - total / counted
-        for k in range(levels):
-            active = (k < reach).astype(jnp.float32)
-            out_ref[0, k] = updated_ref[0, k] + active * shift
-
-
-def finish_state(updated, waves, depth_class):
-    fields, levels, rows, cols = updated.shape
-    whole = pl.BlockSpec((1, levels, rows, cols), lambda f: (f, 0, 0, 0))
-    return pl.pallas_call(
-        finish_kernel,
-        grid=(fields,),
-        out_shape=jax.ShapeDtypeStruct(updated.shape, jnp.float32),
-        in_specs=[
-            pl.BlockSpec((rows, cols), lambda f: (0, 0)),
-            pl.BlockSpec((1, rows, cols), lambda f: (jnp.maximum(f - 1, 0), 0, 0)),
-            whole,
-        ],
-        out_specs=whole,
-        cost_estimate=pl.CostEstimate(
-            flops=4 * updated.size, transcendentals=0, bytes_accessed=4 * 2 * updated.size
-        ),
-    )(depth_class, waves, updated)
 
 
 def body(state, depth_class, vertical_inverse, height, transport):
@@ -379,9 +350,9 @@
         coriolis_row(anchor - rim, y_cells + 2 * rim, y_cells * column_blocks), (8, y_cells + 2 * rim)
     )
     x_cells = depth_class.shape[0]
-    waves = local_waves(fields[0:3], fields[3:6], coriolis_wide, x_cells, y_cells)
-    state_next = finish_state(updated, waves, depth_class)
-    return (state_next, waves[0], waves[1:3])
+    height_next, transport_next = local_waves(fields[0:3], fields[3:6], coriolis_wide, x_cells, y_cells)
+    state_next = finish(updated, transport_next, active, depth_class, level_block, levels)
+    return (state_next, height_next, transport_next)
 
 
 def solution(mesh):

time: 127 us -> 118 us (0.929)
  waiting for transfers between devices: 6.41 us -> 0.03 us
  Pallas kernels: 39.2 us -> 34.4 us
  other arithmetic: 16.9 us -> 20 us
  local copies, waits for them, and re-layouts: 17.6 us -> 16.3 us
    dot_general x1 -> x0, local copies, waits for them, and re-layouts: 10.1 us -> none  [vertical_solve(): jnp.einsum('kl,flxy->fkxy', stacked, provisional, precision=lax.Precision...]
    unnamed x27 -> x40, local copies, waits for them, and re-layouts: 1.12 us -> 10.2 us
    ppermute x3, waiting for transfers between devices: 5.61 us -> 0.01 us  [wide_halo(): lax.ppermute(head, axis, [(i + hop, i) for i in range(count - hop)])]
    pallas_call x2 -> x1, Pallas kernels: 16.5 us -> 11.5 us  [local_waves(): pl.pallas_call(wave_kernel, out_shape=(jax.ShapeDtypeStruct((inner_rows,...]
    add x1, other arithmetic: 5.68 us -> 0.79 us  [vertical_solve(): part = part + chosen[class_index] * every[:, first:first + band]]
    slice x0 -> x1, other arithmetic: none -> 2.91 us  [finish(): return jnp.concatenate([updated[0:2], velocity], axis=0)]
    add x1, other arithmetic: 2.81 us -> 4.75 us  [vertical_solve(): return active * solved + (1.0 - active) * state]
    slice x1 -> x0, local copies, waits for them, and re-layouts: 1.37 us -> none  [body(): return (state_next, waves[0], waves[1:3])]
  transfers between devices with their start and end apart: 10 -> 10, of which waited for: 2 -> 0; matrix products, arithmetic and copies ran while one was open for 29% -> 26% of each run, Pallas kernels for 0% -> 0%
where the time goes in v9:
time: 118 us; the launch traced here: 117 us
  starting transfers between devices  36.3 us (31%)
  Pallas kernels  34.4 us (29%)
  other arithmetic  20 us (17%)
  local copies, waits for them, and re-layouts  16.3 us (14%)
  matrix products  8.77 us (7%)
    pallas_call x1, Pallas kernels, stencil(): pl.pallas_call(stencil_kernel, grid=(steps,), out_shape=(jax.ShapeDtypeSt...  17.9 us
    ppermute x3, starting transfers between devices, wide_halo(): lax.ppermute(tail, axis, [(i, i + hop) for i in range(count - hop)])  11.7 us
    pallas_call x1, Pallas kernels, local_waves(): pl.pallas_call(wave_kernel, out_shape=(jax.ShapeDtypeStruct((inner_rows,...  11.5 us
    unnamed x40, local copies, waits for them, and re-layouts  10.2 us
    ppermute x3, starting transfers between devices, wide_halo(): lax.ppermute(head, axis, [(i + hop, i) for i in range(count - hop)])  10 us
    dot_general x1, matrix products, vertical_solve(): jnp.einsum('kl,flxy->fkxy', stacked, provisional, precision=lax.Precision...  8.77 us
    ppermute x1, starting transfers between devices, body(): lax.ppermute(edges, ('gy', 'mode'), [(i, i + 1) for i in range(y_count -...  5.31 us
    pallas_call x1, Pallas kernels, pack_edges(): pl.pallas_call(pack_kernel, grid=(levels // PACK,), out_shape=jax.ShapeDt...  4.93 us
  transfers between devices with their start and end apart: 10, of which 0 were waited for; matrix products, arithmetic and copies ran while one was open for 26% of the time, Pallas kernels for 0%

profile of v9, /device:TPU:103, one launch (start us, length us, event | category | flops | bytes accessed | tf_op | source)
XLA Modules:
  0.0 116.8 jit_solution(6342557388943297498)
XLA Ops:
  0.7 4.9 %shard_map.76 = f32[4,2,32,128]{3,2,1,0:T(8,128)} custom-call(s32[32,128]{1,0:T(8,128)} %depth_ref.3, f32[4,64,32,128]{3,2,1,0:T(8,128)} %state_ref.3), custom_call_target="tpu_custom_call" | custom-call | flops 4194304 | bytes 4194304 | tf_op jit(solution)/shard_map/pallas_call | solution.py:223
  5.6 5.3 %collective-permute-start.2 = (f32[4,2,32,128]{3,2,1,0:T(8,128)}, f32[4,2,32,128]{3,2,1,0:T(8,128)}, u32[]{:S(2)}, u32[]{:S(2)}) collective-permute-start(f32[4,2,32,128]{3,2,1,0:T(8,128)} %shard_map.76), channel_id=1, source_target_pairs={{0,1},{1,2},{2,3},{3,4},{4,5},{5,6},{6,7},{7,8},{8,9},{9,10},{10,1... | collective-permute-start | bytes 393224 | tf_op jit(solution)/shard_map/ppermute | solution.py:337
  10.9 1.9 %collective-permute-start.3 = (f32[4,2,32,128]{3,2,1,0:T(8,128)}, f32[4,2,32,128]{3,2,1,0:T(8,128)}, u32[]{:S(2)}, u32[]{:S(2)}) collective-permute-start(f32[4,2,32,128]{3,2,1,0:T(8,128)} %shard_map.76), channel_id=1, source_target_pairs={{1,0},{2,1},{3,2},{4,3},{5,4},{6,5},{7,6},{8,7},{9,8},{10,9},{11,1... | collective-permute-start | bytes 393224 | tf_op jit(solution)/shard_map/ppermute | solution.py:338
  13.6 2.6 %slice_multiply_fusion.10 = (f32[4,64,2,128]{3,2,1,0:T(2,128)}, f32[4,64,2,128]{3,2,1,0:T(2,128)}) fusion(f32[4,64,32,128]{3,2,1,0:T(8,128)} %state_ref.3, f32[64,2,128]{2,1,0:T(2,128)S(1)} %get-tuple-element.22, f32[64,2,128]{2,1,0:T(2,128)S(1)} %get-tuple-element.23), kind=kLoop, calls=%fused_computation.29 | loop fusion | flops 131072 | bytes 1179648 | tf_op jit(solution)/shard_map/mul | solution.py:55
  16.2 3.2 %collective-permute-start = (f32[4,64,2,128]{3,2,1,0:T(2,128)}, f32[4,64,2,128]{3,2,1,0:T(2,128)S(1)}, u32[]{:S(2)}, u32[]{:S(2)}) collective-permute-start(f32[4,64,2,128]{3,2,1,0:T(2,128)} %get-tuple-element.21), channel_id=1, source_target_pairs={{0,16},{16,32},{32,48},{48,64},{64,80},{80,96},{96,112},{112,128},... | collective-permute-start | bytes 786440 | tf_op jit(solution)/shard_map/ppermute | solution.py:59
  19.4 4.2 %collective-permute-start.1 = (f32[4,64,2,128]{3,2,1,0:T(2,128)}, f32[4,64,2,128]{3,2,1,0:T(2,128)}, u32[]{:S(2)}, u32[]{:S(2)}) collective-permute-start(f32[4,64,2,128]{3,2,1,0:T(2,128)} %get-tuple-element.20), channel_id=1, source_target_pairs={{16,0},{32,16},{48,32},{64,48},{80,64},{96,80},{112,96},{128,112},... | collective-permute-start | bytes 786440 | tf_op jit(solution)/shard_map/ppermute | solution.py:60
  30.3 0.8 copy.21
  31.1 1.4 %copy.20 = f32[1,32,64]{1,2,0:T(8,128)} copy(f32[1,32,64]{2,1,0:T(8,128)} %slice.88) | data formatting | bytes 16384
  33.9 1.6 %fusion.13.side_ref = f32[4,2,32,128]{3,2,1,0:T(8,128)} fusion(f32[4,2,32,128]{3,2,1,0:T(8,128)} %collective-permute-done.2, f32[4,2,32,128]{3,2,1,0:T(8,128)} %collective-permute-done.3, s32[128]{0:T(128)} %get-tuple-element.37, s32[128]{0:T(128)} %get-tuple-element.38, pred[128]{0:T(512)(128)(4,1)} %compare_and_fusion), kind=kLoop, calls=%fused_computation.32 | loop fusion | flops 98304 | bytes 394368 | tf_op jit(solution)/shard_map/jit(_where)/select_n | solution.py:238
  35.6 1.2 %broadcast_in_dim.4.coriolis_ref = f32[8,128]{1,0:T(8,128)} broadcast(f32[128]{0:T(128)} %multiply_add_fusion.2), dimensions={1} | broadcast | bytes 4608 | tf_op jit(solution)/shard_map/broadcast_in_dim | solution.py:334
  36.8 17.9 %shard_map.77 = (f32[4,64,32,128]{3,2,1,0:T(8,128)}, f32[2,32,128]{2,1,0:T(8,128)}) custom-call(s32[32,128]{1,0:T(8,128)} %depth_ref.3, f32[8,128]{1,0:T(8,128)} %broadcast_in_dim.4.coriolis_ref, f32[4,64,32,128]{3,2,1,0:T(8,128)} %state_ref.3, f32[4,64,2,128]{3,2,1,0:T(2,128)} %copy-done.3, f32[4,64,2,128]{3,2,1,0:T(2,128)} %collective-permute-done.1.east_ref, ...), custom_call_target="tpu_custom_call" | custom-call | flops 62914560 | bytes 8388608 | tf_op jit(solution)/shard_map/pallas_call | solution.py:185
  55.4 2.7 %collective-permute-start.4 = (f32[6,32,128]{2,1,0:T(8,128)S(1)}, f32[6,32,128]{2,1,0:T(8,128)S(1)}, u32[]{:S(2)}, u32[]{:S(2)}) collective-permute-start(f32[6,32,128]{2,1,0:T(8,128)S(1)} %pad_maximum_fusion.2), channel_id=1, source_target_pairs={{0,32},{16,48},{32,64},{48,80},{64,96},{80,112},{96,128},{112,144}... | collective-permute-start | bytes 294920 | tf_op jit(solution)/shard_map/ppermute | solution.py:83
  58.1 3.0 %collective-permute-start.5 = (f32[6,32,128]{2,1,0:T(8,128)S(1)}, f32[6,32,128]{2,1,0:T(8,128)S(1)}, u32[]{:S(2)}, u32[]{:S(2)}) collective-permute-start(f32[6,32,128]{2,1,0:T(8,128)S(1)} %pad_maximum_fusion.2), channel_id=1, source_target_pairs={{0,16},{16,32},{32,48},{48,64},{64,80},{80,96},{96,112},{112,128},... | collective-permute-start | bytes 294920 | tf_op jit(solution)/shard_map/ppermute | solution.py:83
  61.1 4.4 %collective-permute-start.6 = (f32[6,32,128]{2,1,0:T(8,128)S(1)}, f32[6,32,128]{2,1,0:T(8,128)S(1)}, u32[]{:S(2)}, u32[]{:S(2)}) collective-permute-start(f32[6,32,128]{2,1,0:T(8,128)S(1)} %pad_maximum_fusion.2), channel_id=1, source_target_pairs={{16,0},{32,16},{48,32},{64,48},{80,64},{96,80},{112,96},{128,112},... | collective-permute-start | bytes 294920 | tf_op jit(solution)/shard_map/ppermute | solution.py:84
  65.5 2.9 %collective-permute-start.7 = (f32[6,32,128]{2,1,0:T(8,128)S(1)}, f32[6,32,128]{2,1,0:T(8,128)S(1)}, u32[]{:S(2)}, u32[]{:S(2)}) collective-permute-start(f32[6,32,128]{2,1,0:T(8,128)S(1)} %pad_maximum_fusion.2), channel_id=1, source_target_pairs={{32,0},{48,16},{64,32},{80,48},{96,64},{112,80},{128,96},{144,112}... | collective-permute-start | bytes 294920 | tf_op jit(solution)/shard_map/ppermute | solution.py:84
  68.5 8.8 %fusion.3 = f32[4,160,32,128]{3,1,2,0:T(8,128)S(1)} fusion(f32[4,64,32,128]{3,2,1,0:T(8,128)} %get-tuple-element.7, f32[64,64]{0,1:T(8,128)S(1)} %bitcast.16, f32[48,64]{0,1:T(8,128)S(1)} %bitcast.14, f32[32,64]{0,1:T(8,128)S(1)} %bitcast.17, f32[16,64]{0,1:T(8,128)S(1)} %bitcast.15), kind=kOutput, calls=%fused_computation.6 | convolution fusion | flops 1006663680 | bytes 14721024 | tf_op jit(solution)/shard_map/kl,flxy->fkxy/dot_general | solution.py:37
  78.4 2.7 %collective-permute-start.9 = (f32[6,160,64]{2,1,0:T(8,128)S(1)}, f32[6,160,64]{2,1,0:T(8,128)S(1)}, u32[]{:S(2)}, u32[]{:S(2)}) collective-permute-start(f32[6,160,64]{2,1,0:T(8,128)S(1)} %get-tuple-element.27), channel_id=1, source_target_pairs={{1,0},{2,1},{3,2},{4,3},{5,4},{6,5},{7,6},{8,7},{9,8},{10,9},{11,1... | collective-permute-start | bytes 737288 | tf_op jit(solution)/shard_map/ppermute | solution.py:84
  81.2 6.0 %collective-permute-start.8 = (f32[6,160,64]{2,1,0:T(8,128)S(1)}, f32[6,160,64]{2,1,0:T(8,128)S(1)}, u32[]{:S(2)}, u32[]{:S(2)}) collective-permute-start(f32[6,160,64]{2,1,0:T(8,128)S(1)} %get-tuple-element.26), channel_id=1, source_target_pairs={{0,1},{1,2},{2,3},{3,4},{4,5},{5,6},{6,7},{7,8},{8,9},{9,10},{10,1... | collective-permute-start | bytes 737288 | tf_op jit(solution)/shard_map/ppermute | solution.py:83
  87.2 4.7 %fusion = f32[4,64,32,128]{3,1,2,0:T(8,128)S(1)} fusion(f32[4,16,32,128]{3,1,2,0:T(8,128)S(1)} %get-tuple-element.17, f32[4,16,32,128]{3,1,2,0:T(8,128)S(1)} %get-tuple-element.16, f32[4,16,32,128]{3,1,2,0:T(8,128)S(1)} %get-tuple-element.15, f32[4,16,32,128]{3,1,2,0:T(8,128)S(1)} %get-tuple-element.14, f32[4,64,32,128]{3,2,1,0:T(8,128)S(1)} %copy-done, ...), kind=kLoop, calls=%fused_computation.1 | loop fusion | flops 6291456 | bytes 14680064 | tf_op jit(solution)/shard_map/add | solution.py:48
  92.0 2.0 %copy-done.1 = f32[4,64,32,128]{3,1,2,0:T(8,128)} copy-done((f32[4,64,32,128]{3,1,2,0:T(8,128)}, f32[4,64,32,128]{3,1,2,0:T(8,128)S(1)}, u32[]{:S(2)}) %copy-start.1) | copy-done | bytes 4194328
  95.0 1.0 fusion.23
  96.6 11.5 %shard_map.78 = (f32[32,128]{1,0:T(8,128)}, f32[2,32,128]{2,1,0:T(8,128)}) custom-call(f32[3,160,256]{2,1,0:T(8,128)} %get-tuple-element.25.moving_ref, f32[3,160,256]{2,1,0:T(8,128)} %get-tuple-element.24.fixed_ref, f32[8,256]{1,0:T(8,128)} %broadcast_in_dim.5.coriolis_ref), custom_call_target="tpu_custom_call" | custom-call | flops 39321600 | bytes 1146880 | tf_op jit(solution)/shard_map/pallas_call | solution.py:310
  108.9 2.9 %fusion.21 = (f32[2,64,32,128]{3,1,2,0:T(8,128)S(1)}, f32[2,64,32,128]{3,1,2,0:T(8,128)S(1)}) fusion(f32[4,64,32,128]{3,1,2,0:T(8,128)} %copy-done.1, f32[2,32,128]{2,1,0:T(8,128)S(1)} %divide_subtract_fusion, f32[64,32,128]{2,0,1:T(8,128)S(1)} %copy.8), kind=kLoop, calls=%fused_computation.63 | loop fusion | flops 1048576 | bytes 9469952 | tf_op jit(solution)/shard_map/slice | solution.py:70
  112.4 4.4 %copy.17 = f32[4,64,32,128]{3,2,1,0:T(8,128)} copy(f32[4,64,32,128]{3,1,2,0:T(8,128)S(1)} %pad_maximum_fusion) | data formatting | bytes 8388608
  (74 shorter events, 13.6 us)
Async XLA Ops:
  0.6 12.2 %copy-start.2 = (s32[32,128]{1,0:T(8,128)S(1)}, s32[32,128]{1,0:T(8,128)}, u32[]{:S(2)}) copy-start(s32[32,128]{1,0:T(8,128)} %depth_ref.3) | copy-start | bytes 49156
  0.6 25.5 %copy-start.13 = (f32[2,32,128]{2,1,0:T(8,128)S(1)}, f32[2,32,128]{2,1,0:T(8,128)}, u32[]{:S(2)}) copy-start(f32[2,32,128]{2,1,0:T(8,128)} %param.9) | copy-start | bytes 98308
  0.7 25.5 %copy-start.14 = (f32[32,128]{1,0:T(8,128)S(1)}, f32[32,128]{1,0:T(8,128)}, u32[]{:S(2)}) copy-start(f32[32,128]{1,0:T(8,128)} %param.8) | copy-start | bytes 49156
  0.7 26.5 %copy-start.6 = (f32[4,64,64]{2,1,0:T(8,128)S(1)}, f32[4,64,64]{2,1,0:T(8,128)}, u32[]{:S(2)}) copy-start(f32[4,64,64]{2,1,0:T(8,128)} %param.7) | copy-start | bytes 196612
  0.7 28.9 %slice-start = ((f32[4,64,64]{2,1,0:T(8,128)}), f32[1,64,64]{2,1,0:T(8,128)S(1)}, s32[]{:S(2)}) async-start(f32[4,64,64]{2,1,0:T(8,128)} %param.7), calls=%async_computation | async-start | bytes 65536 | tf_op jit(solution)/shard_map/slice | solution.py:35
  5.6 28.3 %collective-permute-start.2 = (f32[4,2,32,128]{3,2,1,0:T(8,128)}, f32[4,2,32,128]{3,2,1,0:T(8,128)}, u32[]{:S(2)}, u32[]{:S(2)}) collective-permute-start(f32[4,2,32,128]{3,2,1,0:T(8,128)} %shard_map.76), channel_id=1, source_target_pairs={{0,1},{1,2},{2,3},{3,4},{4,5},{5,6},{6,7},{7,8},{8,9},{9,10},{10,1... | collective-permute-start | bytes 393224 | tf_op jit(solution)/shard_map/ppermute | solution.py:337
  10.9 23.0 %collective-permute-start.3 = (f32[4,2,32,128]{3,2,1,0:T(8,128)}, f32[4,2,32,128]{3,2,1,0:T(8,128)}, u32[]{:S(2)}, u32[]{:S(2)}) collective-permute-start(f32[4,2,32,128]{3,2,1,0:T(8,128)} %shard_map.76), channel_id=1, source_target_pairs={{1,0},{2,1},{3,2},{4,3},{5,4},{6,5},{7,6},{8,7},{9,8},{10,9},{11,1... | collective-permute-start | bytes 393224 | tf_op jit(solution)/shard_map/ppermute | solution.py:338
  16.2 19.4 %collective-permute-start = (f32[4,64,2,128]{3,2,1,0:T(2,128)}, f32[4,64,2,128]{3,2,1,0:T(2,128)S(1)}, u32[]{:S(2)}, u32[]{:S(2)}) collective-permute-start(f32[4,64,2,128]{3,2,1,0:T(2,128)} %get-tuple-element.21), channel_id=1, source_target_pairs={{0,16},{16,32},{32,48},{48,64},{64,80},{80,96},{96,112},{112,128},... | collective-permute-start | bytes 786440 | tf_op jit(solution)/shard_map/ppermute | solution.py:59
  19.4 16.2 %collective-permute-start.1 = (f32[4,64,2,128]{3,2,1,0:T(2,128)}, f32[4,64,2,128]{3,2,1,0:T(2,128)}, u32[]{:S(2)}, u32[]{:S(2)}) collective-permute-start(f32[4,64,2,128]{3,2,1,0:T(2,128)} %get-tuple-element.20), channel_id=1, source_target_pairs={{16,0},{32,16},{48,32},{64,48},{80,64},{96,80},{112,96},{128,112},... | collective-permute-start | bytes 786440 | tf_op jit(solution)/shard_map/ppermute | solution.py:60
  33.9 34.5 %copy-start.4 = (f32[1,64,64]{1,2,0:T(8,128)S(1)}, f32[1,64,64]{1,2,0:T(8,128)}, u32[]{:S(2)}) copy-start(f32[1,64,64]{1,2,0:T(8,128)} %copy.22) | copy-start | bytes 49156
  33.9 34.5 %copy-start.5 = (f32[1,32,64]{1,2,0:T(8,128)S(1)}, f32[1,32,64]{1,2,0:T(8,128)}, u32[]{:S(2)}) copy-start(f32[1,32,64]{1,2,0:T(8,128)} %copy.20) | copy-start | bytes 24580
  55.4 22.7 %collective-permute-start.4 = (f32[6,32,128]{2,1,0:T(8,128)S(1)}, f32[6,32,128]{2,1,0:T(8,128)S(1)}, u32[]{:S(2)}, u32[]{:S(2)}) collective-permute-start(f32[6,32,128]{2,1,0:T(8,128)S(1)} %pad_maximum_fusion.2), channel_id=1, source_target_pairs={{0,32},{16,48},{32,64},{48,80},{64,96},{80,112},{96,128},{112,144}... | collective-permute-start | bytes 294920 | tf_op jit(solution)/shard_map/ppermute | solution.py:83
  58.1 20.0 %collective-permute-start.5 = (f32[6,32,128]{2,1,0:T(8,128)S(1)}, f32[6,32,128]{2,1,0:T(8,128)S(1)}, u32[]{:S(2)}, u32[]{:S(2)}) collective-permute-start(f32[6,32,128]{2,1,0:T(8,128)S(1)} %pad_maximum_fusion.2), channel_id=1, source_target_pairs={{0,16},{16,32},{32,48},{48,64},{64,80},{80,96},{96,112},{112,128},... | collective-permute-start | bytes 294920 | tf_op jit(solution)/shard_map/ppermute | solution.py:83
  61.1 17.1 %collective-permute-start.6 = (f32[6,32,128]{2,1,0:T(8,128)S(1)}, f32[6,32,128]{2,1,0:T(8,128)S(1)}, u32[]{:S(2)}, u32[]{:S(2)}) collective-permute-start(f32[6,32,128]{2,1,0:T(8,128)S(1)} %pad_maximum_fusion.2), channel_id=1, source_target_pairs={{16,0},{32,16},{48,32},{64,48},{80,64},{96,80},{112,96},{128,112},... | collective-permute-start | bytes 294920 | tf_op jit(solution)/shard_map/ppermute | solution.py:84
  65.5 12.7 %collective-permute-start.7 = (f32[6,32,128]{2,1,0:T(8,128)S(1)}, f32[6,32,128]{2,1,0:T(8,128)S(1)}, u32[]{:S(2)}, u32[]{:S(2)}) collective-permute-start(f32[6,32,128]{2,1,0:T(8,128)S(1)} %pad_maximum_fusion.2), channel_id=1, source_target_pairs={{32,0},{48,16},{64,32},{80,48},{96,64},{112,80},{128,96},{144,112}... | collective-permute-start | bytes 294920 | tf_op jit(solution)/shard_map/ppermute | solution.py:84
  68.4 8.8 %copy-start.8 = (f32[32,128]{1,0:T(8,128)S(1)}, f32[32,128]{1,0:T(8,128)}, u32[]{:S(2)}) copy-start(f32[32,128]{1,0:T(8,128)} %get-tuple-element.34) | copy-start | bytes 49156
  68.5 8.8 %copy-start.9 = (f32[32,128]{1,0:T(8,128)S(1)}, f32[32,128]{1,0:T(8,128)}, u32[]{:S(2)}) copy-start(f32[32,128]{1,0:T(8,128)} %get-tuple-element.35) | copy-start | bytes 49156
  68.5 8.8 %copy-start.10 = (f32[32,128]{1,0:T(8,128)S(1)}, f32[32,128]{1,0:T(8,128)}, u32[]{:S(2)}) copy-start(f32[32,128]{1,0:T(8,128)} %get-tuple-element.36) | copy-start | bytes 49156
  77.3 9.9 %copy-start = (f32[4,64,32,128]{3,2,1,0:T(8,128)S(1)}, f32[4,64,32,128]{3,2,1,0:T(8,128)}, u32[]{:S(2)}) copy-start(f32[4,64,32,128]{3,2,1,0:T(8,128)} %state_ref.3) | copy-start | bytes 12582916
  78.4 16.0 %collective-permute-start.9 = (f32[6,160,64]{2,1,0:T(8,128)S(1)}, f32[6,160,64]{2,1,0:T(8,128)S(1)}, u32[]{:S(2)}, u32[]{:S(2)}) collective-permute-start(f32[6,160,64]{2,1,0:T(8,128)S(1)} %get-tuple-element.27), channel_id=1, source_target_pairs={{1,0},{2,1},{3,2},{4,3},{5,4},{6,5},{7,6},{8,7},{9,8},{10,9},{11,1... | collective-permute-start | bytes 737288 | tf_op jit(solution)/shard_map/ppermute | solution.py:84
  81.2 13.3 %collective-permute-start.8 = (f32[6,160,64]{2,1,0:T(8,128)S(1)}, f32[6,160,64]{2,1,0:T(8,128)S(1)}, u32[]{:S(2)}, u32[]{:S(2)}) collective-permute-start(f32[6,160,64]{2,1,0:T(8,128)S(1)} %get-tuple-element.26), channel_id=1, source_target_pairs={{0,1},{1,2},{2,3},{3,4},{4,5},{5,6},{6,7},{7,8},{8,9},{9,10},{10,1... | collective-permute-start | bytes 737288 | tf_op jit(solution)/shard_map/ppermute | solution.py:83
  92.0 2.0 %copy-start.1 = (f32[4,64,32,128]{3,1,2,0:T(8,128)}, f32[4,64,32,128]{3,1,2,0:T(8,128)S(1)}, u32[]{:S(2)}) copy-start(f32[4,64,32,128]{3,1,2,0:T(8,128)S(1)} %fusion) | copy-start | bytes 12582916
  94.0 14.1 %copy-start.11 = (f32[32,128]{1,0:T(8,128)S(1)}, f32[32,128]{1,0:T(8,128)}, u32[]{:S(2)}) copy-start(f32[32,128]{1,0:T(8,128)} %get-tuple-element.30) | copy-start | bytes 49156
  94.0 14.1 %copy-start.12 = (f32[32,128]{1,0:T(8,128)S(1)}, f32[32,128]{1,0:T(8,128)}, u32[]{:S(2)}) copy-start(f32[32,128]{1,0:T(8,128)} %get-tuple-element.28) | copy-start | bytes 49156
  (3 other events, 4.0 us)

commit v10 on v9

--- a/solution.py
+++ b/solution.py
@@ -1,4 +1,5 @@
 import jax
+import numpy as np
 import jax.numpy as jnp
 from jax import lax
 from jax.experimental import pallas as pl
@@ -31,9 +32,10 @@
     levels = state.shape[1]
     classes = inverse.shape[0]
     band = levels // classes
-    stacked = jnp.concatenate(
-        [inverse[class_index, : band * (class_index + 1)] for class_index in range(classes)], axis=0
+    rows_used = np.concatenate(
+        [class_index * levels + np.arange(band * (class_index + 1)) for class_index in range(classes)]
     )
+    stacked = jnp.take(inverse.reshape(classes * levels, inverse.shape[2]), rows_used, axis=0)
     every = jnp.einsum("kl,flxy->fkxy", stacked, provisional, precision=lax.Precision.HIGH)
     starts = [band * class_index * (class_index + 1) // 2 for class_index in range(classes)]
     chosen = [(depth_class == class_index + 1).astype(jnp.float32) for class_index in range(classes)]
@@ -46,19 +48,6 @@
         bands.append(part)
     solved = jnp.concatenate(bands, axis=1)
     return active * solved + (1.0 - active) * state
-
-
-def edge_halo(state, active, axis, dim, width):
-    count = lax.axis_size(axis)
-    ends = count - 1
-    size = state.shape[dim]
-    head = lax.slice_in_dim(state, 0, width, axis=dim) * lax.slice_in_dim(active, 0, width, axis=dim - 1)
-    tail = lax.slice_in_dim(state, size - width, size, axis=dim) * lax.slice_in_dim(
-        active, size - width, size, axis=dim - 1
-    )
-    before = lax.ppermute(tail, axis, [(i, i + 1) for i in range(ends)])
-    after = lax.ppermute(head, axis, [(i + 1, i) for i in range(ends)])
-    return before, after
 
 
 def finish(updated, transport_next, active, depth_class, level_block, levels):
@@ -187,7 +176,7 @@
         grid=(steps,),
         out_shape=(jax.ShapeDtypeStruct(state.shape, jnp.float32),
                    jax.ShapeDtypeStruct((2, rows, cols), jnp.float32)),
-        in_specs=[flat, pl.BlockSpec((8, cols), lambda c: (0, 0)), big, rim, rim, packed],
+        in_specs=[flat, pl.BlockSpec((1, cols), lambda c: (0, 0)), big, rim, rim, packed],
         out_specs=(big, pl.BlockSpec((2, rows, cols), lambda c: (0, 0, 0))),
         scratch_shapes=[pltpu.VMEM((3, rows, cols), jnp.float32)],
         compiler_params=pltpu.CompilerParams(dimension_semantics=("arbitrary",)),
@@ -197,7 +186,7 @@
     )(depth_class, coriolis, state, west, east, side)
 
 
-def pack_kernel(depth_ref, state_ref, out_ref):
+def pack_kernel(depth_ref, state_ref, out_ref, head_ref, tail_ref):
     block_index = pl.program_id(0)
     fields, depth_levels, rows, cols = state_ref.shape
     block = depth_levels * pl.num_programs(0) // 4
@@ -211,6 +200,8 @@
         second = (lane == low + 2) | (lane == low + 3)
         for f in range(fields):
             masked = state_ref[f, k] * active
+            head_ref[f, k] = masked[0:2]
+            tail_ref[f, k] = masked[rows - 2 : rows]
             near_end = pltpu.roll(masked, low, 1)
             far_end = pltpu.roll(masked, (low + 4) % cols, 1)
             packed[f] = jnp.where(first, near_end, jnp.where(second, far_end, packed[f]))
@@ -220,13 +211,18 @@
 
 def pack_edges(state, depth_class):
     fields, levels, rows, cols = state.shape
+    rim = pl.BlockSpec((fields, PACK, 2, cols), lambda c: (0, c, 0, 0))
     return pl.pallas_call(
         pack_kernel,
         grid=(levels // PACK,),
-        out_shape=jax.ShapeDtypeStruct((fields, levels // PACK, rows, cols), jnp.float32),
+        out_shape=(
+            jax.ShapeDtypeStruct((fields, levels // PACK, rows, cols), jnp.float32),
+            jax.ShapeDtypeStruct((fields, levels, 2, cols), jnp.float32),
+            jax.ShapeDtypeStruct((fields, levels, 2, cols), jnp.float32),
+        ),
         in_specs=[pl.BlockSpec((rows, cols), lambda c: (0, 0)),
                   pl.BlockSpec((fields, PACK, rows, cols), lambda c: (0, c, 0, 0))],
-        out_specs=pl.BlockSpec((fields, 1, rows, cols), lambda c: (0, c, 0, 0)),
+        out_specs=(pl.BlockSpec((fields, 1, rows, cols), lambda c: (0, c, 0, 0)), rim, rim),
         cost_estimate=pl.CostEstimate(
             flops=4 * state.size, transcendentals=0, bytes_accessed=4 * state.size
         ),
@@ -328,11 +324,13 @@
     y_cells = depth_class.shape[1]
     level_ids = lax.broadcasted_iota(jnp.int32, (levels, 1, 1), 0)
     active = (level_ids < depth_class[None] * level_block).astype(jnp.float32)
-    west, east = edge_halo(state, active, "gx", 2, 2)
     column_blocks = lax.axis_size(("gy", "mode"))
     anchor = lax.axis_index(("gy", "mode")) * y_cells
-    coriolis = jnp.broadcast_to(coriolis_row(anchor, y_cells, y_cells * column_blocks), (8, y_cells))
-    edges = pack_edges(state, depth_class)
+    coriolis = coriolis_row(anchor, y_cells, y_cells * column_blocks)
+    edges, head, tail = pack_edges(state, depth_class)
+    x_count = lax.axis_size("gx")
+    west = lax.ppermute(tail, "gx", [(i, i + 1) for i in range(x_count - 1)])
+    east = lax.ppermute(head, "gx", [(i + 1, i) for i in range(x_count - 1)])
     y_count = lax.axis_size(("gy", "mode"))
     from_south = lax.ppermute(edges, ("gy", "mode"), [(i, i + 1) for i in range(y_count - 1)])
     from_north = lax.ppermute(edges, ("gy", "mode"), [(i + 1, i) for i in range(y_count - 1)])
@@ -346,9 +344,7 @@
     rim = 2 * SUB
     fields = wide_halo(fields, "gx", 1, rim)
     fields = wide_halo(fields, ("gy", "mode"), 2, rim)
-    coriolis_wide = jnp.broadcast_to(
-        coriolis_row(anchor - rim, y_cells + 2 * rim, y_cells * column_blocks), (8, y_cells + 2 * rim)
-    )
+    coriolis_wide = coriolis_row(anchor - rim, y_cells + 2 * rim, y_cells * column_blocks)
     x_cells = depth_class.shape[0]
     height_next, transport_next = local_waves(fields[0:3], fields[3:6], coriolis_wide, x_cells, y_cells)
     state_next = finish(updated, transport_next, active, depth_class, level_block, levels)

time: 118 us -> 106 us (0.90)
  local copies, waits for them, and re-layouts: 16.3 us -> 9.14 us
  other arithmetic: 20 us -> 13.6 us
  waiting for transfers between devices: 0.03 us -> 3.32 us
    ppermute x2, waiting for transfers between devices: 0.01 us -> 3.3 us  [the longest x1 1.86 us: body(): east = lax.ppermute(head, 'gx', [(i + 1, i) for i in range(x_count - 1)])]
    unnamed x40 -> x24, local copies, waits for them, and re-layouts: 10.2 us -> 7.22 us
    mul x1 -> x0, other arithmetic: 2.55 us -> none  [edge_halo(): lax.slice_in_dim(state, 0, width, axis=dim)]
    ppermute x3, starting transfers between devices: 11.7 us -> 9.8 us  [wide_halo(): lax.ppermute(tail, axis, [(i, i + hop) for i in range(count - hop)])]
    slice x6 -> x0, local copies, waits for them, and re-layouts: 1.86 us -> none  [the longest x5 1.81 us: vertical_solve(): inverse[class_index, :band * (class_index + 1)]]
    broadcast_in_dim x2 -> x0, local copies, waits for them, and re-layouts: 1.76 us -> none  [the longest x1 1.17 us: body(): jnp.broadcast_to(coriolis_row(anchor, y_cells, y_cells * column_blocks),...]
    ppermute x3, starting transfers between devices: 10 us -> 11.2 us  [wide_halo(): lax.ppermute(head, axis, [(i + hop, i) for i in range(count - hop)])]
  transfers between devices with their start and end apart: 10 -> 10, of which waited for: 0 -> 2; matrix products, arithmetic and copies ran while one was open for 26% -> 16% of each run, Pallas kernels for 0% -> 0%
where the time goes in v10:
time: 106 us
  starting transfers between devices  35.6 us (34%)
  Pallas kernels  34.5 us (33%)
  other arithmetic  13.6 us (13%)
  local copies, waits for them, and re-layouts  9.14 us (9%)
  matrix products  8.64 us (8%)
  waiting for transfers between devices  3.32 us (3%)
    pallas_call x1, Pallas kernels, stencil(): pl.pallas_call(stencil_kernel, grid=(steps,), out_shape=(jax.ShapeDtypeSt...  17.9 us
    pallas_call x1, Pallas kernels, local_waves(): pl.pallas_call(wave_kernel, out_shape=(jax.ShapeDtypeStruct((inner_rows,...  11.5 us
    ppermute x3, starting transfers between devices, wide_halo(): lax.ppermute(head, axis, [(i + hop, i) for i in range(count - hop)])  11.2 us
    ppermute x3, starting transfers between devices, wide_halo(): lax.ppermute(tail, axis, [(i, i + hop) for i in range(count - hop)])  9.8 us
    dot_general x1, matrix products, vertical_solve(): jnp.einsum('kl,flxy->fkxy', stacked, provisional, precision=lax.Precision...  8.64 us
    unnamed x24, local copies, waits for them, and re-layouts  7.22 us
    ppermute x1, starting transfers between devices, body(): lax.ppermute(edges, ('gy', 'mode'), [(i, i + 1) for i in range(y_count -...  5.3 us
    pallas_call x1, Pallas kernels, pack_edges(): pl.pallas_call(pack_kernel, grid=(levels // PACK,), out_shape=(jax.ShapeD...  5.04 us
  transfers between devices with their start and end apart: 10, of which 2 were waited for; matrix products, arithmetic and copies ran while one was open for 16% of the time, Pallas kernels for 0%

profile of v10, /device:TPU:103, one launch (start us, length us, event | category | flops | bytes accessed | tf_op | source)
XLA Modules:
  0.0 105.8 jit_solution(16632668690778057861)
XLA Ops:
  0.7 5.0 %shard_map.85 = (f32[4,2,32,128]{3,2,1,0:T(8,128)}, f32[4,64,2,128]{3,2,1,0:T(2,128)}, f32[4,64,2,128]{3,2,1,0:T(2,128)}) custom-call(s32[32,128]{1,0:T(8,128)} %depth_ref.3, f32[4,64,32,128]{3,2,1,0:T(8,128)} %state_ref.3), custom_call_target="tpu_custom_call" | custom-call | flops 4194304 | bytes 4194304 | tf_op jit(solution)/shard_map/pallas_call | solution.py:215
  5.7 5.3 %collective-permute-start.2 = (f32[4,2,32,128]{3,2,1,0:T(8,128)}, f32[4,2,32,128]{3,2,1,0:T(8,128)S(1)}, u32[]{:S(2)}, u32[]{:S(2)}) collective-permute-start(f32[4,2,32,128]{3,2,1,0:T(8,128)} %get-tuple-element.12), channel_id=1, source_target_pairs={{0,1},{1,2},{2,3},{3,4},{4,5},{5,6},{6,7},{7,8},{8,9},{9,10},{10,1... | collective-permute-start | bytes 393224 | tf_op jit(solution)/shard_map/ppermute | solution.py:335
  11.0 1.9 %collective-permute-start.3 = (f32[4,2,32,128]{3,2,1,0:T(8,128)}, f32[4,2,32,128]{3,2,1,0:T(8,128)S(1)}, u32[]{:S(2)}, u32[]{:S(2)}) collective-permute-start(f32[4,2,32,128]{3,2,1,0:T(8,128)} %get-tuple-element.12), channel_id=1, source_target_pairs={{1,0},{2,1},{3,2},{4,3},{5,4},{6,5},{7,6},{8,7},{9,8},{10,9},{11,1... | collective-permute-start | bytes 393224 | tf_op jit(solution)/shard_map/ppermute | solution.py:336
  13.0 3.2 %collective-permute-start = (f32[4,64,2,128]{3,2,1,0:T(2,128)}, f32[4,64,2,128]{3,2,1,0:T(2,128)S(1)}, u32[]{:S(2)}, u32[]{:S(2)}) collective-permute-start(f32[4,64,2,128]{3,2,1,0:T(2,128)} %get-tuple-element.10), channel_id=1, source_target_pairs={{0,16},{16,32},{32,48},{48,64},{64,80},{80,96},{96,112},{112,128},... | collective-permute-start | bytes 786440 | tf_op jit(solution)/shard_map/ppermute | solution.py:332
  16.2 4.2 %collective-permute-start.1 = (f32[4,64,2,128]{3,2,1,0:T(2,128)}, f32[4,64,2,128]{3,2,1,0:T(2,128)S(1)}, u32[]{:S(2)}, u32[]{:S(2)}) collective-permute-start(f32[4,64,2,128]{3,2,1,0:T(2,128)} %get-tuple-element.11), channel_id=1, source_target_pairs={{16,0},{32,16},{48,32},{64,48},{80,64},{96,80},{112,96},{128,112},... | collective-permute-start | bytes 786440 | tf_op jit(solution)/shard_map/ppermute | solution.py:333
  23.2 1.4 %collective-permute-done.west_ref = f32[4,64,2,128]{3,2,1,0:T(2,128)S(1)} collective-permute-done((f32[4,64,2,128]{3,2,1,0:T(2,128)}, f32[4,64,2,128]{3,2,1,0:T(2,128)S(1)}, u32[]{:S(2)}, u32[]{:S(2)}) %collective-permute-start) | collective-permute-done | bytes 262176 | tf_op jit(solution)/shard_map/ppermute | solution.py:332
  24.7 1.9 %collective-permute-done.1.east_ref = f32[4,64,2,128]{3,2,1,0:T(2,128)S(1)} collective-permute-done((f32[4,64,2,128]{3,2,1,0:T(2,128)}, f32[4,64,2,128]{3,2,1,0:T(2,128)S(1)}, u32[]{:S(2)}, u32[]{:S(2)}) %collective-permute-start.1) | collective-permute-done | bytes 262176 | tf_op jit(solution)/shard_map/ppermute | solution.py:333
  27.2 17.9 %shard_map.86 = (f32[4,64,32,128]{3,2,1,0:T(8,128)}, f32[2,32,128]{2,1,0:T(8,128)}) custom-call(s32[32,128]{1,0:T(8,128)} %depth_ref.3, f32[1,128]{1,0:T(1,128)} %multiply_add_fusion.2.coriolis_ref, f32[4,64,32,128]{3,2,1,0:T(8,128)} %state_ref.3, f32[4,64,2,128]{3,2,1,0:T(2,128)} %copy-done.4, f32[4,64,2,128]{3,2,1,0:T(2,128)} %copy-done.5, ...), custom_call_target="tpu_custom_call" | custom-call | flops 62914560 | bytes 8388608 | tf_op jit(solution)/shard_map/pallas_call | solution.py:174
  45.1 0.8 pad_maximum_fusion.2
  45.9 4.1 %collective-permute-start.4 = (f32[6,32,128]{2,1,0:T(8,128)S(1)}, f32[6,32,128]{2,1,0:T(8,128)S(1)}, u32[]{:S(2)}, u32[]{:S(2)}) collective-permute-start(f32[6,32,128]{2,1,0:T(8,128)S(1)} %pad_maximum_fusion.2), channel_id=1, source_target_pairs={{0,32},{16,48},{32,64},{48,80},{64,96},{80,112},{96,128},{112,144}... | collective-permute-start | bytes 294920 | tf_op jit(solution)/shard_map/ppermute | solution.py:72
  50.0 1.9 %collective-permute-start.5 = (f32[6,32,128]{2,1,0:T(8,128)S(1)}, f32[6,32,128]{2,1,0:T(8,128)S(1)}, u32[]{:S(2)}, u32[]{:S(2)}) collective-permute-start(f32[6,32,128]{2,1,0:T(8,128)S(1)} %pad_maximum_fusion.2), channel_id=1, source_target_pairs={{0,16},{16,32},{32,48},{48,64},{64,80},{80,96},{96,112},{112,128},... | collective-permute-start | bytes 294920 | tf_op jit(solution)/shard_map/ppermute | solution.py:72
  51.9 5.5 %collective-permute-start.6 = (f32[6,32,128]{2,1,0:T(8,128)S(1)}, f32[6,32,128]{2,1,0:T(8,128)S(1)}, u32[]{:S(2)}, u32[]{:S(2)}) collective-permute-start(f32[6,32,128]{2,1,0:T(8,128)S(1)} %pad_maximum_fusion.2), channel_id=1, source_target_pairs={{16,0},{32,16},{48,32},{64,48},{80,64},{96,80},{112,96},{128,112},... | collective-permute-start | bytes 294920 | tf_op jit(solution)/shard_map/ppermute | solution.py:73
  57.4 2.5 %collective-permute-start.7 = (f32[6,32,128]{2,1,0:T(8,128)S(1)}, f32[6,32,128]{2,1,0:T(8,128)S(1)}, u32[]{:S(2)}, u32[]{:S(2)}) collective-permute-start(f32[6,32,128]{2,1,0:T(8,128)S(1)} %pad_maximum_fusion.2), channel_id=1, source_target_pairs={{32,0},{48,16},{64,32},{80,48},{96,64},{112,80},{128,96},{144,112}... | collective-permute-start | bytes 294920 | tf_op jit(solution)/shard_map/ppermute | solution.py:73
  59.8 8.6 %fusion.3 = f32[4,160,32,128]{3,1,2,0:T(8,128)S(1)} fusion(f32[4,64,32,128]{3,2,1,0:T(8,128)} %get-tuple-element.13, f32[160,64]{1,0:T(8,128)S(1)} %gather_fusion), kind=kOutput, calls=%fused_computation.7 | convolution fusion | flops 1006632960 | bytes 14721024 | tf_op jit(solution)/shard_map/kl,flxy->fkxy/dot_general | solution.py:39
  68.5 0.8 fusion.9
  69.7 3.3 %collective-permute-start.9 = (f32[6,160,64]{2,1,0:T(8,128)S(1)}, f32[6,160,64]{2,1,0:T(8,128)S(1)}, u32[]{:S(2)}, u32[]{:S(2)}) collective-permute-start(f32[6,160,64]{2,1,0:T(8,128)S(1)} %get-tuple-element.29), channel_id=1, source_target_pairs={{1,0},{2,1},{3,2},{4,3},{5,4},{6,5},{7,6},{8,7},{9,8},{10,9},{11,1... | collective-permute-start | bytes 737288 | tf_op jit(solution)/shard_map/ppermute | solution.py:73
  72.9 3.8 %collective-permute-start.8 = (f32[6,160,64]{2,1,0:T(8,128)S(1)}, f32[6,160,64]{2,1,0:T(8,128)S(1)}, u32[]{:S(2)}, u32[]{:S(2)}) collective-permute-start(f32[6,160,64]{2,1,0:T(8,128)S(1)} %get-tuple-element.28), channel_id=1, source_target_pairs={{0,1},{1,2},{2,3},{3,4},{4,5},{5,6},{6,7},{7,8},{8,9},{9,10},{10,1... | collective-permute-start | bytes 737288 | tf_op jit(solution)/shard_map/ppermute | solution.py:72
  76.8 4.7 %fusion = f32[4,64,32,128]{3,1,2,0:T(8,128)S(1)} fusion(f32[4,16,32,128]{3,1,2,0:T(8,128)S(1)} %get-tuple-element.23, f32[4,16,32,128]{3,1,2,0:T(8,128)S(1)} %get-tuple-element.22, f32[4,16,32,128]{3,1,2,0:T(8,128)S(1)} %get-tuple-element.21, f32[4,16,32,128]{3,1,2,0:T(8,128)S(1)} %get-tuple-element.20, f32[4,64,32,128]{3,2,1,0:T(8,128)S(1)} %copy-done.1, ...), kind=kLoop, calls=%fused_computation.2 | loop fusion | flops 6291456 | bytes 14680064 | tf_op jit(solution)/shard_map/add | solution.py:50
  81.5 2.0 %copy-done.2 = f32[4,64,32,128]{3,1,2,0:T(8,128)} copy-done((f32[4,64,32,128]{3,1,2,0:T(8,128)}, f32[4,64,32,128]{3,1,2,0:T(8,128)S(1)}, u32[]{:S(2)}) %copy-start.2) | copy-done | bytes 4194328
  84.5 1.0 fusion.16
  85.5 11.5 %shard_map.87 = (f32[32,128]{1,0:T(8,128)}, f32[2,32,128]{2,1,0:T(8,128)}) custom-call(f32[3,160,256]{2,1,0:T(8,128)} %get-tuple-element.27.moving_ref, f32[3,160,256]{2,1,0:T(8,128)} %get-tuple-element.26.fixed_ref, f32[1,256]{1,0:T(1,128)} %multiply_add_fusion.1.coriolis_ref), custom_call_target="tpu_custom_call" | custom-call | flops 39321600 | bytes 1146880 | tf_op jit(solution)/shard_map/pallas_call | solution.py:306
  97.1 0.8 divide_subtract_fusion
  97.8 2.9 %fusion.15 = (f32[2,64,32,128]{3,1,2,0:T(8,128)S(1)}, f32[2,64,32,128]{3,1,2,0:T(8,128)S(1)}) fusion(f32[4,64,32,128]{3,1,2,0:T(8,128)} %copy-done.2, f32[2,32,128]{2,1,0:T(8,128)S(1)} %divide_subtract_fusion, f32[64,32,128]{2,0,1:T(8,128)S(1)} %fusion.12), kind=kLoop, calls=%fused_computation.56 | loop fusion | flops 1048576 | bytes 9469952 | tf_op jit(solution)/shard_map/slice | solution.py:59
  101.3 4.4 %copy.12 = f32[4,64,32,128]{3,2,1,0:T(8,128)} copy(f32[4,64,32,128]{3,1,2,0:T(8,128)S(1)} %pad_maximum_fusion) | data formatting | bytes 8388608
  (49 shorter events, 5.2 us)
Async XLA Ops:
  0.6 21.2 %copy-start = (f32[4,64,64]{2,1,0:T(8,128)S(1)}, f32[4,64,64]{2,1,0:T(8,128)}, u32[]{:S(2)}) copy-start(f32[4,64,64]{2,1,0:T(8,128)} %param.8) | copy-start | bytes 196612
  0.6 20.1 %copy-start.9 = (s32[160]{0:T(256)S(1)}, s32[160]{0:T(256)}, u32[]{:S(2)}) copy-start(s32[160]{0:T(256)} %constant.93) | copy-start | bytes 1924
  0.7 19.7 %copy-start.3 = (s32[32,128]{1,0:T(8,128)S(1)}, s32[32,128]{1,0:T(8,128)}, u32[]{:S(2)}) copy-start(s32[32,128]{1,0:T(8,128)} %depth_ref.3) | copy-start | bytes 49156
  0.7 20.7 %copy-start.7 = (f32[2,32,128]{2,1,0:T(8,128)S(1)}, f32[2,32,128]{2,1,0:T(8,128)}, u32[]{:S(2)}) copy-start(f32[2,32,128]{2,1,0:T(8,128)} %param.10) | copy-start | bytes 98308
  0.7 20.7 %copy-start.8 = (f32[32,128]{1,0:T(8,128)S(1)}, f32[32,128]{1,0:T(8,128)}, u32[]{:S(2)}) copy-start(f32[32,128]{1,0:T(8,128)} %param.9) | copy-start | bytes 49156
  5.7 16.8 %collective-permute-start.2 = (f32[4,2,32,128]{3,2,1,0:T(8,128)}, f32[4,2,32,128]{3,2,1,0:T(8,128)S(1)}, u32[]{:S(2)}, u32[]{:S(2)}) collective-permute-start(f32[4,2,32,128]{3,2,1,0:T(8,128)} %get-tuple-element.12), channel_id=1, source_target_pairs={{0,1},{1,2},{2,3},{3,4},{4,5},{5,6},{6,7},{7,8},{8,9},{9,10},{10,1... | collective-permute-start | bytes 393224 | tf_op jit(solution)/shard_map/ppermute | solution.py:335
  11.0 11.5 %collective-permute-start.3 = (f32[4,2,32,128]{3,2,1,0:T(8,128)}, f32[4,2,32,128]{3,2,1,0:T(8,128)S(1)}, u32[]{:S(2)}, u32[]{:S(2)}) collective-permute-start(f32[4,2,32,128]{3,2,1,0:T(8,128)} %get-tuple-element.12), channel_id=1, source_target_pairs={{1,0},{2,1},{3,2},{4,3},{5,4},{6,5},{7,6},{8,7},{9,8},{10,9},{11,1... | collective-permute-start | bytes 393224 | tf_op jit(solution)/shard_map/ppermute | solution.py:336
  13.0 11.7 %collective-permute-start = (f32[4,64,2,128]{3,2,1,0:T(2,128)}, f32[4,64,2,128]{3,2,1,0:T(2,128)S(1)}, u32[]{:S(2)}, u32[]{:S(2)}) collective-permute-start(f32[4,64,2,128]{3,2,1,0:T(2,128)} %get-tuple-element.10), channel_id=1, source_target_pairs={{0,16},{16,32},{32,48},{48,64},{64,80},{80,96},{96,112},{112,128},... | collective-permute-start | bytes 786440 | tf_op jit(solution)/shard_map/ppermute | solution.py:332
  16.2 10.4 %collective-permute-start.1 = (f32[4,64,2,128]{3,2,1,0:T(2,128)}, f32[4,64,2,128]{3,2,1,0:T(2,128)S(1)}, u32[]{:S(2)}, u32[]{:S(2)}) collective-permute-start(f32[4,64,2,128]{3,2,1,0:T(2,128)} %get-tuple-element.11), channel_id=1, source_target_pairs={{16,0},{32,16},{48,32},{64,48},{80,64},{96,80},{112,96},{128,112},... | collective-permute-start | bytes 786440 | tf_op jit(solution)/shard_map/ppermute | solution.py:333
  24.7 1.9 %copy-start.4 = (f32[4,64,2,128]{3,2,1,0:T(2,128)}, f32[4,64,2,128]{3,2,1,0:T(2,128)S(1)}, u32[]{:S(2)}) copy-start(f32[4,64,2,128]{3,2,1,0:T(2,128)S(1)} %collective-permute-done.west_ref) | copy-start | bytes 786436
  26.5 0.7 copy-start.5
  45.9 23.4 %collective-permute-start.4 = (f32[6,32,128]{2,1,0:T(8,128)S(1)}, f32[6,32,128]{2,1,0:T(8,128)S(1)}, u32[]{:S(2)}, u32[]{:S(2)}) collective-permute-start(f32[6,32,128]{2,1,0:T(8,128)S(1)} %pad_maximum_fusion.2), channel_id=1, source_target_pairs={{0,32},{16,48},{32,64},{48,80},{64,96},{80,112},{96,128},{112,144}... | collective-permute-start | bytes 294920 | tf_op jit(solution)/shard_map/ppermute | solution.py:72
  50.0 19.4 %collective-permute-start.5 = (f32[6,32,128]{2,1,0:T(8,128)S(1)}, f32[6,32,128]{2,1,0:T(8,128)S(1)}, u32[]{:S(2)}, u32[]{:S(2)}) collective-permute-start(f32[6,32,128]{2,1,0:T(8,128)S(1)} %pad_maximum_fusion.2), channel_id=1, source_target_pairs={{0,16},{16,32},{32,48},{48,64},{64,80},{80,96},{96,112},{112,128},... | collective-permute-start | bytes 294920 | tf_op jit(solution)/shard_map/ppermute | solution.py:72
  51.9 17.5 %collective-permute-start.6 = (f32[6,32,128]{2,1,0:T(8,128)S(1)}, f32[6,32,128]{2,1,0:T(8,128)S(1)}, u32[]{:S(2)}, u32[]{:S(2)}) collective-permute-start(f32[6,32,128]{2,1,0:T(8,128)S(1)} %pad_maximum_fusion.2), channel_id=1, source_target_pairs={{16,0},{32,16},{48,32},{64,48},{80,64},{96,80},{112,96},{128,112},... | collective-permute-start | bytes 294920 | tf_op jit(solution)/shard_map/ppermute | solution.py:73
  57.4 12.1 %collective-permute-start.7 = (f32[6,32,128]{2,1,0:T(8,128)S(1)}, f32[6,32,128]{2,1,0:T(8,128)S(1)}, u32[]{:S(2)}, u32[]{:S(2)}) collective-permute-start(f32[6,32,128]{2,1,0:T(8,128)S(1)} %pad_maximum_fusion.2), channel_id=1, source_target_pairs={{32,0},{48,16},{64,32},{80,48},{96,64},{112,80},{128,96},{144,112}... | collective-permute-start | bytes 294920 | tf_op jit(solution)/shard_map/ppermute | solution.py:73
  68.5 0.9 copy-start.6
  68.5 8.2 %copy-start.1 = (f32[4,64,32,128]{3,2,1,0:T(8,128)S(1)}, f32[4,64,32,128]{3,2,1,0:T(8,128)}, u32[]{:S(2)}) copy-start(f32[4,64,32,128]{3,2,1,0:T(8,128)} %state_ref.3) | copy-start | bytes 12582916
  69.7 14.4 %collective-permute-start.9 = (f32[6,160,64]{2,1,0:T(8,128)S(1)}, f32[6,160,64]{2,1,0:T(8,128)S(1)}, u32[]{:S(2)}, u32[]{:S(2)}) collective-permute-start(f32[6,160,64]{2,1,0:T(8,128)S(1)} %get-tuple-element.29), channel_id=1, source_target_pairs={{1,0},{2,1},{3,2},{4,3},{5,4},{6,5},{7,6},{8,7},{9,8},{10,9},{11,1... | collective-permute-start | bytes 737288 | tf_op jit(solution)/shard_map/ppermute | solution.py:73
  72.9 11.1 %collective-permute-start.8 = (f32[6,160,64]{2,1,0:T(8,128)S(1)}, f32[6,160,64]{2,1,0:T(8,128)S(1)}, u32[]{:S(2)}, u32[]{:S(2)}) collective-permute-start(f32[6,160,64]{2,1,0:T(8,128)S(1)} %get-tuple-element.28), channel_id=1, source_target_pairs={{0,1},{1,2},{2,3},{3,4},{4,5},{5,6},{6,7},{7,8},{8,9},{9,10},{10,1... | collective-permute-start | bytes 737288 | tf_op jit(solution)/shard_map/ppermute | solution.py:72
  81.5 2.0 %copy-start.2 = (f32[4,64,32,128]{3,1,2,0:T(8,128)}, f32[4,64,32,128]{3,1,2,0:T(8,128)S(1)}, u32[]{:S(2)}) copy-start(f32[4,64,32,128]{3,1,2,0:T(8,128)S(1)} %fusion) | copy-start | bytes 12582916

commit v11 on v10

--- a/solution.py
+++ b/solution.py
@@ -186,7 +186,7 @@
     )(depth_class, coriolis, state, west, east, side)
 
 
-def pack_kernel(depth_ref, state_ref, out_ref, head_ref, tail_ref):
+def pack_kernel(depth_ref, state_ref, after_ref, out_ref):
     block_index = pl.program_id(0)
     fields, depth_levels, rows, cols = state_ref.shape
     block = depth_levels * pl.num_programs(0) // 4
@@ -200,8 +200,6 @@
         second = (lane == low + 2) | (lane == low + 3)
         for f in range(fields):
             masked = state_ref[f, k] * active
-            head_ref[f, k] = masked[0:2]
-            tail_ref[f, k] = masked[rows - 2 : rows]
             near_end = pltpu.roll(masked, low, 1)
             far_end = pltpu.roll(masked, (low + 4) % cols, 1)
             packed[f] = jnp.where(first, near_end, jnp.where(second, far_end, packed[f]))
@@ -209,24 +207,62 @@
         out_ref[f, 0] = packed[f]
 
 
-def pack_edges(state, depth_class):
+def pack_edges(state, depth_class, after):
     fields, levels, rows, cols = state.shape
-    rim = pl.BlockSpec((fields, PACK, 2, cols), lambda c: (0, c, 0, 0))
     return pl.pallas_call(
         pack_kernel,
         grid=(levels // PACK,),
+        out_shape=jax.ShapeDtypeStruct((fields, levels // PACK, rows, cols), jnp.float32),
+        in_specs=[pl.BlockSpec((rows, cols), lambda c: (0, 0)),
+                  pl.BlockSpec((fields, PACK, rows, cols), lambda c: (0, c, 0, 0)),
+                  pl.BlockSpec(memory_space=pl.ANY)],
+        out_specs=pl.BlockSpec((fields, 1, rows, cols), lambda c: (0, c, 0, 0)),
+        cost_estimate=pl.CostEstimate(
+            flops=4 * state.size, transcendentals=0, bytes_accessed=4 * state.size
+        ),
+    )(depth_class, state, after)
+
+
+def rim_kernel(depth_top_ref, depth_bottom_ref, top_ref, bottom_ref, head_ref, tail_ref):
+    fields, levels = top_ref.shape[0], top_ref.shape[1]
+    block = levels // 4
+    reach_top = depth_top_ref[0:2] * block
+    reach_bottom = depth_bottom_ref[6:8] * block
+
+    def level(k, carry):
+        for f in range(fields):
+            head_ref[f, k] = top_ref[f, k, 0:2] * (k < reach_top).astype(jnp.float32)
+            tail_ref[f, k] = bottom_ref[f, k, 6:8] * (k < reach_bottom).astype(jnp.float32)
+        return carry
+
+    lax.fori_loop(0, levels, level, 0)
+
+
+def rim_rows(state, depth_class):
+    fields, levels, rows, cols = state.shape
+    last = rows // 8 - 1
+    return pl.pallas_call(
+        rim_kernel,
         out_shape=(
-            jax.ShapeDtypeStruct((fields, levels // PACK, rows, cols), jnp.float32),
             jax.ShapeDtypeStruct((fields, levels, 2, cols), jnp.float32),
             jax.ShapeDtypeStruct((fields, levels, 2, cols), jnp.float32),
         ),
-        in_specs=[pl.BlockSpec((rows, cols), lambda c: (0, 0)),
-                  pl.BlockSpec((fields, PACK, rows, cols), lambda c: (0, c, 0, 0))],
-        out_specs=(pl.BlockSpec((fields, 1, rows, cols), lambda c: (0, c, 0, 0)), rim, rim),
+        grid=(1,),
+        in_specs=[
+            pl.BlockSpec((8, cols), lambda i: (0, 0)),
+            pl.BlockSpec((8, cols), lambda i: (last, 0)),
+            pl.BlockSpec((fields, levels, 8, cols), lambda i: (0, 0, 0, 0)),
+            pl.BlockSpec((fields, levels, 8, cols), lambda i: (0, 0, last, 0)),
+        ],
+        out_specs=(
+            pl.BlockSpec((fields, levels, 2, cols), lambda i: (0, 0, 0, 0)),
+            pl.BlockSpec((fields, levels, 2, cols), lambda i: (0, 0, 0, 0)),
+        ),
         cost_estimate=pl.CostEstimate(
-            flops=4 * state.size, transcendentals=0, bytes_accessed=4 * state.size
-        ),
-    )(depth_class, state)
+            flops=fields * levels * 4 * cols, transcendentals=0,
+            bytes_accessed=4 * fields * levels * 20 * cols,
+        ),
+    )(depth_class, depth_class, state, state)
 
 
 def combine(from_south, from_north):
@@ -327,10 +363,11 @@
     column_blocks = lax.axis_size(("gy", "mode"))
     anchor = lax.axis_index(("gy", "mode")) * y_cells
     coriolis = coriolis_row(anchor, y_cells, y_cells * column_blocks)
-    edges, head, tail = pack_edges(state, depth_class)
+    head, tail = rim_rows(state, depth_class)
     x_count = lax.axis_size("gx")
     west = lax.ppermute(tail, "gx", [(i, i + 1) for i in range(x_count - 1)])
     east = lax.ppermute(head, "gx", [(i + 1, i) for i in range(x_count - 1)])
+    edges = pack_edges(state, depth_class, head)
     y_count = lax.axis_size(("gy", "mode"))
     from_south = lax.ppermute(edges, ("gy", "mode"), [(i, i + 1) for i in range(y_count - 1)])
     from_north = lax.ppermute(edges, ("gy", "mode"), [(i + 1, i) for i in range(y_count - 1)])

time: 106 us -> 112 us (1.057)
  waiting for transfers between devices: 3.32 us -> 6.74 us
  Pallas kernels: 34.5 us -> 36.9 us
    ppermute x1, waiting for transfers between devices: 1.44 us -> 5.05 us  [body(): west = lax.ppermute(tail, 'gx', [(i, i + 1) for i in range(x_count - 1)])]
    pallas_call x1 -> x2, Pallas kernels: 5.04 us -> 7.5 us  [the longest x1 4.55 us: pack_edges(): pl.pallas_call(pack_kernel, grid=(levels // PACK,), out_shape=jax.ShapeDt...]
    ppermute x3, starting transfers between devices: 9.8 us -> 7.57 us  [wide_halo(): lax.ppermute(tail, axis, [(i, i + hop) for i in range(count - hop)])]
    ppermute x1, waiting for transfers between devices: 1.86 us -> 0.01 us  [body(): east = lax.ppermute(head, 'gx', [(i + 1, i) for i in range(x_count - 1)])]
    ppermute x1, waiting for transfers between devices: 0.01 us -> 1.67 us  [body(): lax.ppermute(edges, ('gy', 'mode'), [(i + 1, i) for i in range(y_count -...]
    ppermute x1, starting transfers between devices: 3.2 us -> 1.92 us  [body(): west = lax.ppermute(tail, 'gx', [(i, i + 1) for i in range(x_count - 1)])]
    ppermute x3, starting transfers between devices: 11.2 us -> 12.5 us  [wide_halo(): lax.ppermute(head, axis, [(i + hop, i) for i in range(count - hop)])]
    unnamed x24 -> x26, local copies, waits for them, and re-layouts: 7.22 us -> 7.93 us
  transfers between devices with their start and end apart: 10 -> 10, of which waited for: 2 -> 2; matrix products, arithmetic and copies ran while one was open for 16% -> 16% of each run, Pallas kernels for 0% -> 4%
where the time goes in v11:
time: 112 us; the launch traced here: 111 us
  Pallas kernels  36.9 us (33%)
  starting transfers between devices  34.5 us (31%)
  other arithmetic  13.5 us (12%)
  local copies, waits for them, and re-layouts  9.89 us (9%)
  matrix products  8.64 us (8%)
  waiting for transfers between devices  6.74 us (6%)
    pallas_call x1, Pallas kernels, stencil(): pl.pallas_call(stencil_kernel, grid=(steps,), out_shape=(jax.ShapeDtypeSt...  17.9 us
    ppermute x3, starting transfers between devices, wide_halo(): lax.ppermute(head, axis, [(i + hop, i) for i in range(count - hop)])  12.5 us
    pallas_call x1, Pallas kernels, local_waves(): pl.pallas_call(wave_kernel, out_shape=(jax.ShapeDtypeStruct((inner_rows,...  11.5 us
    dot_general x1, matrix products, vertical_solve(): jnp.einsum('kl,flxy->fkxy', stacked, provisional, precision=lax.Precision...  8.64 us
    unnamed x26, local copies, waits for them, and re-layouts  7.93 us
    ppermute x3, starting transfers between devices, wide_halo(): lax.ppermute(tail, axis, [(i, i + hop) for i in range(count - hop)])  7.57 us
    ppermute x1, starting transfers between devices, body(): lax.ppermute(edges, ('gy', 'mode'), [(i, i + 1) for i in range(y_count -...  5.58 us
    ppermute x1, waiting for transfers between devices, body(): west = lax.ppermute(tail, 'gx', [(i, i + 1) for i in range(x_count - 1)])  5.05 us
  transfers between devices with their start and end apart: 10, of which 2 were waited for; matrix products, arithmetic and copies ran while one was open for 16% of the time, Pallas kernels for 4%

profile of v11, /device:TPU:103, one launch (start us, length us, event | category | flops | bytes accessed | tf_op | source)
XLA Modules:
  0.0 111.3 jit_solution(9541580467265926757)
XLA Ops:
  0.6 2.9 %shard_map.85 = (f32[4,64,2,128]{3,2,1,0:T(2,128)}, f32[4,64,2,128]{3,2,1,0:T(2,128)}) custom-call(s32[32,128]{1,0:T(8,128)} %depth_ref.3, s32[32,128]{1,0:T(8,128)} %depth_ref.3, f32[4,64,32,128]{3,2,1,0:T(8,128)} %state_ref.3, f32[4,64,32,128]{3,2,1,0:T(8,128)} %state_ref.3), custom_call_target="tpu_custom_call" | custom-call | flops 131072 | bytes 2621440 | tf_op jit(solution)/shard_map/pallas_call | solution.py:244
  3.6 5.0 %collective-permute-start.1 = (f32[4,64,2,128]{3,2,1,0:T(2,128)}, f32[4,64,2,128]{3,2,1,0:T(2,128)S(1)}, u32[]{:S(2)}, u32[]{:S(2)}) collective-permute-start(f32[4,64,2,128]{3,2,1,0:T(2,128)} %get-tuple-element.10.after_ref), channel_id=1, source_target_pairs={{16,0},{32,16},{48,32},{64,48},{80,64},{96,80},{112,96},{128,112},... | collective-permute-start | bytes 786440 | tf_op jit(solution)/shard_map/ppermute | solution.py:369
  8.7 4.5 %shard_map.86 = f32[4,2,32,128]{3,2,1,0:T(8,128)} custom-call(s32[32,128]{1,0:T(8,128)} %depth_ref.3, f32[4,64,32,128]{3,2,1,0:T(8,128)} %state_ref.3, f32[4,64,2,128]{3,2,1,0:T(2,128)} %get-tuple-element.10.after_ref), custom_call_target="tpu_custom_call" | custom-call | flops 4194304 | bytes 4194304 | tf_op jit(solution)/shard_map/pallas_call | solution.py:212
  13.2 5.6 %collective-permute-start.2 = (f32[4,2,32,128]{3,2,1,0:T(8,128)}, f32[4,2,32,128]{3,2,1,0:T(8,128)S(1)}, u32[]{:S(2)}, u32[]{:S(2)}) collective-permute-start(f32[4,2,32,128]{3,2,1,0:T(8,128)} %shard_map.86), channel_id=1, source_target_pairs={{0,1},{1,2},{2,3},{3,4},{4,5},{5,6},{6,7},{7,8},{8,9},{9,10},{10,1... | collective-permute-start | bytes 393224 | tf_op jit(solution)/shard_map/ppermute | solution.py:372
  18.8 1.9 %collective-permute-start.3 = (f32[4,2,32,128]{3,2,1,0:T(8,128)}, f32[4,2,32,128]{3,2,1,0:T(8,128)S(1)}, u32[]{:S(2)}, u32[]{:S(2)}) collective-permute-start(f32[4,2,32,128]{3,2,1,0:T(8,128)} %shard_map.86), channel_id=1, source_target_pairs={{1,0},{2,1},{3,2},{4,3},{5,4},{6,5},{7,6},{8,7},{9,8},{10,9},{11,1... | collective-permute-start | bytes 393224 | tf_op jit(solution)/shard_map/ppermute | solution.py:373
  20.8 1.9 %collective-permute-start = (f32[4,64,2,128]{3,2,1,0:T(2,128)S(1)}, f32[4,64,2,128]{3,2,1,0:T(2,128)S(1)}, u32[]{:S(2)}, u32[]{:S(2)}) collective-permute-start(f32[4,64,2,128]{3,2,1,0:T(2,128)S(1)} %copy-done.10), channel_id=1, source_target_pairs={{0,16},{16,32},{32,48},{48,64},{64,80},{80,96},{96,112},{112,128},... | collective-permute-start | bytes 786440 | tf_op jit(solution)/shard_map/ppermute | solution.py:368
  24.9 1.7 %collective-permute-done.3 = f32[4,2,32,128]{3,2,1,0:T(8,128)S(1)} collective-permute-done((f32[4,2,32,128]{3,2,1,0:T(8,128)}, f32[4,2,32,128]{3,2,1,0:T(8,128)S(1)}, u32[]{:S(2)}, u32[]{:S(2)}) %collective-permute-start.3) | collective-permute-done | bytes 131104 | tf_op jit(solution)/shard_map/ppermute | solution.py:373
  27.2 5.0 %collective-permute-done.west_ref = f32[4,64,2,128]{3,2,1,0:T(2,128)S(1)} collective-permute-done((f32[4,64,2,128]{3,2,1,0:T(2,128)S(1)}, f32[4,64,2,128]{3,2,1,0:T(2,128)S(1)}, u32[]{:S(2)}, u32[]{:S(2)}) %collective-permute-start) | collective-permute-done | bytes 262176 | tf_op jit(solution)/shard_map/ppermute | solution.py:368
  33.7 17.9 %shard_map.87 = (f32[4,64,32,128]{3,2,1,0:T(8,128)}, f32[2,32,128]{2,1,0:T(8,128)}) custom-call(s32[32,128]{1,0:T(8,128)} %depth_ref.3, f32[1,128]{1,0:T(1,128)} %multiply_add_fusion.2.coriolis_ref, f32[4,64,32,128]{3,2,1,0:T(8,128)} %state_ref.3, f32[4,64,2,128]{3,2,1,0:T(2,128)} %copy-done.5, f32[4,64,2,128]{3,2,1,0:T(2,128)} %copy-done.4, ...), custom_call_target="tpu_custom_call" | custom-call | flops 62914560 | bytes 8388608 | tf_op jit(solution)/shard_map/pallas_call | solution.py:174
  52.3 1.9 %collective-permute-start.4 = (f32[6,32,128]{2,1,0:T(8,128)S(1)}, f32[6,32,128]{2,1,0:T(8,128)S(1)}, u32[]{:S(2)}, u32[]{:S(2)}) collective-permute-start(f32[6,32,128]{2,1,0:T(8,128)S(1)} %pad_maximum_fusion.2), channel_id=1, source_target_pairs={{0,32},{16,48},{32,64},{48,80},{64,96},{80,112},{96,128},{112,144}... | collective-permute-start | bytes 294920 | tf_op jit(solution)/shard_map/ppermute | solution.py:72
  54.2 1.9 %collective-permute-start.5 = (f32[6,32,128]{2,1,0:T(8,128)S(1)}, f32[6,32,128]{2,1,0:T(8,128)S(1)}, u32[]{:S(2)}, u32[]{:S(2)}) collective-permute-start(f32[6,32,128]{2,1,0:T(8,128)S(1)} %pad_maximum_fusion.2), channel_id=1, source_target_pairs={{0,16},{16,32},{32,48},{48,64},{64,80},{80,96},{96,112},{112,128},... | collective-permute-start | bytes 294920 | tf_op jit(solution)/shard_map/ppermute | solution.py:72
  56.1 5.5 %collective-permute-start.6 = (f32[6,32,128]{2,1,0:T(8,128)S(1)}, f32[6,32,128]{2,1,0:T(8,128)S(1)}, u32[]{:S(2)}, u32[]{:S(2)}) collective-permute-start(f32[6,32,128]{2,1,0:T(8,128)S(1)} %pad_maximum_fusion.2), channel_id=1, source_target_pairs={{16,0},{32,16},{48,32},{64,48},{80,64},{96,80},{112,96},{128,112},... | collective-permute-start | bytes 294920 | tf_op jit(solution)/shard_map/ppermute | solution.py:73
  61.6 3.7 %collective-permute-start.7 = (f32[6,32,128]{2,1,0:T(8,128)S(1)}, f32[6,32,128]{2,1,0:T(8,128)S(1)}, u32[]{:S(2)}, u32[]{:S(2)}) collective-permute-start(f32[6,32,128]{2,1,0:T(8,128)S(1)} %pad_maximum_fusion.2), channel_id=1, source_target_pairs={{32,0},{48,16},{64,32},{80,48},{96,64},{112,80},{128,96},{144,112}... | collective-permute-start | bytes 294920 | tf_op jit(solution)/shard_map/ppermute | solution.py:73
  65.3 8.6 %fusion.3 = f32[4,160,32,128]{3,1,2,0:T(8,128)S(1)} fusion(f32[4,64,32,128]{3,2,1,0:T(8,128)} %get-tuple-element.11, f32[160,64]{1,0:T(8,128)S(1)} %gather_fusion), kind=kOutput, calls=%fused_computation.7 | convolution fusion | flops 1006632960 | bytes 14721024 | tf_op jit(solution)/shard_map/kl,flxy->fkxy/dot_general | solution.py:39
  74.0 0.8 fusion.9
  75.1 3.4 %collective-permute-start.9 = (f32[6,160,64]{2,1,0:T(8,128)S(1)}, f32[6,160,64]{2,1,0:T(8,128)S(1)}, u32[]{:S(2)}, u32[]{:S(2)}) collective-permute-start(f32[6,160,64]{2,1,0:T(8,128)S(1)} %get-tuple-element.27), channel_id=1, source_target_pairs={{1,0},{2,1},{3,2},{4,3},{5,4},{6,5},{7,6},{8,7},{9,8},{10,9},{11,1... | collective-permute-start | bytes 737288 | tf_op jit(solution)/shard_map/ppermute | solution.py:73
  78.5 3.7 %collective-permute-start.8 = (f32[6,160,64]{2,1,0:T(8,128)S(1)}, f32[6,160,64]{2,1,0:T(8,128)S(1)}, u32[]{:S(2)}, u32[]{:S(2)}) collective-permute-start(f32[6,160,64]{2,1,0:T(8,128)S(1)} %get-tuple-element.26), channel_id=1, source_target_pairs={{0,1},{1,2},{2,3},{3,4},{4,5},{5,6},{6,7},{7,8},{8,9},{9,10},{10,1... | collective-permute-start | bytes 737288 | tf_op jit(solution)/shard_map/ppermute | solution.py:72
  82.2 4.7 %fusion = f32[4,64,32,128]{3,1,2,0:T(8,128)S(1)} fusion(f32[4,16,32,128]{3,1,2,0:T(8,128)S(1)} %get-tuple-element.21, f32[4,16,32,128]{3,1,2,0:T(8,128)S(1)} %get-tuple-element.20, f32[4,16,32,128]{3,1,2,0:T(8,128)S(1)} %get-tuple-element.19, f32[4,16,32,128]{3,1,2,0:T(8,128)S(1)} %get-tuple-element.18, f32[4,64,32,128]{3,2,1,0:T(8,128)S(1)} %copy-done.1, ...), kind=kLoop, calls=%fused_computation.2 | loop fusion | flops 6291456 | bytes 14680064 | tf_op jit(solution)/shard_map/add | solution.py:50
  87.0 2.0 %copy-done.2 = f32[4,64,32,128]{3,1,2,0:T(8,128)} copy-done((f32[4,64,32,128]{3,1,2,0:T(8,128)}, f32[4,64,32,128]{3,1,2,0:T(8,128)S(1)}, u32[]{:S(2)}) %copy-start.2) | copy-done | bytes 4194328
  90.0 1.1 fusion.16
  91.0 11.5 %shard_map.88 = (f32[32,128]{1,0:T(8,128)}, f32[2,32,128]{2,1,0:T(8,128)}) custom-call(f32[3,160,256]{2,1,0:T(8,128)} %get-tuple-element.25.moving_ref, f32[3,160,256]{2,1,0:T(8,128)} %get-tuple-element.24.fixed_ref, f32[1,256]{1,0:T(1,128)} %multiply_add_fusion.1.coriolis_ref), custom_call_target="tpu_custom_call" | custom-call | flops 39321600 | bytes 1146880 | tf_op jit(solution)/shard_map/pallas_call | solution.py:342
  102.6 0.8 divide_subtract_fusion
  103.4 2.9 %fusion.15 = (f32[2,64,32,128]{3,1,2,0:T(8,128)S(1)}, f32[2,64,32,128]{3,1,2,0:T(8,128)S(1)}) fusion(f32[4,64,32,128]{3,1,2,0:T(8,128)} %copy-done.2, f32[2,32,128]{2,1,0:T(8,128)S(1)} %divide_subtract_fusion, f32[64,32,128]{2,0,1:T(8,128)S(1)} %fusion.12), kind=kLoop, calls=%fused_computation.56 | loop fusion | flops 1048576 | bytes 9469952 | tf_op jit(solution)/shard_map/slice | solution.py:59
  106.8 4.4 %copy.12 = f32[4,64,32,128]{3,2,1,0:T(8,128)} copy(f32[4,64,32,128]{3,1,2,0:T(8,128)S(1)} %pad_maximum_fusion) | data formatting | bytes 8388608
  (52 shorter events, 6.7 us)
Async XLA Ops:
  0.6 23.5 %copy-start = (f32[4,64,64]{2,1,0:T(8,128)S(1)}, f32[4,64,64]{2,1,0:T(8,128)}, u32[]{:S(2)}) copy-start(f32[4,64,64]{2,1,0:T(8,128)} %param.8) | copy-start | bytes 196612
  3.6 17.2 %copy-start.10 = (f32[4,64,2,128]{3,2,1,0:T(2,128)S(1)}, f32[4,64,2,128]{3,2,1,0:T(2,128)}, u32[]{:S(2)}) copy-start(f32[4,64,2,128]{3,2,1,0:T(2,128)} %get-tuple-element.9) | copy-start | bytes 786436
  3.6 19.1 %copy-start.3 = (s32[32,128]{1,0:T(8,128)S(1)}, s32[32,128]{1,0:T(8,128)}, u32[]{:S(2)}) copy-start(s32[32,128]{1,0:T(8,128)} %depth_ref.3) | copy-start | bytes 49156
  3.6 19.4 %copy-start.9 = (s32[160]{0:T(256)S(1)}, s32[160]{0:T(256)}, u32[]{:S(2)}) copy-start(s32[160]{0:T(256)} %constant.93) | copy-start | bytes 1924
  3.6 20.0 %copy-start.7 = (f32[2,32,128]{2,1,0:T(8,128)S(1)}, f32[2,32,128]{2,1,0:T(8,128)}, u32[]{:S(2)}) copy-start(f32[2,32,128]{2,1,0:T(8,128)} %param.10) | copy-start | bytes 98308
  3.6 20.0 %copy-start.8 = (f32[32,128]{1,0:T(8,128)S(1)}, f32[32,128]{1,0:T(8,128)}, u32[]{:S(2)}) copy-start(f32[32,128]{1,0:T(8,128)} %param.9) | copy-start | bytes 49156
  3.6 28.6 %collective-permute-start.1 = (f32[4,64,2,128]{3,2,1,0:T(2,128)}, f32[4,64,2,128]{3,2,1,0:T(2,128)S(1)}, u32[]{:S(2)}, u32[]{:S(2)}) collective-permute-start(f32[4,64,2,128]{3,2,1,0:T(2,128)} %get-tuple-element.10.after_ref), channel_id=1, source_target_pairs={{16,0},{32,16},{48,32},{64,48},{80,64},{96,80},{112,96},{128,112},... | collective-permute-start | bytes 786440 | tf_op jit(solution)/shard_map/ppermute | solution.py:369
  13.2 11.6 %collective-permute-start.2 = (f32[4,2,32,128]{3,2,1,0:T(8,128)}, f32[4,2,32,128]{3,2,1,0:T(8,128)S(1)}, u32[]{:S(2)}, u32[]{:S(2)}) collective-permute-start(f32[4,2,32,128]{3,2,1,0:T(8,128)} %shard_map.86), channel_id=1, source_target_pairs={{0,1},{1,2},{2,3},{3,4},{4,5},{5,6},{6,7},{7,8},{8,9},{9,10},{10,1... | collective-permute-start | bytes 393224 | tf_op jit(solution)/shard_map/ppermute | solution.py:372
  18.8 7.7 %collective-permute-start.3 = (f32[4,2,32,128]{3,2,1,0:T(8,128)}, f32[4,2,32,128]{3,2,1,0:T(8,128)S(1)}, u32[]{:S(2)}, u32[]{:S(2)}) collective-permute-start(f32[4,2,32,128]{3,2,1,0:T(8,128)} %shard_map.86), channel_id=1, source_target_pairs={{1,0},{2,1},{3,2},{4,3},{5,4},{6,5},{7,6},{8,7},{9,8},{10,9},{11,1... | collective-permute-start | bytes 393224 | tf_op jit(solution)/shard_map/ppermute | solution.py:373
  20.8 11.5 %collective-permute-start = (f32[4,64,2,128]{3,2,1,0:T(2,128)S(1)}, f32[4,64,2,128]{3,2,1,0:T(2,128)S(1)}, u32[]{:S(2)}, u32[]{:S(2)}) collective-permute-start(f32[4,64,2,128]{3,2,1,0:T(2,128)S(1)} %copy-done.10), channel_id=1, source_target_pairs={{0,16},{16,32},{32,48},{48,64},{64,80},{80,96},{96,112},{112,128},... | collective-permute-start | bytes 786440 | tf_op jit(solution)/shard_map/ppermute | solution.py:368
  32.2 0.7 copy-start.5
  32.9 0.7 copy-start.4
  52.3 22.5 %collective-permute-start.4 = (f32[6,32,128]{2,1,0:T(8,128)S(1)}, f32[6,32,128]{2,1,0:T(8,128)S(1)}, u32[]{:S(2)}, u32[]{:S(2)}) collective-permute-start(f32[6,32,128]{2,1,0:T(8,128)S(1)} %pad_maximum_fusion.2), channel_id=1, source_target_pairs={{0,32},{16,48},{32,64},{48,80},{64,96},{80,112},{96,128},{112,144}... | collective-permute-start | bytes 294920 | tf_op jit(solution)/shard_map/ppermute | solution.py:72
  54.2 20.6 %collective-permute-start.5 = (f32[6,32,128]{2,1,0:T(8,128)S(1)}, f32[6,32,128]{2,1,0:T(8,128)S(1)}, u32[]{:S(2)}, u32[]{:S(2)}) collective-permute-start(f32[6,32,128]{2,1,0:T(8,128)S(1)} %pad_maximum_fusion.2), channel_id=1, source_target_pairs={{0,16},{16,32},{32,48},{48,64},{64,80},{80,96},{96,112},{112,128},... | collective-permute-start | bytes 294920 | tf_op jit(solution)/shard_map/ppermute | solution.py:72
  56.1 18.7 %collective-permute-start.6 = (f32[6,32,128]{2,1,0:T(8,128)S(1)}, f32[6,32,128]{2,1,0:T(8,128)S(1)}, u32[]{:S(2)}, u32[]{:S(2)}) collective-permute-start(f32[6,32,128]{2,1,0:T(8,128)S(1)} %pad_maximum_fusion.2), channel_id=1, source_target_pairs={{16,0},{32,16},{48,32},{64,48},{80,64},{96,80},{112,96},{128,112},... | collective-permute-start | bytes 294920 | tf_op jit(solution)/shard_map/ppermute | solution.py:73
  61.6 13.2 %collective-permute-start.7 = (f32[6,32,128]{2,1,0:T(8,128)S(1)}, f32[6,32,128]{2,1,0:T(8,128)S(1)}, u32[]{:S(2)}, u32[]{:S(2)}) collective-permute-start(f32[6,32,128]{2,1,0:T(8,128)S(1)} %pad_maximum_fusion.2), channel_id=1, source_target_pairs={{32,0},{48,16},{64,32},{80,48},{96,64},{112,80},{128,96},{144,112}... | collective-permute-start | bytes 294920 | tf_op jit(solution)/shard_map/ppermute | solution.py:73
  73.9 0.9 copy-start.6
  73.9 8.3 %copy-start.1 = (f32[4,64,32,128]{3,2,1,0:T(8,128)S(1)}, f32[4,64,32,128]{3,2,1,0:T(8,128)}, u32[]{:S(2)}) copy-start(f32[4,64,32,128]{3,2,1,0:T(8,128)} %state_ref.3) | copy-start | bytes 12582916
  75.1 14.4 %collective-permute-start.9 = (f32[6,160,64]{2,1,0:T(8,128)S(1)}, f32[6,160,64]{2,1,0:T(8,128)S(1)}, u32[]{:S(2)}, u32[]{:S(2)}) collective-permute-start(f32[6,160,64]{2,1,0:T(8,128)S(1)} %get-tuple-element.27), channel_id=1, source_target_pairs={{1,0},{2,1},{3,2},{4,3},{5,4},{6,5},{7,6},{8,7},{9,8},{10,9},{11,1... | collective-permute-start | bytes 737288 | tf_op jit(solution)/shard_map/ppermute | solution.py:73
  78.5 11.0 %collective-permute-start.8 = (f32[6,160,64]{2,1,0:T(8,128)S(1)}, f32[6,160,64]{2,1,0:T(8,128)S(1)}, u32[]{:S(2)}, u32[]{:S(2)}) collective-permute-start(f32[6,160,64]{2,1,0:T(8,128)S(1)} %get-tuple-element.26), channel_id=1, source_target_pairs={{0,1},{1,2},{2,3},{3,4},{4,5},{5,6},{6,7},{7,8},{8,9},{9,10},{10,1... | collective-permute-start | bytes 737288 | tf_op jit(solution)/shard_map/ppermute | solution.py:72
  87.0 2.0 %copy-start.2 = (f32[4,64,32,128]{3,1,2,0:T(8,128)}, f32[4,64,32,128]{3,1,2,0:T(8,128)S(1)}, u32[]{:S(2)}) copy-start(f32[4,64,32,128]{3,1,2,0:T(8,128)S(1)} %fusion) | copy-start | bytes 12582916

commit v12 on v10

--- a/solution.py
+++ b/solution.py
@@ -7,7 +7,7 @@
 from jax.sharding import PartitionSpec as P
 
 SUB = 32
-LEVEL_CHUNK = 8
+LEVEL_CHUNK = 16
 PACK = 32
 
 
@@ -238,7 +238,7 @@
     rows, cols = moving_ref.shape[1], moving_ref.shape[2]
     inner_rows, inner_cols = height_ref.shape[0], height_ref.shape[1]
     rim = (rows - inner_rows) // 2
-    groups = 4
+    groups = 8
     per_group = SUB // groups
     trim = 2 * per_group
     work_ref[...] = moving_ref[...]

time: 106 us -> 106 us (level)
  no operation moved by 1% of the time
where the time goes in v12:
time: 106 us
  starting transfers between devices  35.6 us (34%)
  Pallas kernels  34.4 us (32%)
  other arithmetic  13.6 us (13%)
  local copies, waits for them, and re-layouts  9.14 us (9%)
  matrix products  8.64 us (8%)
  waiting for transfers between devices  3.32 us (3%)
    pallas_call x1, Pallas kernels, stencil(): pl.pallas_call(stencil_kernel, grid=(steps,), out_shape=(jax.ShapeDtypeSt...  17.9 us
    pallas_call x1, Pallas kernels, local_waves(): pl.pallas_call(wave_kernel, out_shape=(jax.ShapeDtypeStruct((inner_rows,...  11.4 us
    ppermute x3, starting transfers between devices, wide_halo(): lax.ppermute(head, axis, [(i + hop, i) for i in range(count - hop)])  11.2 us
    ppermute x3, starting transfers between devices, wide_halo(): lax.ppermute(tail, axis, [(i, i + hop) for i in range(count - hop)])  9.8 us
    dot_general x1, matrix products, vertical_solve(): jnp.einsum('kl,flxy->fkxy', stacked, provisional, precision=lax.Precision...  8.64 us
    unnamed x24, local copies, waits for them, and re-layouts  7.22 us
    ppermute x1, starting transfers between devices, body(): lax.ppermute(edges, ('gy', 'mode'), [(i, i + 1) for i in range(y_count -...  5.3 us
    pallas_call x1, Pallas kernels, pack_edges(): pl.pallas_call(pack_kernel, grid=(levels // PACK,), out_shape=(jax.ShapeD...  5.04 us
  transfers between devices with their start and end apart: 10, of which 2 were waited for; matrix products, arithmetic and copies ran while one was open for 16% of the time, Pallas kernels for 0%

profile of v12, /device:TPU:103, one launch (start us, length us, event | category | flops | bytes accessed | tf_op | source)
XLA Modules:
  0.0 105.7 jit_solution(4857513159355394661)
XLA Ops:
  0.7 5.0 %shard_map.85 = (f32[4,2,32,128]{3,2,1,0:T(8,128)}, f32[4,64,2,128]{3,2,1,0:T(2,128)}, f32[4,64,2,128]{3,2,1,0:T(2,128)}) custom-call(s32[32,128]{1,0:T(8,128)} %depth_ref.3, f32[4,64,32,128]{3,2,1,0:T(8,128)} %state_ref.3), custom_call_target="tpu_custom_call" | custom-call | flops 4194304 | bytes 4194304 | tf_op jit(solution)/shard_map/pallas_call | solution.py:215
  5.7 5.3 %collective-permute-start.2 = (f32[4,2,32,128]{3,2,1,0:T(8,128)}, f32[4,2,32,128]{3,2,1,0:T(8,128)S(1)}, u32[]{:S(2)}, u32[]{:S(2)}) collective-permute-start(f32[4,2,32,128]{3,2,1,0:T(8,128)} %get-tuple-element.12), channel_id=1, source_target_pairs={{0,1},{1,2},{2,3},{3,4},{4,5},{5,6},{6,7},{7,8},{8,9},{9,10},{10,1... | collective-permute-start | bytes 393224 | tf_op jit(solution)/shard_map/ppermute | solution.py:335
  11.0 1.9 %collective-permute-start.3 = (f32[4,2,32,128]{3,2,1,0:T(8,128)}, f32[4,2,32,128]{3,2,1,0:T(8,128)S(1)}, u32[]{:S(2)}, u32[]{:S(2)}) collective-permute-start(f32[4,2,32,128]{3,2,1,0:T(8,128)} %get-tuple-element.12), channel_id=1, source_target_pairs={{1,0},{2,1},{3,2},{4,3},{5,4},{6,5},{7,6},{8,7},{9,8},{10,9},{11,1... | collective-permute-start | bytes 393224 | tf_op jit(solution)/shard_map/ppermute | solution.py:336
  13.0 3.2 %collective-permute-start = (f32[4,64,2,128]{3,2,1,0:T(2,128)}, f32[4,64,2,128]{3,2,1,0:T(2,128)S(1)}, u32[]{:S(2)}, u32[]{:S(2)}) collective-permute-start(f32[4,64,2,128]{3,2,1,0:T(2,128)} %get-tuple-element.10), channel_id=1, source_target_pairs={{0,16},{16,32},{32,48},{48,64},{64,80},{80,96},{96,112},{112,128},... | collective-permute-start | bytes 786440 | tf_op jit(solution)/shard_map/ppermute | solution.py:332
  16.2 4.2 %collective-permute-start.1 = (f32[4,64,2,128]{3,2,1,0:T(2,128)}, f32[4,64,2,128]{3,2,1,0:T(2,128)S(1)}, u32[]{:S(2)}, u32[]{:S(2)}) collective-permute-start(f32[4,64,2,128]{3,2,1,0:T(2,128)} %get-tuple-element.11), channel_id=1, source_target_pairs={{16,0},{32,16},{48,32},{64,48},{80,64},{96,80},{112,96},{128,112},... | collective-permute-start | bytes 786440 | tf_op jit(solution)/shard_map/ppermute | solution.py:333
  23.2 1.4 %collective-permute-done.west_ref = f32[4,64,2,128]{3,2,1,0:T(2,128)S(1)} collective-permute-done((f32[4,64,2,128]{3,2,1,0:T(2,128)}, f32[4,64,2,128]{3,2,1,0:T(2,128)S(1)}, u32[]{:S(2)}, u32[]{:S(2)}) %collective-permute-start) | collective-permute-done | bytes 262176 | tf_op jit(solution)/shard_map/ppermute | solution.py:332
  24.7 1.9 %collective-permute-done.1.east_ref = f32[4,64,2,128]{3,2,1,0:T(2,128)S(1)} collective-permute-done((f32[4,64,2,128]{3,2,1,0:T(2,128)}, f32[4,64,2,128]{3,2,1,0:T(2,128)S(1)}, u32[]{:S(2)}, u32[]{:S(2)}) %collective-permute-start.1) | collective-permute-done | bytes 262176 | tf_op jit(solution)/shard_map/ppermute | solution.py:333
  27.2 17.9 %shard_map.86 = (f32[4,64,32,128]{3,2,1,0:T(8,128)}, f32[2,32,128]{2,1,0:T(8,128)}) custom-call(s32[32,128]{1,0:T(8,128)} %depth_ref.3, f32[1,128]{1,0:T(1,128)} %multiply_add_fusion.2.coriolis_ref, f32[4,64,32,128]{3,2,1,0:T(8,128)} %state_ref.3, f32[4,64,2,128]{3,2,1,0:T(2,128)} %copy-done.4, f32[4,64,2,128]{3,2,1,0:T(2,128)} %copy-done.5, ...), custom_call_target="tpu_custom_call" | custom-call | flops 62914560 | bytes 8388608 | tf_op jit(solution)/shard_map/pallas_call | solution.py:174
  45.2 0.8 pad_maximum_fusion.2
  45.9 4.1 %collective-permute-start.4 = (f32[6,32,128]{2,1,0:T(8,128)S(1)}, f32[6,32,128]{2,1,0:T(8,128)S(1)}, u32[]{:S(2)}, u32[]{:S(2)}) collective-permute-start(f32[6,32,128]{2,1,0:T(8,128)S(1)} %pad_maximum_fusion.2), channel_id=1, source_target_pairs={{0,32},{16,48},{32,64},{48,80},{64,96},{80,112},{96,128},{112,144}... | collective-permute-start | bytes 294920 | tf_op jit(solution)/shard_map/ppermute | solution.py:72
  50.0 1.9 %collective-permute-start.5 = (f32[6,32,128]{2,1,0:T(8,128)S(1)}, f32[6,32,128]{2,1,0:T(8,128)S(1)}, u32[]{:S(2)}, u32[]{:S(2)}) collective-permute-start(f32[6,32,128]{2,1,0:T(8,128)S(1)} %pad_maximum_fusion.2), channel_id=1, source_target_pairs={{0,16},{16,32},{32,48},{48,64},{64,80},{80,96},{96,112},{112,128},... | collective-permute-start | bytes 294920 | tf_op jit(solution)/shard_map/ppermute | solution.py:72
  51.9 5.5 %collective-permute-start.6 = (f32[6,32,128]{2,1,0:T(8,128)S(1)}, f32[6,32,128]{2,1,0:T(8,128)S(1)}, u32[]{:S(2)}, u32[]{:S(2)}) collective-permute-start(f32[6,32,128]{2,1,0:T(8,128)S(1)} %pad_maximum_fusion.2), channel_id=1, source_target_pairs={{16,0},{32,16},{48,32},{64,48},{80,64},{96,80},{112,96},{128,112},... | collective-permute-start | bytes 294920 | tf_op jit(solution)/shard_map/ppermute | solution.py:73
  57.4 2.5 %collective-permute-start.7 = (f32[6,32,128]{2,1,0:T(8,128)S(1)}, f32[6,32,128]{2,1,0:T(8,128)S(1)}, u32[]{:S(2)}, u32[]{:S(2)}) collective-permute-start(f32[6,32,128]{2,1,0:T(8,128)S(1)} %pad_maximum_fusion.2), channel_id=1, source_target_pairs={{32,0},{48,16},{64,32},{80,48},{96,64},{112,80},{128,96},{144,112}... | collective-permute-start | bytes 294920 | tf_op jit(solution)/shard_map/ppermute | solution.py:73
  59.9 8.6 %fusion.3 = f32[4,160,32,128]{3,1,2,0:T(8,128)S(1)} fusion(f32[4,64,32,128]{3,2,1,0:T(8,128)} %get-tuple-element.13, f32[160,64]{1,0:T(8,128)S(1)} %gather_fusion), kind=kOutput, calls=%fused_computation.7 | convolution fusion | flops 1006632960 | bytes 14721024 | tf_op jit(solution)/shard_map/kl,flxy->fkxy/dot_general | solution.py:39
  68.6 0.8 fusion.9
  69.7 3.3 %collective-permute-start.9 = (f32[6,160,64]{2,1,0:T(8,128)S(1)}, f32[6,160,64]{2,1,0:T(8,128)S(1)}, u32[]{:S(2)}, u32[]{:S(2)}) collective-permute-start(f32[6,160,64]{2,1,0:T(8,128)S(1)} %get-tuple-element.29), channel_id=1, source_target_pairs={{1,0},{2,1},{3,2},{4,3},{5,4},{6,5},{7,6},{8,7},{9,8},{10,9},{11,1... | collective-permute-start | bytes 737288 | tf_op jit(solution)/shard_map/ppermute | solution.py:73
  73.0 3.8 %collective-permute-start.8 = (f32[6,160,64]{2,1,0:T(8,128)S(1)}, f32[6,160,64]{2,1,0:T(8,128)S(1)}, u32[]{:S(2)}, u32[]{:S(2)}) collective-permute-start(f32[6,160,64]{2,1,0:T(8,128)S(1)} %get-tuple-element.28), channel_id=1, source_target_pairs={{0,1},{1,2},{2,3},{3,4},{4,5},{5,6},{6,7},{7,8},{8,9},{9,10},{10,1... | collective-permute-start | bytes 737288 | tf_op jit(solution)/shard_map/ppermute | solution.py:72
  76.8 4.7 %fusion = f32[4,64,32,128]{3,1,2,0:T(8,128)S(1)} fusion(f32[4,16,32,128]{3,1,2,0:T(8,128)S(1)} %get-tuple-element.23, f32[4,16,32,128]{3,1,2,0:T(8,128)S(1)} %get-tuple-element.22, f32[4,16,32,128]{3,1,2,0:T(8,128)S(1)} %get-tuple-element.21, f32[4,16,32,128]{3,1,2,0:T(8,128)S(1)} %get-tuple-element.20, f32[4,64,32,128]{3,2,1,0:T(8,128)S(1)} %copy-done.1, ...), kind=kLoop, calls=%fused_computation.2 | loop fusion | flops 6291456 | bytes 14680064 | tf_op jit(solution)/shard_map/add | solution.py:50
  81.6 2.0 %copy-done.2 = f32[4,64,32,128]{3,1,2,0:T(8,128)} copy-done((f32[4,64,32,128]{3,1,2,0:T(8,128)}, f32[4,64,32,128]{3,1,2,0:T(8,128)S(1)}, u32[]{:S(2)}) %copy-start.2) | copy-done | bytes 4194328
  84.5 1.0 fusion.16
  85.6 11.4 %shard_map.87 = (f32[32,128]{1,0:T(8,128)}, f32[2,32,128]{2,1,0:T(8,128)}) custom-call(f32[3,160,256]{2,1,0:T(8,128)} %get-tuple-element.27.moving_ref, f32[3,160,256]{2,1,0:T(8,128)} %get-tuple-element.26.fixed_ref, f32[1,256]{1,0:T(1,128)} %multiply_add_fusion.1.coriolis_ref), custom_call_target="tpu_custom_call" | custom-call | flops 39321600 | bytes 1146880 | tf_op jit(solution)/shard_map/pallas_call | solution.py:306
  97.0 0.8 divide_subtract_fusion
  97.7 2.9 %fusion.15 = (f32[2,64,32,128]{3,1,2,0:T(8,128)S(1)}, f32[2,64,32,128]{3,1,2,0:T(8,128)S(1)}) fusion(f32[4,64,32,128]{3,1,2,0:T(8,128)} %copy-done.2, f32[2,32,128]{2,1,0:T(8,128)S(1)} %divide_subtract_fusion, f32[64,32,128]{2,0,1:T(8,128)S(1)} %fusion.12), kind=kLoop, calls=%fused_computation.56 | loop fusion | flops 1048576 | bytes 9469952 | tf_op jit(solution)/shard_map/slice | solution.py:59
  101.2 4.4 %copy.12 = f32[4,64,32,128]{3,2,1,0:T(8,128)} copy(f32[4,64,32,128]{3,1,2,0:T(8,128)S(1)} %pad_maximum_fusion) | data formatting | bytes 8388608
  (49 shorter events, 5.2 us)
Async XLA Ops:
  0.6 21.2 %copy-start = (f32[4,64,64]{2,1,0:T(8,128)S(1)}, f32[4,64,64]{2,1,0:T(8,128)}, u32[]{:S(2)}) copy-start(f32[4,64,64]{2,1,0:T(8,128)} %param.8) | copy-start | bytes 196612
  0.6 20.1 %copy-start.9 = (s32[160]{0:T(256)S(1)}, s32[160]{0:T(256)}, u32[]{:S(2)}) copy-start(s32[160]{0:T(256)} %constant.93) | copy-start | bytes 1924
  0.7 19.7 %copy-start.3 = (s32[32,128]{1,0:T(8,128)S(1)}, s32[32,128]{1,0:T(8,128)}, u32[]{:S(2)}) copy-start(s32[32,128]{1,0:T(8,128)} %depth_ref.3) | copy-start | bytes 49156
  0.7 20.7 %copy-start.7 = (f32[2,32,128]{2,1,0:T(8,128)S(1)}, f32[2,32,128]{2,1,0:T(8,128)}, u32[]{:S(2)}) copy-start(f32[2,32,128]{2,1,0:T(8,128)} %param.10) | copy-start | bytes 98308
  0.7 20.7 %copy-start.8 = (f32[32,128]{1,0:T(8,128)S(1)}, f32[32,128]{1,0:T(8,128)}, u32[]{:S(2)}) copy-start(f32[32,128]{1,0:T(8,128)} %param.9) | copy-start | bytes 49156
  5.7 16.8 %collective-permute-start.2 = (f32[4,2,32,128]{3,2,1,0:T(8,128)}, f32[4,2,32,128]{3,2,1,0:T(8,128)S(1)}, u32[]{:S(2)}, u32[]{:S(2)}) collective-permute-start(f32[4,2,32,128]{3,2,1,0:T(8,128)} %get-tuple-element.12), channel_id=1, source_target_pairs={{0,1},{1,2},{2,3},{3,4},{4,5},{5,6},{6,7},{7,8},{8,9},{9,10},{10,1... | collective-permute-start | bytes 393224 | tf_op jit(solution)/shard_map/ppermute | solution.py:335
  11.0 11.5 %collective-permute-start.3 = (f32[4,2,32,128]{3,2,1,0:T(8,128)}, f32[4,2,32,128]{3,2,1,0:T(8,128)S(1)}, u32[]{:S(2)}, u32[]{:S(2)}) collective-permute-start(f32[4,2,32,128]{3,2,1,0:T(8,128)} %get-tuple-element.12), channel_id=1, source_target_pairs={{1,0},{2,1},{3,2},{4,3},{5,4},{6,5},{7,6},{8,7},{9,8},{10,9},{11,1... | collective-permute-start | bytes 393224 | tf_op jit(solution)/shard_map/ppermute | solution.py:336
  13.0 11.7 %collective-permute-start = (f32[4,64,2,128]{3,2,1,0:T(2,128)}, f32[4,64,2,128]{3,2,1,0:T(2,128)S(1)}, u32[]{:S(2)}, u32[]{:S(2)}) collective-permute-start(f32[4,64,2,128]{3,2,1,0:T(2,128)} %get-tuple-element.10), channel_id=1, source_target_pairs={{0,16},{16,32},{32,48},{48,64},{64,80},{80,96},{96,112},{112,128},... | collective-permute-start | bytes 786440 | tf_op jit(solution)/shard_map/ppermute | solution.py:332
  16.2 10.4 %collective-permute-start.1 = (f32[4,64,2,128]{3,2,1,0:T(2,128)}, f32[4,64,2,128]{3,2,1,0:T(2,128)S(1)}, u32[]{:S(2)}, u32[]{:S(2)}) collective-permute-start(f32[4,64,2,128]{3,2,1,0:T(2,128)} %get-tuple-element.11), channel_id=1, source_target_pairs={{16,0},{32,16},{48,32},{64,48},{80,64},{96,80},{112,96},{128,112},... | collective-permute-start | bytes 786440 | tf_op jit(solution)/shard_map/ppermute | solution.py:333
  24.7 1.9 %copy-start.4 = (f32[4,64,2,128]{3,2,1,0:T(2,128)}, f32[4,64,2,128]{3,2,1,0:T(2,128)S(1)}, u32[]{:S(2)}) copy-start(f32[4,64,2,128]{3,2,1,0:T(2,128)S(1)} %collective-permute-done.west_ref) | copy-start | bytes 786436
  26.5 0.7 copy-start.5
  45.9 23.4 %collective-permute-start.4 = (f32[6,32,128]{2,1,0:T(8,128)S(1)}, f32[6,32,128]{2,1,0:T(8,128)S(1)}, u32[]{:S(2)}, u32[]{:S(2)}) collective-permute-start(f32[6,32,128]{2,1,0:T(8,128)S(1)} %pad_maximum_fusion.2), channel_id=1, source_target_pairs={{0,32},{16,48},{32,64},{48,80},{64,96},{80,112},{96,128},{112,144}... | collective-permute-start | bytes 294920 | tf_op jit(solution)/shard_map/ppermute | solution.py:72
  50.0 19.4 %collective-permute-start.5 = (f32[6,32,128]{2,1,0:T(8,128)S(1)}, f32[6,32,128]{2,1,0:T(8,128)S(1)}, u32[]{:S(2)}, u32[]{:S(2)}) collective-permute-start(f32[6,32,128]{2,1,0:T(8,128)S(1)} %pad_maximum_fusion.2), channel_id=1, source_target_pairs={{0,16},{16,32},{32,48},{48,64},{64,80},{80,96},{96,112},{112,128},... | collective-permute-start | bytes 294920 | tf_op jit(solution)/shard_map/ppermute | solution.py:72
  51.9 17.5 %collective-permute-start.6 = (f32[6,32,128]{2,1,0:T(8,128)S(1)}, f32[6,32,128]{2,1,0:T(8,128)S(1)}, u32[]{:S(2)}, u32[]{:S(2)}) collective-permute-start(f32[6,32,128]{2,1,0:T(8,128)S(1)} %pad_maximum_fusion.2), channel_id=1, source_target_pairs={{16,0},{32,16},{48,32},{64,48},{80,64},{96,80},{112,96},{128,112},... | collective-permute-start | bytes 294920 | tf_op jit(solution)/shard_map/ppermute | solution.py:73
  57.4 12.1 %collective-permute-start.7 = (f32[6,32,128]{2,1,0:T(8,128)S(1)}, f32[6,32,128]{2,1,0:T(8,128)S(1)}, u32[]{:S(2)}, u32[]{:S(2)}) collective-permute-start(f32[6,32,128]{2,1,0:T(8,128)S(1)} %pad_maximum_fusion.2), channel_id=1, source_target_pairs={{32,0},{48,16},{64,32},{80,48},{96,64},{112,80},{128,96},{144,112}... | collective-permute-start | bytes 294920 | tf_op jit(solution)/shard_map/ppermute | solution.py:73
  68.6 0.9 copy-start.6
  68.6 8.2 %copy-start.1 = (f32[4,64,32,128]{3,2,1,0:T(8,128)S(1)}, f32[4,64,32,128]{3,2,1,0:T(8,128)}, u32[]{:S(2)}) copy-start(f32[4,64,32,128]{3,2,1,0:T(8,128)} %state_ref.3) | copy-start | bytes 12582916
  69.7 14.4 %collective-permute-start.9 = (f32[6,160,64]{2,1,0:T(8,128)S(1)}, f32[6,160,64]{2,1,0:T(8,128)S(1)}, u32[]{:S(2)}, u32[]{:S(2)}) collective-permute-start(f32[6,160,64]{2,1,0:T(8,128)S(1)} %get-tuple-element.29), channel_id=1, source_target_pairs={{1,0},{2,1},{3,2},{4,3},{5,4},{6,5},{7,6},{8,7},{9,8},{10,9},{11,1... | collective-permute-start | bytes 737288 | tf_op jit(solution)/shard_map/ppermute | solution.py:73
  73.0 11.1 %collective-permute-start.8 = (f32[6,160,64]{2,1,0:T(8,128)S(1)}, f32[6,160,64]{2,1,0:T(8,128)S(1)}, u32[]{:S(2)}, u32[]{:S(2)}) collective-permute-start(f32[6,160,64]{2,1,0:T(8,128)S(1)} %get-tuple-element.28), channel_id=1, source_target_pairs={{0,1},{1,2},{2,3},{3,4},{4,5},{5,6},{6,7},{7,8},{8,9},{9,10},{10,1... | collective-permute-start | bytes 737288 | tf_op jit(solution)/shard_map/ppermute | solution.py:72
  81.6 2.0 %copy-start.2 = (f32[4,64,32,128]{3,1,2,0:T(8,128)}, f32[4,64,32,128]{3,1,2,0:T(8,128)S(1)}, u32[]{:S(2)}) copy-start(f32[4,64,32,128]{3,1,2,0:T(8,128)S(1)} %fusion) | copy-start | bytes 12582916

commit v13 on v12

--- a/solution.py
+++ b/solution.py
@@ -157,7 +157,7 @@
     def _():
         forcing_ref[...] = jnp.zeros_like(forcing_ref)
 
-    lax.fori_loop(0, depth_levels, level, 0)
+    lax.fori_loop(0, depth_levels, level, 0, unroll=4)
 
     @pl.when(chunk == pl.num_programs(0) - 1)
     def _():

time: 106 us -> 105 us (level)
  Pallas kernels: 34.4 us -> 32.9 us
    pallas_call x1, Pallas kernels: 17.9 us -> 16.5 us  [stencil(): pl.pallas_call(stencil_kernel, grid=(steps,), out_shape=(jax.ShapeDtypeSt...]
  transfers between devices with their start and end apart: 10 -> 10, of which waited for: 2 -> 2; matrix products, arithmetic and copies ran while one was open for 16% -> 17% of each run, Pallas kernels for 0% -> 0%
where the time goes in v13:
time: 105 us; the launch traced here: 104 us
  starting transfers between devices  35.6 us (34%)
  Pallas kernels  32.9 us (31%)
  other arithmetic  13.6 us (13%)
  local copies, waits for them, and re-layouts  9.14 us (9%)
  matrix products  8.65 us (8%)
  waiting for transfers between devices  3.32 us (3%)
    pallas_call x1, Pallas kernels, stencil(): pl.pallas_call(stencil_kernel, grid=(steps,), out_shape=(jax.ShapeDtypeSt...  16.5 us
    pallas_call x1, Pallas kernels, local_waves(): pl.pallas_call(wave_kernel, out_shape=(jax.ShapeDtypeStruct((inner_rows,...  11.4 us
    ppermute x3, starting transfers between devices, wide_halo(): lax.ppermute(head, axis, [(i + hop, i) for i in range(count - hop)])  11.2 us
    ppermute x3, starting transfers between devices, wide_halo(): lax.ppermute(tail, axis, [(i, i + hop) for i in range(count - hop)])  9.81 us
    dot_general x1, matrix products, vertical_solve(): jnp.einsum('kl,flxy->fkxy', stacked, provisional, precision=lax.Precision...  8.65 us
    unnamed x24, local copies, waits for them, and re-layouts  7.22 us
    ppermute x1, starting transfers between devices, body(): lax.ppermute(edges, ('gy', 'mode'), [(i, i + 1) for i in range(y_count -...  5.3 us
    pallas_call x1, Pallas kernels, pack_edges(): pl.pallas_call(pack_kernel, grid=(levels // PACK,), out_shape=(jax.ShapeD...  5.04 us
  transfers between devices with their start and end apart: 10, of which 2 were waited for; matrix products, arithmetic and copies ran while one was open for 17% of the time, Pallas kernels for 0%

profile of v13, /device:TPU:103, one launch (start us, length us, event | category | flops | bytes accessed | tf_op | source)
XLA Modules:
  0.0 104.3 jit_solution(14414122891911208748)
XLA Ops:
  0.7 5.0 %shard_map.85 = (f32[4,2,32,128]{3,2,1,0:T(8,128)}, f32[4,64,2,128]{3,2,1,0:T(2,128)}, f32[4,64,2,128]{3,2,1,0:T(2,128)}) custom-call(s32[32,128]{1,0:T(8,128)} %depth_ref.3, f32[4,64,32,128]{3,2,1,0:T(8,128)} %state_ref.3), custom_call_target="tpu_custom_call" | custom-call | flops 4194304 | bytes 4194304 | tf_op jit(solution)/shard_map/pallas_call | solution.py:215
  5.7 5.3 %collective-permute-start.2 = (f32[4,2,32,128]{3,2,1,0:T(8,128)}, f32[4,2,32,128]{3,2,1,0:T(8,128)S(1)}, u32[]{:S(2)}, u32[]{:S(2)}) collective-permute-start(f32[4,2,32,128]{3,2,1,0:T(8,128)} %get-tuple-element.12), channel_id=1, source_target_pairs={{0,1},{1,2},{2,3},{3,4},{4,5},{5,6},{6,7},{7,8},{8,9},{9,10},{10,1... | collective-permute-start | bytes 393224 | tf_op jit(solution)/shard_map/ppermute | solution.py:335
  11.0 1.9 %collective-permute-start.3 = (f32[4,2,32,128]{3,2,1,0:T(8,128)}, f32[4,2,32,128]{3,2,1,0:T(8,128)S(1)}, u32[]{:S(2)}, u32[]{:S(2)}) collective-permute-start(f32[4,2,32,128]{3,2,1,0:T(8,128)} %get-tuple-element.12), channel_id=1, source_target_pairs={{1,0},{2,1},{3,2},{4,3},{5,4},{6,5},{7,6},{8,7},{9,8},{10,9},{11,1... | collective-permute-start | bytes 393224 | tf_op jit(solution)/shard_map/ppermute | solution.py:336
  13.0 3.2 %collective-permute-start = (f32[4,64,2,128]{3,2,1,0:T(2,128)}, f32[4,64,2,128]{3,2,1,0:T(2,128)S(1)}, u32[]{:S(2)}, u32[]{:S(2)}) collective-permute-start(f32[4,64,2,128]{3,2,1,0:T(2,128)} %get-tuple-element.10), channel_id=1, source_target_pairs={{0,16},{16,32},{32,48},{48,64},{64,80},{80,96},{96,112},{112,128},... | collective-permute-start | bytes 786440 | tf_op jit(solution)/shard_map/ppermute | solution.py:332
  16.2 4.2 %collective-permute-start.1 = (f32[4,64,2,128]{3,2,1,0:T(2,128)}, f32[4,64,2,128]{3,2,1,0:T(2,128)S(1)}, u32[]{:S(2)}, u32[]{:S(2)}) collective-permute-start(f32[4,64,2,128]{3,2,1,0:T(2,128)} %get-tuple-element.11), channel_id=1, source_target_pairs={{16,0},{32,16},{48,32},{64,48},{80,64},{96,80},{112,96},{128,112},... | collective-permute-start | bytes 786440 | tf_op jit(solution)/shard_map/ppermute | solution.py:333
  23.2 1.4 %collective-permute-done.west_ref = f32[4,64,2,128]{3,2,1,0:T(2,128)S(1)} collective-permute-done((f32[4,64,2,128]{3,2,1,0:T(2,128)}, f32[4,64,2,128]{3,2,1,0:T(2,128)S(1)}, u32[]{:S(2)}, u32[]{:S(2)}) %collective-permute-start) | collective-permute-done | bytes 262176 | tf_op jit(solution)/shard_map/ppermute | solution.py:332
  24.7 1.9 %collective-permute-done.1.east_ref = f32[4,64,2,128]{3,2,1,0:T(2,128)S(1)} collective-permute-done((f32[4,64,2,128]{3,2,1,0:T(2,128)}, f32[4,64,2,128]{3,2,1,0:T(2,128)S(1)}, u32[]{:S(2)}, u32[]{:S(2)}) %collective-permute-start.1) | collective-permute-done | bytes 262176 | tf_op jit(solution)/shard_map/ppermute | solution.py:333
  27.2 16.5 %shard_map.86 = (f32[4,64,32,128]{3,2,1,0:T(8,128)}, f32[2,32,128]{2,1,0:T(8,128)}) custom-call(s32[32,128]{1,0:T(8,128)} %depth_ref.3, f32[1,128]{1,0:T(1,128)} %multiply_add_fusion.2.coriolis_ref, f32[4,64,32,128]{3,2,1,0:T(8,128)} %state_ref.3, f32[4,64,2,128]{3,2,1,0:T(2,128)} %copy-done.4, f32[4,64,2,128]{3,2,1,0:T(2,128)} %copy-done.5, ...), custom_call_target="tpu_custom_call" | custom-call | flops 62914560 | bytes 8388608 | tf_op jit(solution)/shard_map/pallas_call | solution.py:174
  43.7 0.8 pad_maximum_fusion.2
  44.5 4.1 %collective-permute-start.4 = (f32[6,32,128]{2,1,0:T(8,128)S(1)}, f32[6,32,128]{2,1,0:T(8,128)S(1)}, u32[]{:S(2)}, u32[]{:S(2)}) collective-permute-start(f32[6,32,128]{2,1,0:T(8,128)S(1)} %pad_maximum_fusion.2), channel_id=1, source_target_pairs={{0,32},{16,48},{32,64},{48,80},{64,96},{80,112},{96,128},{112,144}... | collective-permute-start | bytes 294920 | tf_op jit(solution)/shard_map/ppermute | solution.py:72
  48.6 1.9 %collective-permute-start.5 = (f32[6,32,128]{2,1,0:T(8,128)S(1)}, f32[6,32,128]{2,1,0:T(8,128)S(1)}, u32[]{:S(2)}, u32[]{:S(2)}) collective-permute-start(f32[6,32,128]{2,1,0:T(8,128)S(1)} %pad_maximum_fusion.2), channel_id=1, source_target_pairs={{0,16},{16,32},{32,48},{48,64},{64,80},{80,96},{96,112},{112,128},... | collective-permute-start | bytes 294920 | tf_op jit(solution)/shard_map/ppermute | solution.py:72
  50.5 5.5 %collective-permute-start.6 = (f32[6,32,128]{2,1,0:T(8,128)S(1)}, f32[6,32,128]{2,1,0:T(8,128)S(1)}, u32[]{:S(2)}, u32[]{:S(2)}) collective-permute-start(f32[6,32,128]{2,1,0:T(8,128)S(1)} %pad_maximum_fusion.2), channel_id=1, source_target_pairs={{16,0},{32,16},{48,32},{64,48},{80,64},{96,80},{112,96},{128,112},... | collective-permute-start | bytes 294920 | tf_op jit(solution)/shard_map/ppermute | solution.py:73
  56.0 2.5 %collective-permute-start.7 = (f32[6,32,128]{2,1,0:T(8,128)S(1)}, f32[6,32,128]{2,1,0:T(8,128)S(1)}, u32[]{:S(2)}, u32[]{:S(2)}) collective-permute-start(f32[6,32,128]{2,1,0:T(8,128)S(1)} %pad_maximum_fusion.2), channel_id=1, source_target_pairs={{32,0},{48,16},{64,32},{80,48},{96,64},{112,80},{128,96},{144,112}... | collective-permute-start | bytes 294920 | tf_op jit(solution)/shard_map/ppermute | solution.py:73
  58.5 8.6 %fusion.3 = f32[4,160,32,128]{3,1,2,0:T(8,128)S(1)} fusion(f32[4,64,32,128]{3,2,1,0:T(8,128)} %get-tuple-element.13, f32[160,64]{1,0:T(8,128)S(1)} %gather_fusion), kind=kOutput, calls=%fused_computation.7 | convolution fusion | flops 1006632960 | bytes 14721024 | tf_op jit(solution)/shard_map/kl,flxy->fkxy/dot_general | solution.py:39
  67.2 0.8 fusion.9
  68.3 3.3 %collective-permute-start.9 = (f32[6,160,64]{2,1,0:T(8,128)S(1)}, f32[6,160,64]{2,1,0:T(8,128)S(1)}, u32[]{:S(2)}, u32[]{:S(2)}) collective-permute-start(f32[6,160,64]{2,1,0:T(8,128)S(1)} %get-tuple-element.29), channel_id=1, source_target_pairs={{1,0},{2,1},{3,2},{4,3},{5,4},{6,5},{7,6},{8,7},{9,8},{10,9},{11,1... | collective-permute-start | bytes 737288 | tf_op jit(solution)/shard_map/ppermute | solution.py:73
  71.6 3.8 %collective-permute-start.8 = (f32[6,160,64]{2,1,0:T(8,128)S(1)}, f32[6,160,64]{2,1,0:T(8,128)S(1)}, u32[]{:S(2)}, u32[]{:S(2)}) collective-permute-start(f32[6,160,64]{2,1,0:T(8,128)S(1)} %get-tuple-element.28), channel_id=1, source_target_pairs={{0,1},{1,2},{2,3},{3,4},{4,5},{5,6},{6,7},{7,8},{8,9},{9,10},{10,1... | collective-permute-start | bytes 737288 | tf_op jit(solution)/shard_map/ppermute | solution.py:72
  75.4 4.7 %fusion = f32[4,64,32,128]{3,1,2,0:T(8,128)S(1)} fusion(f32[4,16,32,128]{3,1,2,0:T(8,128)S(1)} %get-tuple-element.23, f32[4,16,32,128]{3,1,2,0:T(8,128)S(1)} %get-tuple-element.22, f32[4,16,32,128]{3,1,2,0:T(8,128)S(1)} %get-tuple-element.21, f32[4,16,32,128]{3,1,2,0:T(8,128)S(1)} %get-tuple-element.20, f32[4,64,32,128]{3,2,1,0:T(8,128)S(1)} %copy-done.1, ...), kind=kLoop, calls=%fused_computation.2 | loop fusion | flops 6291456 | bytes 14680064 | tf_op jit(solution)/shard_map/add | solution.py:50
  80.2 2.0 %copy-done.2 = f32[4,64,32,128]{3,1,2,0:T(8,128)} copy-done((f32[4,64,32,128]{3,1,2,0:T(8,128)}, f32[4,64,32,128]{3,1,2,0:T(8,128)S(1)}, u32[]{:S(2)}) %copy-start.2) | copy-done | bytes 4194328
  83.1 1.0 fusion.16
  84.2 11.4 %shard_map.87 = (f32[32,128]{1,0:T(8,128)}, f32[2,32,128]{2,1,0:T(8,128)}) custom-call(f32[3,160,256]{2,1,0:T(8,128)} %get-tuple-element.27.moving_ref, f32[3,160,256]{2,1,0:T(8,128)} %get-tuple-element.26.fixed_ref, f32[1,256]{1,0:T(1,128)} %multiply_add_fusion.1.coriolis_ref), custom_call_target="tpu_custom_call" | custom-call | flops 39321600 | bytes 1146880 | tf_op jit(solution)/shard_map/pallas_call | solution.py:306
  95.5 0.8 divide_subtract_fusion
  96.3 2.9 %fusion.15 = (f32[2,64,32,128]{3,1,2,0:T(8,128)S(1)}, f32[2,64,32,128]{3,1,2,0:T(8,128)S(1)}) fusion(f32[4,64,32,128]{3,1,2,0:T(8,128)} %copy-done.2, f32[2,32,128]{2,1,0:T(8,128)S(1)} %divide_subtract_fusion, f32[64,32,128]{2,0,1:T(8,128)S(1)} %fusion.12), kind=kLoop, calls=%fused_computation.56 | loop fusion | flops 1048576 | bytes 9469952 | tf_op jit(solution)/shard_map/slice | solution.py:59
  99.8 4.4 %copy.12 = f32[4,64,32,128]{3,2,1,0:T(8,128)} copy(f32[4,64,32,128]{3,1,2,0:T(8,128)S(1)} %pad_maximum_fusion) | data formatting | bytes 8388608
  (49 shorter events, 5.2 us)
Async XLA Ops:
  0.6 21.2 %copy-start = (f32[4,64,64]{2,1,0:T(8,128)S(1)}, f32[4,64,64]{2,1,0:T(8,128)}, u32[]{:S(2)}) copy-start(f32[4,64,64]{2,1,0:T(8,128)} %param.8) | copy-start | bytes 196612
  0.6 20.1 %copy-start.9 = (s32[160]{0:T(256)S(1)}, s32[160]{0:T(256)}, u32[]{:S(2)}) copy-start(s32[160]{0:T(256)} %constant.93) | copy-start | bytes 1924
  0.7 19.7 %copy-start.3 = (s32[32,128]{1,0:T(8,128)S(1)}, s32[32,128]{1,0:T(8,128)}, u32[]{:S(2)}) copy-start(s32[32,128]{1,0:T(8,128)} %depth_ref.3) | copy-start | bytes 49156
  0.7 20.7 %copy-start.7 = (f32[2,32,128]{2,1,0:T(8,128)S(1)}, f32[2,32,128]{2,1,0:T(8,128)}, u32[]{:S(2)}) copy-start(f32[2,32,128]{2,1,0:T(8,128)} %param.10) | copy-start | bytes 98308
  0.7 20.7 %copy-start.8 = (f32[32,128]{1,0:T(8,128)S(1)}, f32[32,128]{1,0:T(8,128)}, u32[]{:S(2)}) copy-start(f32[32,128]{1,0:T(8,128)} %param.9) | copy-start | bytes 49156
  5.7 16.8 %collective-permute-start.2 = (f32[4,2,32,128]{3,2,1,0:T(8,128)}, f32[4,2,32,128]{3,2,1,0:T(8,128)S(1)}, u32[]{:S(2)}, u32[]{:S(2)}) collective-permute-start(f32[4,2,32,128]{3,2,1,0:T(8,128)} %get-tuple-element.12), channel_id=1, source_target_pairs={{0,1},{1,2},{2,3},{3,4},{4,5},{5,6},{6,7},{7,8},{8,9},{9,10},{10,1... | collective-permute-start | bytes 393224 | tf_op jit(solution)/shard_map/ppermute | solution.py:335
  11.0 11.5 %collective-permute-start.3 = (f32[4,2,32,128]{3,2,1,0:T(8,128)}, f32[4,2,32,128]{3,2,1,0:T(8,128)S(1)}, u32[]{:S(2)}, u32[]{:S(2)}) collective-permute-start(f32[4,2,32,128]{3,2,1,0:T(8,128)} %get-tuple-element.12), channel_id=1, source_target_pairs={{1,0},{2,1},{3,2},{4,3},{5,4},{6,5},{7,6},{8,7},{9,8},{10,9},{11,1... | collective-permute-start | bytes 393224 | tf_op jit(solution)/shard_map/ppermute | solution.py:336
  13.0 11.7 %collective-permute-start = (f32[4,64,2,128]{3,2,1,0:T(2,128)}, f32[4,64,2,128]{3,2,1,0:T(2,128)S(1)}, u32[]{:S(2)}, u32[]{:S(2)}) collective-permute-start(f32[4,64,2,128]{3,2,1,0:T(2,128)} %get-tuple-element.10), channel_id=1, source_target_pairs={{0,16},{16,32},{32,48},{48,64},{64,80},{80,96},{96,112},{112,128},... | collective-permute-start | bytes 786440 | tf_op jit(solution)/shard_map/ppermute | solution.py:332
  16.2 10.4 %collective-permute-start.1 = (f32[4,64,2,128]{3,2,1,0:T(2,128)}, f32[4,64,2,128]{3,2,1,0:T(2,128)S(1)}, u32[]{:S(2)}, u32[]{:S(2)}) collective-permute-start(f32[4,64,2,128]{3,2,1,0:T(2,128)} %get-tuple-element.11), channel_id=1, source_target_pairs={{16,0},{32,16},{48,32},{64,48},{80,64},{96,80},{112,96},{128,112},... | collective-permute-start | bytes 786440 | tf_op jit(solution)/shard_map/ppermute | solution.py:333
  24.7 1.9 %copy-start.4 = (f32[4,64,2,128]{3,2,1,0:T(2,128)}, f32[4,64,2,128]{3,2,1,0:T(2,128)S(1)}, u32[]{:S(2)}) copy-start(f32[4,64,2,128]{3,2,1,0:T(2,128)S(1)} %collective-permute-done.west_ref) | copy-start | bytes 786436
  26.5 0.7 copy-start.5
  44.5 23.5 %collective-permute-start.4 = (f32[6,32,128]{2,1,0:T(8,128)S(1)}, f32[6,32,128]{2,1,0:T(8,128)S(1)}, u32[]{:S(2)}, u32[]{:S(2)}) collective-permute-start(f32[6,32,128]{2,1,0:T(8,128)S(1)} %pad_maximum_fusion.2), channel_id=1, source_target_pairs={{0,32},{16,48},{32,64},{48,80},{64,96},{80,112},{96,128},{112,144}... | collective-permute-start | bytes 294920 | tf_op jit(solution)/shard_map/ppermute | solution.py:72
  48.6 19.4 %collective-permute-start.5 = (f32[6,32,128]{2,1,0:T(8,128)S(1)}, f32[6,32,128]{2,1,0:T(8,128)S(1)}, u32[]{:S(2)}, u32[]{:S(2)}) collective-permute-start(f32[6,32,128]{2,1,0:T(8,128)S(1)} %pad_maximum_fusion.2), channel_id=1, source_target_pairs={{0,16},{16,32},{32,48},{48,64},{64,80},{80,96},{96,112},{112,128},... | collective-permute-start | bytes 294920 | tf_op jit(solution)/shard_map/ppermute | solution.py:72
  50.5 17.5 %collective-permute-start.6 = (f32[6,32,128]{2,1,0:T(8,128)S(1)}, f32[6,32,128]{2,1,0:T(8,128)S(1)}, u32[]{:S(2)}, u32[]{:S(2)}) collective-permute-start(f32[6,32,128]{2,1,0:T(8,128)S(1)} %pad_maximum_fusion.2), channel_id=1, source_target_pairs={{16,0},{32,16},{48,32},{64,48},{80,64},{96,80},{112,96},{128,112},... | collective-permute-start | bytes 294920 | tf_op jit(solution)/shard_map/ppermute | solution.py:73
  56.0 12.1 %collective-permute-start.7 = (f32[6,32,128]{2,1,0:T(8,128)S(1)}, f32[6,32,128]{2,1,0:T(8,128)S(1)}, u32[]{:S(2)}, u32[]{:S(2)}) collective-permute-start(f32[6,32,128]{2,1,0:T(8,128)S(1)} %pad_maximum_fusion.2), channel_id=1, source_target_pairs={{32,0},{48,16},{64,32},{80,48},{96,64},{112,80},{128,96},{144,112}... | collective-permute-start | bytes 294920 | tf_op jit(solution)/shard_map/ppermute | solution.py:73
  67.1 0.9 copy-start.6
  67.2 8.2 %copy-start.1 = (f32[4,64,32,128]{3,2,1,0:T(8,128)S(1)}, f32[4,64,32,128]{3,2,1,0:T(8,128)}, u32[]{:S(2)}) copy-start(f32[4,64,32,128]{3,2,1,0:T(8,128)} %state_ref.3) | copy-start | bytes 12582916
  68.3 14.4 %collective-permute-start.9 = (f32[6,160,64]{2,1,0:T(8,128)S(1)}, f32[6,160,64]{2,1,0:T(8,128)S(1)}, u32[]{:S(2)}, u32[]{:S(2)}) collective-permute-start(f32[6,160,64]{2,1,0:T(8,128)S(1)} %get-tuple-element.29), channel_id=1, source_target_pairs={{1,0},{2,1},{3,2},{4,3},{5,4},{6,5},{7,6},{8,7},{9,8},{10,9},{11,1... | collective-permute-start | bytes 737288 | tf_op jit(solution)/shard_map/ppermute | solution.py:73
  71.6 11.1 %collective-permute-start.8 = (f32[6,160,64]{2,1,0:T(8,128)S(1)}, f32[6,160,64]{2,1,0:T(8,128)S(1)}, u32[]{:S(2)}, u32[]{:S(2)}) collective-permute-start(f32[6,160,64]{2,1,0:T(8,128)S(1)} %get-tuple-element.28), channel_id=1, source_target_pairs={{0,1},{1,2},{2,3},{3,4},{4,5},{5,6},{6,7},{7,8},{8,9},{9,10},{10,1... | collective-permute-start | bytes 737288 | tf_op jit(solution)/shard_map/ppermute | solution.py:72
  80.2 2.0 %copy-start.2 = (f32[4,64,32,128]{3,1,2,0:T(8,128)}, f32[4,64,32,128]{3,1,2,0:T(8,128)S(1)}, u32[]{:S(2)}) copy-start(f32[4,64,32,128]{3,1,2,0:T(8,128)S(1)} %fusion) | copy-start | bytes 12582916

commit v14 on v13

--- a/solution.py
+++ b/solution.py
@@ -290,7 +290,7 @@
             work_ref[2, low:high] = north_new
             return carry
 
-        lax.fori_loop(0, per_group, step, 0)
+        lax.fori_loop(0, per_group, step, 0, unroll=True)
     for field in range(3):
         middle = work_ref[field, rim : rim + inner_rows]
         inner = pltpu.roll(middle, cols - rim, 1)[:, :inner_cols]

time: 105 us -> 103 us (0.981)
  Pallas kernels: 32.9 us -> 31 us
    pallas_call x1, Pallas kernels: 11.4 us -> 9.52 us  [local_waves(): pl.pallas_call(wave_kernel, out_shape=(jax.ShapeDtypeStruct((inner_rows,...]
where the time goes in v14:
time: 103 us; the launch traced here: 102 us
  starting transfers between devices  35.5 us (34%)
  Pallas kernels  31 us (30%)
  other arithmetic  13.7 us (13%)
  local copies, waits for them, and re-layouts  9.14 us (9%)
  matrix products  8.65 us (8%)
  waiting for transfers between devices  3.32 us (3%)
  between operations  1.04 us (1%)
    pallas_call x1, Pallas kernels, stencil(): pl.pallas_call(stencil_kernel, grid=(steps,), out_shape=(jax.ShapeDtypeSt...  16.5 us
    ppermute x3, starting transfers between devices, wide_halo(): lax.ppermute(head, axis, [(i + hop, i) for i in range(count - hop)])  11.2 us
    ppermute x3, starting transfers between devices, wide_halo(): lax.ppermute(tail, axis, [(i, i + hop) for i in range(count - hop)])  9.63 us
    pallas_call x1, Pallas kernels, local_waves(): pl.pallas_call(wave_kernel, out_shape=(jax.ShapeDtypeStruct((inner_rows,...  9.52 us
    dot_general x1, matrix products, vertical_solve(): jnp.einsum('kl,flxy->fkxy', stacked, provisional, precision=lax.Precision...  8.65 us
    unnamed x24, local copies, waits for them, and re-layouts  7.22 us
    ppermute x1, starting transfers between devices, body(): lax.ppermute(edges, ('gy', 'mode'), [(i, i + 1) for i in range(y_count -...  5.3 us
    add x1, other arithmetic, vertical_solve(): return active * solved + (1.0 - active) * state  4.93 us
  transfers between devices with their start and end apart: 10, of which 2 were waited for; matrix products, arithmetic and copies ran while one was open for 17% of the time, Pallas kernels for 0%

profile of v14, /device:TPU:103, one launch (start us, length us, event | category | flops | bytes accessed | tf_op | source)
XLA Modules:
  0.0 102.3 jit_solution(1972860726712449657)
XLA Ops:
  0.7 4.9 %shard_map.85 = (f32[4,2,32,128]{3,2,1,0:T(8,128)}, f32[4,64,2,128]{3,2,1,0:T(2,128)}, f32[4,64,2,128]{3,2,1,0:T(2,128)}) custom-call(s32[32,128]{1,0:T(8,128)} %depth_ref.3, f32[4,64,32,128]{3,2,1,0:T(8,128)} %state_ref.3), custom_call_target="tpu_custom_call" | custom-call | flops 4194304 | bytes 4194304 | tf_op jit(solution)/shard_map/pallas_call | solution.py:215
  5.6 5.3 %collective-permute-start.2 = (f32[4,2,32,128]{3,2,1,0:T(8,128)}, f32[4,2,32,128]{3,2,1,0:T(8,128)S(1)}, u32[]{:S(2)}, u32[]{:S(2)}) collective-permute-start(f32[4,2,32,128]{3,2,1,0:T(8,128)} %get-tuple-element.12), channel_id=1, source_target_pairs={{0,1},{1,2},{2,3},{3,4},{4,5},{5,6},{6,7},{7,8},{8,9},{9,10},{10,1... | collective-permute-start | bytes 393224 | tf_op jit(solution)/shard_map/ppermute | solution.py:335
  10.9 1.9 %collective-permute-start.3 = (f32[4,2,32,128]{3,2,1,0:T(8,128)}, f32[4,2,32,128]{3,2,1,0:T(8,128)S(1)}, u32[]{:S(2)}, u32[]{:S(2)}) collective-permute-start(f32[4,2,32,128]{3,2,1,0:T(8,128)} %get-tuple-element.12), channel_id=1, source_target_pairs={{1,0},{2,1},{3,2},{4,3},{5,4},{6,5},{7,6},{8,7},{9,8},{10,9},{11,1... | collective-permute-start | bytes 393224 | tf_op jit(solution)/shard_map/ppermute | solution.py:336
  12.8 3.2 %collective-permute-start = (f32[4,64,2,128]{3,2,1,0:T(2,128)}, f32[4,64,2,128]{3,2,1,0:T(2,128)S(1)}, u32[]{:S(2)}, u32[]{:S(2)}) collective-permute-start(f32[4,64,2,128]{3,2,1,0:T(2,128)} %get-tuple-element.10), channel_id=1, source_target_pairs={{0,16},{16,32},{32,48},{48,64},{64,80},{80,96},{96,112},{112,128},... | collective-permute-start | bytes 786440 | tf_op jit(solution)/shard_map/ppermute | solution.py:332
  16.1 4.2 %collective-permute-start.1 = (f32[4,64,2,128]{3,2,1,0:T(2,128)}, f32[4,64,2,128]{3,2,1,0:T(2,128)S(1)}, u32[]{:S(2)}, u32[]{:S(2)}) collective-permute-start(f32[4,64,2,128]{3,2,1,0:T(2,128)} %get-tuple-element.11), channel_id=1, source_target_pairs={{16,0},{32,16},{48,32},{64,48},{80,64},{96,80},{112,96},{128,112},... | collective-permute-start | bytes 786440 | tf_op jit(solution)/shard_map/ppermute | solution.py:333
  23.1 1.4 %collective-permute-done.west_ref = f32[4,64,2,128]{3,2,1,0:T(2,128)S(1)} collective-permute-done((f32[4,64,2,128]{3,2,1,0:T(2,128)}, f32[4,64,2,128]{3,2,1,0:T(2,128)S(1)}, u32[]{:S(2)}, u32[]{:S(2)}) %collective-permute-start) | collective-permute-done | bytes 262176 | tf_op jit(solution)/shard_map/ppermute | solution.py:332
  24.6 1.9 %collective-permute-done.1.east_ref = f32[4,64,2,128]{3,2,1,0:T(2,128)S(1)} collective-permute-done((f32[4,64,2,128]{3,2,1,0:T(2,128)}, f32[4,64,2,128]{3,2,1,0:T(2,128)S(1)}, u32[]{:S(2)}, u32[]{:S(2)}) %collective-permute-start.1) | collective-permute-done | bytes 262176 | tf_op jit(solution)/shard_map/ppermute | solution.py:333
  27.1 16.5 %shard_map.86 = (f32[4,64,32,128]{3,2,1,0:T(8,128)}, f32[2,32,128]{2,1,0:T(8,128)}) custom-call(s32[32,128]{1,0:T(8,128)} %depth_ref.3, f32[1,128]{1,0:T(1,128)} %multiply_add_fusion.2.coriolis_ref, f32[4,64,32,128]{3,2,1,0:T(8,128)} %state_ref.3, f32[4,64,2,128]{3,2,1,0:T(2,128)} %copy-done.4, f32[4,64,2,128]{3,2,1,0:T(2,128)} %copy-done.5, ...), custom_call_target="tpu_custom_call" | custom-call | flops 62914560 | bytes 8388608 | tf_op jit(solution)/shard_map/pallas_call | solution.py:174
  43.6 0.8 pad_maximum_fusion.2
  44.4 4.1 %collective-permute-start.4 = (f32[6,32,128]{2,1,0:T(8,128)S(1)}, f32[6,32,128]{2,1,0:T(8,128)S(1)}, u32[]{:S(2)}, u32[]{:S(2)}) collective-permute-start(f32[6,32,128]{2,1,0:T(8,128)S(1)} %pad_maximum_fusion.2), channel_id=1, source_target_pairs={{0,32},{16,48},{32,64},{48,80},{64,96},{80,112},{96,128},{112,144}... | collective-permute-start | bytes 294920 | tf_op jit(solution)/shard_map/ppermute | solution.py:72
  48.5 1.9 %collective-permute-start.5 = (f32[6,32,128]{2,1,0:T(8,128)S(1)}, f32[6,32,128]{2,1,0:T(8,128)S(1)}, u32[]{:S(2)}, u32[]{:S(2)}) collective-permute-start(f32[6,32,128]{2,1,0:T(8,128)S(1)} %pad_maximum_fusion.2), channel_id=1, source_target_pairs={{0,16},{16,32},{32,48},{48,64},{64,80},{80,96},{96,112},{112,128},... | collective-permute-start | bytes 294920 | tf_op jit(solution)/shard_map/ppermute | solution.py:72
  50.4 5.5 %collective-permute-start.6 = (f32[6,32,128]{2,1,0:T(8,128)S(1)}, f32[6,32,128]{2,1,0:T(8,128)S(1)}, u32[]{:S(2)}, u32[]{:S(2)}) collective-permute-start(f32[6,32,128]{2,1,0:T(8,128)S(1)} %pad_maximum_fusion.2), channel_id=1, source_target_pairs={{16,0},{32,16},{48,32},{64,48},{80,64},{96,80},{112,96},{128,112},... | collective-permute-start | bytes 294920 | tf_op jit(solution)/shard_map/ppermute | solution.py:73
  55.9 2.5 %collective-permute-start.7 = (f32[6,32,128]{2,1,0:T(8,128)S(1)}, f32[6,32,128]{2,1,0:T(8,128)S(1)}, u32[]{:S(2)}, u32[]{:S(2)}) collective-permute-start(f32[6,32,128]{2,1,0:T(8,128)S(1)} %pad_maximum_fusion.2), channel_id=1, source_target_pairs={{32,0},{48,16},{64,32},{80,48},{96,64},{112,80},{128,96},{144,112}... | collective-permute-start | bytes 294920 | tf_op jit(solution)/shard_map/ppermute | solution.py:73
  58.4 8.6 %fusion.3 = f32[4,160,32,128]{3,1,2,0:T(8,128)S(1)} fusion(f32[4,64,32,128]{3,2,1,0:T(8,128)} %get-tuple-element.13, f32[160,64]{1,0:T(8,128)S(1)} %gather_fusion), kind=kOutput, calls=%fused_computation.7 | convolution fusion | flops 1006632960 | bytes 14721024 | tf_op jit(solution)/shard_map/kl,flxy->fkxy/dot_general | solution.py:39
  67.0 0.8 fusion.9
  68.2 3.3 %collective-permute-start.9 = (f32[6,160,64]{2,1,0:T(8,128)S(1)}, f32[6,160,64]{2,1,0:T(8,128)S(1)}, u32[]{:S(2)}, u32[]{:S(2)}) collective-permute-start(f32[6,160,64]{2,1,0:T(8,128)S(1)} %get-tuple-element.29), channel_id=1, source_target_pairs={{1,0},{2,1},{3,2},{4,3},{5,4},{6,5},{7,6},{8,7},{9,8},{10,9},{11,1... | collective-permute-start | bytes 737288 | tf_op jit(solution)/shard_map/ppermute | solution.py:73
  71.4 3.6 %collective-permute-start.8 = (f32[6,160,64]{2,1,0:T(8,128)S(1)}, f32[6,160,64]{2,1,0:T(8,128)S(1)}, u32[]{:S(2)}, u32[]{:S(2)}) collective-permute-start(f32[6,160,64]{2,1,0:T(8,128)S(1)} %get-tuple-element.28), channel_id=1, source_target_pairs={{0,1},{1,2},{2,3},{3,4},{4,5},{5,6},{6,7},{7,8},{8,9},{9,10},{10,1... | collective-permute-start | bytes 737288 | tf_op jit(solution)/shard_map/ppermute | solution.py:72
  75.1 4.9 %fusion = f32[4,64,32,128]{3,1,2,0:T(8,128)S(1)} fusion(f32[4,16,32,128]{3,1,2,0:T(8,128)S(1)} %get-tuple-element.23, f32[4,16,32,128]{3,1,2,0:T(8,128)S(1)} %get-tuple-element.22, f32[4,16,32,128]{3,1,2,0:T(8,128)S(1)} %get-tuple-element.21, f32[4,16,32,128]{3,1,2,0:T(8,128)S(1)} %get-tuple-element.20, f32[4,64,32,128]{3,2,1,0:T(8,128)S(1)} %copy-done.1, ...), kind=kLoop, calls=%fused_computation.2 | loop fusion | flops 6291456 | bytes 14680064 | tf_op jit(solution)/shard_map/add | solution.py:50
  80.1 2.0 %copy-done.2 = f32[4,64,32,128]{3,1,2,0:T(8,128)} copy-done((f32[4,64,32,128]{3,1,2,0:T(8,128)}, f32[4,64,32,128]{3,1,2,0:T(8,128)S(1)}, u32[]{:S(2)}) %copy-start.2) | copy-done | bytes 4194328
  83.0 1.0 %fusion.16 = (f32[3,160,256]{2,1,0:T(8,128)}, f32[3,160,256]{2,1,0:T(8,128)}) fusion(f32[6,160,256]{2,1,0:T(8,128)S(1)} %pad_maximum_fusion.1), kind=kLoop, calls=%fused_computation.57 | loop fusion | bytes 1966080 | tf_op jit(solution)/shard_map/slice | solution.py:349
  84.0 9.5 %shard_map.87 = (f32[32,128]{1,0:T(8,128)}, f32[2,32,128]{2,1,0:T(8,128)}) custom-call(f32[3,160,256]{2,1,0:T(8,128)} %get-tuple-element.27.moving_ref, f32[3,160,256]{2,1,0:T(8,128)} %get-tuple-element.26.fixed_ref, f32[1,256]{1,0:T(1,128)} %multiply_add_fusion.1.coriolis_ref), custom_call_target="tpu_custom_call" | custom-call | flops 39321600 | bytes 1146880 | tf_op jit(solution)/shard_map/pallas_call | solution.py:306
  93.6 0.8 divide_subtract_fusion
  94.3 2.9 %fusion.15 = (f32[2,64,32,128]{3,1,2,0:T(8,128)S(1)}, f32[2,64,32,128]{3,1,2,0:T(8,128)S(1)}) fusion(f32[4,64,32,128]{3,1,2,0:T(8,128)} %copy-done.2, f32[2,32,128]{2,1,0:T(8,128)S(1)} %divide_subtract_fusion, f32[64,32,128]{2,0,1:T(8,128)S(1)} %fusion.12), kind=kLoop, calls=%fused_computation.56 | loop fusion | flops 1048576 | bytes 9469952 | tf_op jit(solution)/shard_map/slice | solution.py:59
  97.8 4.4 %copy.12 = f32[4,64,32,128]{3,2,1,0:T(8,128)} copy(f32[4,64,32,128]{3,1,2,0:T(8,128)S(1)} %pad_maximum_fusion) | data formatting | bytes 8388608
  (49 shorter events, 5.2 us)
Async XLA Ops:
  0.6 21.1 %copy-start = (f32[4,64,64]{2,1,0:T(8,128)S(1)}, f32[4,64,64]{2,1,0:T(8,128)}, u32[]{:S(2)}) copy-start(f32[4,64,64]{2,1,0:T(8,128)} %param.8) | copy-start | bytes 196612
  0.6 19.9 %copy-start.9 = (s32[160]{0:T(256)S(1)}, s32[160]{0:T(256)}, u32[]{:S(2)}) copy-start(s32[160]{0:T(256)} %constant.93) | copy-start | bytes 1924
  0.7 19.6 %copy-start.3 = (s32[32,128]{1,0:T(8,128)S(1)}, s32[32,128]{1,0:T(8,128)}, u32[]{:S(2)}) copy-start(s32[32,128]{1,0:T(8,128)} %depth_ref.3) | copy-start | bytes 49156
  0.7 20.5 %copy-start.7 = (f32[2,32,128]{2,1,0:T(8,128)S(1)}, f32[2,32,128]{2,1,0:T(8,128)}, u32[]{:S(2)}) copy-start(f32[2,32,128]{2,1,0:T(8,128)} %param.10) | copy-start | bytes 98308
  0.7 20.5 %copy-start.8 = (f32[32,128]{1,0:T(8,128)S(1)}, f32[32,128]{1,0:T(8,128)}, u32[]{:S(2)}) copy-start(f32[32,128]{1,0:T(8,128)} %param.9) | copy-start | bytes 49156
  5.6 16.8 %collective-permute-start.2 = (f32[4,2,32,128]{3,2,1,0:T(8,128)}, f32[4,2,32,128]{3,2,1,0:T(8,128)S(1)}, u32[]{:S(2)}, u32[]{:S(2)}) collective-permute-start(f32[4,2,32,128]{3,2,1,0:T(8,128)} %get-tuple-element.12), channel_id=1, source_target_pairs={{0,1},{1,2},{2,3},{3,4},{4,5},{5,6},{6,7},{7,8},{8,9},{9,10},{10,1... | collective-permute-start | bytes 393224 | tf_op jit(solution)/shard_map/ppermute | solution.py:335
  10.9 11.5 %collective-permute-start.3 = (f32[4,2,32,128]{3,2,1,0:T(8,128)}, f32[4,2,32,128]{3,2,1,0:T(8,128)S(1)}, u32[]{:S(2)}, u32[]{:S(2)}) collective-permute-start(f32[4,2,32,128]{3,2,1,0:T(8,128)} %get-tuple-element.12), channel_id=1, source_target_pairs={{1,0},{2,1},{3,2},{4,3},{5,4},{6,5},{7,6},{8,7},{9,8},{10,9},{11,1... | collective-permute-start | bytes 393224 | tf_op jit(solution)/shard_map/ppermute | solution.py:336
  12.8 11.7 %collective-permute-start = (f32[4,64,2,128]{3,2,1,0:T(2,128)}, f32[4,64,2,128]{3,2,1,0:T(2,128)S(1)}, u32[]{:S(2)}, u32[]{:S(2)}) collective-permute-start(f32[4,64,2,128]{3,2,1,0:T(2,128)} %get-tuple-element.10), channel_id=1, source_target_pairs={{0,16},{16,32},{32,48},{48,64},{64,80},{80,96},{96,112},{112,128},... | collective-permute-start | bytes 786440 | tf_op jit(solution)/shard_map/ppermute | solution.py:332
  16.1 10.4 %collective-permute-start.1 = (f32[4,64,2,128]{3,2,1,0:T(2,128)}, f32[4,64,2,128]{3,2,1,0:T(2,128)S(1)}, u32[]{:S(2)}, u32[]{:S(2)}) collective-permute-start(f32[4,64,2,128]{3,2,1,0:T(2,128)} %get-tuple-element.11), channel_id=1, source_target_pairs={{16,0},{32,16},{48,32},{64,48},{80,64},{96,80},{112,96},{128,112},... | collective-permute-start | bytes 786440 | tf_op jit(solution)/shard_map/ppermute | solution.py:333
  24.6 1.9 %copy-start.4 = (f32[4,64,2,128]{3,2,1,0:T(2,128)}, f32[4,64,2,128]{3,2,1,0:T(2,128)S(1)}, u32[]{:S(2)}) copy-start(f32[4,64,2,128]{3,2,1,0:T(2,128)S(1)} %collective-permute-done.west_ref) | copy-start | bytes 786436
  26.4 0.7 copy-start.5
  44.4 23.5 %collective-permute-start.4 = (f32[6,32,128]{2,1,0:T(8,128)S(1)}, f32[6,32,128]{2,1,0:T(8,128)S(1)}, u32[]{:S(2)}, u32[]{:S(2)}) collective-permute-start(f32[6,32,128]{2,1,0:T(8,128)S(1)} %pad_maximum_fusion.2), channel_id=1, source_target_pairs={{0,32},{16,48},{32,64},{48,80},{64,96},{80,112},{96,128},{112,144}... | collective-permute-start | bytes 294920 | tf_op jit(solution)/shard_map/ppermute | solution.py:72
  48.5 19.4 %collective-permute-start.5 = (f32[6,32,128]{2,1,0:T(8,128)S(1)}, f32[6,32,128]{2,1,0:T(8,128)S(1)}, u32[]{:S(2)}, u32[]{:S(2)}) collective-permute-start(f32[6,32,128]{2,1,0:T(8,128)S(1)} %pad_maximum_fusion.2), channel_id=1, source_target_pairs={{0,16},{16,32},{32,48},{48,64},{64,80},{80,96},{96,112},{112,128},... | collective-permute-start | bytes 294920 | tf_op jit(solution)/shard_map/ppermute | solution.py:72
  50.4 17.5 %collective-permute-start.6 = (f32[6,32,128]{2,1,0:T(8,128)S(1)}, f32[6,32,128]{2,1,0:T(8,128)S(1)}, u32[]{:S(2)}, u32[]{:S(2)}) collective-permute-start(f32[6,32,128]{2,1,0:T(8,128)S(1)} %pad_maximum_fusion.2), channel_id=1, source_target_pairs={{16,0},{32,16},{48,32},{64,48},{80,64},{96,80},{112,96},{128,112},... | collective-permute-start | bytes 294920 | tf_op jit(solution)/shard_map/ppermute | solution.py:73
  55.9 12.1 %collective-permute-start.7 = (f32[6,32,128]{2,1,0:T(8,128)S(1)}, f32[6,32,128]{2,1,0:T(8,128)S(1)}, u32[]{:S(2)}, u32[]{:S(2)}) collective-permute-start(f32[6,32,128]{2,1,0:T(8,128)S(1)} %pad_maximum_fusion.2), channel_id=1, source_target_pairs={{32,0},{48,16},{64,32},{80,48},{96,64},{112,80},{128,96},{144,112}... | collective-permute-start | bytes 294920 | tf_op jit(solution)/shard_map/ppermute | solution.py:73
  67.0 0.9 copy-start.6
  67.0 8.1 %copy-start.1 = (f32[4,64,32,128]{3,2,1,0:T(8,128)S(1)}, f32[4,64,32,128]{3,2,1,0:T(8,128)}, u32[]{:S(2)}) copy-start(f32[4,64,32,128]{3,2,1,0:T(8,128)} %state_ref.3) | copy-start | bytes 12582916
  68.2 14.4 %collective-permute-start.9 = (f32[6,160,64]{2,1,0:T(8,128)S(1)}, f32[6,160,64]{2,1,0:T(8,128)S(1)}, u32[]{:S(2)}, u32[]{:S(2)}) collective-permute-start(f32[6,160,64]{2,1,0:T(8,128)S(1)} %get-tuple-element.29), channel_id=1, source_target_pairs={{1,0},{2,1},{3,2},{4,3},{5,4},{6,5},{7,6},{8,7},{9,8},{10,9},{11,1... | collective-permute-start | bytes 737288 | tf_op jit(solution)/shard_map/ppermute | solution.py:73
  71.4 11.1 %collective-permute-start.8 = (f32[6,160,64]{2,1,0:T(8,128)S(1)}, f32[6,160,64]{2,1,0:T(8,128)S(1)}, u32[]{:S(2)}, u32[]{:S(2)}) collective-permute-start(f32[6,160,64]{2,1,0:T(8,128)S(1)} %get-tuple-element.28), channel_id=1, source_target_pairs={{0,1},{1,2},{2,3},{3,4},{4,5},{5,6},{6,7},{7,8},{8,9},{9,10},{10,1... | collective-permute-start | bytes 737288 | tf_op jit(solution)/shard_map/ppermute | solution.py:72
  80.0 2.0 %copy-start.2 = (f32[4,64,32,128]{3,1,2,0:T(8,128)}, f32[4,64,32,128]{3,1,2,0:T(8,128)S(1)}, u32[]{:S(2)}) copy-start(f32[4,64,32,128]{3,1,2,0:T(8,128)S(1)} %fusion) | copy-start | bytes 12582916

commit v15 on v14

--- a/solution.py
+++ b/solution.py
@@ -157,7 +157,7 @@
     def _():
         forcing_ref[...] = jnp.zeros_like(forcing_ref)
 
-    lax.fori_loop(0, depth_levels, level, 0, unroll=4)
+    lax.fori_loop(0, depth_levels, level, 0, unroll=True)
 
     @pl.when(chunk == pl.num_programs(0) - 1)
     def _():

time: 103 us -> 102 us (level)
  no operation moved by 1% of the time
where the time goes in v15:
time: 102 us
  starting transfers between devices  35.6 us (35%)
  Pallas kernels  30.6 us (30%)
  other arithmetic  13.6 us (13%)
  local copies, waits for them, and re-layouts  9.14 us (9%)
  matrix products  8.64 us (8%)
  waiting for transfers between devices  3.32 us (3%)
  between operations  1.04 us (1%)
    pallas_call x1, Pallas kernels, stencil(): pl.pallas_call(stencil_kernel, grid=(steps,), out_shape=(jax.ShapeDtypeSt...  16.1 us
    ppermute x3, starting transfers between devices, wide_halo(): lax.ppermute(head, axis, [(i + hop, i) for i in range(count - hop)])  11.2 us
    ppermute x3, starting transfers between devices, wide_halo(): lax.ppermute(tail, axis, [(i, i + hop) for i in range(count - hop)])  9.8 us
    pallas_call x1, Pallas kernels, local_waves(): pl.pallas_call(wave_kernel, out_shape=(jax.ShapeDtypeStruct((inner_rows,...  9.52 us
    dot_general x1, matrix products, vertical_solve(): jnp.einsum('kl,flxy->fkxy', stacked, provisional, precision=lax.Precision...  8.64 us
    unnamed x24, local copies, waits for them, and re-layouts  7.22 us
    ppermute x1, starting transfers between devices, body(): lax.ppermute(edges, ('gy', 'mode'), [(i, i + 1) for i in range(y_count -...  5.3 us
    pallas_call x1, Pallas kernels, pack_edges(): pl.pallas_call(pack_kernel, grid=(levels // PACK,), out_shape=(jax.ShapeD...  4.92 us
  transfers between devices with their start and end apart: 10, of which 2 were waited for; matrix products, arithmetic and copies ran while one was open for 17% of the time, Pallas kernels for 0%

profile of v15, /device:TPU:103, one launch (start us, length us, event | category | flops | bytes accessed | tf_op | source)
XLA Modules:
  0.0 101.9 jit_solution(11693203982267757711)
XLA Ops:
  0.7 4.9 %shard_map.85 = (f32[4,2,32,128]{3,2,1,0:T(8,128)}, f32[4,64,2,128]{3,2,1,0:T(2,128)}, f32[4,64,2,128]{3,2,1,0:T(2,128)}) custom-call(s32[32,128]{1,0:T(8,128)} %depth_ref.3, f32[4,64,32,128]{3,2,1,0:T(8,128)} %state_ref.3), custom_call_target="tpu_custom_call" | custom-call | flops 4194304 | bytes 4194304 | tf_op jit(solution)/shard_map/pallas_call | solution.py:215
  5.6 5.3 %collective-permute-start.2 = (f32[4,2,32,128]{3,2,1,0:T(8,128)}, f32[4,2,32,128]{3,2,1,0:T(8,128)S(1)}, u32[]{:S(2)}, u32[]{:S(2)}) collective-permute-start(f32[4,2,32,128]{3,2,1,0:T(8,128)} %get-tuple-element.12), channel_id=1, source_target_pairs={{0,1},{1,2},{2,3},{3,4},{4,5},{5,6},{6,7},{7,8},{8,9},{9,10},{10,1... | collective-permute-start | bytes 393224 | tf_op jit(solution)/shard_map/ppermute | solution.py:335
  10.9 1.9 %collective-permute-start.3 = (f32[4,2,32,128]{3,2,1,0:T(8,128)}, f32[4,2,32,128]{3,2,1,0:T(8,128)S(1)}, u32[]{:S(2)}, u32[]{:S(2)}) collective-permute-start(f32[4,2,32,128]{3,2,1,0:T(8,128)} %get-tuple-element.12), channel_id=1, source_target_pairs={{1,0},{2,1},{3,2},{4,3},{5,4},{6,5},{7,6},{8,7},{9,8},{10,9},{11,1... | collective-permute-start | bytes 393224 | tf_op jit(solution)/shard_map/ppermute | solution.py:336
  12.8 3.2 %collective-permute-start = (f32[4,64,2,128]{3,2,1,0:T(2,128)}, f32[4,64,2,128]{3,2,1,0:T(2,128)S(1)}, u32[]{:S(2)}, u32[]{:S(2)}) collective-permute-start(f32[4,64,2,128]{3,2,1,0:T(2,128)} %get-tuple-element.10), channel_id=1, source_target_pairs={{0,16},{16,32},{32,48},{48,64},{64,80},{80,96},{96,112},{112,128},... | collective-permute-start | bytes 786440 | tf_op jit(solution)/shard_map/ppermute | solution.py:332
  16.1 4.2 %collective-permute-start.1 = (f32[4,64,2,128]{3,2,1,0:T(2,128)}, f32[4,64,2,128]{3,2,1,0:T(2,128)S(1)}, u32[]{:S(2)}, u32[]{:S(2)}) collective-permute-start(f32[4,64,2,128]{3,2,1,0:T(2,128)} %get-tuple-element.11), channel_id=1, source_target_pairs={{16,0},{32,16},{48,32},{64,48},{80,64},{96,80},{112,96},{128,112},... | collective-permute-start | bytes 786440 | tf_op jit(solution)/shard_map/ppermute | solution.py:333
  23.1 1.4 %collective-permute-done.west_ref = f32[4,64,2,128]{3,2,1,0:T(2,128)S(1)} collective-permute-done((f32[4,64,2,128]{3,2,1,0:T(2,128)}, f32[4,64,2,128]{3,2,1,0:T(2,128)S(1)}, u32[]{:S(2)}, u32[]{:S(2)}) %collective-permute-start) | collective-permute-done | bytes 262176 | tf_op jit(solution)/shard_map/ppermute | solution.py:332
  24.6 1.9 %collective-permute-done.1.east_ref = f32[4,64,2,128]{3,2,1,0:T(2,128)S(1)} collective-permute-done((f32[4,64,2,128]{3,2,1,0:T(2,128)}, f32[4,64,2,128]{3,2,1,0:T(2,128)S(1)}, u32[]{:S(2)}, u32[]{:S(2)}) %collective-permute-start.1) | collective-permute-done | bytes 262176 | tf_op jit(solution)/shard_map/ppermute | solution.py:333
  27.1 16.1 %shard_map.86 = (f32[4,64,32,128]{3,2,1,0:T(8,128)}, f32[2,32,128]{2,1,0:T(8,128)}) custom-call(s32[32,128]{1,0:T(8,128)} %depth_ref.3, f32[1,128]{1,0:T(1,128)} %multiply_add_fusion.2.coriolis_ref, f32[4,64,32,128]{3,2,1,0:T(8,128)} %state_ref.3, f32[4,64,2,128]{3,2,1,0:T(2,128)} %copy-done.4, f32[4,64,2,128]{3,2,1,0:T(2,128)} %copy-done.5, ...), custom_call_target="tpu_custom_call" | custom-call | flops 62914560 | bytes 8388608 | tf_op jit(solution)/shard_map/pallas_call | solution.py:174
  43.2 0.8 pad_maximum_fusion.2
  44.0 4.1 %collective-permute-start.4 = (f32[6,32,128]{2,1,0:T(8,128)S(1)}, f32[6,32,128]{2,1,0:T(8,128)S(1)}, u32[]{:S(2)}, u32[]{:S(2)}) collective-permute-start(f32[6,32,128]{2,1,0:T(8,128)S(1)} %pad_maximum_fusion.2), channel_id=1, source_target_pairs={{0,32},{16,48},{32,64},{48,80},{64,96},{80,112},{96,128},{112,144}... | collective-permute-start | bytes 294920 | tf_op jit(solution)/shard_map/ppermute | solution.py:72
  48.1 1.9 %collective-permute-start.5 = (f32[6,32,128]{2,1,0:T(8,128)S(1)}, f32[6,32,128]{2,1,0:T(8,128)S(1)}, u32[]{:S(2)}, u32[]{:S(2)}) collective-permute-start(f32[6,32,128]{2,1,0:T(8,128)S(1)} %pad_maximum_fusion.2), channel_id=1, source_target_pairs={{0,16},{16,32},{32,48},{48,64},{64,80},{80,96},{96,112},{112,128},... | collective-permute-start | bytes 294920 | tf_op jit(solution)/shard_map/ppermute | solution.py:72
  50.0 5.5 %collective-permute-start.6 = (f32[6,32,128]{2,1,0:T(8,128)S(1)}, f32[6,32,128]{2,1,0:T(8,128)S(1)}, u32[]{:S(2)}, u32[]{:S(2)}) collective-permute-start(f32[6,32,128]{2,1,0:T(8,128)S(1)} %pad_maximum_fusion.2), channel_id=1, source_target_pairs={{16,0},{32,16},{48,32},{64,48},{80,64},{96,80},{112,96},{128,112},... | collective-permute-start | bytes 294920 | tf_op jit(solution)/shard_map/ppermute | solution.py:73
  55.5 2.5 %collective-permute-start.7 = (f32[6,32,128]{2,1,0:T(8,128)S(1)}, f32[6,32,128]{2,1,0:T(8,128)S(1)}, u32[]{:S(2)}, u32[]{:S(2)}) collective-permute-start(f32[6,32,128]{2,1,0:T(8,128)S(1)} %pad_maximum_fusion.2), channel_id=1, source_target_pairs={{32,0},{48,16},{64,32},{80,48},{96,64},{112,80},{128,96},{144,112}... | collective-permute-start | bytes 294920 | tf_op jit(solution)/shard_map/ppermute | solution.py:73
  58.0 8.6 %fusion.3 = f32[4,160,32,128]{3,1,2,0:T(8,128)S(1)} fusion(f32[4,64,32,128]{3,2,1,0:T(8,128)} %get-tuple-element.13, f32[160,64]{1,0:T(8,128)S(1)} %gather_fusion), kind=kOutput, calls=%fused_computation.7 | convolution fusion | flops 1006632960 | bytes 14721024 | tf_op jit(solution)/shard_map/kl,flxy->fkxy/dot_general | solution.py:39
  66.6 0.8 fusion.9
  67.8 3.3 %collective-permute-start.9 = (f32[6,160,64]{2,1,0:T(8,128)S(1)}, f32[6,160,64]{2,1,0:T(8,128)S(1)}, u32[]{:S(2)}, u32[]{:S(2)}) collective-permute-start(f32[6,160,64]{2,1,0:T(8,128)S(1)} %get-tuple-element.29), channel_id=1, source_target_pairs={{1,0},{2,1},{3,2},{4,3},{5,4},{6,5},{7,6},{8,7},{9,8},{10,9},{11,1... | collective-permute-start | bytes 737288 | tf_op jit(solution)/shard_map/ppermute | solution.py:73
  71.1 3.8 %collective-permute-start.8 = (f32[6,160,64]{2,1,0:T(8,128)S(1)}, f32[6,160,64]{2,1,0:T(8,128)S(1)}, u32[]{:S(2)}, u32[]{:S(2)}) collective-permute-start(f32[6,160,64]{2,1,0:T(8,128)S(1)} %get-tuple-element.28), channel_id=1, source_target_pairs={{0,1},{1,2},{2,3},{3,4},{4,5},{5,6},{6,7},{7,8},{8,9},{9,10},{10,1... | collective-permute-start | bytes 737288 | tf_op jit(solution)/shard_map/ppermute | solution.py:72
  74.9 4.7 %fusion = f32[4,64,32,128]{3,1,2,0:T(8,128)S(1)} fusion(f32[4,16,32,128]{3,1,2,0:T(8,128)S(1)} %get-tuple-element.23, f32[4,16,32,128]{3,1,2,0:T(8,128)S(1)} %get-tuple-element.22, f32[4,16,32,128]{3,1,2,0:T(8,128)S(1)} %get-tuple-element.21, f32[4,16,32,128]{3,1,2,0:T(8,128)S(1)} %get-tuple-element.20, f32[4,64,32,128]{3,2,1,0:T(8,128)S(1)} %copy-done.1, ...), kind=kLoop, calls=%fused_computation.2 | loop fusion | flops 6291456 | bytes 14680064 | tf_op jit(solution)/shard_map/add | solution.py:50
  79.7 2.0 %copy-done.2 = f32[4,64,32,128]{3,1,2,0:T(8,128)} copy-done((f32[4,64,32,128]{3,1,2,0:T(8,128)}, f32[4,64,32,128]{3,1,2,0:T(8,128)S(1)}, u32[]{:S(2)}) %copy-start.2) | copy-done | bytes 4194328
  82.6 1.0 %fusion.16 = (f32[3,160,256]{2,1,0:T(8,128)}, f32[3,160,256]{2,1,0:T(8,128)}) fusion(f32[6,160,256]{2,1,0:T(8,128)S(1)} %pad_maximum_fusion.1), kind=kLoop, calls=%fused_computation.57 | loop fusion | bytes 1966080 | tf_op jit(solution)/shard_map/slice | solution.py:349
  83.6 9.5 %shard_map.87 = (f32[32,128]{1,0:T(8,128)}, f32[2,32,128]{2,1,0:T(8,128)}) custom-call(f32[3,160,256]{2,1,0:T(8,128)} %get-tuple-element.27.moving_ref, f32[3,160,256]{2,1,0:T(8,128)} %get-tuple-element.26.fixed_ref, f32[1,256]{1,0:T(1,128)} %multiply_add_fusion.1.coriolis_ref), custom_call_target="tpu_custom_call" | custom-call | flops 39321600 | bytes 1146880 | tf_op jit(solution)/shard_map/pallas_call | solution.py:306
  93.2 0.8 divide_subtract_fusion
  93.9 2.9 %fusion.15 = (f32[2,64,32,128]{3,1,2,0:T(8,128)S(1)}, f32[2,64,32,128]{3,1,2,0:T(8,128)S(1)}) fusion(f32[4,64,32,128]{3,1,2,0:T(8,128)} %copy-done.2, f32[2,32,128]{2,1,0:T(8,128)S(1)} %divide_subtract_fusion, f32[64,32,128]{2,0,1:T(8,128)S(1)} %fusion.12), kind=kLoop, calls=%fused_computation.56 | loop fusion | flops 1048576 | bytes 9469952 | tf_op jit(solution)/shard_map/slice | solution.py:59
  97.4 4.4 %copy.12 = f32[4,64,32,128]{3,2,1,0:T(8,128)} copy(f32[4,64,32,128]{3,1,2,0:T(8,128)S(1)} %pad_maximum_fusion) | data formatting | bytes 8388608
  (49 shorter events, 5.2 us)
Async XLA Ops:
  0.6 21.1 %copy-start = (f32[4,64,64]{2,1,0:T(8,128)S(1)}, f32[4,64,64]{2,1,0:T(8,128)}, u32[]{:S(2)}) copy-start(f32[4,64,64]{2,1,0:T(8,128)} %param.8) | copy-start | bytes 196612
  0.6 19.9 %copy-start.9 = (s32[160]{0:T(256)S(1)}, s32[160]{0:T(256)}, u32[]{:S(2)}) copy-start(s32[160]{0:T(256)} %constant.93) | copy-start | bytes 1924
  0.7 19.6 %copy-start.3 = (s32[32,128]{1,0:T(8,128)S(1)}, s32[32,128]{1,0:T(8,128)}, u32[]{:S(2)}) copy-start(s32[32,128]{1,0:T(8,128)} %depth_ref.3) | copy-start | bytes 49156
  0.7 20.5 %copy-start.7 = (f32[2,32,128]{2,1,0:T(8,128)S(1)}, f32[2,32,128]{2,1,0:T(8,128)}, u32[]{:S(2)}) copy-start(f32[2,32,128]{2,1,0:T(8,128)} %param.10) | copy-start | bytes 98308
  0.7 20.5 %copy-start.8 = (f32[32,128]{1,0:T(8,128)S(1)}, f32[32,128]{1,0:T(8,128)}, u32[]{:S(2)}) copy-start(f32[32,128]{1,0:T(8,128)} %param.9) | copy-start | bytes 49156
  5.6 16.8 %collective-permute-start.2 = (f32[4,2,32,128]{3,2,1,0:T(8,128)}, f32[4,2,32,128]{3,2,1,0:T(8,128)S(1)}, u32[]{:S(2)}, u32[]{:S(2)}) collective-permute-start(f32[4,2,32,128]{3,2,1,0:T(8,128)} %get-tuple-element.12), channel_id=1, source_target_pairs={{0,1},{1,2},{2,3},{3,4},{4,5},{5,6},{6,7},{7,8},{8,9},{9,10},{10,1... | collective-permute-start | bytes 393224 | tf_op jit(solution)/shard_map/ppermute | solution.py:335
  10.9 11.5 %collective-permute-start.3 = (f32[4,2,32,128]{3,2,1,0:T(8,128)}, f32[4,2,32,128]{3,2,1,0:T(8,128)S(1)}, u32[]{:S(2)}, u32[]{:S(2)}) collective-permute-start(f32[4,2,32,128]{3,2,1,0:T(8,128)} %get-tuple-element.12), channel_id=1, source_target_pairs={{1,0},{2,1},{3,2},{4,3},{5,4},{6,5},{7,6},{8,7},{9,8},{10,9},{11,1... | collective-permute-start | bytes 393224 | tf_op jit(solution)/shard_map/ppermute | solution.py:336
  12.8 11.7 %collective-permute-start = (f32[4,64,2,128]{3,2,1,0:T(2,128)}, f32[4,64,2,128]{3,2,1,0:T(2,128)S(1)}, u32[]{:S(2)}, u32[]{:S(2)}) collective-permute-start(f32[4,64,2,128]{3,2,1,0:T(2,128)} %get-tuple-element.10), channel_id=1, source_target_pairs={{0,16},{16,32},{32,48},{48,64},{64,80},{80,96},{96,112},{112,128},... | collective-permute-start | bytes 786440 | tf_op jit(solution)/shard_map/ppermute | solution.py:332
  16.1 10.4 %collective-permute-start.1 = (f32[4,64,2,128]{3,2,1,0:T(2,128)}, f32[4,64,2,128]{3,2,1,0:T(2,128)S(1)}, u32[]{:S(2)}, u32[]{:S(2)}) collective-permute-start(f32[4,64,2,128]{3,2,1,0:T(2,128)} %get-tuple-element.11), channel_id=1, source_target_pairs={{16,0},{32,16},{48,32},{64,48},{80,64},{96,80},{112,96},{128,112},... | collective-permute-start | bytes 786440 | tf_op jit(solution)/shard_map/ppermute | solution.py:333
  24.6 1.9 %copy-start.4 = (f32[4,64,2,128]{3,2,1,0:T(2,128)}, f32[4,64,2,128]{3,2,1,0:T(2,128)S(1)}, u32[]{:S(2)}) copy-start(f32[4,64,2,128]{3,2,1,0:T(2,128)S(1)} %collective-permute-done.west_ref) | copy-start | bytes 786436
  26.4 0.7 copy-start.5
  44.0 23.4 %collective-permute-start.4 = (f32[6,32,128]{2,1,0:T(8,128)S(1)}, f32[6,32,128]{2,1,0:T(8,128)S(1)}, u32[]{:S(2)}, u32[]{:S(2)}) collective-permute-start(f32[6,32,128]{2,1,0:T(8,128)S(1)} %pad_maximum_fusion.2), channel_id=1, source_target_pairs={{0,32},{16,48},{32,64},{48,80},{64,96},{80,112},{96,128},{112,144}... | collective-permute-start | bytes 294920 | tf_op jit(solution)/shard_map/ppermute | solution.py:72
  48.1 19.4 %collective-permute-start.5 = (f32[6,32,128]{2,1,0:T(8,128)S(1)}, f32[6,32,128]{2,1,0:T(8,128)S(1)}, u32[]{:S(2)}, u32[]{:S(2)}) collective-permute-start(f32[6,32,128]{2,1,0:T(8,128)S(1)} %pad_maximum_fusion.2), channel_id=1, source_target_pairs={{0,16},{16,32},{32,48},{48,64},{64,80},{80,96},{96,112},{112,128},... | collective-permute-start | bytes 294920 | tf_op jit(solution)/shard_map/ppermute | solution.py:72
  50.0 17.5 %collective-permute-start.6 = (f32[6,32,128]{2,1,0:T(8,128)S(1)}, f32[6,32,128]{2,1,0:T(8,128)S(1)}, u32[]{:S(2)}, u32[]{:S(2)}) collective-permute-start(f32[6,32,128]{2,1,0:T(8,128)S(1)} %pad_maximum_fusion.2), channel_id=1, source_target_pairs={{16,0},{32,16},{48,32},{64,48},{80,64},{96,80},{112,96},{128,112},... | collective-permute-start | bytes 294920 | tf_op jit(solution)/shard_map/ppermute | solution.py:73
  55.5 12.1 %collective-permute-start.7 = (f32[6,32,128]{2,1,0:T(8,128)S(1)}, f32[6,32,128]{2,1,0:T(8,128)S(1)}, u32[]{:S(2)}, u32[]{:S(2)}) collective-permute-start(f32[6,32,128]{2,1,0:T(8,128)S(1)} %pad_maximum_fusion.2), channel_id=1, source_target_pairs={{32,0},{48,16},{64,32},{80,48},{96,64},{112,80},{128,96},{144,112}... | collective-permute-start | bytes 294920 | tf_op jit(solution)/shard_map/ppermute | solution.py:73
  66.6 0.9 copy-start.6
  66.6 8.2 %copy-start.1 = (f32[4,64,32,128]{3,2,1,0:T(8,128)S(1)}, f32[4,64,32,128]{3,2,1,0:T(8,128)}, u32[]{:S(2)}) copy-start(f32[4,64,32,128]{3,2,1,0:T(8,128)} %state_ref.3) | copy-start | bytes 12582916
  67.8 14.4 %collective-permute-start.9 = (f32[6,160,64]{2,1,0:T(8,128)S(1)}, f32[6,160,64]{2,1,0:T(8,128)S(1)}, u32[]{:S(2)}, u32[]{:S(2)}) collective-permute-start(f32[6,160,64]{2,1,0:T(8,128)S(1)} %get-tuple-element.29), channel_id=1, source_target_pairs={{1,0},{2,1},{3,2},{4,3},{5,4},{6,5},{7,6},{8,7},{9,8},{10,9},{11,1... | collective-permute-start | bytes 737288 | tf_op jit(solution)/shard_map/ppermute | solution.py:73
  71.1 11.1 %collective-permute-start.8 = (f32[6,160,64]{2,1,0:T(8,128)S(1)}, f32[6,160,64]{2,1,0:T(8,128)S(1)}, u32[]{:S(2)}, u32[]{:S(2)}) collective-permute-start(f32[6,160,64]{2,1,0:T(8,128)S(1)} %get-tuple-element.28), channel_id=1, source_target_pairs={{0,1},{1,2},{2,3},{3,4},{4,5},{5,6},{6,7},{7,8},{8,9},{9,10},{10,1... | collective-permute-start | bytes 737288 | tf_op jit(solution)/shard_map/ppermute | solution.py:72
  79.6 2.0 %copy-start.2 = (f32[4,64,32,128]{3,1,2,0:T(8,128)}, f32[4,64,32,128]{3,1,2,0:T(8,128)S(1)}, u32[]{:S(2)}) copy-start(f32[4,64,32,128]{3,1,2,0:T(8,128)S(1)} %fusion) | copy-start | bytes 12582916
